TPU v7x, 512 devices: a whole 4x8x8 slice. The times are simulated.
512 devices in a mesh: space: 64 (over z_hi, y, core), member: 8 (over z_lo, x).
Axes of the slice: x: 4, y: 8, z: 8 (z_hi: 4, z_lo: 2; z = z_hi * 2 + z_lo), core: 2. Of those that a mesh axis runs over, the one named last changes fastest.
Arguments:
- pressure: float32 [32, 10, 131072], P('member', None, 'space'), may hold values from -6 to 6
- heat: float32 [32, 10, 131072], P('member', None, 'space'), may hold values from -6 to 6
- log_cond: float32 [10, 131072], P(None, 'space'), may hold values from -1 to 1
- log_therm: float32 [10, 131072], P(None, 'space'), may hold values from -1 to 1
- frozen: float32 [10, 131072], P(None, 'space'), may hold values from 0 to 1
- frozen_flag: int32 [10, 131072], P(None, 'space'), may hold values 0 or 1
- recharge: float32 [32, 131072], P('member', 'space'), may hold values from -6 to 6
- face_cols: int32 [4, 16384], P(None, 'space'), may hold values from 0 to 2047
- face_weight: float32 [4, 16384], P(None, 'space'), may hold values from 0.05 to 0.3
- cot_pressure: float32 [32, 10, 131072], P('member', None, 'space'), may hold values from -6 to 6
- cot_heat: float32 [32, 10, 131072], P('member', None, 'space'), may hold values from -6 to 6
Outputs:
- new_pressure: float32 [32, 10, 131072], P('member', None, 'space')
- new_heat: float32 [32, 10, 131072], P('member', None, 'space')
- adj_pressure: float32 [32, 10, 131072], P('member', None, 'space')
- adj_heat: float32 [32, 10, 131072], P('member', None, 'space')
- param_grads: float32 [2, 10, 131072], P(None, None, ('space', 'member'))
All inputs are finite; a program needn't handle non-finite values. No bound on the sum of `frozen_flag` on one device may be relied on, other than what follows from the above.
Results may differ from a plain program's by a relative error of at most 0.00007.
Values sent between devices are 32-bit elements; how exact they have to be, the bound alone decides.
No kernel may reach another device: no remote copies, remote signals or barrier semaphores. Data moves between devices by JAX's collectives and lax.ppermute only.
A program may use at most 64 MiB of HBM per device.

v0:
```python
import jax
import jax.numpy as jnp
from jax import lax
from jax.sharding import PartitionSpec as P


def from_partner(value, axis, stride):
    mask = 2**stride
    pairs = [(source, source ^ mask) for source in range(lax.axis_size(axis))]
    return lax.ppermute(value, axis, pairs)


def spread(grad_iface):
    return jnp.pad(grad_iface, ((0, 0), (0, 1), (0, 0))) - jnp.pad(
        grad_iface, ((0, 0), (1, 0), (0, 0))
    )


def selector(columns, width):
    return (columns[:, None] == jnp.arange(width, dtype=jnp.int32)[None, :]).astype(jnp.float32)


def pick(values, select):
    return jnp.einsum("...c,kc->...k", values, select, precision=lax.Precision.HIGHEST)


def place(values, select):
    return jnp.einsum("...k,kc->...c", values, select, precision=lax.Precision.HIGHEST)


def body(
    pressure,
    heat,
    log_cond,
    log_therm,
    frozen,
    frozen_flag,
    recharge,
    face_cols,
    face_weight,
    cot_pressure,
    cot_heat,
):
    rounds = face_cols.shape[0]
    width = pressure.shape[2]
    blocked = frozen * frozen_flag.astype(jnp.float32)
    selects = [selector(face_cols[index], width) for index in range(rounds)]

    def advance(p_old, t_old, log_k, log_t, far_faces):
        cond = jnp.exp(log_k - 3.0 * blocked)
        therm = jnp.exp(log_t) * (1.0 + blocked)
        flow = 0.5 * (cond[:-1] + cond[1:]) * (p_old[:, 1:] - p_old[:, :-1])
        conduct = 0.5 * (therm[:-1] + therm[1:]) * (t_old[:, 1:] - t_old[:, :-1])
        carried = flow * 0.5 * (t_old[:, :-1] + t_old[:, 1:])
        p_rate = spread(flow)
        p_rate = p_rate.at[:, 0].add(recharge)
        t_rate = spread(conduct) + 0.5 * spread(carried)
        fields = jnp.stack([p_old, t_old])
        coeffs = jnp.stack([cond, therm])
        for index in range(rounds):
            select = selects[index]
            weight = face_weight[index]
            own = pick(fields, select)
            coef = pick(coeffs, select)
            update = weight * coef[:, None] * (far_faces[index] - own)
            added = place(update, select)
            p_rate = p_rate + added[0]
            t_rate = t_rate + added[1]
        return (p_old + 0.1 * p_rate, t_old + 0.1 * t_rate)

    fields_in = jnp.stack([pressure, heat])
    remotes = []
    for index in range(rounds):
        sending = pick(fields_in, selects[index])
        remotes.append(from_partner(sending, "space", index))
    remotes = jnp.stack(remotes)
    (new_pressure, new_heat), pullback = jax.vjp(
        advance, pressure, heat, log_cond, log_therm, remotes
    )
    adj_pressure, adj_heat, grad_k, grad_t, grad_far = pullback((cot_pressure, cot_heat))
    extra = None
    for index in range(rounds):
        coming = from_partner(grad_far[index], "space", index)
        term = place(coming, selects[index])
        extra = term if extra is None else extra + term
    adj_pressure = adj_pressure + extra[0]
    adj_heat = adj_heat + extra[1]
    grads = jnp.stack([grad_k, grad_t])
    summed = lax.psum(grads, "member")
    share = grads.shape[2] // lax.axis_size("member")
    owned = lax.dynamic_slice_in_dim(summed, lax.axis_index("member") * share, share, 2)
    return (new_pressure, new_heat, adj_pressure, adj_heat, owned)


def solution(mesh):
    placed = (
        P("member", None, "space"),
        P("member", None, "space"),
        P(None, "space"),
        P(None, "space"),
        P(None, "space"),
        P(None, "space"),
        P("member", "space"),
        P(None, "space"),
        P(None, "space"),
        P("member", None, "space"),
        P("member", None, "space"),
    )
    return jax.shard_map(
        body,
        mesh=mesh,
        in_specs=placed,
        out_specs=(
            P("member", None, "space"),
            P("member", None, "space"),
            P("member", None, "space"),
            P("member", None, "space"),
            P(None, None, ("space", "member")),
        ),
        check_vma=False,
    )
```

profile of v0, /device:TPU:24, one launch (start us, length us, event | category | flops | bytes accessed | tf_op | source)
XLA Modules:
  0.0 170.9 jit_solution(9766011143822614567)
XLA Ops:
  7.2 0.0 all-reduce.24.cloned.1.call-start
  7.2 0.8 fusion.185
  8.1 1.5 fusion.182
  9.6 2.1 %fusion.26 = f32[2,4,10,256]{3,2,1,0:T(8,128)} fusion(s32[256]{0:T(256)S(1)} %bitcast.222, f32[1,4,10,2048]{3,2,1,0:T(8,128)S(1)} %get-tuple-element.51, f32[1,4,10,2048]{3,2,1,0:T(8,128)S(1)} %get-tuple-element.72), kind=kOutput, calls=%fused_computation.24 | convolution fusion | flops 504004608 | bytes 738304 | tf_op jit(solution)/shard_map/...c,kc->...k/dot_general | solution.py:24
  11.6 2.2 %collective-permute-start.2 = (f32[2,4,10,256]{3,2,1,0:T(8,128)}, f32[2,4,10,256]{3,2,1,0:T(8,128)}, u32[]{:S(2)}, u32[]{:S(2)}) collective-permute-start(f32[2,4,10,256]{3,2,1,0:T(8,128)} %fusion.26), channel_id=1, source_target_pairs={{0,32},{8,40},{16,48},{24,56},{32,0},{40,8},{48,16},{56,24},{64,96... | collective-permute-start | bytes 245768 | tf_op jit(solution)/shard_map/ppermute | solution.py:10
  13.9 2.1 %fusion.12 = f32[2,4,10,256]{3,2,1,0:T(8,128)} fusion(s32[256]{0:T(256)S(1)} %bitcast.229, f32[1,4,10,2048]{3,2,1,0:T(8,128)S(1)} %get-tuple-element.51, f32[1,4,10,2048]{3,2,1,0:T(8,128)S(1)} %get-tuple-element.72), kind=kOutput, calls=%fused_computation.16 | convolution fusion | flops 504004608 | bytes 738304 | tf_op jit(solution)/shard_map/...c,kc->...k/dot_general | solution.py:24
  15.9 6.8 %collective-permute-start.3 = (f32[2,4,10,256]{3,2,1,0:T(8,128)}, f32[2,4,10,256]{3,2,1,0:T(8,128)}, u32[]{:S(2)}, u32[]{:S(2)}) collective-permute-start(f32[2,4,10,256]{3,2,1,0:T(8,128)} %fusion.12), channel_id=1, source_target_pairs={{0,64},{8,72},{16,80},{24,88},{32,96},{40,104},{48,112},{56,120},{... | collective-permute-start | bytes 245768 | tf_op jit(solution)/shard_map/ppermute | solution.py:10
  22.8 2.1 %fusion.41 = f32[2,4,10,256]{3,2,1,0:T(8,128)} fusion(s32[256]{0:T(256)S(1)} %bitcast.215, f32[1,4,10,2048]{3,2,1,0:T(8,128)S(1)} %get-tuple-element.51, f32[1,4,10,2048]{3,2,1,0:T(8,128)S(1)} %get-tuple-element.72), kind=kOutput, calls=%fused_computation.33 | convolution fusion | flops 504004608 | bytes 738304 | tf_op jit(solution)/shard_map/...c,kc->...k/dot_general | solution.py:24
  24.8 3.4 %collective-permute-start.1 = (f32[2,4,10,256]{3,2,1,0:T(8,128)}, f32[2,4,10,256]{3,2,1,0:T(8,128)}, u32[]{:S(2)}, u32[]{:S(2)}) collective-permute-start(f32[2,4,10,256]{3,2,1,0:T(8,128)} %fusion.41), channel_id=1, source_target_pairs={{0,16},{8,24},{16,0},{24,8},{32,48},{40,56},{48,32},{56,40},{64,80... | collective-permute-start | bytes 245768 | tf_op jit(solution)/shard_map/ppermute | solution.py:10
  28.2 0.0 copy-start.7
  28.2 2.1 %fusion.54 = f32[2,4,10,256]{3,2,1,0:T(8,128)} fusion(s32[256]{0:T(256)S(1)} %bitcast.208, f32[1,4,10,2048]{3,2,1,0:T(8,128)S(1)} %get-tuple-element.51, f32[1,4,10,2048]{3,2,1,0:T(8,128)S(1)} %get-tuple-element.72), kind=kOutput, calls=%fused_computation.40 | convolution fusion | flops 504004608 | bytes 738304 | tf_op jit(solution)/shard_map/...c,kc->...k/dot_general | solution.py:24
  30.3 2.1 %collective-permute-start = (f32[2,4,10,256]{3,2,1,0:T(8,128)}, f32[2,4,10,256]{3,2,1,0:T(8,128)}, u32[]{:S(2)}, u32[]{:S(2)}) collective-permute-start(f32[2,4,10,256]{3,2,1,0:T(8,128)} %fusion.54), channel_id=1, source_target_pairs={{0,8},{8,0},{16,24},{24,16},{32,40},{40,32},{48,56},{56,48},{64,72... | collective-permute-start | bytes 245768 | tf_op jit(solution)/shard_map/ppermute | solution.py:10
  32.5 1.3 copy_multiply_fusion.1
  33.8 1.4 fusion.180
  35.3 0.0 copy-start.25
  35.3 2.6 %multiply_reduce_fusion.4 = (f32[2,10,256]{2,1,0:T(8,128)S(1)}, f32[2,4,10,256]{3,2,1,0:T(8,128)S(1)}) fusion(f32[2,4,10,256]{3,2,1,0:T(8,128)} %collective-permute-done.2, f32[2,4,10,256]{3,2,1,0:T(8,128)} %fusion.26, s32[256]{0:T(256)S(1)} %bitcast.223, f32[1,4,10,2048]{3,2,1,0:T(8,128)} %get-tuple-element.74, f32[1,4,10,2048]{3,2,1,0:T(8,128)S(1)} %get-tuple-element.46), kind=kOutput, calls=%fused_computation.160 | convolution fusion | flops 504060928 | bytes 922624 | tf_op jit(solution)/shard_map/transpose(jvp(...k,kc->...c))/dot_general | solution.py:28
  37.9 0.9 fusion.28
  38.8 2.4 %multiply_reduce_fusion.5 = (f32[2,10,256]{2,1,0:T(8,128)S(1)}, f32[2,4,10,256]{3,2,1,0:T(8,128)S(1)}) fusion(f32[2,4,10,256]{3,2,1,0:T(8,128)} %collective-permute-done.3, f32[2,4,10,256]{3,2,1,0:T(8,128)} %fusion.12, s32[256]{0:T(256)S(1)} %bitcast.230, f32[1,4,10,2048]{3,2,1,0:T(8,128)S(1)} %copy-done.11, f32[1,4,10,2048]{3,2,1,0:T(8,128)S(1)} %get-tuple-element.46), kind=kOutput, calls=%fused_computation.161 | convolution fusion | flops 504060928 | bytes 922624 | tf_op jit(solution)/shard_map/transpose(jvp(...k,kc->...c))/dot_general | solution.py:28
  41.2 0.9 convolution_add_fusion.6
  42.2 2.4 %multiply_reduce_fusion.3 = (f32[2,10,256]{2,1,0:T(8,128)S(1)}, f32[2,4,10,256]{3,2,1,0:T(8,128)S(1)}) fusion(f32[2,4,10,256]{3,2,1,0:T(8,128)} %collective-permute-done.1, f32[2,4,10,256]{3,2,1,0:T(8,128)} %fusion.41, s32[256]{0:T(256)S(1)} %bitcast.216, f32[1,4,10,2048]{3,2,1,0:T(8,128)S(1)} %copy-done.11, f32[1,4,10,2048]{3,2,1,0:T(8,128)S(1)} %get-tuple-element.46), kind=kOutput, calls=%fused_computation.159 | convolution fusion | flops 504060928 | bytes 922624 | tf_op jit(solution)/shard_map/transpose(jvp(...k,kc->...c))/dot_general | solution.py:28
  44.5 0.9 convolution_add_fusion.5
  45.5 0.0 copy-start.16
  45.5 2.4 %multiply_reduce_fusion.2 = (f32[2,10,256]{2,1,0:T(8,128)S(1)}, f32[2,4,10,256]{3,2,1,0:T(8,128)S(1)}) fusion(f32[2,4,10,256]{3,2,1,0:T(8,128)} %collective-permute-done, f32[2,4,10,256]{3,2,1,0:T(8,128)} %fusion.54, s32[256]{0:T(256)S(1)} %bitcast.209, f32[1,4,10,2048]{3,2,1,0:T(8,128)S(1)} %copy-done.11, f32[1,4,10,2048]{3,2,1,0:T(8,128)S(1)} %get-tuple-element.46), kind=kOutput, calls=%fused_computation.158 | convolution fusion | flops 504060928 | bytes 922624 | tf_op jit(solution)/shard_map/transpose(jvp(...k,kc->...c))/dot_general | solution.py:28
  48.0 0.9 convolution_add_fusion.4
  48.9 0.1 fusion.128
  49.1 1.2 fusion.68
  50.3 1.2 fusion.65
  51.5 1.2 fusion.62
  52.7 1.2 fusion.59
  53.9 0.2 copy-start.17
  54.1 0.9 fusion.6
  55.1 1.3 fusion.181
  56.4 0.1 pad_subtract_fusion
  56.5 0.1 multiply_multiply_fusion.1
  56.6 1.0 convolution_add_fusion.3
  57.6 0.9 convolution_add_fusion.2
  58.6 0.9 convolution_add_fusion.1
  59.5 0.1 pad_add_fusion.1
  59.6 0.8 slice_bitcast_fusion.17
  60.4 2.8 %collective-permute-start.6 = (f32[2,4,10,256]{3,2,1,0:T(8,128)}, f32[2,4,10,256]{3,2,1,0:T(8,128)}, u32[]{:S(2)}, u32[]{:S(2)}) collective-permute-start(f32[2,4,10,256]{3,2,1,0:T(8,128)} %get-tuple-element.43), channel_id=1, source_target_pairs={{0,32},{8,40},{16,48},{24,56},{32,0},{40,8},{48,16},{56,24},{64,96... | collective-permute-start | bytes 245768 | tf_op jit(solution)/shard_map/ppermute | solution.py:10
  63.2 2.6 %collective-permute-start.5 = (f32[2,4,10,256]{3,2,1,0:T(8,128)}, f32[2,4,10,256]{3,2,1,0:T(8,128)}, u32[]{:S(2)}, u32[]{:S(2)}) collective-permute-start(f32[2,4,10,256]{3,2,1,0:T(8,128)} %get-tuple-element.44), channel_id=1, source_target_pairs={{0,16},{8,24},{16,0},{24,8},{32,48},{40,56},{48,32},{56,40},{64,80... | collective-permute-start | bytes 245768 | tf_op jit(solution)/shard_map/ppermute | solution.py:10
  65.8 5.9 %collective-permute-start.7 = (f32[2,4,10,256]{3,2,1,0:T(8,128)}, f32[2,4,10,256]{3,2,1,0:T(8,128)}, u32[]{:S(2)}, u32[]{:S(2)}) collective-permute-start(f32[2,4,10,256]{3,2,1,0:T(8,128)} %get-tuple-element.42), channel_id=1, source_target_pairs={{0,64},{8,72},{16,80},{24,88},{32,96},{40,104},{48,112},{56,120},{... | collective-permute-start | bytes 245768 | tf_op jit(solution)/shard_map/ppermute | solution.py:10
  71.8 2.1 %collective-permute-start.4 = (f32[2,4,10,256]{3,2,1,0:T(8,128)}, f32[2,4,10,256]{3,2,1,0:T(8,128)}, u32[]{:S(2)}, u32[]{:S(2)}) collective-permute-start(f32[2,4,10,256]{3,2,1,0:T(8,128)} %get-tuple-element.41), channel_id=1, source_target_pairs={{0,8},{8,0},{16,24},{24,16},{32,40},{40,32},{48,56},{56,48},{64,72... | collective-permute-start | bytes 245768 | tf_op jit(solution)/shard_map/ppermute | solution.py:10
  73.9 0.7 pad_maximum_fusion.6
  74.7 0.0 all-reduce.24.cloned.1.call-update
  74.7 0.8 fusion.158
  75.5 0.1 scatter-add.4
  75.6 1.9 %fusion.52 = f32[2,4,10,2048]{3,2,1,0:T(8,128)S(1)} fusion(s32[256]{0:T(256)S(1)} %bitcast.213, f32[2,10,256]{2,1,0:T(8,128)S(1)} %copy-done.18, f32[2,4,10,256]{3,2,1,0:T(8,128)} %collective-permute-done, f32[2,4,10,256]{3,2,1,0:T(8,128)} %fusion.54), kind=kOutput, calls=%fused_computation.39 | convolution fusion | flops 503881728 | bytes 840704 | tf_op jit(solution)/shard_map/jvp(...k,kc->...c)/dot_general | solution.py:28
  77.6 1.9 %fusion.39 = f32[2,4,10,2048]{3,2,1,0:T(8,128)S(1)} fusion(s32[256]{0:T(256)S(1)} %bitcast.220, f32[2,10,256]{2,1,0:T(8,128)S(1)} %fusion.62, f32[2,4,10,256]{3,2,1,0:T(8,128)} %collective-permute-done.1, f32[2,4,10,256]{3,2,1,0:T(8,128)} %fusion.41), kind=kOutput, calls=%fused_computation.32 | convolution fusion | flops 503881728 | bytes 840704 | tf_op jit(solution)/shard_map/jvp(...k,kc->...c)/dot_general | solution.py:28
  79.5 2.0 %fusion.24 = f32[2,4,10,2048]{3,2,1,0:T(8,128)S(1)} fusion(s32[256]{0:T(256)S(1)} %bitcast.227, f32[2,10,256]{2,1,0:T(8,128)S(1)} %fusion.65, f32[2,4,10,256]{3,2,1,0:T(8,128)} %collective-permute-done.2, f32[2,4,10,256]{3,2,1,0:T(8,128)} %fusion.26), kind=kOutput, calls=%fused_computation.23 | convolution fusion | flops 503881728 | bytes 840704 | tf_op jit(solution)/shard_map/jvp(...k,kc->...c)/dot_general | solution.py:28
  81.5 1.9 %fusion.10 = f32[2,4,10,2048]{3,2,1,0:T(8,128)S(1)} fusion(s32[256]{0:T(256)S(1)} %bitcast.234, f32[2,10,256]{2,1,0:T(8,128)S(1)} %copy-done.20, f32[2,4,10,256]{3,2,1,0:T(8,128)} %collective-permute-done.3, f32[2,4,10,256]{3,2,1,0:T(8,128)} %fusion.12), kind=kOutput, calls=%fused_computation.15 | convolution fusion | flops 503881728 | bytes 840704 | tf_op jit(solution)/shard_map/jvp(...k,kc->...c)/dot_general | solution.py:28
  83.5 0.8 fusion.110
  84.3 0.9 copy.29
  85.2 0.9 copy.30
  86.2 1.8 %fusion.19 = f32[2,4,10,2048]{3,2,1,0:T(8,128)S(1)} fusion(f32[2,4,10,256]{3,2,1,0:T(8,128)} %collective-permute-done.6, s32[256]{0:T(256)S(1)} %bitcast.228), kind=kOutput, calls=%fused_computation.21 | convolution fusion | flops 503840768 | bytes 738304 | tf_op jit(solution)/shard_map/...k,kc->...c/dot_general | solution.py:28
  88.0 1.8 %fusion.34 = f32[2,4,10,2048]{3,2,1,0:T(8,128)S(1)} fusion(f32[2,4,10,256]{3,2,1,0:T(8,128)} %collective-permute-done.5, s32[256]{0:T(256)S(1)} %bitcast.221), kind=kOutput, calls=%fused_computation.30 | convolution fusion | flops 503840768 | bytes 738304 | tf_op jit(solution)/shard_map/...k,kc->...c/dot_general | solution.py:28
  89.8 1.8 %fusion.4 = f32[2,4,10,2048]{3,2,1,0:T(8,128)S(1)} fusion(f32[2,4,10,256]{3,2,1,0:T(8,128)} %collective-permute-done.7, s32[256]{0:T(256)S(1)} %bitcast.235), kind=kOutput, calls=%fused_computation.12 | convolution fusion | flops 503840768 | bytes 738304 | tf_op jit(solution)/shard_map/...k,kc->...c/dot_general | solution.py:28
  91.7 2.1 %fusion.1 = f32[2,4,10,2048]{3,2,1,0:T(8,128)S(1)} fusion(f32[2,4,10,2048]{3,2,1,0:T(8,128)S(1)} %fusion.4, f32[2,4,10,2048]{3,2,1,0:T(8,128)S(1)} %fusion.19, f32[2,4,10,2048]{3,2,1,0:T(8,128)S(1)} %fusion.34, f32[2,4,10,256]{3,2,1,0:T(8,128)} %collective-permute-done.4, s32[256]{0:T(256)S(1)} %bitcast.214), kind=kOutput, calls=%fused_computation.2 | convolution fusion | flops 504332288 | bytes 2704384 | tf_op jit(solution)/shard_map/...k,kc->...c/dot_general | solution.py:28
  93.9 0.8 fusion.106
  94.7 0.9 copy.31
  95.7 0.9 copy.32
  96.6 66.0 %all-reduce.24.cloned.1.call-done = f32[2,10,2048]{2,1,0:T(8,128)} async-done(((f32[2,10,2048]{2,1,0:T(8,128)}), f32[2,10,2048]{2,1,0:T(8,128)}) %all-reduce.24.cloned.1.call-update) | async-done | bytes 163856 | tf_op jit(solution)/shard_map/psum | solution.py:89
  162.6 0.8 constant_dynamic-slice_fusion
  163.4 0.6 copy.33
  (68 shorter events, 0.3 us)
Async XLA Ops:
  7.2 155.5 %all-reduce.24.cloned.1.call-start = ((), (), s32[]{:S(2)}) async-start(), calls=%async_computation | async-start | bytes 524288 | tf_op jit(solution)/shard_map/psum | solution.py:89
  11.6 23.7 %collective-permute-start.2 = (f32[2,4,10,256]{3,2,1,0:T(8,128)}, f32[2,4,10,256]{3,2,1,0:T(8,128)}, u32[]{:S(2)}, u32[]{:S(2)}) collective-permute-start(f32[2,4,10,256]{3,2,1,0:T(8,128)} %fusion.26), channel_id=1, source_target_pairs={{0,32},{8,40},{16,48},{24,56},{32,0},{40,8},{48,16},{56,24},{64,96... | collective-permute-start | bytes 245768 | tf_op jit(solution)/shard_map/ppermute | solution.py:10
  15.9 22.9 %collective-permute-start.3 = (f32[2,4,10,256]{3,2,1,0:T(8,128)}, f32[2,4,10,256]{3,2,1,0:T(8,128)}, u32[]{:S(2)}, u32[]{:S(2)}) collective-permute-start(f32[2,4,10,256]{3,2,1,0:T(8,128)} %fusion.12), channel_id=1, source_target_pairs={{0,64},{8,72},{16,80},{24,88},{32,96},{40,104},{48,112},{56,120},{... | collective-permute-start | bytes 245768 | tf_op jit(solution)/shard_map/ppermute | solution.py:10
  24.8 7.6 %copy-start.12 = (f32[10,2048]{1,0:T(8,128)S(1)}, f32[10,2048]{1,0:T(8,128)}, u32[]{:S(2)}) copy-start(f32[10,2048]{1,0:T(8,128)} %param.16) | copy-start | bytes 245764
  24.8 7.6 %copy-start.13 = (f32[10,2048]{1,0:T(8,128)S(1)}, f32[10,2048]{1,0:T(8,128)}, u32[]{:S(2)}) copy-start(f32[10,2048]{1,0:T(8,128)} %param.17) | copy-start | bytes 245764
  24.8 7.6 %copy-start.15 = (s32[10,2048]{1,0:T(8,128)S(1)}, s32[10,2048]{1,0:T(8,128)}, u32[]{:S(2)}) copy-start(s32[10,2048]{1,0:T(8,128)} %param.18) | copy-start | bytes 245764
  24.8 17.3 %collective-permute-start.1 = (f32[2,4,10,256]{3,2,1,0:T(8,128)}, f32[2,4,10,256]{3,2,1,0:T(8,128)}, u32[]{:S(2)}, u32[]{:S(2)}) collective-permute-start(f32[2,4,10,256]{3,2,1,0:T(8,128)} %fusion.41), channel_id=1, source_target_pairs={{0,16},{8,24},{16,0},{24,8},{32,48},{40,56},{48,32},{56,40},{64,80... | collective-permute-start | bytes 245768 | tf_op jit(solution)/shard_map/ppermute | solution.py:10
  28.2 4.3 %copy-start.6 = (f32[4,10,2048]{2,0,1:T(4,128)S(1)}, f32[4,10,2048]{2,0,1:T(4,128)}, u32[]{:S(2)}) copy-start(f32[4,10,2048]{2,0,1:T(4,128)} %param.23) | copy-start | bytes 983044
  28.2 4.3 %copy-start.7 = (f32[4,10,2048]{2,0,1:T(4,128)S(1)}, f32[4,10,2048]{2,0,1:T(4,128)}, u32[]{:S(2)}) copy-start(f32[4,10,2048]{2,0,1:T(4,128)} %param.22) | copy-start | bytes 983044
  30.3 15.2 %collective-permute-start = (f32[2,4,10,256]{3,2,1,0:T(8,128)}, f32[2,4,10,256]{3,2,1,0:T(8,128)}, u32[]{:S(2)}, u32[]{:S(2)}) collective-permute-start(f32[2,4,10,256]{3,2,1,0:T(8,128)} %fusion.54), channel_id=1, source_target_pairs={{0,8},{8,0},{16,24},{24,16},{32,40},{40,32},{48,56},{56,48},{64,72... | collective-permute-start | bytes 245768 | tf_op jit(solution)/shard_map/ppermute | solution.py:10
  33.8 1.4 copy-start.22
  35.3 9.3 %copy-start.25 = (f32[1,256]{1,0:T(1,128)}, f32[1,256]{1,0:T(1,128)S(1)}, u32[]{:S(2)}) copy-start(f32[1,256]{1,0:T(1,128)S(1)} %get-tuple-element.57) | copy-start | bytes 3076
  35.3 12.7 %copy-start.23 = (f32[1,256]{1,0:T(1,128)}, f32[1,256]{1,0:T(1,128)S(1)}, u32[]{:S(2)}) copy-start(f32[1,256]{1,0:T(1,128)S(1)} %get-tuple-element.56) | copy-start | bytes 3076
  35.3 3.5 %copy-start.11 = (f32[1,4,10,2048]{3,2,1,0:T(8,128)S(1)}, f32[1,4,10,2048]{3,2,1,0:T(8,128)}, u32[]{:S(2)}) copy-start(f32[1,4,10,2048]{3,2,1,0:T(8,128)} %get-tuple-element.74) | copy-start | bytes 983044
  45.5 3.4 %copy-start.14 = (f32[10,2048]{1,0:T(8,128)S(1)}, f32[10,2048]{1,0:T(8,128)}, u32[]{:S(2)}) copy-start(f32[10,2048]{1,0:T(8,128)} %param.17) | copy-start | bytes 245764
  45.5 3.4 %copy-start.16 = (s32[10,2048]{1,0:T(8,128)S(1)}, s32[10,2048]{1,0:T(8,128)}, u32[]{:S(2)}) copy-start(s32[10,2048]{1,0:T(8,128)} %param.18) | copy-start | bytes 245764
  45.5 3.4 %copy-start.21 = (f32[10,2048]{1,0:T(8,128)S(1)}, f32[10,2048]{1,0:T(8,128)}, u32[]{:S(2)}) copy-start(f32[10,2048]{1,0:T(8,128)} %param.15) | copy-start | bytes 245764
  49.0 2.4 %copy-start.26 = (f32[1,256]{1,0:T(1,128)S(1)}, f32[1,256]{1,0:T(1,128)}, u32[]{:S(2)}) copy-start(f32[1,256]{1,0:T(1,128)} %copy-done.25) | copy-start | bytes 3076
  49.0 3.6 %copy-start.24 = (f32[1,256]{1,0:T(1,128)S(1)}, f32[1,256]{1,0:T(1,128)}, u32[]{:S(2)}) copy-start(f32[1,256]{1,0:T(1,128)} %copy-done.23) | copy-start | bytes 3076
  50.3 4.8 %copy-start.19 = (f32[2,10,256]{2,1,0:T(8,128)}, f32[2,10,256]{2,1,0:T(8,128)S(1)}, u32[]{:S(2)}) copy-start(f32[2,10,256]{2,1,0:T(8,128)S(1)} %fusion.68) | copy-start | bytes 61444
  53.9 4.7 %copy-start.17 = (f32[2,10,256]{2,1,0:T(8,128)}, f32[2,10,256]{2,1,0:T(8,128)S(1)}, u32[]{:S(2)}) copy-start(f32[2,10,256]{2,1,0:T(8,128)S(1)} %fusion.59) | copy-start | bytes 61444
  60.4 15.2 %copy-start.18 = (f32[2,10,256]{2,1,0:T(8,128)S(1)}, f32[2,10,256]{2,1,0:T(8,128)}, u32[]{:S(2)}) copy-start(f32[2,10,256]{2,1,0:T(8,128)} %copy-done.17) | copy-start | bytes 61444
  60.4 25.7 %collective-permute-start.6 = (f32[2,4,10,256]{3,2,1,0:T(8,128)}, f32[2,4,10,256]{3,2,1,0:T(8,128)}, u32[]{:S(2)}, u32[]{:S(2)}) collective-permute-start(f32[2,4,10,256]{3,2,1,0:T(8,128)} %get-tuple-element.43), channel_id=1, source_target_pairs={{0,32},{8,40},{16,48},{24,56},{32,0},{40,8},{48,16},{56,24},{64,96... | collective-permute-start | bytes 245768 | tf_op jit(solution)/shard_map/ppermute | solution.py:10
  63.2 24.8 %collective-permute-start.5 = (f32[2,4,10,256]{3,2,1,0:T(8,128)}, f32[2,4,10,256]{3,2,1,0:T(8,128)}, u32[]{:S(2)}, u32[]{:S(2)}) collective-permute-start(f32[2,4,10,256]{3,2,1,0:T(8,128)} %get-tuple-element.44), channel_id=1, source_target_pairs={{0,16},{8,24},{16,0},{24,8},{32,48},{40,56},{48,32},{56,40},{64,80... | collective-permute-start | bytes 245768 | tf_op jit(solution)/shard_map/ppermute | solution.py:10
  65.8 24.0 %collective-permute-start.7 = (f32[2,4,10,256]{3,2,1,0:T(8,128)}, f32[2,4,10,256]{3,2,1,0:T(8,128)}, u32[]{:S(2)}, u32[]{:S(2)}) collective-permute-start(f32[2,4,10,256]{3,2,1,0:T(8,128)} %get-tuple-element.42), channel_id=1, source_target_pairs={{0,64},{8,72},{16,80},{24,88},{32,96},{40,104},{48,112},{56,120},{... | collective-permute-start | bytes 245768 | tf_op jit(solution)/shard_map/ppermute | solution.py:10
  71.8 19.9 %collective-permute-start.4 = (f32[2,4,10,256]{3,2,1,0:T(8,128)}, f32[2,4,10,256]{3,2,1,0:T(8,128)}, u32[]{:S(2)}, u32[]{:S(2)}) collective-permute-start(f32[2,4,10,256]{3,2,1,0:T(8,128)} %get-tuple-element.41), channel_id=1, source_target_pairs={{0,8},{8,0},{16,24},{24,16},{32,40},{40,32},{48,56},{56,48},{64,72... | collective-permute-start | bytes 245768 | tf_op jit(solution)/shard_map/ppermute | solution.py:10
  77.6 4.0 %copy-start.20 = (f32[2,10,256]{2,1,0:T(8,128)S(1)}, f32[2,10,256]{2,1,0:T(8,128)}, u32[]{:S(2)}) copy-start(f32[2,10,256]{2,1,0:T(8,128)} %copy-done.19) | copy-start | bytes 61444
  79.5 4.0 %copy-start = (f32[4,9,2048]{2,1,0:T(8,128)S(1)}, f32[4,9,2048]{2,1,0:T(8,128)}, u32[]{:S(2)}) copy-start(f32[4,9,2048]{2,1,0:T(8,128)} %get-tuple-element.38) | copy-start | bytes 884740
  79.5 4.0 %copy-start.9 = (f32[4,10,2048]{2,0,1:T(4,128)S(1)}, f32[4,10,2048]{2,0,1:T(4,128)}, u32[]{:S(2)}) copy-start(f32[4,10,2048]{2,0,1:T(4,128)} %param.14) | copy-start | bytes 983044
  79.5 4.0 %copy-start.10 = (f32[4,10,2048]{2,0,1:T(4,128)S(1)}, f32[4,10,2048]{2,0,1:T(4,128)}, u32[]{:S(2)}) copy-start(f32[4,10,2048]{2,0,1:T(4,128)} %param.13) | copy-start | bytes 983044
  91.7 2.2 %copy-start.1 = (f32[4,9,2048]{2,1,0:T(8,128)S(1)}, f32[4,9,2048]{2,1,0:T(8,128)}, u32[]{:S(2)}) copy-start(f32[4,9,2048]{2,1,0:T(8,128)} %get-tuple-element.30) | copy-start | bytes 884740
  91.7 2.2 %copy-start.2 = (f32[4,9,2048]{2,1,0:T(8,128)S(1)}, f32[4,9,2048]{2,1,0:T(8,128)}, u32[]{:S(2)}) copy-start(f32[4,9,2048]{2,1,0:T(8,128)} %get-tuple-element.31) | copy-start | bytes 884740
  91.7 2.2 %copy-start.3 = (f32[4,9,2048]{2,1,0:T(8,128)S(1)}, f32[4,9,2048]{2,1,0:T(8,128)}, u32[]{:S(2)}) copy-start(f32[4,9,2048]{2,1,0:T(8,128)} %get-tuple-element.54) | copy-start | bytes 884740
  91.7 2.2 %copy-start.4 = (f32[4,9,2048]{2,1,0:T(8,128)S(1)}, f32[4,9,2048]{2,1,0:T(8,128)}, u32[]{:S(2)}) copy-start(f32[4,9,2048]{2,1,0:T(8,128)} %get-tuple-element.28) | copy-start | bytes 884740
  91.7 2.2 %copy-start.5 = (f32[4,9,2048]{2,1,0:T(8,128)S(1)}, f32[4,9,2048]{2,1,0:T(8,128)}, u32[]{:S(2)}) copy-start(f32[4,9,2048]{2,1,0:T(8,128)} %get-tuple-element.29) | copy-start | bytes 884740
  91.7 2.2 %copy-start.8 = (f32[4,10,2048]{2,0,1:T(4,128)S(1)}, f32[4,10,2048]{2,0,1:T(4,128)}, u32[]{:S(2)}) copy-start(f32[4,10,2048]{2,0,1:T(4,128)} %param.22) | copy-start | bytes 983044
Sparse Core Ops, SparseCore 0:
  74.8 87.8 all-reduce.23
where the time goes:
time: 172 us; the launch traced here: 171 us
  waiting for transfers between devices  66.1 us (38%)
  matrix products  45.5 us (26%)
  starting transfers between devices  28 us (16%)
  between operations  14.8 us (9%)
  local copies, waits for them, and re-layouts  8.84 us (5%)
  other arithmetic  7.6 us (4%)
    psum x1, waiting for transfers between devices, body(): summed = lax.psum(grads, 'member')  66 us
    ppermute x8, starting transfers between devices, from_partner(): return lax.ppermute(value, axis, pairs)  28 us
    dot_general x12, matrix products, place(): jnp.einsum('...k,kc->...c', values, select, precision=lax.Precision.HIGHEST)  25 us
    dot_general x16, matrix products, pick(): jnp.einsum('...c,kc->...k', values, select, precision=lax.Precision.HIGHEST)  20.4 us
    unnamed x60, local copies, waits for them, and re-layouts  6.25 us
  transfers between devices with their start and end apart: 9, of which 1 were waited for; matrix products, arithmetic and copies ran while one was open for 24% of the time, Pallas kernels for 0%

commit v1 on v0

v1 whole, which is shorter than its diff:
```python
import jax
import jax.numpy as jnp
from jax import lax
from jax.sharding import PartitionSpec as P


def from_partner(value, axis, mask):
    pairs = [(source, source ^ mask) for source in range(lax.axis_size(axis))]
    return lax.ppermute(value, axis, pairs)


def spread(grad_iface):
    return jnp.pad(grad_iface, ((0, 0), (0, 1), (0, 0))) - jnp.pad(
        grad_iface, ((0, 0), (1, 0), (0, 0))
    )


def pad_sum(grad_iface, axis):
    pads = [(0, 0)] * grad_iface.ndim
    low, high = list(pads), list(pads)
    low[axis], high[axis] = (0, 1), (1, 0)
    return jnp.pad(grad_iface, low) + jnp.pad(grad_iface, high)


def split3(x):
    hi = lax.reduce_precision(x, exponent_bits=8, mantissa_bits=7)
    rest = x - hi
    mid = lax.reduce_precision(rest, exponent_bits=8, mantissa_bits=7)
    lo = rest - mid
    return jnp.concatenate(
        [hi.astype(jnp.bfloat16), mid.astype(jnp.bfloat16), lo.astype(jnp.bfloat16)]
    )


def exact_select(rows, select, contract):
    n = rows.shape[0]
    parts = lax.dot_general(
        split3(rows),
        select,
        (((1,), (contract,)), ((), ())),
        preferred_element_type=jnp.float32,
    )
    return (parts[:n] + parts[n : 2 * n]) + parts[2 * n :]


def reduce_scatter(value, axis):
    size = lax.axis_size(axis)
    index = lax.axis_index(axis)
    width = value.shape[-1] // size
    cur = value.reshape(value.shape[:-1] + (size, width))
    dist = size // 2
    while dist >= 1:
        half = cur.shape[-2] // 2
        lower, upper = cur[..., :half, :], cur[..., half:, :]
        bit = (index // dist) % 2 == 1
        keep = jnp.where(bit, upper, lower)
        send = jnp.where(bit, lower, upper)
        cur = keep + from_partner(send, axis, dist)
        dist //= 2
    return cur.reshape(value.shape[:-1] + (width,))


def body(
    pressure,
    heat,
    log_cond,
    log_therm,
    frozen,
    frozen_flag,
    recharge,
    face_cols,
    face_weight,
    cot_pressure,
    cot_heat,
):
    members, layers, width = pressure.shape
    rounds, face = face_cols.shape
    blocked = frozen * frozen_flag.astype(jnp.float32)
    cond = jnp.exp(log_cond - 3.0 * blocked)
    therm = jnp.exp(log_therm) * (1.0 + blocked)
    g_p = 0.1 * cot_pressure
    g_t = 0.1 * cot_heat

    cols = face_cols.reshape(rounds * face)
    select = (cols[:, None] == jnp.arange(width, dtype=jnp.int32)[None, :]).astype(
        jnp.bfloat16
    )

    n_field = members * layers
    rows = jnp.concatenate(
        [
            jnp.stack([pressure, heat, g_p, g_t]).reshape(4 * n_field, width),
            jnp.stack([cond, therm]).reshape(2 * layers, width),
        ]
    )
    picked = exact_select(rows, select, 1)
    fields_f = picked[: 4 * n_field].reshape(4, members, layers, rounds, face)
    coefs_f = picked[4 * n_field :].reshape(2, 1, layers, rounds, face)
    wc = face_weight * coefs_f
    own = fields_f[:2]
    g_own = fields_f[2:] * wc
    sending = jnp.concatenate([own, g_own])

    far = []
    for index in range(rounds):
        far.append(from_partner(sending[..., index, :], "space", 1 << index))
    far = jnp.stack(far, axis=-2)

    diff = far[:2] - own
    update = wc * diff
    adj_lat = far[2:] - g_own
    param_lat = face_weight * jnp.sum(fields_f[2:] * diff, axis=1)

    kf = 0.5 * (cond[:-1] + cond[1:])
    kt = 0.5 * (therm[:-1] + therm[1:])
    d_p = pressure[:, 1:] - pressure[:, :-1]
    d_t = heat[:, 1:] - heat[:, :-1]
    flow = kf * d_p
    conduct = kt * d_t
    t_mean = 0.5 * (heat[:, :-1] + heat[:, 1:])
    carried = flow * t_mean
    da = g_p[:, :-1] - g_p[:, 1:]
    db = g_t[:, :-1] - g_t[:, 1:]
    g_carried = 0.5 * db
    g_flow = da + g_carried * t_mean
    g_kf = jnp.sum(g_flow * d_p, axis=0)
    g_kt = jnp.sum(db * d_t, axis=0)
    vert_grads = jnp.stack([0.5 * pad_sum(g_kf, 0), 0.5 * pad_sum(g_kt, 0)])

    lat_grads = exact_select(
        param_lat.reshape(2 * layers, rounds * face), select, 0
    ).reshape(2, layers, width)
    grads = (vert_grads + lat_grads) * jnp.stack([cond, therm])
    owned = reduce_scatter(grads, "member")

    lat = exact_select(
        jnp.concatenate([update, adj_lat]).reshape(4 * n_field, rounds * face),
        select,
        0,
    ).reshape(4, members, layers, width)

    p_rate = spread(flow)
    p_rate = p_rate.at[:, 0].add(recharge)
    t_rate = spread(conduct) + 0.5 * spread(carried)
    new_pressure = pressure + 0.1 * (p_rate + lat[0])
    new_heat = heat + 0.1 * (t_rate + lat[1])
    adj_pressure = cot_pressure - spread(g_flow * kf[None]) + lat[2]
    adj_heat = (
        cot_heat
        - spread(db * kt[None])
        + 0.5 * pad_sum(g_carried * flow, 1)
        + lat[3]
    )
    return (new_pressure, new_heat, adj_pressure, adj_heat, owned)


def solution(mesh):
    placed = (
        P("member", None, "space"),
        P("member", None, "space"),
        P(None, "space"),
        P(None, "space"),
        P(None, "space"),
        P(None, "space"),
        P("member", "space"),
        P(None, "space"),
        P(None, "space"),
        P("member", None, "space"),
        P("member", None, "space"),
    )
    return jax.shard_map(
        body,
        mesh=mesh,
        in_specs=placed,
        out_specs=(
            P("member", None, "space"),
            P("member", None, "space"),
            P("member", None, "space"),
            P("member", None, "space"),
            P(None, None, ("space", "member")),
        ),
        check_vma=False,
    )
```

time: 172 us -> 80.2 us (0.47)
  the two profiles are of different devices: /device:TPU:24 before, /device:TPU:1 now
where the time goes in v1:
time: 80.2 us; the launch traced here: 78.8 us
  starting transfers between devices  26.8 us (33%)
  local copies, waits for them, and re-layouts  18.2 us (23%)
  other arithmetic  16.9 us (21%)
  waiting for transfers between devices  8.55 us (11%)
  matrix products  7.05 us (9%)
  between operations  1.26 us (2%)
    ppermute x7, starting transfers between devices, from_partner(): return lax.ppermute(value, axis, pairs)  26.8 us
    ppermute x7, waiting for transfers between devices, from_partner(): return lax.ppermute(value, axis, pairs)  8.55 us
    dot_general x3, matrix products, exact_select(): lax.dot_general(split3(rows), select, (((1,), (contract,)), ((), ())), pr...  7.05 us
    unnamed x49, local copies, waits for them, and re-layouts  6.78 us
    add x1, other arithmetic, body(): new_pressure = pressure + 0.1 * (p_rate + lat[0])  2.1 us
    another operation x2, other arithmetic, body(): jnp.stack([pressure, heat, g_p, g_t]).reshape(4 * n_field, width)  1.68 us
  transfers between devices with their start and end apart: 7, of which 2 were waited for; matrix products, arithmetic and copies ran while one was open for 28% of the time, Pallas kernels for 0%

profile of v1, /device:TPU:1, one launch (start us, length us, event | category | flops | bytes accessed | tf_op | source)
XLA Modules:
  0.0 78.8 jit_solution(6069956160226796037)
XLA Ops:
  0.6 0.7 copy.118
  1.3 1.2 %add_multiply_fusion.3 = (f32[10,2048]{1,0:T(8,128)S(1)}, f32[10,2048]{1,0:T(8,128)S(1)}) fusion(f32[10,2048]{1,0:T(8,128)} %param.16, f32[10,2048]{1,0:T(8,128)} %param.17, s32[10,2048]{1,0:T(8,128)} %param.18, f32[10,2048]{1,0:T(8,128)} %param.15), kind=kLoop, calls=%fused_computation.101 | loop fusion | flops 122880 | bytes 491520 | tf_op jit(solution)/shard_map/mul | solution.py:80
  2.6 0.7 reshape.103
  3.3 1.5 %copy_bitcast_fusion = (f32[1,4,10,2048]{3,2,1,0:T(8,128)S(1)}, f32[4,10,2048]{2,1,0:T(8,128)S(1)}, f32[4,10,2048]{2,1,0:T(8,128)S(1)}, f32[1,4,10,2048]{3,2,1,0:T(8,128)S(1)}) fusion(f32[4,10,2048]{2,0,1:T(4,128)} %param.13, f32[4,10,2048]{2,0,1:T(4,128)} %param.14), kind=kLoop, calls=%fused_computation.88 | loop fusion | bytes 1966080 | tf_op jit(solution)/shard_map/stack | solution.py:92
  4.8 1.4 %fusion.39 = (f32[1,4,10,2048]{3,2,1,0:T(8,128)S(1)}, f32[4,10,2048]{2,1,0:T(8,128)}, f32[4,10,2048]{2,1,0:T(8,128)}, f32[1,4,10,2048]{3,2,1,0:T(8,128)S(1)}) fusion(f32[4,10,2048]{2,0,1:T(4,128)S(1)} %copy-done.7, f32[4,10,2048]{2,0,1:T(4,128)S(1)} %copy-done.6), kind=kLoop, calls=%fused_computation.116 | loop fusion | flops 163840 | bytes 1966080 | tf_op jit(solution)/shard_map/stack | solution.py:92
  6.2 0.2 pad_maximum_fusion
  6.5 1.3 %reshape.102 = f32[160,2048]{1,0:T(8,128)} reshape(f32[4,4,10,2048]{3,2,1,0:T(8,128)S(1)} %pad_maximum_fusion) | data formatting | bytes 2621440 | tf_op jit(solution)/shard_map/reshape | solution.py:92
  7.7 1.4 %constant_dynamic-update-slice_fusion.1 = f32[180,2048]{1,0:T(8,128)S(1)} fusion(f32[160,2048]{1,0:T(8,128)} %reshape.102), kind=kLoop, calls=%fused_computation.123 | loop fusion | bytes 2621440
  9.2 0.4 reduce-precision_convert_fusion.1
  9.6 2.8 %fusion.2 = f32[540,1024]{1,0:T(8,128)S(1)} fusion(s32[1024]{0:T(1024)S(1)} %bitcast.88, bf16[180,2048]{1,0:T(8,128)(2,1)S(1)} %get-tuple-element.43, bf16[180,2048]{1,0:T(8,128)(2,1)S(1)} %get-tuple-element.44, bf16[180,2048]{1,0:T(8,128)(2,1)S(1)} %get-tuple-element.42), kind=kOutput, calls=%fused_computation.3 | convolution fusion | flops 2273656832 | bytes 4427776 | tf_op jit(solution)/shard_map/dot_general | solution.py:37
  12.4 0.2 slice_add_fusion.2
  12.6 0.1 fusion.49
  12.7 0.2 slice.168
  12.9 0.2 copy-done.15
  13.1 0.2 slice.170
  13.3 0.1 copy.102
  13.4 0.2 copy_multiply_fusion.2
  13.6 0.9 %fusion.25 = (f32[4,4,10,256]{3,1,2,0:T(4,128)}, f32[4,4,10,256]{3,1,2,0:T(4,128)}, f32[4,4,10,256]{3,1,2,0:T(4,128)}, f32[4,4,10,256]{3,1,2,0:T(4,128)}) fusion(f32[2,4,10,4,256]{4,1,2,0,3:T(4,128)S(1)} %copy.102, f32[2,4,10,4,256]{4,1,2,0,3:T(4,128)S(1)} %copy_multiply_fusion.2), kind=kLoop, calls=%fused_computation.75 | loop fusion | flops 163840 | bytes 1310720 | tf_op jit(solution)/shard_map/squeeze | solution.py:106
  14.5 8.8 %collective-permute-start = (f32[4,4,10,256]{3,1,2,0:T(4,128)}, f32[4,4,10,256]{3,1,2,0:T(4,128)}, u32[]{:S(2)}, u32[]{:S(2)}) collective-permute-start(f32[4,4,10,256]{3,1,2,0:T(4,128)} %get-tuple-element.57), channel_id=1, source_target_pairs={{0,8},{8,0},{16,24},{24,16},{32,40},{40,32},{48,56},{56,48},{64,72... | collective-permute-start | bytes 491528 | tf_op jit(solution)/shard_map/ppermute | solution.py:9
  23.3 1.9 %collective-permute-start.1 = (f32[4,4,10,256]{3,1,2,0:T(4,128)}, f32[4,4,10,256]{3,1,2,0:T(4,128)}, u32[]{:S(2)}, u32[]{:S(2)}) collective-permute-start(f32[4,4,10,256]{3,1,2,0:T(4,128)} %get-tuple-element.58), channel_id=1, source_target_pairs={{0,16},{8,24},{16,0},{24,8},{32,48},{40,56},{48,32},{56,40},{64,80... | collective-permute-start | bytes 491528 | tf_op jit(solution)/shard_map/ppermute | solution.py:9
  25.2 2.5 %collective-permute-start.3 = (f32[4,4,10,256]{3,1,2,0:T(4,128)}, f32[4,4,10,256]{3,1,2,0:T(4,128)}, u32[]{:S(2)}, u32[]{:S(2)}) collective-permute-start(f32[4,4,10,256]{3,1,2,0:T(4,128)} %get-tuple-element.59), channel_id=1, source_target_pairs={{0,64},{8,72},{16,80},{24,88},{32,96},{40,104},{48,112},{56,120},{... | collective-permute-start | bytes 491528 | tf_op jit(solution)/shard_map/ppermute | solution.py:9
  27.7 2.4 %collective-permute-start.2 = (f32[4,4,10,256]{3,1,2,0:T(4,128)}, f32[4,4,10,256]{3,1,2,0:T(4,128)}, u32[]{:S(2)}, u32[]{:S(2)}) collective-permute-start(f32[4,4,10,256]{3,1,2,0:T(4,128)} %get-tuple-element.60), channel_id=1, source_target_pairs={{0,32},{8,40},{16,48},{24,56},{32,0},{40,8},{48,16},{56,24},{64,96... | collective-permute-start | bytes 491528 | tf_op jit(solution)/shard_map/ppermute | solution.py:9
  30.2 0.7 fusion.31
  31.0 0.3 multiply_reduce_fusion.1
  31.4 0.6 slice_bitcast_fusion.3
  32.1 1.2 %multiply_multiply_fusion = (f32[4,9,2048]{2,1,0:T(8,128)}, f32[4,9,2048]{2,1,0:T(8,128)S(1)}, f32[4,9,2048]{2,1,0:T(8,128)}) fusion(f32[4,9,2048]{2,1,0:T(8,128)S(1)} %get-tuple-element.39, f32[4,10,2048]{2,1,0:T(8,128)S(1)} %get-tuple-element.66, f32[9,2048]{1,0:T(8,128)S(1)} %get-tuple-element.84, f32[4,9,2048]{2,1,0:T(8,128)S(1)} %get-tuple-element.38), kind=kLoop, calls=%fused_computation.57 | loop fusion | flops 368640 | bytes 2138112 | tf_op jit(solution)/shard_map/mul | solution.py:151
  33.2 0.1 pad_subtract_fusion
  33.3 0.7 fusion.42
  34.0 0.2 multiply_reduce_fusion
  34.3 0.7 slice_bitcast_fusion
  35.0 0.9 %scatter-add.4 = f32[4,10,2048]{2,1,0:T(8,128)S(1)} dynamic-update-slice(f32[4,10,2048]{2,1,0:T(8,128)S(1)} %pad_subtract_fusion, f32[4,1,2048]{2,1,0:T(1,128)} %fusion.42, s32[]{:T(128)} %constant.88.clone.1, s32[]{:T(128)} %constant.88.clone.1, s32[]{:T(128)} %constant.88.clone.1) | dynamic-update-slice | bytes 65540 | tf_op jit(solution)/shard_map/scatter-add | solution.py:143
  35.9 3.9 %collective-permute-done.3 = f32[4,4,10,256]{3,1,2,0:T(4,128)} collective-permute-done((f32[4,4,10,256]{3,1,2,0:T(4,128)}, f32[4,4,10,256]{3,1,2,0:T(4,128)}, u32[]{:S(2)}, u32[]{:S(2)}) %collective-permute-start.3) | collective-permute-done | bytes 163872 | tf_op jit(solution)/shard_map/ppermute | solution.py:9
  39.8 4.6 %collective-permute-done.2 = f32[4,4,10,256]{3,1,2,0:T(4,128)} collective-permute-done((f32[4,4,10,256]{3,1,2,0:T(4,128)}, f32[4,4,10,256]{3,1,2,0:T(4,128)}, u32[]{:S(2)}, u32[]{:S(2)}) %collective-permute-start.2) | collective-permute-done | bytes 163872 | tf_op jit(solution)/shard_map/ppermute | solution.py:9
  44.4 1.3 %pad_maximum_fusion.1 = f32[4,4,10,4,256]{4,1,2,0,3:T(4,128)S(1)} fusion(f32[4,4,10,1,256]{4,1,2,0,3:T(4,128)} %bitcast.13, f32[4,4,10,1,256]{4,1,2,0,3:T(4,128)} %bitcast.11, f32[4,4,10,1,256]{4,1,2,0,3:T(4,128)} %bitcast.9, f32[4,4,10,1,256]{4,1,2,0,3:T(4,128)} %bitcast.7), kind=kLoop, calls=%fused_computation.38 | loop fusion | flops 491520 | bytes 1310720 | tf_op jit(solution)/shard_map/stack | solution.py:107
  45.7 0.5 multiply_reduce_fusion.2
  46.3 0.1 copy.112
  46.4 1.8 %fusion = f32[60,2048]{1,0:T(8,128)S(1)} fusion(s32[1024]{0:T(1024)S(1)} %bitcast.89, bf16[20,1024]{1,0:T(8,128)(2,1)S(1)} %get-tuple-element.77, bf16[20,1024]{1,0:T(8,128)(2,1)S(1)} %get-tuple-element.78, bf16[20,1024]{1,0:T(8,128)(2,1)S(1)} %get-tuple-element.76), kind=kOutput, calls=%fused_computation.1 | convolution fusion | flops 254124032 | bytes 618496 | tf_op jit(solution)/shard_map/dot_general | solution.py:37
  48.3 0.1 copy.124
  48.4 0.2 pad_maximum_fusion.2
  48.6 0.4 copy.104
  49.0 0.1 copy.119
  49.2 0.1 reduce-precision_convert_fusion.3
  49.3 0.2 copy-done.11
  49.5 0.0 copy-done.12
  49.5 0.0 copy-done.13
  49.6 0.7 slice_select_fusion
  50.2 4.2 %collective-permute-start.4 = (f32[2,10,4,256]{3,2,1,0:T(4,128)}, f32[2,10,4,256]{3,2,1,0:T(4,128)S(1)}, u32[]{:S(2)}, u32[]{:S(2)}) collective-permute-start(f32[2,10,4,256]{3,2,1,0:T(4,128)} %slice_select_fusion), channel_id=1, source_target_pairs={{0,4},{1,5},{2,6},{3,7},{4,0},{5,1},{6,2},{7,3},{8,12},{9,13},{10,... | collective-permute-start | bytes 245768 | tf_op jit(solution)/shard_map/ppermute | solution.py:9
  54.5 2.5 %fusion.1 = f32[480,2048]{1,0:T(8,128)S(1)} fusion(s32[1024]{0:T(1024)S(1)} %bitcast.90, bf16[160,1024]{1,0:T(8,128)(2,1)S(1)} %get-tuple-element.55, bf16[160,1024]{1,0:T(8,128)(2,1)S(1)} %get-tuple-element.56, bf16[160,1024]{1,0:T(8,128)(2,1)S(1)} %get-tuple-element.54), kind=kOutput, calls=%fused_computation.2 | convolution fusion | flops 2018312192 | bytes 4919296 | tf_op jit(solution)/shard_map/dot_general | solution.py:37
  56.9 0.2 slice_add_fusion
  57.2 1.0 %fusion.48 = (f32[40,2048]{1,0:T(8,128)}, f32[40,2048]{1,0:T(8,128)S(1)}, f32[40,2048]{1,0:T(8,128)}, f32[40,2048]{1,0:T(8,128)}) fusion(f32[160,2048]{1,0:T(8,128)S(1)} %slice_add_fusion), kind=kLoop, calls=%fused_computation.127 | loop fusion | bytes 2621440 | tf_op jit(solution)/shard_map/slice | solution.py:152
  58.2 1.0 %squeeze.28 = f32[4,10,2048]{2,1,0:T(8,128)S(1)} reshape(f32[40,2048]{1,0:T(8,128)} %get-tuple-element.48) | data formatting | bytes 655360 | tf_op jit(solution)/shard_map/squeeze | solution.py:145
  59.2 2.1 %multiply_add_fusion.1 = f32[4,10,2048]{2,1,0:T(8,128)} fusion(f32[4,10,2048]{2,1,0:T(8,128)S(1)} %scatter-add.4, f32[4,10,2048]{2,1,0:T(8,128)S(1)} %squeeze.28, f32[4,10,2048]{2,0,1:T(4,128)} %param.13), kind=kLoop, calls=%fused_computation.55 | loop fusion | flops 245760 | bytes 1310720 | tf_op jit(solution)/shard_map/add | solution.py:145
  61.4 1.1 %fusion.18 = f32[4,10,2048]{2,1,0:T(8,128)} fusion(f32[4,10,2048]{2,1,0:T(8,128)S(1)} %squeeze.30, f32[4,10,2048]{2,0,1:T(4,128)S(1)} %copy-done.8, f32[4,9,2048]{2,1,0:T(8,128)S(1)} %copy-done.5), kind=kLoop, calls=%fused_computation.44 | loop fusion | flops 245760 | bytes 1277952 | tf_op jit(solution)/shard_map/add | solution.py:147
  62.4 1.0 %squeeze.31 = f32[4,10,2048]{2,1,0:T(8,128)S(1)} reshape(f32[40,2048]{1,0:T(8,128)} %get-tuple-element.45) | data formatting | bytes 655360 | tf_op jit(solution)/shard_map/squeeze | solution.py:152
  63.5 4.7 %collective-permute-start.5 = (f32[2,10,2,256]{3,2,1,0:T(2,128)S(1)}, f32[2,10,2,256]{3,2,1,0:T(2,128)S(1)}, u32[]{:S(2)}, u32[]{:S(2)}) collective-permute-start(f32[2,10,2,256]{3,2,1,0:T(2,128)S(1)} %broadcast_select_fusion), channel_id=1, source_target_pairs={{0,2},{1,3},{2,0},{3,1},{4,6},{5,7},{6,4},{7,5},{8,10},{9,11},{10,... | collective-permute-start | bytes 122888 | tf_op jit(solution)/shard_map/ppermute | solution.py:9
  68.2 1.3 %fusion.20 = f32[4,10,2048]{2,1,0:T(8,128)S(1)} fusion(f32[4,10,2048]{2,1,0:T(8,128)S(1)} %squeeze.31, f32[4,10,2048]{2,0,1:T(4,128)} %param.23, f32[4,9,2048]{2,1,0:T(8,128)S(1)} %copy-done.2, f32[4,9,2048]{2,1,0:T(8,128)S(1)} %get-tuple-element.63), kind=kLoop, calls=%fused_computation.46 | loop fusion | flops 491520 | bytes 1572864 | tf_op jit(solution)/shard_map/add | solution.py:149
  69.5 1.1 %squeeze.29 = f32[4,10,2048]{2,1,0:T(8,128)S(1)} reshape(f32[40,2048]{1,0:T(8,128)} %get-tuple-element.47) | data formatting | bytes 655360 | tf_op jit(solution)/shard_map/squeeze | solution.py:146
  70.7 2.3 %collective-permute-start.6 = (f32[2,10,1,256]{3,2,1,0:T(1,128)S(1)}, f32[2,10,1,256]{3,2,1,0:T(1,128)S(1)}, u32[]{:S(2)}, u32[]{:S(2)}) collective-permute-start(f32[2,10,1,256]{3,2,1,0:T(1,128)S(1)} %broadcast_select_fusion.1), channel_id=1, source_target_pairs={{0,1},{1,0},{2,3},{3,2},{4,5},{5,4},{6,7},{7,6},{8,9},{9,8},{10,11... | collective-permute-start | bytes 61448 | tf_op jit(solution)/shard_map/ppermute | solution.py:9
  73.0 1.4 %multiply_add_fusion = f32[4,10,2048]{2,1,0:T(8,128)S(1)} fusion(f32[4,10,2048]{2,1,0:T(8,128)S(1)} %squeeze.29, f32[4,9,2048]{2,1,0:T(8,128)S(1)} %get-tuple-element.64, f32[4,9,2048]{2,1,0:T(8,128)S(1)} %get-tuple-element.62, f32[4,10,2048]{2,0,1:T(4,128)} %param.14), kind=kLoop, calls=%fused_computation.53 | loop fusion | flops 573440 | bytes 1572864 | tf_op jit(solution)/shard_map/add | solution.py:146
  74.4 0.9 %copy.117 = f32[4,10,2048]{2,0,1:T(4,128)} copy(f32[4,10,2048]{2,1,0:T(8,128)S(1)} %fusion.20) | data formatting | bytes 655360
  75.3 0.9 %copy.116 = f32[4,10,2048]{2,0,1:T(4,128)} copy(f32[4,10,2048]{2,1,0:T(8,128)S(1)} %copy-done.4) | data formatting | bytes 655360
  76.2 0.9 %copy.115 = f32[4,10,2048]{2,0,1:T(4,128)} copy(f32[4,10,2048]{2,1,0:T(8,128)S(1)} %multiply_add_fusion) | data formatting | bytes 655360
  77.2 0.9 %copy.114 = f32[4,10,2048]{2,0,1:T(4,128)} copy(f32[4,10,2048]{2,1,0:T(8,128)S(1)} %copy-done.3) | data formatting | bytes 655360
  78.2 0.6 copy.154
  (60 shorter events, 0.8 us)
Async XLA Ops:
  1.3 3.4 %copy-start.6 = (f32[4,10,2048]{2,0,1:T(4,128)S(1)}, f32[4,10,2048]{2,0,1:T(4,128)}, u32[]{:S(2)}) copy-start(f32[4,10,2048]{2,0,1:T(4,128)} %param.23) | copy-start | bytes 983044
  1.3 3.4 %copy-start.7 = (f32[4,10,2048]{2,0,1:T(4,128)S(1)}, f32[4,10,2048]{2,0,1:T(4,128)}, u32[]{:S(2)}) copy-start(f32[4,10,2048]{2,0,1:T(4,128)} %param.22) | copy-start | bytes 983044
  7.7 1.5 %copy-start.9 = (f32[20,2048]{1,0:T(8,128)S(1)}, f32[20,2048]{1,0:T(8,128)}, u32[]{:S(2)}) copy-start(f32[20,2048]{1,0:T(8,128)} %reshape.103) | copy-start | bytes 491524
  12.4 0.7 copy-start.15
  13.3 17.7 %copy-start = (f32[4,10,2048]{2,1,0:T(8,128)S(1)}, f32[4,10,2048]{2,1,0:T(8,128)}, u32[]{:S(2)}) copy-start(f32[4,10,2048]{2,1,0:T(8,128)} %get-tuple-element.70) | copy-start | bytes 983044
  13.3 17.7 %copy-start.1 = (f32[4,10,2048]{2,1,0:T(8,128)S(1)}, f32[4,10,2048]{2,1,0:T(8,128)}, u32[]{:S(2)}) copy-start(f32[4,10,2048]{2,1,0:T(8,128)} %get-tuple-element.81) | copy-start | bytes 983044
  14.5 21.4 %collective-permute-start = (f32[4,4,10,256]{3,1,2,0:T(4,128)}, f32[4,4,10,256]{3,1,2,0:T(4,128)}, u32[]{:S(2)}, u32[]{:S(2)}) collective-permute-start(f32[4,4,10,256]{3,1,2,0:T(4,128)} %get-tuple-element.57), channel_id=1, source_target_pairs={{0,8},{8,0},{16,24},{24,16},{32,40},{40,32},{48,56},{56,48},{64,72... | collective-permute-start | bytes 491528 | tf_op jit(solution)/shard_map/ppermute | solution.py:9
  23.3 12.6 %collective-permute-start.1 = (f32[4,4,10,256]{3,1,2,0:T(4,128)}, f32[4,4,10,256]{3,1,2,0:T(4,128)}, u32[]{:S(2)}, u32[]{:S(2)}) collective-permute-start(f32[4,4,10,256]{3,1,2,0:T(4,128)} %get-tuple-element.58), channel_id=1, source_target_pairs={{0,16},{8,24},{16,0},{24,8},{32,48},{40,56},{48,32},{56,40},{64,80... | collective-permute-start | bytes 491528 | tf_op jit(solution)/shard_map/ppermute | solution.py:9
  25.2 14.6 %collective-permute-start.3 = (f32[4,4,10,256]{3,1,2,0:T(4,128)}, f32[4,4,10,256]{3,1,2,0:T(4,128)}, u32[]{:S(2)}, u32[]{:S(2)}) collective-permute-start(f32[4,4,10,256]{3,1,2,0:T(4,128)} %get-tuple-element.59), channel_id=1, source_target_pairs={{0,64},{8,72},{16,80},{24,88},{32,96},{40,104},{48,112},{56,120},{... | collective-permute-start | bytes 491528 | tf_op jit(solution)/shard_map/ppermute | solution.py:9
  27.7 16.7 %collective-permute-start.2 = (f32[4,4,10,256]{3,1,2,0:T(4,128)}, f32[4,4,10,256]{3,1,2,0:T(4,128)}, u32[]{:S(2)}, u32[]{:S(2)}) collective-permute-start(f32[4,4,10,256]{3,1,2,0:T(4,128)} %get-tuple-element.60), channel_id=1, source_target_pairs={{0,32},{8,40},{16,48},{24,56},{32,0},{40,8},{48,16},{56,24},{64,96... | collective-permute-start | bytes 491528 | tf_op jit(solution)/shard_map/ppermute | solution.py:9
  32.1 1.2 %copy-start.14 = (f32[4,2048]{1,0:T(4,128)S(1)}, f32[4,2048]{1,0:T(4,128)}, u32[]{:S(2)}) copy-start(f32[4,2048]{1,0:T(4,128)} %param.19) | copy-start | bytes 98308
  32.1 1.9 %copy-start.10 = (f32[9,2048]{1,0:T(8,128)S(1)}, f32[9,2048]{1,0:T(8,128)}, u32[]{:S(2)}) copy-start(f32[9,2048]{1,0:T(8,128)} %get-tuple-element.83) | copy-start | bytes 221188
  48.6 0.9 %copy-start.11 = (f32[1,10,8,256]{3,2,1,0:T(8,128)S(1)}, f32[1,10,8,256]{3,2,1,0:T(8,128)}, u32[]{:S(2)}) copy-start(f32[1,10,8,256]{3,2,1,0:T(8,128)} %get-tuple-element.85) | copy-start | bytes 245764
  48.6 0.9 %copy-start.12 = (f32[1,10,8,256]{3,2,1,0:T(8,128)S(1)}, f32[1,10,8,256]{3,2,1,0:T(8,128)}, u32[]{:S(2)}) copy-start(f32[1,10,8,256]{3,2,1,0:T(8,128)} %get-tuple-element.86) | copy-start | bytes 245764
  48.6 1.0 %copy-start.13 = (f32[1,10,8,256]{3,2,1,0:T(8,128)S(1)}, f32[1,10,8,256]{3,2,1,0:T(8,128)}, u32[]{:S(2)}) copy-start(f32[1,10,8,256]{3,2,1,0:T(8,128)} %slice_bitcast_fusion.3) | copy-start | bytes 245764
  50.2 13.2 %collective-permute-start.4 = (f32[2,10,4,256]{3,2,1,0:T(4,128)}, f32[2,10,4,256]{3,2,1,0:T(4,128)S(1)}, u32[]{:S(2)}, u32[]{:S(2)}) collective-permute-start(f32[2,10,4,256]{3,2,1,0:T(4,128)} %slice_select_fusion), channel_id=1, source_target_pairs={{0,4},{1,5},{2,6},{3,7},{4,0},{5,1},{6,2},{7,3},{8,12},{9,13},{10,... | collective-permute-start | bytes 245768 | tf_op jit(solution)/shard_map/ppermute | solution.py:9
  59.2 2.1 %copy-start.5 = (f32[4,9,2048]{2,1,0:T(8,128)S(1)}, f32[4,9,2048]{2,1,0:T(8,128)}, u32[]{:S(2)}) copy-start(f32[4,9,2048]{2,1,0:T(8,128)} %get-tuple-element.75) | copy-start | bytes 884740
  59.2 2.1 %copy-start.8 = (f32[4,10,2048]{2,0,1:T(4,128)S(1)}, f32[4,10,2048]{2,0,1:T(4,128)}, u32[]{:S(2)}) copy-start(f32[4,10,2048]{2,0,1:T(4,128)} %param.22) | copy-start | bytes 983044
  61.4 6.8 %copy-start.2 = (f32[4,9,2048]{2,1,0:T(8,128)S(1)}, f32[4,9,2048]{2,1,0:T(8,128)}, u32[]{:S(2)}) copy-start(f32[4,9,2048]{2,1,0:T(8,128)} %get-tuple-element.40) | copy-start | bytes 884740
  63.5 7.1 %collective-permute-start.5 = (f32[2,10,2,256]{3,2,1,0:T(2,128)S(1)}, f32[2,10,2,256]{3,2,1,0:T(2,128)S(1)}, u32[]{:S(2)}, u32[]{:S(2)}) collective-permute-start(f32[2,10,2,256]{3,2,1,0:T(2,128)S(1)} %broadcast_select_fusion), channel_id=1, source_target_pairs={{0,2},{1,3},{2,0},{3,1},{4,6},{5,7},{6,4},{7,5},{8,10},{9,11},{10,... | collective-permute-start | bytes 122888 | tf_op jit(solution)/shard_map/ppermute | solution.py:9
  69.5 5.8 %copy-start.4 = (f32[4,10,2048]{2,1,0:T(8,128)S(1)}, f32[4,10,2048]{2,1,0:T(8,128)}, u32[]{:S(2)}) copy-start(f32[4,10,2048]{2,1,0:T(8,128)} %fusion.18) | copy-start | bytes 983044
  70.7 7.4 %collective-permute-start.6 = (f32[2,10,1,256]{3,2,1,0:T(1,128)S(1)}, f32[2,10,1,256]{3,2,1,0:T(1,128)S(1)}, u32[]{:S(2)}, u32[]{:S(2)}) collective-permute-start(f32[2,10,1,256]{3,2,1,0:T(1,128)S(1)} %broadcast_select_fusion.1), channel_id=1, source_target_pairs={{0,1},{1,0},{2,3},{3,2},{4,5},{5,4},{6,7},{7,6},{8,9},{9,8},{10,11... | collective-permute-start | bytes 61448 | tf_op jit(solution)/shard_map/ppermute | solution.py:9
  73.0 4.2 %copy-start.3 = (f32[4,10,2048]{2,1,0:T(8,128)S(1)}, f32[4,10,2048]{2,1,0:T(8,128)}, u32[]{:S(2)}) copy-start(f32[4,10,2048]{2,1,0:T(8,128)} %multiply_add_fusion.1) | copy-start | bytes 983044

commit v2 on v1

--- a/solution.py
+++ b/solution.py
@@ -15,10 +15,16 @@
     )
 
 
-def pad_sum(grad_iface, axis):
+def spread0(grad_iface):
+    return pad_sum(grad_iface, 0, -1.0)
+
+
+def pad_sum(grad_iface, axis, sign=1.0):
     pads = [(0, 0)] * grad_iface.ndim
     low, high = list(pads), list(pads)
     low[axis], high[axis] = (0, 1), (1, 0)
+    if sign < 0:
+        return jnp.pad(grad_iface, low) - jnp.pad(grad_iface, high)
     return jnp.pad(grad_iface, low) + jnp.pad(grad_iface, high)
 
 
@@ -75,11 +81,15 @@
 ):
     members, layers, width = pressure.shape
     rounds, face = face_cols.shape
+    p_old = pressure.transpose(1, 0, 2)
+    t_old = heat.transpose(1, 0, 2)
+    c_p = cot_pressure.transpose(1, 0, 2)
+    c_t = cot_heat.transpose(1, 0, 2)
     blocked = frozen * frozen_flag.astype(jnp.float32)
     cond = jnp.exp(log_cond - 3.0 * blocked)
     therm = jnp.exp(log_therm) * (1.0 + blocked)
-    g_p = 0.1 * cot_pressure
-    g_t = 0.1 * cot_heat
+    g_p = 0.1 * c_p
+    g_t = 0.1 * c_t
 
     cols = face_cols.reshape(rounds * face)
     select = (cols[:, None] == jnp.arange(width, dtype=jnp.int32)[None, :]).astype(
@@ -89,13 +99,13 @@
     n_field = members * layers
     rows = jnp.concatenate(
         [
-            jnp.stack([pressure, heat, g_p, g_t]).reshape(4 * n_field, width),
+            jnp.stack([p_old, t_old, g_p, g_t]).reshape(4 * n_field, width),
             jnp.stack([cond, therm]).reshape(2 * layers, width),
         ]
     )
     picked = exact_select(rows, select, 1)
-    fields_f = picked[: 4 * n_field].reshape(4, members, layers, rounds, face)
-    coefs_f = picked[4 * n_field :].reshape(2, 1, layers, rounds, face)
+    fields_f = picked[: 4 * n_field].reshape(4, layers, members, rounds, face)
+    coefs_f = picked[4 * n_field :].reshape(2, layers, 1, rounds, face)
     wc = face_weight * coefs_f
     own = fields_f[:2]
     g_own = fields_f[2:] * wc
@@ -109,22 +119,22 @@
     diff = far[:2] - own
     update = wc * diff
     adj_lat = far[2:] - g_own
-    param_lat = face_weight * jnp.sum(fields_f[2:] * diff, axis=1)
+    param_lat = face_weight * jnp.sum(fields_f[2:] * diff, axis=2)
 
-    kf = 0.5 * (cond[:-1] + cond[1:])
-    kt = 0.5 * (therm[:-1] + therm[1:])
-    d_p = pressure[:, 1:] - pressure[:, :-1]
-    d_t = heat[:, 1:] - heat[:, :-1]
+    kf = (0.5 * (cond[:-1] + cond[1:]))[:, None]
+    kt = (0.5 * (therm[:-1] + therm[1:]))[:, None]
+    d_p = p_old[1:] - p_old[:-1]
+    d_t = t_old[1:] - t_old[:-1]
     flow = kf * d_p
     conduct = kt * d_t
-    t_mean = 0.5 * (heat[:, :-1] + heat[:, 1:])
+    t_mean = 0.5 * (t_old[:-1] + t_old[1:])
     carried = flow * t_mean
-    da = g_p[:, :-1] - g_p[:, 1:]
-    db = g_t[:, :-1] - g_t[:, 1:]
+    da = g_p[:-1] - g_p[1:]
+    db = g_t[:-1] - g_t[1:]
     g_carried = 0.5 * db
     g_flow = da + g_carried * t_mean
-    g_kf = jnp.sum(g_flow * d_p, axis=0)
-    g_kt = jnp.sum(db * d_t, axis=0)
+    g_kf = jnp.sum(g_flow * d_p, axis=1)
+    g_kt = jnp.sum(db * d_t, axis=1)
     vert_grads = jnp.stack([0.5 * pad_sum(g_kf, 0), 0.5 * pad_sum(g_kt, 0)])
 
     lat_grads = exact_select(
@@ -137,21 +147,17 @@
         jnp.concatenate([update, adj_lat]).reshape(4 * n_field, rounds * face),
         select,
         0,
-    ).reshape(4, members, layers, width)
+    ).reshape(4, layers, members, width)
 
-    p_rate = spread(flow)
-    p_rate = p_rate.at[:, 0].add(recharge)
-    t_rate = spread(conduct) + 0.5 * spread(carried)
-    new_pressure = pressure + 0.1 * (p_rate + lat[0])
-    new_heat = heat + 0.1 * (t_rate + lat[1])
-    adj_pressure = cot_pressure - spread(g_flow * kf[None]) + lat[2]
-    adj_heat = (
-        cot_heat
-        - spread(db * kt[None])
-        + 0.5 * pad_sum(g_carried * flow, 1)
-        + lat[3]
-    )
-    return (new_pressure, new_heat, adj_pressure, adj_heat, owned)
+    p_rate = spread0(flow)
+    p_rate = p_rate.at[0].add(recharge)
+    t_rate = spread0(conduct) + 0.5 * spread0(carried)
+    new_pressure = p_old + 0.1 * (p_rate + lat[0])
+    new_heat = t_old + 0.1 * (t_rate + lat[1])
+    adj_pressure = c_p - spread0(g_flow * kf) + lat[2]
+    adj_heat = c_t - spread0(db * kt) + 0.5 * pad_sum(g_carried * flow, 0) + lat[3]
+    outs = [new_pressure, new_heat, adj_pressure, adj_heat]
+    return tuple(o.transpose(1, 0, 2) for o in outs) + (owned,)
 
 
 def solution(mesh):

time: 80.2 us -> 68.7 us (0.86)
  the two profiles are of different devices: /device:TPU:1 before, /device:TPU:140 now
where the time goes in v2:
time: 68.7 us; the launch traced here: 68.3 us
  starting transfers between devices  24.6 us (36%)
  waiting for transfers between devices  14.7 us (21%)
  other arithmetic  13.5 us (20%)
  matrix products  7.05 us (10%)
  local copies, waits for them, and re-layouts  6.99 us (10%)
  between operations  1.37 us (2%)
    ppermute x7, starting transfers between devices, from_partner(): return lax.ppermute(value, axis, pairs)  24.6 us
    ppermute x7, waiting for transfers between devices, from_partner(): return lax.ppermute(value, axis, pairs)  14.7 us
    dot_general x3, matrix products, exact_select(): lax.dot_general(split3(rows), select, (((1,), (contract,)), ((), ())), pr...  7.05 us
    unnamed x53, local copies, waits for them, and re-layouts  4.87 us
    transpose x4, other arithmetic, body(): return tuple((o.transpose(1, 0, 2) for o in outs)) + (owned,)  3.55 us
    another operation x2, other arithmetic, body(): jnp.stack([p_old, t_old, g_p, g_t]).reshape(4 * n_field, width)  2.66 us
  transfers between devices with their start and end apart: 7, of which 4 were waited for; matrix products, arithmetic and copies ran while one was open for 18% of the time, Pallas kernels for 0%

profile of v2, /device:TPU:140, one launch (start us, length us, event | category | flops | bytes accessed | tf_op | source)
XLA Modules:
  0.0 68.3 jit_solution(2878487665814784998)
XLA Ops:
  0.7 2.2 %fusion.44 = (f32[1,10,4,2048]{3,2,1,0:T(4,128)S(1)}, f32[10,4,2048]{2,1,0:T(4,128)}, f32[10,4,2048]{2,1,0:T(4,128)}, f32[1,10,4,2048]{3,2,1,0:T(4,128)S(1)}) fusion(f32[4,10,2048]{2,0,1:T(4,128)} %param.22, f32[4,10,2048]{2,0,1:T(4,128)} %param.23), kind=kLoop, calls=%fused_computation.126 | loop fusion | flops 163840 | bytes 1966080 | tf_op jit(solution)/shard_map/stack | solution.py:102
  2.9 0.4 pad_maximum_fusion
  3.3 0.5 reshape.102
  3.8 0.0 copy-start.11
  3.8 0.0 copy-start.12
  3.8 0.1 constant_dynamic-update-slice_fusion.1
  4.0 0.7 %copy-done.11 = f32[10,2048]{1,0:T(8,128)S(1)} copy-done((f32[10,2048]{1,0:T(8,128)S(1)}, f32[10,2048]{1,0:T(8,128)}, u32[]{:S(2)}) %copy-start.11) | copy-done | bytes 81944
  4.7 0.1 copy-done.12
  4.8 0.1 copy-done.13
  4.8 0.1 copy-done.14
  4.9 0.1 add_multiply_fusion.3
  5.0 0.0 copy-start.17
  5.0 0.4 reduce-precision_convert_fusion.1
  5.5 0.3 copy-done.17
  5.7 2.8 %fusion.2 = f32[540,1024]{1,0:T(8,128)S(1)} fusion(s32[1024]{0:T(1024)S(1)} %bitcast.135, bf16[180,2048]{1,0:T(8,128)(2,1)S(1)} %get-tuple-element.28, bf16[180,2048]{1,0:T(8,128)(2,1)S(1)} %get-tuple-element.29, bf16[180,2048]{1,0:T(8,128)(2,1)S(1)} %get-tuple-element.27), kind=kOutput, calls=%fused_computation.3 | convolution fusion | flops 2273656832 | bytes 4427776 | tf_op jit(solution)/shard_map/dot_general | solution.py:43
  8.5 0.2 slice_add_fusion.2
  8.7 0.1 fusion.48
  8.8 0.2 slice.170
  9.0 0.2 slice.168
  9.1 0.2 copy-done.16
  9.4 0.0 copy-start.3
  9.4 0.1 broadcast_multiply_fusion.1
  9.5 0.5 fusion.25
  10.0 0.7 %copy.60 = f32[4,10,4,1,256]{4,2,1,0,3:T(4,128)} copy(f32[4,10,4,1,256]{4,3,2,1,0:T(1,128)S(1)} %get-tuple-element.43) | data formatting | bytes 327680
  10.7 1.9 %collective-permute-start = (f32[4,10,4,256]{3,2,1,0:T(4,128)}, f32[4,10,4,256]{3,2,1,0:T(4,128)S(1)}, u32[]{:S(2)}, u32[]{:S(2)}) collective-permute-start(f32[4,10,4,256]{3,2,1,0:T(4,128)} %bitcast.95), channel_id=1, source_target_pairs={{0,8},{8,0},{16,24},{24,16},{32,40},{40,32},{48,56},{56,48},{64,72... | collective-permute-start | bytes 491528 | tf_op jit(solution)/shard_map/ppermute | solution.py:9
  12.6 0.7 %copy.59 = f32[4,10,4,1,256]{4,2,1,0,3:T(4,128)} copy(f32[4,10,4,1,256]{4,3,2,1,0:T(1,128)S(1)} %get-tuple-element.44) | data formatting | bytes 327680
  13.3 2.3 %collective-permute-start.1 = (f32[4,10,4,256]{3,2,1,0:T(4,128)}, f32[4,10,4,256]{3,2,1,0:T(4,128)}, u32[]{:S(2)}, u32[]{:S(2)}) collective-permute-start(f32[4,10,4,256]{3,2,1,0:T(4,128)} %bitcast.94), channel_id=1, source_target_pairs={{0,16},{8,24},{16,0},{24,8},{32,48},{40,56},{48,32},{56,40},{64,80... | collective-permute-start | bytes 491528 | tf_op jit(solution)/shard_map/ppermute | solution.py:9
  15.7 0.7 %copy.58 = f32[4,10,4,1,256]{4,2,1,0,3:T(4,128)} copy(f32[4,10,4,1,256]{4,3,2,1,0:T(1,128)S(1)} %get-tuple-element.46) | data formatting | bytes 327680
  16.4 4.5 %collective-permute-start.2 = (f32[4,10,4,256]{3,2,1,0:T(4,128)}, f32[4,10,4,256]{3,2,1,0:T(4,128)}, u32[]{:S(2)}, u32[]{:S(2)}) collective-permute-start(f32[4,10,4,256]{3,2,1,0:T(4,128)} %bitcast.93), channel_id=1, source_target_pairs={{0,32},{8,40},{16,48},{24,56},{32,0},{40,8},{48,16},{56,24},{64,96... | collective-permute-start | bytes 491528 | tf_op jit(solution)/shard_map/ppermute | solution.py:9
  20.9 0.7 %copy.61 = f32[4,10,4,1,256]{4,2,3,1,0:T(4,128)} copy(f32[4,10,4,1,256]{4,3,2,1,0:T(1,128)S(1)} %get-tuple-element.45) | data formatting | bytes 327680
  21.6 5.9 %collective-permute-start.3 = (f32[4,10,4,256]{3,2,1,0:T(4,128)}, f32[4,10,4,256]{3,2,1,0:T(4,128)}, u32[]{:S(2)}, u32[]{:S(2)}) collective-permute-start(f32[4,10,4,256]{3,2,1,0:T(4,128)} %bitcast.96), channel_id=1, source_target_pairs={{0,64},{8,72},{16,80},{24,88},{32,96},{40,104},{48,112},{56,120},{... | collective-permute-start | bytes 491528 | tf_op jit(solution)/shard_map/ppermute | solution.py:9
  27.6 0.4 multiply_reduce_fusion.2
  28.0 1.1 %multiply_multiply_fusion = (f32[9,4,2048]{2,1,0:T(4,128)}, f32[9,4,2048]{2,1,0:T(4,128)S(1)}, f32[9,4,2048]{2,1,0:T(4,128)}) fusion(f32[9,4,2048]{2,1,0:T(4,128)S(1)} %get-tuple-element.24, f32[10,4,2048]{2,1,0:T(4,128)S(1)} %bitcast.106, f32[9,2048]{1,0:T(8,128)S(1)} %get-tuple-element.64, f32[9,4,2048]{2,1,0:T(4,128)S(1)} %get-tuple-element.23), kind=kLoop, calls=%fused_computation.66 | loop fusion | flops 368640 | bytes 2138112 | tf_op jit(solution)/shard_map/mul | solution.py:158
  29.1 0.1 pad_subtract_fusion
  29.2 1.1 %multiply_reduce_fusion.1 = (f32[9,2048]{1,0:T(8,128)S(1)}, f32[9,4,2048]{2,1,0:T(4,128)}, f32[9,4,2048]{2,1,0:T(4,128)}, f32[9,4,2048]{2,1,0:T(4,128)}) fusion(f32[9,4,2048]{2,1,0:T(4,128)S(1)} %get-tuple-element.24, f32[10,4,2048]{2,1,0:T(4,128)S(1)} %bitcast.103, f32[9,2048]{1,0:T(8,128)S(1)} %get-tuple-element.63, f32[9,4,2048]{2,1,0:T(4,128)S(1)} %get-tuple-element.26), kind=kLoop, calls=%fused_computation.61 | loop fusion | flops 571392 | bytes 2211840 | tf_op jit(solution)/shard_map/reduce_sum | solution.py:137
  30.7 2.4 %collective-permute-done.2 = f32[4,10,4,256]{3,2,1,0:T(4,128)} collective-permute-done((f32[4,10,4,256]{3,2,1,0:T(4,128)}, f32[4,10,4,256]{3,2,1,0:T(4,128)}, u32[]{:S(2)}, u32[]{:S(2)}) %collective-permute-start.2) | collective-permute-done | bytes 163872 | tf_op jit(solution)/shard_map/ppermute | solution.py:9
  33.1 6.8 %collective-permute-done.3 = f32[4,10,4,256]{3,2,1,0:T(4,128)} collective-permute-done((f32[4,10,4,256]{3,2,1,0:T(4,128)}, f32[4,10,4,256]{3,2,1,0:T(4,128)}, u32[]{:S(2)}, u32[]{:S(2)}) %collective-permute-start.3) | collective-permute-done | bytes 163872 | tf_op jit(solution)/shard_map/ppermute | solution.py:9
  39.9 1.2 %pad_maximum_fusion.1 = f32[4,10,4,4,256]{4,2,1,0,3:T(4,128)S(1)} fusion(f32[4,10,4,1,256]{4,2,1,0,3:T(4,128)} %bitcast.17, f32[4,10,4,1,256]{4,2,1,0,3:T(4,128)} %bitcast.16, f32[4,10,4,1,256]{4,2,1,0,3:T(4,128)} %bitcast.14, f32[4,10,4,1,256]{4,2,1,0,3:T(4,128)S(1)} %bitcast.129), kind=kLoop, calls=%fused_computation.38 | loop fusion | flops 491520 | bytes 1310720 | tf_op jit(solution)/shard_map/stack | solution.py:117
  41.1 0.1 fusion.49
  41.2 0.3 multiply_reduce_fusion
  41.6 1.8 %fusion = f32[60,2048]{1,0:T(8,128)S(1)} fusion(s32[1024]{0:T(1024)S(1)} %bitcast.136, bf16[20,1024]{1,0:T(8,128)(2,1)S(1)} %get-tuple-element.59, bf16[20,1024]{1,0:T(8,128)(2,1)S(1)} %get-tuple-element.60, bf16[20,1024]{1,0:T(8,128)(2,1)S(1)} %get-tuple-element.58), kind=kOutput, calls=%fused_computation.1 | convolution fusion | flops 254124032 | bytes 618496 | tf_op jit(solution)/shard_map/dot_general | solution.py:43
  43.5 0.1 copy.44
  43.6 0.7 slice_select_fusion
  44.3 4.5 %collective-permute-start.4 = (f32[2,10,4,256]{3,2,1,0:T(4,128)}, f32[2,10,4,256]{3,2,1,0:T(4,128)S(1)}, u32[]{:S(2)}, u32[]{:S(2)}) collective-permute-start(f32[2,10,4,256]{3,2,1,0:T(4,128)} %slice_select_fusion), channel_id=1, source_target_pairs={{0,4},{1,5},{2,6},{3,7},{4,0},{5,1},{6,2},{7,3},{8,12},{9,13},{10,... | collective-permute-start | bytes 245768 | tf_op jit(solution)/shard_map/ppermute | solution.py:9
  48.7 0.3 copy_subtract_fusion
  49.0 0.2 pad_maximum_fusion.2
  49.2 0.1 copy.39
  49.3 0.2 reduce-precision_convert_fusion.3
  49.5 2.5 %fusion.1 = f32[480,2048]{1,0:T(8,128)S(1)} fusion(s32[1024]{0:T(1024)S(1)} %bitcast.137, bf16[160,1024]{1,0:T(8,128)(2,1)S(1)} %get-tuple-element.39, bf16[160,1024]{1,0:T(8,128)(2,1)S(1)} %get-tuple-element.40, bf16[160,1024]{1,0:T(8,128)(2,1)S(1)} %get-tuple-element.38), kind=kOutput, calls=%fused_computation.2 | convolution fusion | flops 2018312192 | bytes 4919296 | tf_op jit(solution)/shard_map/dot_general | solution.py:43
  52.0 0.2 slice_add_fusion
  52.2 0.1 fusion.47
  52.3 0.1 squeeze.30
  52.4 0.1 squeeze.28
  52.5 0.9 %add_bitcast_fusion.1 = f32[4,10,2048]{2,0,1:T(4,128)} fusion(f32[10,4,2048]{2,1,0:T(4,128)S(1)} %fusion.38, f32[10,4,2048]{2,1,0:T(4,128)S(1)} %squeeze.28, f32[4,10,2048]{2,0,1:T(4,128)S(1)} %copy-done.1), kind=kLoop, calls=%fused_computation.53 | loop fusion | flops 245760 | bytes 1310720 | tf_op jit(solution)/shard_map/transpose | solution.py:160
  53.4 0.8 %fusion.22 = f32[4,10,2048]{2,0,1:T(4,128)} fusion(f32[10,4,2048]{2,1,0:T(4,128)S(1)} %squeeze.30, f32[4,10,2048]{2,0,1:T(4,128)S(1)} %copy-done.4, f32[9,4,2048]{2,1,0:T(4,128)S(1)} %copy-done.6), kind=kLoop, calls=%fused_computation.48 | loop fusion | flops 245760 | bytes 1277952 | tf_op jit(solution)/shard_map/transpose | solution.py:160
  54.3 0.1 squeeze.31
  54.5 2.4 %collective-permute-start.5 = (f32[2,10,2,256]{3,2,1,0:T(2,128)S(1)}, f32[2,10,2,256]{3,2,1,0:T(2,128)S(1)}, u32[]{:S(2)}, u32[]{:S(2)}) collective-permute-start(f32[2,10,2,256]{3,2,1,0:T(2,128)S(1)} %broadcast_select_fusion), channel_id=1, source_target_pairs={{0,2},{1,3},{2,0},{3,1},{4,6},{5,7},{6,4},{7,5},{8,10},{9,11},{10,... | collective-permute-start | bytes 122888 | tf_op jit(solution)/shard_map/ppermute | solution.py:9
  56.9 0.9 %fusion.20 = f32[4,10,2048]{2,0,1:T(4,128)} fusion(f32[10,4,2048]{2,1,0:T(4,128)S(1)} %squeeze.31, f32[4,10,2048]{2,0,1:T(4,128)S(1)} %copy-done.5, f32[9,4,2048]{2,1,0:T(4,128)S(1)} %copy-done.9, f32[9,4,2048]{2,1,0:T(4,128)S(1)} %copy-done.10), kind=kLoop, calls=%fused_computation.44 | loop fusion | flops 491520 | bytes 1572864 | tf_op jit(solution)/shard_map/transpose | solution.py:160
  57.8 0.1 squeeze.29
  57.9 4.0 %collective-permute-done.5 = f32[2,10,2,256]{3,2,1,0:T(2,128)S(1)} collective-permute-done((f32[2,10,2,256]{3,2,1,0:T(2,128)S(1)}, f32[2,10,2,256]{3,2,1,0:T(2,128)S(1)}, u32[]{:S(2)}, u32[]{:S(2)}) %collective-permute-start.5) | collective-permute-done | bytes 40992 | tf_op jit(solution)/shard_map/ppermute | solution.py:9
  61.9 3.1 %collective-permute-start.6 = (f32[2,10,1,256]{3,2,1,0:T(1,128)S(1)}, f32[2,10,1,256]{3,2,1,0:T(1,128)S(1)}, u32[]{:S(2)}, u32[]{:S(2)}) collective-permute-start(f32[2,10,1,256]{3,2,1,0:T(1,128)S(1)} %broadcast_select_fusion.1), channel_id=1, source_target_pairs={{0,1},{1,0},{2,3},{3,2},{4,5},{5,4},{6,7},{7,6},{8,9},{9,8},{10,11... | collective-permute-start | bytes 61448 | tf_op jit(solution)/shard_map/ppermute | solution.py:9
  65.1 0.9 %add_bitcast_fusion = f32[4,10,2048]{2,0,1:T(4,128)} fusion(f32[10,4,2048]{2,1,0:T(4,128)S(1)} %squeeze.29, f32[9,4,2048]{2,1,0:T(4,128)S(1)} %copy-done.8, f32[9,4,2048]{2,1,0:T(4,128)S(1)} %copy-done.7, f32[4,10,2048]{2,0,1:T(4,128)S(1)} %copy-done), kind=kLoop, calls=%fused_computation.52 | loop fusion | flops 573440 | bytes 1572864 | tf_op jit(solution)/shard_map/transpose | solution.py:160
  66.0 1.6 %collective-permute-done.6 = f32[2,10,1,256]{3,2,1,0:T(1,128)S(1)} collective-permute-done((f32[2,10,1,256]{3,2,1,0:T(1,128)S(1)}, f32[2,10,1,256]{3,2,1,0:T(1,128)S(1)}, u32[]{:S(2)}, u32[]{:S(2)}) %collective-permute-start.6) | collective-permute-done | bytes 20512 | tf_op jit(solution)/shard_map/ppermute | solution.py:9
  67.6 0.6 copy.62
  (60 shorter events, 0.8 us)
Async XLA Ops:
  0.6 2.2 %copy-start.1 = (f32[4,10,2048]{2,0,1:T(4,128)S(1)}, f32[4,10,2048]{2,0,1:T(4,128)}, u32[]{:S(2)}) copy-start(f32[4,10,2048]{2,0,1:T(4,128)} %param.13) | copy-start | bytes 983044
  0.6 2.2 %copy-start = (f32[4,10,2048]{2,0,1:T(4,128)S(1)}, f32[4,10,2048]{2,0,1:T(4,128)}, u32[]{:S(2)}) copy-start(f32[4,10,2048]{2,0,1:T(4,128)} %param.14) | copy-start | bytes 983044
  3.8 0.9 %copy-start.11 = (f32[10,2048]{1,0:T(8,128)S(1)}, f32[10,2048]{1,0:T(8,128)}, u32[]{:S(2)}) copy-start(f32[10,2048]{1,0:T(8,128)} %param.16) | copy-start | bytes 245764
  3.8 1.0 %copy-start.12 = (f32[10,2048]{1,0:T(8,128)S(1)}, f32[10,2048]{1,0:T(8,128)}, u32[]{:S(2)}) copy-start(f32[10,2048]{1,0:T(8,128)} %param.17) | copy-start | bytes 245764
  3.8 1.0 %copy-start.13 = (s32[10,2048]{1,0:T(8,128)S(1)}, s32[10,2048]{1,0:T(8,128)}, u32[]{:S(2)}) copy-start(s32[10,2048]{1,0:T(8,128)} %param.18) | copy-start | bytes 245764
  3.8 1.1 %copy-start.14 = (f32[10,2048]{1,0:T(8,128)S(1)}, f32[10,2048]{1,0:T(8,128)}, u32[]{:S(2)}) copy-start(f32[10,2048]{1,0:T(8,128)} %param.15) | copy-start | bytes 245764
  5.0 0.7 %copy-start.17 = (s32[4,256]{1,0:T(4,128)S(1)}, s32[4,256]{1,0:T(4,128)}, u32[]{:S(2)}) copy-start(s32[4,256]{1,0:T(4,128)} %param.20) | copy-start | bytes 12292
  8.7 0.7 %copy-start.16 = (f32[4,256]{1,0:T(4,128)S(1)}, f32[4,256]{1,0:T(4,128)}, u32[]{:S(2)}) copy-start(f32[4,256]{1,0:T(4,128)} %param.21) | copy-start | bytes 12292
  9.4 18.2 %copy-start.2 = (f32[10,4,2048]{2,1,0:T(4,128)S(1)}, f32[10,4,2048]{2,1,0:T(4,128)}, u32[]{:S(2)}) copy-start(f32[10,4,2048]{2,1,0:T(4,128)} %get-tuple-element.52) | copy-start | bytes 983044
  9.4 18.2 %copy-start.3 = (f32[10,4,2048]{2,1,0:T(4,128)S(1)}, f32[10,4,2048]{2,1,0:T(4,128)}, u32[]{:S(2)}) copy-start(f32[10,4,2048]{2,1,0:T(4,128)} %get-tuple-element.61) | copy-start | bytes 983044
  10.7 20.0 %collective-permute-start = (f32[4,10,4,256]{3,2,1,0:T(4,128)}, f32[4,10,4,256]{3,2,1,0:T(4,128)S(1)}, u32[]{:S(2)}, u32[]{:S(2)}) collective-permute-start(f32[4,10,4,256]{3,2,1,0:T(4,128)} %bitcast.95), channel_id=1, source_target_pairs={{0,8},{8,0},{16,24},{24,16},{32,40},{40,32},{48,56},{56,48},{64,72... | collective-permute-start | bytes 491528 | tf_op jit(solution)/shard_map/ppermute | solution.py:9
  13.3 17.4 %collective-permute-start.1 = (f32[4,10,4,256]{3,2,1,0:T(4,128)}, f32[4,10,4,256]{3,2,1,0:T(4,128)}, u32[]{:S(2)}, u32[]{:S(2)}) collective-permute-start(f32[4,10,4,256]{3,2,1,0:T(4,128)} %bitcast.94), channel_id=1, source_target_pairs={{0,16},{8,24},{16,0},{24,8},{32,48},{40,56},{48,32},{56,40},{64,80... | collective-permute-start | bytes 491528 | tf_op jit(solution)/shard_map/ppermute | solution.py:9
  16.4 16.7 %collective-permute-start.2 = (f32[4,10,4,256]{3,2,1,0:T(4,128)}, f32[4,10,4,256]{3,2,1,0:T(4,128)}, u32[]{:S(2)}, u32[]{:S(2)}) collective-permute-start(f32[4,10,4,256]{3,2,1,0:T(4,128)} %bitcast.93), channel_id=1, source_target_pairs={{0,32},{8,40},{16,48},{24,56},{32,0},{40,8},{48,16},{56,24},{64,96... | collective-permute-start | bytes 491528 | tf_op jit(solution)/shard_map/ppermute | solution.py:9
  21.6 18.3 %collective-permute-start.3 = (f32[4,10,4,256]{3,2,1,0:T(4,128)}, f32[4,10,4,256]{3,2,1,0:T(4,128)}, u32[]{:S(2)}, u32[]{:S(2)}) collective-permute-start(f32[4,10,4,256]{3,2,1,0:T(4,128)} %bitcast.96), channel_id=1, source_target_pairs={{0,64},{8,72},{16,80},{24,88},{32,96},{40,104},{48,112},{56,120},{... | collective-permute-start | bytes 491528 | tf_op jit(solution)/shard_map/ppermute | solution.py:9
  29.2 1.5 %copy-start.15 = (f32[4,2048]{1,0:T(4,128)S(1)}, f32[4,2048]{1,0:T(4,128)}, u32[]{:S(2)}) copy-start(f32[4,2048]{1,0:T(4,128)} %param.19) | copy-start | bytes 98308
  44.3 10.1 %collective-permute-start.4 = (f32[2,10,4,256]{3,2,1,0:T(4,128)}, f32[2,10,4,256]{3,2,1,0:T(4,128)S(1)}, u32[]{:S(2)}, u32[]{:S(2)}) collective-permute-start(f32[2,10,4,256]{3,2,1,0:T(4,128)} %slice_select_fusion), channel_id=1, source_target_pairs={{0,4},{1,5},{2,6},{3,7},{4,0},{5,1},{6,2},{7,3},{8,12},{9,13},{10,... | collective-permute-start | bytes 245768 | tf_op jit(solution)/shard_map/ppermute | solution.py:9
  52.3 1.1 %copy-start.4 = (f32[4,10,2048]{2,0,1:T(4,128)S(1)}, f32[4,10,2048]{2,0,1:T(4,128)}, u32[]{:S(2)}) copy-start(f32[4,10,2048]{2,0,1:T(4,128)} %param.22) | copy-start | bytes 983044
  52.3 1.1 %copy-start.6 = (f32[9,4,2048]{2,1,0:T(4,128)S(1)}, f32[9,4,2048]{2,1,0:T(4,128)}, u32[]{:S(2)}) copy-start(f32[9,4,2048]{2,1,0:T(4,128)} %get-tuple-element.57) | copy-start | bytes 884740
  52.5 4.3 %copy-start.5 = (f32[4,10,2048]{2,0,1:T(4,128)S(1)}, f32[4,10,2048]{2,0,1:T(4,128)}, u32[]{:S(2)}) copy-start(f32[4,10,2048]{2,0,1:T(4,128)} %param.23) | copy-start | bytes 983044
  53.4 3.5 %copy-start.9 = (f32[9,4,2048]{2,1,0:T(4,128)S(1)}, f32[9,4,2048]{2,1,0:T(4,128)}, u32[]{:S(2)}) copy-start(f32[9,4,2048]{2,1,0:T(4,128)} %get-tuple-element.25) | copy-start | bytes 884740
  53.4 3.5 %copy-start.10 = (f32[9,4,2048]{2,1,0:T(4,128)S(1)}, f32[9,4,2048]{2,1,0:T(4,128)}, u32[]{:S(2)}) copy-start(f32[9,4,2048]{2,1,0:T(4,128)} %get-tuple-element.49) | copy-start | bytes 884740
  54.3 10.8 %copy-start.7 = (f32[9,4,2048]{2,1,0:T(4,128)S(1)}, f32[9,4,2048]{2,1,0:T(4,128)}, u32[]{:S(2)}) copy-start(f32[9,4,2048]{2,1,0:T(4,128)} %get-tuple-element.48) | copy-start | bytes 884740
  54.3 10.8 %copy-start.8 = (f32[9,4,2048]{2,1,0:T(4,128)S(1)}, f32[9,4,2048]{2,1,0:T(4,128)}, u32[]{:S(2)}) copy-start(f32[9,4,2048]{2,1,0:T(4,128)} %get-tuple-element.50) | copy-start | bytes 884740
  54.5 7.4 %collective-permute-start.5 = (f32[2,10,2,256]{3,2,1,0:T(2,128)S(1)}, f32[2,10,2,256]{3,2,1,0:T(2,128)S(1)}, u32[]{:S(2)}, u32[]{:S(2)}) collective-permute-start(f32[2,10,2,256]{3,2,1,0:T(2,128)S(1)} %broadcast_select_fusion), channel_id=1, source_target_pairs={{0,2},{1,3},{2,0},{3,1},{4,6},{5,7},{6,4},{7,5},{8,10},{9,11},{10,... | collective-permute-start | bytes 122888 | tf_op jit(solution)/shard_map/ppermute | solution.py:9
  61.9 5.7 %collective-permute-start.6 = (f32[2,10,1,256]{3,2,1,0:T(1,128)S(1)}, f32[2,10,1,256]{3,2,1,0:T(1,128)S(1)}, u32[]{:S(2)}, u32[]{:S(2)}) collective-permute-start(f32[2,10,1,256]{3,2,1,0:T(1,128)S(1)} %broadcast_select_fusion.1), channel_id=1, source_target_pairs={{0,1},{1,0},{2,3},{3,2},{4,5},{5,4},{6,7},{7,6},{8,9},{9,8},{10,11... | collective-permute-start | bytes 61448 | tf_op jit(solution)/shard_map/ppermute | solution.py:9

commit v3 on v2

--- a/solution.py
+++ b/solution.py
@@ -64,6 +64,14 @@
         cur = keep + from_partner(send, axis, dist)
         dist //= 2
     return cur.reshape(value.shape[:-1] + (width,))
+
+
+def sum_scatter(value, axis):
+    size = lax.axis_size(axis)
+    width = value.shape[-1] // size
+    parts = value.reshape(value.shape[:-1] + (size, width))
+    got = lax.all_to_all(parts, axis, parts.ndim - 2, parts.ndim - 2, tiled=True)
+    return jnp.sum(got, axis=-2)
 
 
 def body(
@@ -141,7 +149,7 @@
         param_lat.reshape(2 * layers, rounds * face), select, 0
     ).reshape(2, layers, width)
     grads = (vert_grads + lat_grads) * jnp.stack([cond, therm])
-    owned = reduce_scatter(grads, "member")
+    owned = sum_scatter(grads, "member")
 
     lat = exact_select(
         jnp.concatenate([update, adj_lat]).reshape(4 * n_field, rounds * face),

time: 68.7 us -> 59 us (0.86)
  the two profiles are of different devices: /device:TPU:140 before, /device:TPU:1 now
where the time goes in v3:
time: 59 us; the launch traced here: 58.6 us
  starting transfers between devices  19.8 us (34%)
  other arithmetic  14.4 us (24%)
  waiting for transfers between devices  11.1 us (19%)
  matrix products  7.05 us (12%)
  local copies, waits for them, and re-layouts  5.03 us (9%)
  between operations  1.24 us (2%)
    ppermute x4, starting transfers between devices, from_partner(): return lax.ppermute(value, axis, pairs)  15.6 us
    ppermute x4, waiting for transfers between devices, from_partner(): return lax.ppermute(value, axis, pairs)  11.1 us
    dot_general x3, matrix products, exact_select(): lax.dot_general(split3(rows), select, (((1,), (contract,)), ((), ())), pr...  7.05 us
    transpose x4, other arithmetic, body(): return tuple((o.transpose(1, 0, 2) for o in outs)) + (owned,)  4.69 us
    all_to_all x1, starting transfers between devices, sum_scatter(): lax.all_to_all(parts, axis, parts.ndim - 2, parts.ndim - 2, tiled=True)  4.18 us
    unnamed x51, local copies, waits for them, and re-layouts  2.73 us
    another operation x2, other arithmetic, body(): jnp.stack([p_old, t_old, g_p, g_t]).reshape(4 * n_field, width)  2.66 us
    reduce_sum x1, other arithmetic, sum_scatter(): return jnp.sum(got, axis=-2)  1.58 us
  transfers between devices with their start and end apart: 5, of which 1 were waited for; matrix products, arithmetic and copies ran while one was open for 20% of the time, Pallas kernels for 0%

profile of v3, /device:TPU:1, one launch (start us, length us, event | category | flops | bytes accessed | tf_op | source)
XLA Modules:
  0.0 58.6 jit_solution(4701884352600851751)
XLA Ops:
  0.7 2.2 %fusion.43 = (f32[1,10,4,2048]{3,2,1,0:T(4,128)S(1)}, f32[10,4,2048]{2,1,0:T(4,128)}, f32[10,4,2048]{2,1,0:T(4,128)}, f32[1,10,4,2048]{3,2,1,0:T(4,128)S(1)}) fusion(f32[4,10,2048]{2,0,1:T(4,128)} %param.22, f32[4,10,2048]{2,0,1:T(4,128)} %param.23), kind=kLoop, calls=%fused_computation.118 | loop fusion | flops 163840 | bytes 1966080 | tf_op jit(solution)/shard_map/stack | solution.py:110
  2.9 0.4 pad_maximum_fusion
  3.3 0.5 reshape.99
  3.8 0.0 copy-start.10
  3.8 0.0 copy-start.11
  3.8 0.0 copy-start.12
  3.8 0.0 copy-start.13
  3.8 0.1 constant_dynamic-update-slice_fusion.1
  4.0 0.7 %copy-done.10 = f32[10,2048]{1,0:T(8,128)S(1)} copy-done((f32[10,2048]{1,0:T(8,128)S(1)}, f32[10,2048]{1,0:T(8,128)}, u32[]{:S(2)}) %copy-start.10) | copy-done | bytes 81944
  4.7 0.1 copy-done.11
  4.8 0.1 copy-done.12
  4.8 0.1 copy-done.13
  4.9 0.1 add_multiply_fusion.3
  5.0 0.0 copy-start.16
  5.0 0.4 reduce-precision_convert_fusion.1
  5.5 0.3 copy-done.16
  5.7 2.8 %fusion.2 = f32[540,1024]{1,0:T(8,128)S(1)} fusion(s32[1024]{0:T(1024)S(1)} %bitcast.138, bf16[180,2048]{1,0:T(8,128)(2,1)S(1)} %get-tuple-element.38, bf16[180,2048]{1,0:T(8,128)(2,1)S(1)} %get-tuple-element.39, bf16[180,2048]{1,0:T(8,128)(2,1)S(1)} %get-tuple-element.37), kind=kOutput, calls=%fused_computation.3 | convolution fusion | flops 2273656832 | bytes 4427776 | tf_op jit(solution)/shard_map/dot_general | solution.py:43
  8.5 0.2 slice_add_fusion.2
  8.7 0.0 copy-start.15
  8.7 0.1 fusion.47
  8.8 0.2 slice.152
  9.0 0.2 slice.150
  9.1 0.2 copy-done.15
  9.4 0.0 copy-start.2
  9.4 0.0 copy-start.3
  9.4 0.1 broadcast_multiply_fusion.1
  9.5 0.5 fusion.25
  10.0 8.8 %collective-permute-start = (f32[4,10,4,256]{3,2,1,0:T(4,128)S(1)}, f32[4,10,4,256]{3,2,1,0:T(4,128)S(1)}, u32[]{:S(2)}, u32[]{:S(2)}) collective-permute-start(f32[4,10,4,256]{3,2,1,0:T(4,128)S(1)} %bitcast.130), channel_id=1, source_target_pairs={{0,8},{8,0},{16,24},{24,16},{32,40},{40,32},{48,56},{56,48},{64,72... | collective-permute-start | bytes 491528 | tf_op jit(solution)/shard_map/ppermute | solution.py:9
  18.9 1.9 %collective-permute-start.1 = (f32[4,10,4,256]{3,2,1,0:T(4,128)S(1)}, f32[4,10,4,256]{3,2,1,0:T(4,128)S(1)}, u32[]{:S(2)}, u32[]{:S(2)}) collective-permute-start(f32[4,10,4,256]{3,2,1,0:T(4,128)S(1)} %bitcast.131), channel_id=1, source_target_pairs={{0,16},{8,24},{16,0},{24,8},{32,48},{40,56},{48,32},{56,40},{64,80... | collective-permute-start | bytes 491528 | tf_op jit(solution)/shard_map/ppermute | solution.py:9
  20.9 1.9 %collective-permute-start.2 = (f32[4,10,4,256]{3,2,1,0:T(4,128)S(1)}, f32[4,10,4,256]{3,2,1,0:T(4,128)S(1)}, u32[]{:S(2)}, u32[]{:S(2)}) collective-permute-start(f32[4,10,4,256]{3,2,1,0:T(4,128)S(1)} %bitcast.132), channel_id=1, source_target_pairs={{0,32},{8,40},{16,48},{24,56},{32,0},{40,8},{48,16},{56,24},{64,96... | collective-permute-start | bytes 491528 | tf_op jit(solution)/shard_map/ppermute | solution.py:9
  22.8 3.0 %collective-permute-start.3 = (f32[4,10,4,256]{3,2,1,0:T(4,128)S(1)}, f32[4,10,4,256]{3,2,1,0:T(4,128)S(1)}, u32[]{:S(2)}, u32[]{:S(2)}) collective-permute-start(f32[4,10,4,256]{3,2,1,0:T(4,128)S(1)} %bitcast.133), channel_id=1, source_target_pairs={{0,64},{8,72},{16,80},{24,88},{32,96},{40,104},{48,112},{56,120},{... | collective-permute-start | bytes 491528 | tf_op jit(solution)/shard_map/ppermute | solution.py:9
  25.9 0.4 multiply_reduce_fusion.2
  26.3 1.1 %multiply_multiply_fusion = (f32[9,4,2048]{2,1,0:T(4,128)}, f32[9,4,2048]{2,1,0:T(4,128)S(1)}, f32[9,4,2048]{2,1,0:T(4,128)}) fusion(f32[9,4,2048]{2,1,0:T(4,128)S(1)} %get-tuple-element.34, f32[10,4,2048]{2,1,0:T(4,128)S(1)} %bitcast.103, f32[9,2048]{1,0:T(8,128)S(1)} %get-tuple-element.74, f32[9,4,2048]{2,1,0:T(4,128)S(1)} %get-tuple-element.33), kind=kLoop, calls=%fused_computation.66 | loop fusion | flops 368640 | bytes 2138112 | tf_op jit(solution)/shard_map/mul | solution.py:166
  27.4 0.1 pad_subtract_fusion
  27.4 0.0 copy-start.14
  27.4 1.2 %multiply_reduce_fusion.1 = (f32[9,2048]{1,0:T(8,128)S(1)}, f32[9,4,2048]{2,1,0:T(4,128)}, f32[9,4,2048]{2,1,0:T(4,128)}, f32[9,4,2048]{2,1,0:T(4,128)}) fusion(f32[9,4,2048]{2,1,0:T(4,128)S(1)} %get-tuple-element.34, f32[10,4,2048]{2,1,0:T(4,128)S(1)} %bitcast.100, f32[9,2048]{1,0:T(8,128)S(1)} %get-tuple-element.73, f32[9,4,2048]{2,1,0:T(4,128)S(1)} %get-tuple-element.36), kind=kLoop, calls=%fused_computation.61 | loop fusion | flops 571392 | bytes 2211840 | tf_op jit(solution)/shard_map/reduce_sum | solution.py:145
  29.0 11.1 %collective-permute-done.2 = f32[4,10,4,256]{3,2,1,0:T(4,128)S(1)} collective-permute-done((f32[4,10,4,256]{3,2,1,0:T(4,128)S(1)}, f32[4,10,4,256]{3,2,1,0:T(4,128)S(1)}, u32[]{:S(2)}, u32[]{:S(2)}) %collective-permute-start.2) | collective-permute-done | bytes 163872 | tf_op jit(solution)/shard_map/ppermute | solution.py:9
  40.1 0.1 pad_maximum_fusion.1
  40.2 0.1 fusion.48
  40.3 0.3 multiply_reduce_fusion
  40.8 1.8 %fusion = f32[60,2048]{1,0:T(8,128)S(1)} fusion(s32[1024]{0:T(1024)S(1)} %bitcast.139, bf16[20,1024]{1,0:T(8,128)(2,1)S(1)} %get-tuple-element.69, bf16[20,1024]{1,0:T(8,128)(2,1)S(1)} %get-tuple-element.70, bf16[20,1024]{1,0:T(8,128)(2,1)S(1)} %get-tuple-element.68), kind=kOutput, calls=%fused_computation.1 | convolution fusion | flops 254124032 | bytes 618496 | tf_op jit(solution)/shard_map/dot_general | solution.py:43
  42.6 0.1 copy.61
  42.8 0.8 %copy.47 = f32[2,10,8,256]{3,0,1,2:T(2,128)} copy(f32[2,10,8,256]{3,2,1,0:T(8,128)S(1)} %fusion.27) | data formatting | bytes 327680 | tf_op jit(solution)/shard_map/mul | solution.py:151
  43.5 4.2 %all-to-all-start = ((f32[2,10,8,256]{3,0,1,2:T(2,128)}), f32[2,10,8,256]{3,0,1,2:T(2,128)}, u32[]{:S(2)}, u32[]{:S(2)}) async-start(f32[2,10,8,256]{3,0,1,2:T(2,128)} %copy.47), calls=%async_computation | async-start | bytes 327680 | tf_op jit(solution)/shard_map/all_to_all | solution.py:73
  47.7 0.3 copy_subtract_fusion
  48.0 0.2 pad_maximum_fusion.2
  48.2 0.1 copy.56
  48.3 0.2 reduce-precision_convert_fusion.3
  48.5 2.5 %fusion.1 = f32[480,2048]{1,0:T(8,128)S(1)} fusion(s32[1024]{0:T(1024)S(1)} %bitcast.140, bf16[160,1024]{1,0:T(8,128)(2,1)S(1)} %get-tuple-element.49, bf16[160,1024]{1,0:T(8,128)(2,1)S(1)} %get-tuple-element.50, bf16[160,1024]{1,0:T(8,128)(2,1)S(1)} %get-tuple-element.48), kind=kOutput, calls=%fused_computation.2 | convolution fusion | flops 2018312192 | bytes 4919296 | tf_op jit(solution)/shard_map/dot_general | solution.py:43
  51.0 0.2 slice_add_fusion
  51.2 0.1 fusion.46
  51.3 0.0 copy-start.4
  51.3 0.1 squeeze.31
  51.4 0.1 squeeze.30
  51.5 0.0 copy-start.5
  51.5 0.1 squeeze.29
  51.6 0.1 squeeze.28
  51.7 0.0 copy-start.6
  51.8 0.5 copy-done.4
  52.3 2.0 %fusion.22 = f32[4,10,2048]{2,0,1:T(4,128)} fusion(f32[10,4,2048]{2,1,0:T(4,128)S(1)} %squeeze.30, f32[4,10,2048]{2,0,1:T(4,128)S(1)} %copy-done.4, f32[9,4,2048]{2,1,0:T(4,128)} %get-tuple-element.67), kind=kLoop, calls=%fused_computation.48 | loop fusion | flops 245760 | bytes 1277952 | tf_op jit(solution)/shard_map/transpose | solution.py:168
  54.3 0.9 %add_bitcast_fusion.1 = f32[4,10,2048]{2,0,1:T(4,128)} fusion(f32[10,4,2048]{2,1,0:T(4,128)S(1)} %fusion.38, f32[10,4,2048]{2,1,0:T(4,128)S(1)} %squeeze.28, f32[4,10,2048]{2,0,1:T(4,128)S(1)} %copy-done.1), kind=kLoop, calls=%fused_computation.53 | loop fusion | flops 245760 | bytes 1310720 | tf_op jit(solution)/shard_map/transpose | solution.py:168
  55.1 0.9 %fusion.20 = f32[4,10,2048]{2,0,1:T(4,128)} fusion(f32[10,4,2048]{2,1,0:T(4,128)S(1)} %squeeze.31, f32[4,10,2048]{2,0,1:T(4,128)S(1)} %copy-done.5, f32[9,4,2048]{2,1,0:T(4,128)S(1)} %copy-done.6, f32[9,4,2048]{2,1,0:T(4,128)S(1)} %copy-done.9), kind=kLoop, calls=%fused_computation.44 | loop fusion | flops 491520 | bytes 1572864 | tf_op jit(solution)/shard_map/transpose | solution.py:168
  56.1 0.9 %add_bitcast_fusion = f32[4,10,2048]{2,0,1:T(4,128)} fusion(f32[10,4,2048]{2,1,0:T(4,128)S(1)} %squeeze.29, f32[9,4,2048]{2,1,0:T(4,128)S(1)} %copy-done.8, f32[9,4,2048]{2,1,0:T(4,128)S(1)} %copy-done.7, f32[4,10,2048]{2,0,1:T(4,128)S(1)} %copy-done), kind=kLoop, calls=%fused_computation.52 | loop fusion | flops 573440 | bytes 1572864 | tf_op jit(solution)/shard_map/transpose | solution.py:168
  57.0 1.6 %reduce_sum.42 = f32[2,10,256]{2,0,1:T(2,128)} reduce(f32[2,10,8,256]{3,0,1,2:T(2,128)} %all-to-all-done, f32[]{:T(128)} %constant.38.clone.1), dimensions={2}, to_apply=%region_3.4 | reduce | flops 35840 | bytes 184324 | tf_op jit(solution)/shard_map/reduce_sum | solution.py:74
  (49 shorter events, 0.8 us)
Async XLA Ops:
  0.6 2.2 %copy-start.1 = (f32[4,10,2048]{2,0,1:T(4,128)S(1)}, f32[4,10,2048]{2,0,1:T(4,128)}, u32[]{:S(2)}) copy-start(f32[4,10,2048]{2,0,1:T(4,128)} %param.13) | copy-start | bytes 983044
  0.6 2.2 %copy-start = (f32[4,10,2048]{2,0,1:T(4,128)S(1)}, f32[4,10,2048]{2,0,1:T(4,128)}, u32[]{:S(2)}) copy-start(f32[4,10,2048]{2,0,1:T(4,128)} %param.14) | copy-start | bytes 983044
  3.8 0.9 %copy-start.10 = (f32[10,2048]{1,0:T(8,128)S(1)}, f32[10,2048]{1,0:T(8,128)}, u32[]{:S(2)}) copy-start(f32[10,2048]{1,0:T(8,128)} %param.16) | copy-start | bytes 245764
  3.8 1.0 %copy-start.11 = (f32[10,2048]{1,0:T(8,128)S(1)}, f32[10,2048]{1,0:T(8,128)}, u32[]{:S(2)}) copy-start(f32[10,2048]{1,0:T(8,128)} %param.17) | copy-start | bytes 245764
  3.8 1.0 %copy-start.12 = (s32[10,2048]{1,0:T(8,128)S(1)}, s32[10,2048]{1,0:T(8,128)}, u32[]{:S(2)}) copy-start(s32[10,2048]{1,0:T(8,128)} %param.18) | copy-start | bytes 245764
  3.8 1.1 %copy-start.13 = (f32[10,2048]{1,0:T(8,128)S(1)}, f32[10,2048]{1,0:T(8,128)}, u32[]{:S(2)}) copy-start(f32[10,2048]{1,0:T(8,128)} %param.15) | copy-start | bytes 245764
  5.0 0.7 %copy-start.16 = (s32[4,256]{1,0:T(4,128)S(1)}, s32[4,256]{1,0:T(4,128)}, u32[]{:S(2)}) copy-start(s32[4,256]{1,0:T(4,128)} %param.20) | copy-start | bytes 12292
  8.7 0.7 %copy-start.15 = (f32[4,256]{1,0:T(4,128)S(1)}, f32[4,256]{1,0:T(4,128)}, u32[]{:S(2)}) copy-start(f32[4,256]{1,0:T(4,128)} %param.21) | copy-start | bytes 12292
  9.4 16.5 %copy-start.2 = (f32[10,4,2048]{2,1,0:T(4,128)S(1)}, f32[10,4,2048]{2,1,0:T(4,128)}, u32[]{:S(2)}) copy-start(f32[10,4,2048]{2,1,0:T(4,128)} %get-tuple-element.62) | copy-start | bytes 983044
  9.4 16.5 %copy-start.3 = (f32[10,4,2048]{2,1,0:T(4,128)S(1)}, f32[10,4,2048]{2,1,0:T(4,128)}, u32[]{:S(2)}) copy-start(f32[10,4,2048]{2,1,0:T(4,128)} %get-tuple-element.71) | copy-start | bytes 983044
  10.0 18.9 %collective-permute-start = (f32[4,10,4,256]{3,2,1,0:T(4,128)S(1)}, f32[4,10,4,256]{3,2,1,0:T(4,128)S(1)}, u32[]{:S(2)}, u32[]{:S(2)}) collective-permute-start(f32[4,10,4,256]{3,2,1,0:T(4,128)S(1)} %bitcast.130), channel_id=1, source_target_pairs={{0,8},{8,0},{16,24},{24,16},{32,40},{40,32},{48,56},{56,48},{64,72... | collective-permute-start | bytes 491528 | tf_op jit(solution)/shard_map/ppermute | solution.py:9
  18.9 10.1 %collective-permute-start.1 = (f32[4,10,4,256]{3,2,1,0:T(4,128)S(1)}, f32[4,10,4,256]{3,2,1,0:T(4,128)S(1)}, u32[]{:S(2)}, u32[]{:S(2)}) collective-permute-start(f32[4,10,4,256]{3,2,1,0:T(4,128)S(1)} %bitcast.131), channel_id=1, source_target_pairs={{0,16},{8,24},{16,0},{24,8},{32,48},{40,56},{48,32},{56,40},{64,80... | collective-permute-start | bytes 491528 | tf_op jit(solution)/shard_map/ppermute | solution.py:9
  20.9 19.2 %collective-permute-start.2 = (f32[4,10,4,256]{3,2,1,0:T(4,128)S(1)}, f32[4,10,4,256]{3,2,1,0:T(4,128)S(1)}, u32[]{:S(2)}, u32[]{:S(2)}) collective-permute-start(f32[4,10,4,256]{3,2,1,0:T(4,128)S(1)} %bitcast.132), channel_id=1, source_target_pairs={{0,32},{8,40},{16,48},{24,56},{32,0},{40,8},{48,16},{56,24},{64,96... | collective-permute-start | bytes 491528 | tf_op jit(solution)/shard_map/ppermute | solution.py:9
  22.8 17.2 %collective-permute-start.3 = (f32[4,10,4,256]{3,2,1,0:T(4,128)S(1)}, f32[4,10,4,256]{3,2,1,0:T(4,128)S(1)}, u32[]{:S(2)}, u32[]{:S(2)}) collective-permute-start(f32[4,10,4,256]{3,2,1,0:T(4,128)S(1)} %bitcast.133), channel_id=1, source_target_pairs={{0,64},{8,72},{16,80},{24,88},{32,96},{40,104},{48,112},{56,120},{... | collective-permute-start | bytes 491528 | tf_op jit(solution)/shard_map/ppermute | solution.py:9
  27.4 1.5 %copy-start.14 = (f32[4,2048]{1,0:T(4,128)S(1)}, f32[4,2048]{1,0:T(4,128)}, u32[]{:S(2)}) copy-start(f32[4,2048]{1,0:T(4,128)} %param.19) | copy-start | bytes 98308
  43.5 13.5 %all-to-all-start = ((f32[2,10,8,256]{3,0,1,2:T(2,128)}), f32[2,10,8,256]{3,0,1,2:T(2,128)}, u32[]{:S(2)}, u32[]{:S(2)}) async-start(f32[2,10,8,256]{3,0,1,2:T(2,128)} %copy.47), calls=%async_computation | async-start | bytes 327680 | tf_op jit(solution)/shard_map/all_to_all | solution.py:73
  51.3 1.0 %copy-start.4 = (f32[4,10,2048]{2,0,1:T(4,128)S(1)}, f32[4,10,2048]{2,0,1:T(4,128)}, u32[]{:S(2)}) copy-start(f32[4,10,2048]{2,0,1:T(4,128)} %param.22) | copy-start | bytes 983044
  51.5 3.6 %copy-start.5 = (f32[4,10,2048]{2,0,1:T(4,128)S(1)}, f32[4,10,2048]{2,0,1:T(4,128)}, u32[]{:S(2)}) copy-start(f32[4,10,2048]{2,0,1:T(4,128)} %param.23) | copy-start | bytes 983044
  51.7 3.4 %copy-start.6 = (f32[9,4,2048]{2,1,0:T(4,128)S(1)}, f32[9,4,2048]{2,1,0:T(4,128)}, u32[]{:S(2)}) copy-start(f32[9,4,2048]{2,1,0:T(4,128)} %get-tuple-element.35) | copy-start | bytes 884740
  51.7 3.4 %copy-start.9 = (f32[9,4,2048]{2,1,0:T(4,128)S(1)}, f32[9,4,2048]{2,1,0:T(4,128)}, u32[]{:S(2)}) copy-start(f32[9,4,2048]{2,1,0:T(4,128)} %get-tuple-element.59) | copy-start | bytes 884740
  52.3 3.8 %copy-start.7 = (f32[9,4,2048]{2,1,0:T(4,128)S(1)}, f32[9,4,2048]{2,1,0:T(4,128)}, u32[]{:S(2)}) copy-start(f32[9,4,2048]{2,1,0:T(4,128)} %get-tuple-element.58) | copy-start | bytes 884740
  52.3 3.8 %copy-start.8 = (f32[9,4,2048]{2,1,0:T(4,128)S(1)}, f32[9,4,2048]{2,1,0:T(4,128)}, u32[]{:S(2)}) copy-start(f32[9,4,2048]{2,1,0:T(4,128)} %get-tuple-element.60) | copy-start | bytes 884740

commit v4 on v3

--- a/solution.py
+++ b/solution.py
@@ -39,13 +39,17 @@
 
 
 def exact_select(rows, select, contract):
-    n = rows.shape[0]
     parts = lax.dot_general(
         split3(rows),
         select,
         (((1,), (contract,)), ((), ())),
         preferred_element_type=jnp.float32,
     )
+    return combine3(parts)
+
+
+def combine3(parts):
+    n = parts.shape[0] // 3
     return (parts[:n] + parts[n : 2 * n]) + parts[2 * n :]
 
 
@@ -111,23 +115,40 @@
             jnp.stack([cond, therm]).reshape(2 * layers, width),
         ]
     )
-    picked = exact_select(rows, select, 1)
-    fields_f = picked[: 4 * n_field].reshape(4, layers, members, rounds, face)
-    coefs_f = picked[4 * n_field :].reshape(2, layers, 1, rounds, face)
-    wc = face_weight * coefs_f
-    own = fields_f[:2]
-    g_own = fields_f[2:] * wc
-    sending = jnp.concatenate([own, g_own])
-
-    far = []
-    for index in range(rounds):
-        far.append(from_partner(sending[..., index, :], "space", 1 << index))
-    far = jnp.stack(far, axis=-2)
-
-    diff = far[:2] - own
-    update = wc * diff
-    adj_lat = far[2:] - g_own
-    param_lat = face_weight * jnp.sum(fields_f[2:] * diff, axis=2)
+    row_parts = split3(rows)
+
+    placed = None
+    for index in reversed(range(rounds)):
+        choose = select[index * face : (index + 1) * face]
+        weight = face_weight[index]
+        picked = combine3(
+            lax.dot_general(
+                row_parts,
+                choose,
+                (((1,), (1,)), ((), ())),
+                preferred_element_type=jnp.float32,
+            )
+        )
+        fields_f = picked[: 4 * n_field].reshape(4, layers, members, face)
+        coefs_f = picked[4 * n_field :].reshape(2, layers, 1, face)
+        wc = weight * coefs_f
+        own = fields_f[:2]
+        g_own = fields_f[2:] * wc
+        far = from_partner(jnp.concatenate([own, g_own]), "space", 1 << index)
+        diff = far[:2] - own
+        param_lat = weight * jnp.sum(fields_f[2:] * diff, axis=2)
+        back = jnp.concatenate(
+            [
+                param_lat.reshape(2 * layers, face),
+                jnp.concatenate([wc * diff, far[2:] - g_own]).reshape(
+                    4 * n_field, face
+                ),
+            ]
+        )
+        term = exact_select(back, choose, 0)
+        placed = term if placed is None else placed + term
+    lat_grads = placed[: 2 * layers].reshape(2, layers, width)
+    lat = placed[2 * layers :].reshape(4, layers, members, width)
 
     kf = (0.5 * (cond[:-1] + cond[1:]))[:, None]
     kt = (0.5 * (therm[:-1] + therm[1:]))[:, None]
@@ -145,17 +166,9 @@
     g_kt = jnp.sum(db * d_t, axis=1)
     vert_grads = jnp.stack([0.5 * pad_sum(g_kf, 0), 0.5 * pad_sum(g_kt, 0)])
 
-    lat_grads = exact_select(
-        param_lat.reshape(2 * layers, rounds * face), select, 0
-    ).reshape(2, layers, width)
     grads = (vert_grads + lat_grads) * jnp.stack([cond, therm])
     owned = sum_scatter(grads, "member")
 
-    lat = exact_select(
-        jnp.concatenate([update, adj_lat]).reshape(4 * n_field, rounds * face),
-        select,
-        0,
-    ).reshape(4, layers, members, width)
 
     p_rate = spread0(flow)
     p_rate = p_rate.at[0].add(recharge)

time: 59 us -> 92.1 us (1.56)
  other arithmetic: 14.4 us -> 35.1 us
  local copies, waits for them, and re-layouts: 5.03 us -> 18.1 us
  waiting for transfers between devices: 11.1 us -> 0.01 us
  matrix products: 7.05 us -> 13.6 us
  starting transfers between devices: 19.8 us -> 22.5 us
    ppermute x4, waiting for transfers between devices: 11.1 us -> 0.01 us  [from_partner(): return lax.ppermute(value, axis, pairs)]
    dot_general x0 -> x4, matrix products: none -> 8.08 us  [body(): lax.dot_general(row_parts, choose, (((1,), (1,)), ((), ())), preferred_el...]
    reduce_sum x1 -> x4, other arithmetic: 0.33 us -> 5.38 us  [body(): param_lat = weight * jnp.sum(fields_f[2:] * diff, axis=2)]
    reshape x1 -> x8, local copies, waits for them, and re-layouts: 0.04 us -> 4.87 us  [the longest x4 3.63 us: body(): jnp.concatenate([wc * diff, far[2:] - g_own]).reshape(4 * n_field, face)]
    concatenate x2 -> x8, other arithmetic: 0.65 us -> 4.92 us  [the longest x4 2.77 us: body(): far = from_partner(jnp.concatenate([own, g_own]), 'space', 1 << index)]
    add x3 -> x5, other arithmetic: 0.45 us -> 4.63 us  [the longest x1 4.48 us: body(): placed = term if placed is None else placed + term]
    mul x1 -> x8, other arithmetic: 0.01 us -> 2.25 us  [the longest x4 1.62 us: body(): wc = weight * coefs_f]
    all_to_all x1, starting transfers between devices: 4.18 us -> 5.96 us  [sum_scatter(): lax.all_to_all(parts, axis, parts.ndim - 2, parts.ndim - 2, tiled=True)]
  transfers between devices with their start and end apart: 5 -> 5, of which waited for: 1 -> 0; matrix products, arithmetic and copies ran while one was open for 20% -> 43% of each run, Pallas kernels for 0% -> 0%
where the time goes in v4:
time: 92.1 us; the launch traced here: 90.8 us
  other arithmetic  35.1 us (38%)
  starting transfers between devices  22.5 us (24%)
  local copies, waits for them, and re-layouts  18.1 us (20%)
  matrix products  13.6 us (15%)
  between operations  1.57 us (2%)
    ppermute x4, starting transfers between devices, from_partner(): return lax.ppermute(value, axis, pairs)  16.6 us
    dot_general x4, matrix products, body(): lax.dot_general(row_parts, choose, (((1,), (1,)), ((), ())), preferred_el...  8.08 us
    transpose x4, other arithmetic, body(): return tuple((o.transpose(1, 0, 2) for o in outs)) + (owned,)  6.11 us
    all_to_all x1, starting transfers between devices, sum_scatter(): lax.all_to_all(parts, axis, parts.ndim - 2, parts.ndim - 2, tiled=True)  5.96 us
    dot_general x4, matrix products, exact_select(): lax.dot_general(split3(rows), select, (((1,), (contract,)), ((), ())), pr...  5.48 us
    reduce_sum x4, other arithmetic, body(): param_lat = weight * jnp.sum(fields_f[2:] * diff, axis=2)  5.38 us
    add x1, other arithmetic, body(): placed = term if placed is None else placed + term  4.48 us
    reshape x4, local copies, waits for them, and re-layouts, body(): jnp.concatenate([wc * diff, far[2:] - g_own]).reshape(4 * n_field, face)  3.63 us
  transfers between devices with their start and end apart: 5, of which 0 were waited for; matrix products, arithmetic and copies ran while one was open for 43% of the time, Pallas kernels for 0%

profile of v4, /device:TPU:1, one launch (start us, length us, event | category | flops | bytes accessed | tf_op | source)
XLA Modules:
  0.0 90.8 jit_solution(5637528927312655987)
XLA Ops:
  0.7 2.2 %fusion.61 = (f32[1,10,4,2048]{3,2,1,0:T(4,128)S(1)}, f32[10,4,2048]{2,1,0:T(4,128)}, f32[10,4,2048]{2,1,0:T(4,128)}, f32[1,10,4,2048]{3,2,1,0:T(4,128)S(1)}) fusion(f32[4,10,2048]{2,0,1:T(4,128)} %param.22, f32[4,10,2048]{2,0,1:T(4,128)} %param.23), kind=kLoop, calls=%fused_computation.176 | loop fusion | flops 163840 | bytes 1966080 | tf_op jit(solution)/shard_map/stack | solution.py:114
  2.9 0.4 pad_maximum_fusion.1
  3.4 1.6 %reshape.163 = f32[160,2048]{1,0:T(8,128)} reshape(f32[4,10,4,2048]{3,2,1,0:T(4,128)S(1)} %pad_maximum_fusion.1) | data formatting | bytes 2621440 | tf_op jit(solution)/shard_map/reshape | solution.py:114
  4.9 1.4 %constant_dynamic-update-slice_fusion.1 = f32[180,2048]{1,0:T(8,128)S(1)} fusion(f32[160,2048]{1,0:T(8,128)} %reshape.163), kind=kLoop, calls=%fused_computation.171 | loop fusion | bytes 2621440
  6.6 0.4 reduce-precision_convert_fusion.1
  7.0 0.2 copy-done.34
  7.2 1.7 %iota_compare_fusion = pred[1024,2048]{1,0:T(32,128)(4,1)S(1)} fusion(s32[1024]{0:T(1024)S(1)} %bitcast.93), kind=kLoop, calls=%fused_computation | loop fusion | flops 2097152 | bytes 2101248 | tf_op jit(solution)/shard_map/eq | solution.py:107
  8.9 0.9 %fusion.14 = f32[540,256]{1,0:T(8,128)S(1)} fusion(pred[1024,2048]{1,0:T(32,128)(4,1)S(1)} %iota_compare_fusion, bf16[180,2048]{1,0:T(8,128)(2,1)S(1)} %get-tuple-element.42, bf16[180,2048]{1,0:T(8,128)(2,1)S(1)} %get-tuple-element.43, bf16[180,2048]{1,0:T(8,128)(2,1)S(1)} %get-tuple-element.41), kind=kOutput, calls=%fused_computation.20 | convolution fusion | flops 572866560 | bytes 3338240 | tf_op jit(solution)/shard_map/dot_general | solution.py:125
  10.1 0.7 pad_maximum_fusion.7
  10.8 8.3 %collective-permute-start = (f32[4,10,4,256]{3,2,1,0:T(4,128)}, f32[4,10,4,256]{3,2,1,0:T(4,128)}, u32[]{:S(2)}, u32[]{:S(2)}) collective-permute-start(f32[4,10,4,256]{3,2,1,0:T(4,128)} %pad_maximum_fusion.7), channel_id=1, source_target_pairs={{0,64},{8,72},{16,80},{24,88},{32,96},{40,104},{48,112},{56,120},{... | collective-permute-start | bytes 491528 | tf_op jit(solution)/shard_map/ppermute | solution.py:9
  19.1 2.4 %fusion.10 = f32[540,256]{1,0:T(8,128)S(1)} fusion(pred[1024,2048]{1,0:T(32,128)(4,1)S(1)} %iota_compare_fusion, bf16[180,2048]{1,0:T(8,128)(2,1)} %copy-done.9, bf16[180,2048]{1,0:T(8,128)(2,1)} %copy-done.10, bf16[180,2048]{1,0:T(8,128)(2,1)} %copy-done.8), kind=kOutput, calls=%fused_computation.16 | convolution fusion | flops 572866560 | bytes 3289088 | tf_op jit(solution)/shard_map/dot_general | solution.py:125
  21.7 0.7 pad_maximum_fusion.9
  22.4 2.4 %collective-permute-start.1 = (f32[4,10,4,256]{3,2,1,0:T(4,128)}, f32[4,10,4,256]{3,2,1,0:T(4,128)}, u32[]{:S(2)}, u32[]{:S(2)}) collective-permute-start(f32[4,10,4,256]{3,2,1,0:T(4,128)} %pad_maximum_fusion.9), channel_id=1, source_target_pairs={{0,32},{8,40},{16,48},{24,56},{32,0},{40,8},{48,16},{56,24},{64,96... | collective-permute-start | bytes 491528 | tf_op jit(solution)/shard_map/ppermute | solution.py:9
  24.8 2.4 %fusion.6 = f32[540,256]{1,0:T(8,128)S(1)} fusion(pred[1024,2048]{1,0:T(32,128)(4,1)S(1)} %iota_compare_fusion, bf16[180,2048]{1,0:T(8,128)(2,1)} %copy-done.9, bf16[180,2048]{1,0:T(8,128)(2,1)} %copy-done.10, bf16[180,2048]{1,0:T(8,128)(2,1)} %copy-done.8), kind=kOutput, calls=%fused_computation.12 | convolution fusion | flops 572866560 | bytes 3289088 | tf_op jit(solution)/shard_map/dot_general | solution.py:125
  27.3 0.6 fusion.67
  27.9 0.6 reshape.169
  28.6 0.9 %slice.321 = f32[2,10,4,256]{3,2,1,0:T(4,128)S(1)} reshape(f32[80,256]{1,0:T(8,128)} %get-tuple-element.76) | data formatting | bytes 163840 | tf_op jit(solution)/shard_map/slice | solution.py:139
  29.5 0.8 broadcast_multiply_fusion.13
  30.3 0.7 pad_maximum_fusion.11
  31.0 2.3 %collective-permute-start.2 = (f32[4,10,4,256]{3,2,1,0:T(4,128)}, f32[4,10,4,256]{3,2,1,0:T(4,128)}, u32[]{:S(2)}, u32[]{:S(2)}) collective-permute-start(f32[4,10,4,256]{3,2,1,0:T(4,128)} %pad_maximum_fusion.11), channel_id=1, source_target_pairs={{0,16},{8,24},{16,0},{24,8},{32,48},{40,56},{48,32},{56,40},{64,80... | collective-permute-start | bytes 491528 | tf_op jit(solution)/shard_map/ppermute | solution.py:9
  33.4 2.4 %fusion.2 = f32[540,256]{1,0:T(8,128)S(1)} fusion(pred[1024,2048]{1,0:T(32,128)(4,1)S(1)} %iota_compare_fusion, bf16[180,2048]{1,0:T(8,128)(2,1)} %copy-done.9, bf16[180,2048]{1,0:T(8,128)(2,1)} %copy-done.10, bf16[180,2048]{1,0:T(8,128)(2,1)} %copy-done.8), kind=kOutput, calls=%fused_computation.8 | convolution fusion | flops 572866560 | bytes 3289088 | tf_op jit(solution)/shard_map/dot_general | solution.py:125
  35.8 0.6 fusion.68
  36.5 0.6 reshape.171
  37.1 0.9 %slice.336 = f32[2,10,4,256]{3,2,1,0:T(4,128)S(1)} reshape(f32[80,256]{1,0:T(8,128)} %get-tuple-element.81) | data formatting | bytes 163840 | tf_op jit(solution)/shard_map/slice | solution.py:139
  38.1 0.8 broadcast_multiply_fusion.12
  38.9 0.7 pad_maximum_fusion.13
  39.6 3.6 %collective-permute-start.3 = (f32[4,10,4,256]{3,2,1,0:T(4,128)}, f32[4,10,4,256]{3,2,1,0:T(4,128)}, u32[]{:S(2)}, u32[]{:S(2)}) collective-permute-start(f32[4,10,4,256]{3,2,1,0:T(4,128)} %pad_maximum_fusion.13), channel_id=1, source_target_pairs={{0,8},{8,0},{16,24},{24,16},{32,40},{40,32},{48,56},{56,48},{64,72... | collective-permute-start | bytes 491528 | tf_op jit(solution)/shard_map/ppermute | solution.py:9
  43.3 1.8 %multiply_reduce_fusion.1 = (f32[9,2048]{1,0:T(8,128)S(1)}, f32[9,4,2048]{2,1,0:T(4,128)S(1)}, f32[9,4,2048]{2,1,0:T(4,128)S(1)}) fusion(f32[10,4,2048]{2,1,0:T(4,128)S(1)} %bitcast.78, f32[10,4,2048]{2,1,0:T(4,128)S(1)} %bitcast.75, f32[10,4,2048]{2,1,0:T(4,128)} %get-tuple-element.49, f32[10,4,2048]{2,1,0:T(4,128)} %get-tuple-element.91), kind=kLoop, calls=%fused_computation.54 | loop fusion | flops 718848 | bytes 3022848 | tf_op jit(solution)/shard_map/reduce_sum | solution.py:165
  45.0 1.1 %multiply_multiply_fusion = (f32[9,4,2048]{2,1,0:T(4,128)}, f32[9,4,2048]{2,1,0:T(4,128)S(1)}, f32[9,4,2048]{2,1,0:T(4,128)}) fusion(f32[9,4,2048]{2,1,0:T(4,128)S(1)} %get-tuple-element.34, f32[10,4,2048]{2,1,0:T(4,128)S(1)} %bitcast.79, f32[9,2048]{1,0:T(8,128)S(1)} %get-tuple-element.94, f32[9,4,2048]{2,1,0:T(4,128)S(1)} %get-tuple-element.33), kind=kLoop, calls=%fused_computation.94 | loop fusion | flops 368640 | bytes 2138112 | tf_op jit(solution)/shard_map/mul | solution.py:179
  46.2 1.1 %multiply_reduce_fusion = (f32[9,2048]{1,0:T(8,128)S(1)}, f32[9,4,2048]{2,1,0:T(4,128)}, f32[9,4,2048]{2,1,0:T(4,128)}, f32[9,4,2048]{2,1,0:T(4,128)}) fusion(f32[9,4,2048]{2,1,0:T(4,128)S(1)} %get-tuple-element.34, f32[10,4,2048]{2,1,0:T(4,128)S(1)} %bitcast.76, f32[9,2048]{1,0:T(8,128)S(1)} %get-tuple-element.93, f32[9,4,2048]{2,1,0:T(4,128)S(1)} %get-tuple-element.36), kind=kLoop, calls=%fused_computation.53 | loop fusion | flops 571392 | bytes 2211840 | tf_op jit(solution)/shard_map/reduce_sum | solution.py:166
  47.4 0.7 slice_bitcast_fusion.2
  48.3 0.7 slice_bitcast_fusion
  49.0 0.7 copy-done.2
  49.7 0.6 slice_bitcast_fusion.3
  50.3 1.6 %multiply_reduce_fusion.5 = (f32[2,10,256]{2,1,0:T(8,128)}, f32[2,10,4,256]{3,2,1,0:T(4,128)S(1)}, f32[2,10,4,256]{3,2,1,0:T(4,128)S(1)}) fusion(f32[2,10,4,256]{3,2,1,0:T(4,128)S(1)} %copy-done.16, f32[2,10,4,256]{3,2,1,0:T(4,128)S(1)} %slice.293, f32[4,10,4,256]{3,2,1,0:T(4,128)} %collective-permute-done, f32[2,10,256]{2,1,0:T(8,128)S(1)} %broadcast_multiply_fusion.15), kind=kLoop, calls=%fused_computation.149 | loop fusion | flops 117760 | bytes 532480 | tf_op jit(solution)/shard_map/reduce_sum | solution.py:139
  52.1 0.8 reduce_sum.72
  52.8 0.6 broadcast_multiply_fusion.19
  53.4 1.6 %multiply_reduce_fusion.4 = (f32[2,10,256]{2,1,0:T(8,128)}, f32[2,10,4,256]{3,2,1,0:T(4,128)S(1)}, f32[2,10,4,256]{3,2,1,0:T(4,128)S(1)}) fusion(f32[2,10,4,256]{3,2,1,0:T(4,128)S(1)} %copy-done.18, f32[2,10,4,256]{3,2,1,0:T(4,128)S(1)} %slice.308, f32[4,10,4,256]{3,2,1,0:T(4,128)} %collective-permute-done.1, f32[2,10,256]{2,1,0:T(8,128)S(1)} %broadcast_multiply_fusion.14), kind=kLoop, calls=%fused_computation.148 | loop fusion | flops 117760 | bytes 532480 | tf_op jit(solution)/shard_map/reduce_sum | solution.py:139
  55.1 0.7 pad_maximum_fusion.10
  55.8 1.0 %reshape.168 = f32[160,256]{1,0:T(8,128)S(1)} reshape(f32[4,10,4,256]{3,2,1,0:T(4,128)} %pad_maximum_fusion.10) | data formatting | bytes 327680 | tf_op jit(solution)/shard_map/reshape | solution.py:143
  56.8 0.8 reduce_sum.74
  57.6 1.1 %multiply_reduce_fusion.3 = (f32[2,10,256]{2,1,0:T(8,128)S(1)}, f32[2,10,4,256]{3,2,1,0:T(4,128)S(1)}, f32[2,10,4,256]{3,2,1,0:T(4,128)S(1)}) fusion(f32[2,10,4,256]{3,2,1,0:T(4,128)} %copy-done.19, f32[2,10,4,256]{3,2,1,0:T(4,128)S(1)} %copy-done.12, f32[4,10,4,256]{3,2,1,0:T(4,128)} %collective-permute-done.2, f32[2,10,256]{2,1,0:T(8,128)} %copy-done.26), kind=kLoop, calls=%fused_computation.147 | loop fusion | flops 117760 | bytes 532480 | tf_op jit(solution)/shard_map/reduce_sum | solution.py:139
  58.6 0.7 pad_maximum_fusion.12
  59.3 1.6 %reshape.170 = f32[160,256]{1,0:T(8,128)} reshape(f32[4,10,4,256]{3,2,1,0:T(4,128)} %pad_maximum_fusion.12) | data formatting | bytes 327680 | tf_op jit(solution)/shard_map/reshape | solution.py:143
  61.0 1.0 %multiply_reduce_fusion.2 = (f32[2,10,256]{2,1,0:T(8,128)S(1)}, f32[2,10,4,256]{3,2,1,0:T(4,128)S(1)}, f32[2,10,4,256]{3,2,1,0:T(4,128)S(1)}) fusion(f32[2,10,4,256]{3,2,1,0:T(4,128)S(1)} %copy-done.21, f32[2,10,4,256]{3,2,1,0:T(4,128)S(1)} %copy-done.14, f32[4,10,4,256]{3,2,1,0:T(4,128)} %collective-permute-done.3, f32[2,10,256]{2,1,0:T(8,128)} %copy-done.27), kind=kLoop, calls=%fused_computation.146 | loop fusion | flops 117760 | bytes 532480 | tf_op jit(solution)/shard_map/reduce_sum | solution.py:139
  62.0 0.7 pad_maximum_fusion.14
  62.7 1.0 %reshape.172 = f32[160,256]{1,0:T(8,128)S(1)} reshape(f32[4,10,4,256]{3,2,1,0:T(4,128)} %pad_maximum_fusion.14) | data formatting | bytes 327680 | tf_op jit(solution)/shard_map/reshape | solution.py:143
  63.9 1.0 %reduce-precision_convert_fusion.5 = (bf16[180,256]{1,0:T(8,128)(2,1)S(1)}, bf16[180,256]{1,0:T(8,128)(2,1)S(1)}, bf16[180,256]{1,0:T(8,128)(2,1)S(1)}) fusion(f32[160,256]{1,0:T(8,128)} %reshape.170, f32[20,256]{1,0:T(8,128)S(1)} %broadcast_multiply_fusion.17), kind=kLoop, calls=%fused_computation.83 | loop fusion | flops 368640 | bytes 460800 | tf_op jit(solution)/shard_map/convert_element_type | solution.py:37
  64.9 0.9 fusion.12
  65.8 0.9 fusion.8
  66.6 0.9 fusion.4
  67.5 2.9 %fusion = f32[540,2048]{1,0:T(8,128)} fusion(pred[1024,2048]{1,0:T(32,128)(4,1)S(1)} %iota_compare_fusion, bf16[180,256]{1,0:T(8,128)(2,1)S(1)} %get-tuple-element.79, bf16[180,256]{1,0:T(8,128)(2,1)S(1)} %get-tuple-element.78, bf16[180,256]{1,0:T(8,128)(2,1)S(1)} %get-tuple-element.77), kind=kOutput, calls=%fused_computation.6 | convolution fusion | flops 567060480 | bytes 5230592 | tf_op jit(solution)/shard_map/dot_general | solution.py:42
  70.4 4.5 %fusion.17 = f32[180,2048]{1,0:T(8,128)S(1)} fusion(f32[540,2048]{1,0:T(8,128)} %fusion, f32[540,2048]{1,0:T(8,128)S(1)} %fusion.4, f32[540,2048]{1,0:T(8,128)S(1)} %fusion.8, f32[540,2048]{1,0:T(8,128)S(1)} %fusion.12), kind=kLoop, calls=%fused_computation.24 | loop fusion | flops 4055040 | bytes 19169280 | tf_op jit(solution)/shard_map/add | solution.py:149
  74.9 0.8 fusion.64
  75.9 0.8 copy.22
  76.7 6.0 %all-to-all-start = ((f32[2,10,8,256]{3,0,1,2:T(2,128)}), f32[2,10,8,256]{3,0,1,2:T(2,128)}, u32[]{:S(2)}, u32[]{:S(2)}) async-start(f32[2,10,8,256]{3,0,1,2:T(2,128)} %copy.22), calls=%async_computation | async-start | bytes 327680 | tf_op jit(solution)/shard_map/all_to_all | solution.py:77
  82.7 0.1 squeeze.15
  82.9 0.1 squeeze.13
  83.0 0.1 squeeze.12
  83.1 2.1 %fusion.24 = f32[4,10,2048]{2,0,1:T(4,128)} fusion(f32[10,4,2048]{2,1,0:T(4,128)S(1)} %squeeze.14, f32[4,10,2048]{2,0,1:T(4,128)} %param.22, f32[9,4,2048]{2,1,0:T(4,128)} %get-tuple-element.86), kind=kLoop, calls=%fused_computation.43 | loop fusion | flops 245760 | bytes 1277952 | tf_op jit(solution)/shard_map/transpose | solution.py:181
  85.2 0.9 add_bitcast_fusion.1
  86.1 2.2 %fusion.22 = f32[4,10,2048]{2,0,1:T(4,128)} fusion(f32[10,4,2048]{2,1,0:T(4,128)S(1)} %squeeze.15, f32[4,10,2048]{2,0,1:T(4,128)S(1)} %copy-done.5, f32[9,4,2048]{2,1,0:T(4,128)} %get-tuple-element.35, f32[9,4,2048]{2,1,0:T(4,128)} %get-tuple-element.46), kind=kLoop, calls=%fused_computation.39 | loop fusion | flops 491520 | bytes 1572864 | tf_op jit(solution)/shard_map/transpose | solution.py:181
  88.3 0.9 %add_bitcast_fusion = f32[4,10,2048]{2,0,1:T(4,128)} fusion(f32[10,4,2048]{2,1,0:T(4,128)S(1)} %squeeze.13, f32[9,4,2048]{2,1,0:T(4,128)S(1)} %copy-done.7, f32[9,4,2048]{2,1,0:T(4,128)S(1)} %copy-done.6, f32[4,10,2048]{2,0,1:T(4,128)S(1)} %copy-done), kind=kLoop, calls=%fused_computation.44 | loop fusion | flops 573440 | bytes 1572864 | tf_op jit(solution)/shard_map/transpose | solution.py:181
  89.3 1.6 %reduce_sum.81 = f32[2,10,256]{2,0,1:T(2,128)} reduce(f32[2,10,8,256]{3,0,1,2:T(2,128)} %all-to-all-done, f32[]{:T(128)} %constant.38.clone.1), dimensions={2}, to_apply=%region_6.7 | reduce | flops 35840 | bytes 184324 | tf_op jit(solution)/shard_map/reduce_sum | solution.py:78
  (129 shorter events, 1.6 us)
Async XLA Ops:
  0.6 2.2 %copy-start.1 = (f32[4,10,2048]{2,0,1:T(4,128)S(1)}, f32[4,10,2048]{2,0,1:T(4,128)}, u32[]{:S(2)}) copy-start(f32[4,10,2048]{2,0,1:T(4,128)} %param.13) | copy-start | bytes 983044
  0.6 2.2 %copy-start = (f32[4,10,2048]{2,0,1:T(4,128)S(1)}, f32[4,10,2048]{2,0,1:T(4,128)}, u32[]{:S(2)}) copy-start(f32[4,10,2048]{2,0,1:T(4,128)} %param.14) | copy-start | bytes 983044
  3.3 3.0 %copy-start.28 = (f32[10,2048]{1,0:T(8,128)S(1)}, f32[10,2048]{1,0:T(8,128)}, u32[]{:S(2)}) copy-start(f32[10,2048]{1,0:T(8,128)} %param.16) | copy-start | bytes 245764
  3.3 3.0 %copy-start.29 = (f32[10,2048]{1,0:T(8,128)S(1)}, f32[10,2048]{1,0:T(8,128)}, u32[]{:S(2)}) copy-start(f32[10,2048]{1,0:T(8,128)} %param.17) | copy-start | bytes 245764
  3.3 3.0 %copy-start.30 = (s32[10,2048]{1,0:T(8,128)S(1)}, s32[10,2048]{1,0:T(8,128)}, u32[]{:S(2)}) copy-start(s32[10,2048]{1,0:T(8,128)} %param.18) | copy-start | bytes 245764
  3.4 3.0 %copy-start.31 = (f32[10,2048]{1,0:T(8,128)S(1)}, f32[10,2048]{1,0:T(8,128)}, u32[]{:S(2)}) copy-start(f32[10,2048]{1,0:T(8,128)} %param.15) | copy-start | bytes 245764
  6.5 0.7 copy-start.34
  7.0 2.9 %copy-start.8 = (bf16[180,2048]{1,0:T(8,128)(2,1)}, bf16[180,2048]{1,0:T(8,128)(2,1)S(1)}, u32[]{:S(2)}) copy-start(bf16[180,2048]{1,0:T(8,128)(2,1)S(1)} %get-tuple-element.41) | copy-start | bytes 2211844
  7.0 2.9 %copy-start.9 = (bf16[180,2048]{1,0:T(8,128)(2,1)}, bf16[180,2048]{1,0:T(8,128)(2,1)S(1)}, u32[]{:S(2)}) copy-start(bf16[180,2048]{1,0:T(8,128)(2,1)S(1)} %get-tuple-element.42) | copy-start | bytes 2211844
  7.0 2.9 %copy-start.10 = (bf16[180,2048]{1,0:T(8,128)(2,1)}, bf16[180,2048]{1,0:T(8,128)(2,1)S(1)}, u32[]{:S(2)}) copy-start(bf16[180,2048]{1,0:T(8,128)(2,1)S(1)} %get-tuple-element.43) | copy-start | bytes 2211844
  8.9 1.1 %copy-start.35 = (f32[4,256]{1,0:T(4,128)S(1)}, f32[4,256]{1,0:T(4,128)}, u32[]{:S(2)}) copy-start(f32[4,256]{1,0:T(4,128)} %param.21) | copy-start | bytes 12292
  10.0 9.1 %copy-start.15 = (f32[2,10,4,256]{3,2,1,0:T(4,128)}, f32[2,10,4,256]{3,2,1,0:T(4,128)S(1)}, u32[]{:S(2)}) copy-start(f32[2,10,4,256]{3,2,1,0:T(4,128)S(1)} %slice.291) | copy-start | bytes 245764
  10.8 39.5 %collective-permute-start = (f32[4,10,4,256]{3,2,1,0:T(4,128)}, f32[4,10,4,256]{3,2,1,0:T(4,128)}, u32[]{:S(2)}, u32[]{:S(2)}) collective-permute-start(f32[4,10,4,256]{3,2,1,0:T(4,128)} %pad_maximum_fusion.7), channel_id=1, source_target_pairs={{0,64},{8,72},{16,80},{24,88},{32,96},{40,104},{48,112},{56,120},{... | collective-permute-start | bytes 491528 | tf_op jit(solution)/shard_map/ppermute | solution.py:9
  21.6 3.2 %copy-start.17 = (f32[2,10,4,256]{3,2,1,0:T(4,128)}, f32[2,10,4,256]{3,2,1,0:T(4,128)S(1)}, u32[]{:S(2)}) copy-start(f32[2,10,4,256]{3,2,1,0:T(4,128)S(1)} %slice.306) | copy-start | bytes 245764
  22.4 31.0 %collective-permute-start.1 = (f32[4,10,4,256]{3,2,1,0:T(4,128)}, f32[4,10,4,256]{3,2,1,0:T(4,128)}, u32[]{:S(2)}, u32[]{:S(2)}) collective-permute-start(f32[4,10,4,256]{3,2,1,0:T(4,128)} %pad_maximum_fusion.9), channel_id=1, source_target_pairs={{0,32},{8,40},{16,48},{24,56},{32,0},{40,8},{48,16},{56,24},{64,96... | collective-permute-start | bytes 491528 | tf_op jit(solution)/shard_map/ppermute | solution.py:9
  29.5 3.9 %copy-start.19 = (f32[2,10,4,256]{3,2,1,0:T(4,128)}, f32[2,10,4,256]{3,2,1,0:T(4,128)S(1)}, u32[]{:S(2)}) copy-start(f32[2,10,4,256]{3,2,1,0:T(4,128)S(1)} %slice.321) | copy-start | bytes 245764
  29.5 3.8 %copy-start.11 = (f32[2,10,4,256]{3,2,1,0:T(4,128)}, f32[2,10,4,256]{3,2,1,0:T(4,128)S(1)}, u32[]{:S(2)}) copy-start(f32[2,10,4,256]{3,2,1,0:T(4,128)S(1)} %slice.323) | copy-start | bytes 245764
  30.3 5.4 %copy-start.26 = (f32[2,10,256]{2,1,0:T(8,128)}, f32[2,10,256]{2,1,0:T(8,128)S(1)}, u32[]{:S(2)}) copy-start(f32[2,10,256]{2,1,0:T(8,128)S(1)} %broadcast_multiply_fusion.13) | copy-start | bytes 61444
  31.0 26.5 %collective-permute-start.2 = (f32[4,10,4,256]{3,2,1,0:T(4,128)}, f32[4,10,4,256]{3,2,1,0:T(4,128)}, u32[]{:S(2)}, u32[]{:S(2)}) collective-permute-start(f32[4,10,4,256]{3,2,1,0:T(4,128)} %pad_maximum_fusion.11), channel_id=1, source_target_pairs={{0,16},{8,24},{16,0},{24,8},{32,48},{40,56},{48,32},{56,40},{64,80... | collective-permute-start | bytes 491528 | tf_op jit(solution)/shard_map/ppermute | solution.py:9
  38.0 5.2 %copy-start.20 = (f32[2,10,4,256]{3,2,1,0:T(4,128)}, f32[2,10,4,256]{3,2,1,0:T(4,128)S(1)}, u32[]{:S(2)}) copy-start(f32[2,10,4,256]{3,2,1,0:T(4,128)S(1)} %slice.336) | copy-start | bytes 245764
  38.0 5.2 %copy-start.13 = (f32[2,10,4,256]{3,2,1,0:T(4,128)}, f32[2,10,4,256]{3,2,1,0:T(4,128)S(1)}, u32[]{:S(2)}) copy-start(f32[2,10,4,256]{3,2,1,0:T(4,128)S(1)} %slice.338) | copy-start | bytes 245764
  38.9 4.4 %copy-start.27 = (f32[2,10,256]{2,1,0:T(8,128)}, f32[2,10,256]{2,1,0:T(8,128)S(1)}, u32[]{:S(2)}) copy-start(f32[2,10,256]{2,1,0:T(8,128)S(1)} %broadcast_multiply_fusion.12) | copy-start | bytes 61444
  39.6 21.4 %collective-permute-start.3 = (f32[4,10,4,256]{3,2,1,0:T(4,128)}, f32[4,10,4,256]{3,2,1,0:T(4,128)}, u32[]{:S(2)}, u32[]{:S(2)}) collective-permute-start(f32[4,10,4,256]{3,2,1,0:T(4,128)} %pad_maximum_fusion.13), channel_id=1, source_target_pairs={{0,8},{8,0},{16,24},{24,16},{32,40},{40,32},{48,56},{56,48},{64,72... | collective-permute-start | bytes 491528 | tf_op jit(solution)/shard_map/ppermute | solution.py:9
  46.2 2.8 %copy-start.33 = (f32[4,2048]{1,0:T(4,128)S(1)}, f32[4,2048]{1,0:T(4,128)}, u32[]{:S(2)}) copy-start(f32[4,2048]{1,0:T(4,128)} %param.19) | copy-start | bytes 98308
  46.2 4.1 %copy-start.16 = (f32[2,10,4,256]{3,2,1,0:T(4,128)S(1)}, f32[2,10,4,256]{3,2,1,0:T(4,128)}, u32[]{:S(2)}) copy-start(f32[2,10,4,256]{3,2,1,0:T(4,128)} %copy-done.15) | copy-start | bytes 245764
  47.3 6.1 %copy-start.18 = (f32[2,10,4,256]{3,2,1,0:T(4,128)S(1)}, f32[2,10,4,256]{3,2,1,0:T(4,128)}, u32[]{:S(2)}) copy-start(f32[2,10,4,256]{3,2,1,0:T(4,128)} %copy-done.17) | copy-start | bytes 245764
  48.1 9.4 %copy-start.12 = (f32[2,10,4,256]{3,2,1,0:T(4,128)S(1)}, f32[2,10,4,256]{3,2,1,0:T(4,128)}, u32[]{:S(2)}) copy-start(f32[2,10,4,256]{3,2,1,0:T(4,128)} %copy-done.11) | copy-start | bytes 245764
  48.9 0.7 copy-start.2
  49.7 11.3 %copy-start.14 = (f32[2,10,4,256]{3,2,1,0:T(4,128)S(1)}, f32[2,10,4,256]{3,2,1,0:T(4,128)}, u32[]{:S(2)}) copy-start(f32[2,10,4,256]{3,2,1,0:T(4,128)} %copy-done.13) | copy-start | bytes 245764
  49.7 11.3 %copy-start.21 = (f32[2,10,4,256]{3,2,1,0:T(4,128)S(1)}, f32[2,10,4,256]{3,2,1,0:T(4,128)}, u32[]{:S(2)}) copy-start(f32[2,10,4,256]{3,2,1,0:T(4,128)} %copy-done.20) | copy-start | bytes 245764
  55.1 8.6 %copy-start.32 = (f32[20,256]{1,0:T(8,128)S(1)}, f32[20,256]{1,0:T(8,128)}, u32[]{:S(2)}) copy-start(f32[20,256]{1,0:T(8,128)} %broadcast_multiply_fusion.19) | copy-start | bytes 61444
  74.9 1.0 %copy-start.22 = (f32[1,10,8,256]{3,2,1,0:T(8,128)S(1)}, f32[1,10,8,256]{3,2,1,0:T(8,128)}, u32[]{:S(2)}) copy-start(f32[1,10,8,256]{3,2,1,0:T(8,128)} %get-tuple-element.95) | copy-start | bytes 245764
  74.9 1.0 %copy-start.23 = (f32[1,10,8,256]{3,2,1,0:T(8,128)S(1)}, f32[1,10,8,256]{3,2,1,0:T(8,128)}, u32[]{:S(2)}) copy-start(f32[1,10,8,256]{3,2,1,0:T(8,128)} %get-tuple-element.96) | copy-start | bytes 245764
  74.9 1.0 %copy-start.24 = (f32[1,10,8,256]{3,2,1,0:T(8,128)S(1)}, f32[1,10,8,256]{3,2,1,0:T(8,128)}, u32[]{:S(2)}) copy-start(f32[1,10,8,256]{3,2,1,0:T(8,128)} %slice_bitcast_fusion.2) | copy-start | bytes 245764
  74.9 1.0 %copy-start.25 = (f32[1,10,8,256]{3,2,1,0:T(8,128)S(1)}, f32[1,10,8,256]{3,2,1,0:T(8,128)}, u32[]{:S(2)}) copy-start(f32[1,10,8,256]{3,2,1,0:T(8,128)} %slice_bitcast_fusion.3) | copy-start | bytes 245764
  75.8 6.9 %copy-start.4 = (f32[40,2048]{1,0:T(8,128)S(1)}, f32[40,2048]{1,0:T(8,128)}, u32[]{:S(2)}) copy-start(f32[40,2048]{1,0:T(8,128)} %get-tuple-element.37) | copy-start | bytes 983044
  76.7 8.5 %copy-start.3 = (f32[10,4,2048]{2,1,0:T(4,128)S(1)}, f32[10,4,2048]{2,1,0:T(4,128)}, u32[]{:S(2)}) copy-start(f32[10,4,2048]{2,1,0:T(4,128)} %copy-done.2) | copy-start | bytes 983044
  76.7 12.5 %all-to-all-start = ((f32[2,10,8,256]{3,0,1,2:T(2,128)}), f32[2,10,8,256]{3,0,1,2:T(2,128)}, u32[]{:S(2)}, u32[]{:S(2)}) async-start(f32[2,10,8,256]{3,0,1,2:T(2,128)} %copy.22), calls=%async_computation | async-start | bytes 327680 | tf_op jit(solution)/shard_map/all_to_all | solution.py:77
  82.9 3.2 %copy-start.5 = (f32[4,10,2048]{2,0,1:T(4,128)S(1)}, f32[4,10,2048]{2,0,1:T(4,128)}, u32[]{:S(2)}) copy-start(f32[4,10,2048]{2,0,1:T(4,128)} %param.23) | copy-start | bytes 983044
  83.1 5.2 %copy-start.6 = (f32[9,4,2048]{2,1,0:T(4,128)S(1)}, f32[9,4,2048]{2,1,0:T(4,128)}, u32[]{:S(2)}) copy-start(f32[9,4,2048]{2,1,0:T(4,128)} %get-tuple-element.45) | copy-start | bytes 884740
  83.1 5.2 %copy-start.7 = (f32[9,4,2048]{2,1,0:T(4,128)S(1)}, f32[9,4,2048]{2,1,0:T(4,128)}, u32[]{:S(2)}) copy-start(f32[9,4,2048]{2,1,0:T(4,128)} %get-tuple-element.47) | copy-start | bytes 884740

commit v5 on v3

--- a/solution.py
+++ b/solution.py
@@ -28,25 +28,21 @@
     return jnp.pad(grad_iface, low) + jnp.pad(grad_iface, high)
 
 
-def split3(x):
+def split2(x):
     hi = lax.reduce_precision(x, exponent_bits=8, mantissa_bits=7)
-    rest = x - hi
-    mid = lax.reduce_precision(rest, exponent_bits=8, mantissa_bits=7)
-    lo = rest - mid
-    return jnp.concatenate(
-        [hi.astype(jnp.bfloat16), mid.astype(jnp.bfloat16), lo.astype(jnp.bfloat16)]
-    )
+    lo = x - hi
+    return jnp.concatenate([hi.astype(jnp.bfloat16), lo.astype(jnp.bfloat16)])
 
 
 def exact_select(rows, select, contract):
     n = rows.shape[0]
     parts = lax.dot_general(
-        split3(rows),
+        split2(rows),
         select,
         (((1,), (contract,)), ((), ())),
         preferred_element_type=jnp.float32,
     )
-    return (parts[:n] + parts[n : 2 * n]) + parts[2 * n :]
+    return parts[:n] + parts[n:]
 
 
 def reduce_scatter(value, axis):
@@ -69,9 +65,9 @@
 def sum_scatter(value, axis):
     size = lax.axis_size(axis)
     width = value.shape[-1] // size
-    parts = value.reshape(value.shape[:-1] + (size, width))
-    got = lax.all_to_all(parts, axis, parts.ndim - 2, parts.ndim - 2, tiled=True)
-    return jnp.sum(got, axis=-2)
+    parts = jnp.moveaxis(value.reshape(value.shape[:-1] + (size, width)), -2, 0)
+    got = lax.all_to_all(parts, axis, 0, 0, tiled=True)
+    return jnp.sum(got, axis=0)
 
 
 def body(
@@ -107,7 +103,7 @@
     n_field = members * layers
     rows = jnp.concatenate(
         [
-            jnp.stack([p_old, t_old, g_p, g_t]).reshape(4 * n_field, width),
+            jnp.stack([p_old, t_old, c_p, c_t]).reshape(4 * n_field, width),
             jnp.stack([cond, therm]).reshape(2 * layers, width),
         ]
     )
@@ -116,7 +112,8 @@
     coefs_f = picked[4 * n_field :].reshape(2, layers, 1, rounds, face)
     wc = face_weight * coefs_f
     own = fields_f[:2]
-    g_own = fields_f[2:] * wc
+    g_f = 0.1 * fields_f[2:]
+    g_own = g_f * wc
     sending = jnp.concatenate([own, g_own])
 
     far = []
@@ -127,7 +124,7 @@
     diff = far[:2] - own
     update = wc * diff
     adj_lat = far[2:] - g_own
-    param_lat = face_weight * jnp.sum(fields_f[2:] * diff, axis=2)
+    param_lat = face_weight * jnp.sum(g_f * diff, axis=2)
 
     kf = (0.5 * (cond[:-1] + cond[1:]))[:, None]
     kt = (0.5 * (therm[:-1] + therm[1:]))[:, None]

time: 59 us -> 56.5 us (0.958)
  other arithmetic: 14.4 us -> 12.3 us
  local copies, waits for them, and re-layouts: 5.03 us -> 6.45 us
  matrix products: 7.05 us -> 5.83 us
  waiting for transfers between devices: 11.1 us -> 10.4 us
    another operation x2 -> x1, other arithmetic: 2.66 us -> 0.58 us  [body(): jnp.stack([p_old, t_old, c_p, c_t]).reshape(4 * n_field, width)]
    dot_general x3, matrix products: 7.05 us -> 5.83 us  [exact_select(): lax.dot_general(split2(rows), select, (((1,), (contract,)), ((), ())), pr...]
    mul x1, other arithmetic: 0.05 us -> 1.24 us  [body(): therm = jnp.exp(log_therm) * (1.0 + blocked)]
    transpose x4, other arithmetic: 4.69 us -> 3.55 us  [body(): return tuple((o.transpose(1, 0, 2) for o in outs)) + (owned,)]
    transpose x0 -> x1, local copies, waits for them, and re-layouts: none -> 0.78 us  [sum_scatter(): parts = jnp.moveaxis(value.reshape(value.shape[:-1] + (size, width)), -2, 0)]
    mul x1 -> x0, local copies, waits for them, and re-layouts: 0.78 us -> none  [body(): grads = (vert_grads + lat_grads) * jnp.stack([cond, therm])]
    squeeze x1, local copies, waits for them, and re-layouts: 0.09 us -> 0.82 us  [body(): lat[3]]
    ppermute x4, waiting for transfers between devices: 11.1 us -> 10.4 us  [from_partner(): return lax.ppermute(value, axis, pairs)]
  transfers between devices with their start and end apart: 5 -> 5, of which waited for: 1 -> 1; matrix products, arithmetic and copies ran while one was open for 20% -> 19% of each run, Pallas kernels for 0% -> 0%
where the time goes in v5:
time: 56.5 us; the launch traced here: 56 us
  starting transfers between devices  19.8 us (35%)
  other arithmetic  12.3 us (22%)
  waiting for transfers between devices  10.4 us (18%)
  local copies, waits for them, and re-layouts  6.45 us (11%)
  matrix products  5.83 us (10%)
  between operations  1.21 us (2%)
    ppermute x4, starting transfers between devices, from_partner(): return lax.ppermute(value, axis, pairs)  15.6 us
    ppermute x4, waiting for transfers between devices, from_partner(): return lax.ppermute(value, axis, pairs)  10.4 us
    dot_general x3, matrix products, exact_select(): lax.dot_general(split2(rows), select, (((1,), (contract,)), ((), ())), pr...  5.83 us
    all_to_all x1, starting transfers between devices, sum_scatter(): got = lax.all_to_all(parts, axis, 0, 0, tiled=True)  4.18 us
    transpose x4, other arithmetic, body(): return tuple((o.transpose(1, 0, 2) for o in outs)) + (owned,)  3.55 us
    unnamed x48, local copies, waits for them, and re-layouts  2.75 us
    reduce_sum x1, other arithmetic, sum_scatter(): return jnp.sum(got, axis=0)  1.58 us
    mul x1, other arithmetic, body(): therm = jnp.exp(log_therm) * (1.0 + blocked)  1.24 us
  transfers between devices with their start and end apart: 5, of which 1 were waited for; matrix products, arithmetic and copies ran while one was open for 19% of the time, Pallas kernels for 0%

profile of v5, /device:TPU:1, one launch (start us, length us, event | category | flops | bytes accessed | tf_op | source)
XLA Modules:
  0.0 56.0 jit_solution(7239068452915554970)
XLA Ops:
  0.7 0.0 copy-start.2
  0.7 0.0 copy-start.4
  0.7 1.2 %add_multiply_fusion.3 = (f32[10,2048]{1,0:T(8,128)S(1)}, f32[10,2048]{1,0:T(8,128)S(1)}) fusion(f32[10,2048]{1,0:T(8,128)} %param.16, f32[10,2048]{1,0:T(8,128)} %param.17, s32[10,2048]{1,0:T(8,128)} %param.18, f32[10,2048]{1,0:T(8,128)} %param.15), kind=kLoop, calls=%fused_computation.83 | loop fusion | flops 122880 | bytes 491520 | tf_op jit(solution)/shard_map/mul | solution.py:94
  2.0 0.7 %reshape.100 = f32[20,2048]{1,0:T(8,128)} reshape(f32[2,10,2048]{2,1,0:T(8,128)S(1)} %pad_maximum_fusion.3) | data formatting | bytes 327680 | tf_op jit(solution)/shard_map/reshape | solution.py:107
  2.7 0.0 copy-done
  2.7 0.6 %pad_maximum_fusion = f32[4,10,4,2048]{3,2,1,0:T(4,128)S(1)} fusion(f32[1,10,4,2048]{3,2,1,0:T(4,128)S(1)} %bitcast.104, f32[1,10,4,2048]{3,2,1,0:T(4,128)S(1)} %bitcast.103, f32[1,10,4,2048]{3,2,1,0:T(4,128)S(1)} %bitcast.93, f32[1,10,4,2048]{3,2,1,0:T(4,128)S(1)} %bitcast.96), kind=kLoop, calls=%fused_computation.14 | loop fusion | flops 983040 | bytes 2621440 | tf_op jit(solution)/shard_map/stack | solution.py:106
  3.3 0.5 reshape.99
  3.7 0.0 copy-start.12
  3.7 0.1 constant_dynamic-update-slice_fusion.1
  3.8 0.8 %copy-done.12 = f32[20,2048]{1,0:T(8,128)S(1)} copy-done((f32[20,2048]{1,0:T(8,128)S(1)}, f32[20,2048]{1,0:T(8,128)}, u32[]{:S(2)}) %copy-start.12) | copy-done | bytes 163864
  4.7 0.0 copy-start.15
  4.7 0.2 reduce-precision_convert_fusion
  4.9 0.5 copy-done.15
  5.4 2.2 %fusion.2 = f32[360,1024]{1,0:T(8,128)S(1)} fusion(s32[1024]{0:T(1024)S(1)} %bitcast.130, bf16[180,2048]{1,0:T(8,128)(2,1)S(1)} %get-tuple-element.40, bf16[180,2048]{1,0:T(8,128)(2,1)S(1)} %get-tuple-element.39), kind=kOutput, calls=%fused_computation.3 | convolution fusion | flops 1514995712 | bytes 2953216 | tf_op jit(solution)/shard_map/dot_general | solution.py:39
  7.5 0.1 slice_add_fusion.1
  7.7 0.0 copy-start.14
  7.7 0.1 fusion.40
  7.8 0.2 slice.141
  8.0 0.2 slice.139
  8.2 0.2 copy-done.14
  8.4 0.0 copy-start.3
  8.4 0.0 copy-start.5
  8.4 0.1 broadcast_multiply_fusion
  8.5 0.5 fusion.21
  9.1 8.8 %collective-permute-start = (f32[4,10,4,256]{3,2,1,0:T(4,128)S(1)}, f32[4,10,4,256]{3,2,1,0:T(4,128)S(1)}, u32[]{:S(2)}, u32[]{:S(2)}) collective-permute-start(f32[4,10,4,256]{3,2,1,0:T(4,128)S(1)} %bitcast.123), channel_id=1, source_target_pairs={{0,8},{8,0},{16,24},{24,16},{32,40},{40,32},{48,56},{56,48},{64,72... | collective-permute-start | bytes 491528 | tf_op jit(solution)/shard_map/ppermute | solution.py:9
  17.9 1.9 %collective-permute-start.1 = (f32[4,10,4,256]{3,2,1,0:T(4,128)S(1)}, f32[4,10,4,256]{3,2,1,0:T(4,128)S(1)}, u32[]{:S(2)}, u32[]{:S(2)}) collective-permute-start(f32[4,10,4,256]{3,2,1,0:T(4,128)S(1)} %bitcast.124), channel_id=1, source_target_pairs={{0,16},{8,24},{16,0},{24,8},{32,48},{40,56},{48,32},{56,40},{64,80... | collective-permute-start | bytes 491528 | tf_op jit(solution)/shard_map/ppermute | solution.py:9
  19.9 1.9 %collective-permute-start.2 = (f32[4,10,4,256]{3,2,1,0:T(4,128)S(1)}, f32[4,10,4,256]{3,2,1,0:T(4,128)S(1)}, u32[]{:S(2)}, u32[]{:S(2)}) collective-permute-start(f32[4,10,4,256]{3,2,1,0:T(4,128)S(1)} %bitcast.125), channel_id=1, source_target_pairs={{0,32},{8,40},{16,48},{24,56},{32,0},{40,8},{48,16},{56,24},{64,96... | collective-permute-start | bytes 491528 | tf_op jit(solution)/shard_map/ppermute | solution.py:9
  21.9 3.0 %collective-permute-start.3 = (f32[4,10,4,256]{3,2,1,0:T(4,128)S(1)}, f32[4,10,4,256]{3,2,1,0:T(4,128)S(1)}, u32[]{:S(2)}, u32[]{:S(2)}) collective-permute-start(f32[4,10,4,256]{3,2,1,0:T(4,128)S(1)} %bitcast.126), channel_id=1, source_target_pairs={{0,64},{8,72},{16,80},{24,88},{32,96},{40,104},{48,112},{56,120},{... | collective-permute-start | bytes 491528 | tf_op jit(solution)/shard_map/ppermute | solution.py:9
  24.8 0.2 bitcast_multiply_fusion
  25.1 0.5 multiply_reduce_fusion.2
  25.6 1.1 %multiply_multiply_fusion = (f32[9,4,2048]{2,1,0:T(4,128)}, f32[9,4,2048]{2,1,0:T(4,128)S(1)}, f32[9,4,2048]{2,1,0:T(4,128)}) fusion(f32[9,4,2048]{2,1,0:T(4,128)S(1)} %get-tuple-element.34, f32[10,4,2048]{2,1,0:T(4,128)S(1)} %bitcast.98, f32[9,2048]{1,0:T(8,128)S(1)} %get-tuple-element.69, f32[9,4,2048]{2,1,0:T(4,128)S(1)} %get-tuple-element.33), kind=kLoop, calls=%fused_computation.56 | loop fusion | flops 368640 | bytes 2138112 | tf_op jit(solution)/shard_map/mul | solution.py:163
  26.7 0.1 pad_subtract_fusion
  26.7 1.2 %multiply_reduce_fusion.1 = (f32[9,2048]{1,0:T(8,128)S(1)}, f32[9,4,2048]{2,1,0:T(4,128)}, f32[9,4,2048]{2,1,0:T(4,128)}, f32[9,4,2048]{2,1,0:T(4,128)}) fusion(f32[9,4,2048]{2,1,0:T(4,128)S(1)} %get-tuple-element.34, f32[10,4,2048]{2,1,0:T(4,128)S(1)} %bitcast.95, f32[9,2048]{1,0:T(8,128)S(1)} %get-tuple-element.68, f32[9,4,2048]{2,1,0:T(4,128)S(1)} %get-tuple-element.36), kind=kLoop, calls=%fused_computation.51 | loop fusion | flops 571392 | bytes 2211840 | tf_op jit(solution)/shard_map/reduce_sum | solution.py:142
  28.2 0.5 copy-done.13
  28.7 0.0 collective-permute-done
  28.7 0.0 collective-permute-done.1
  28.7 10.4 %collective-permute-done.2 = f32[4,10,4,256]{3,2,1,0:T(4,128)S(1)} collective-permute-done((f32[4,10,4,256]{3,2,1,0:T(4,128)S(1)}, f32[4,10,4,256]{3,2,1,0:T(4,128)S(1)}, u32[]{:S(2)}, u32[]{:S(2)}) %collective-permute-start.2) | collective-permute-done | bytes 163872 | tf_op jit(solution)/shard_map/ppermute | solution.py:9
  39.1 0.0 collective-permute-done.3
  39.1 0.1 pad_maximum_fusion.1
  39.2 0.1 fusion.41
  39.4 0.7 %multiply_reduce_fusion = (f32[2,10,4,256]{3,2,1,0:T(4,128)S(1)}, f32[2,10,4,4,256]{4,3,2,1,0:T(4,128)S(1)}, f32[2,10,4,4,256]{4,3,2,1,0:T(4,128)S(1)}) fusion(f32[2,10,4,4,256]{4,3,2,1,0:T(4,128)S(1)} %slice.141, f32[2,10,4,4,256]{4,3,2,1,0:T(4,128)S(1)} %slice.139, f32[2,10,4,4,256]{4,2,1,0,3:T(4,128)S(1)} %get-tuple-element.51, ...), kind=kLoop, calls=%fused_computation.41 | loop fusion | flops 552960 | bytes 2211840 | tf_op jit(solution)/shard_map/reduce_sum | solution.py:127
  40.1 1.8 %fusion = f32[40,2048]{1,0:T(8,128)S(1)} fusion(s32[1024]{0:T(1024)S(1)} %bitcast.131, bf16[20,1024]{1,0:T(8,128)(2,1)S(1)} %get-tuple-element.65, bf16[20,1024]{1,0:T(8,128)(2,1)S(1)} %get-tuple-element.64), kind=kOutput, calls=%fused_computation.1 | convolution fusion | flops 170033152 | bytes 413696 | tf_op jit(solution)/shard_map/dot_general | solution.py:39
  41.9 0.1 copy.61
  42.1 0.8 %copy.47 = f32[8,2,10,256]{3,1,2,0:T(2,128)} copy(f32[8,2,10,256]{3,0,2,1:T(8,128)S(1)} %fusion.24) | data formatting | bytes 327680 | tf_op jit(solution)/shard_map/transpose | solution.py:68
  42.9 4.2 %all-to-all-start = ((f32[8,2,10,256]{3,1,2,0:T(2,128)}), f32[8,2,10,256]{3,1,2,0:T(2,128)}, u32[]{:S(2)}, u32[]{:S(2)}) async-start(f32[8,2,10,256]{3,1,2,0:T(2,128)} %copy.47), calls=%async_computation | async-start | bytes 327680 | tf_op jit(solution)/shard_map/all_to_all | solution.py:69
  47.0 0.2 pad_maximum_fusion.2
  47.3 0.1 copy.56
  47.4 0.1 reduce-precision_convert_fusion.1
  47.5 1.9 %fusion.1 = f32[320,2048]{1,0:T(8,128)S(1)} fusion(s32[1024]{0:T(1024)S(1)} %bitcast.132, bf16[160,1024]{1,0:T(8,128)(2,1)S(1)} %get-tuple-element.50, bf16[160,1024]{1,0:T(8,128)(2,1)S(1)} %get-tuple-element.49), kind=kOutput, calls=%fused_computation.2 | convolution fusion | flops 1345585152 | bytes 3280896 | tf_op jit(solution)/shard_map/dot_general | solution.py:39
  49.4 0.1 slice_add_fusion
  49.6 0.1 fusion.39
  49.6 0.0 copy-start.7
  49.7 0.8 %squeeze.31 = f32[10,4,2048]{2,1,0:T(4,128)} reshape(f32[40,2048]{1,0:T(8,128)S(1)} %get-tuple-element.41) | data formatting | bytes 655360 | tf_op jit(solution)/shard_map/squeeze | solution.py:163
  50.5 0.1 squeeze.30
  50.6 0.1 squeeze.29
  50.7 0.0 copy-start.8
  50.7 0.1 squeeze.28
  50.8 0.0 copy-start.6
  50.8 0.8 %fusion.18 = f32[4,10,2048]{2,0,1:T(4,128)} fusion(f32[10,4,2048]{2,1,0:T(4,128)S(1)} %squeeze.30, f32[4,10,2048]{2,0,1:T(4,128)S(1)} %copy-done.3, f32[9,4,2048]{2,1,0:T(4,128)S(1)} %copy-done.7), kind=kLoop, calls=%fused_computation.38 | loop fusion | flops 245760 | bytes 1277952 | tf_op jit(solution)/shard_map/transpose | solution.py:165
  51.7 0.9 %add_bitcast_fusion.1 = f32[4,10,2048]{2,0,1:T(4,128)} fusion(f32[10,4,2048]{2,1,0:T(4,128)S(1)} %fusion.33, f32[10,4,2048]{2,1,0:T(4,128)S(1)} %squeeze.28, f32[4,10,2048]{2,0,1:T(4,128)S(1)} %copy-done.1), kind=kLoop, calls=%fused_computation.43 | loop fusion | flops 245760 | bytes 1310720 | tf_op jit(solution)/shard_map/transpose | solution.py:165
  52.6 0.9 %fusion.16 = f32[4,10,2048]{2,0,1:T(4,128)} fusion(f32[10,4,2048]{2,1,0:T(4,128)S(1)} %copy-done.6, f32[4,10,2048]{2,0,1:T(4,128)S(1)} %copy-done.5, f32[9,4,2048]{2,1,0:T(4,128)S(1)} %copy-done.8, f32[9,4,2048]{2,1,0:T(4,128)S(1)} %copy-done.11), kind=kLoop, calls=%fused_computation.34 | loop fusion | flops 491520 | bytes 1572864 | tf_op jit(solution)/shard_map/transpose | solution.py:165
  53.5 0.9 %add_bitcast_fusion = f32[4,10,2048]{2,0,1:T(4,128)} fusion(f32[10,4,2048]{2,1,0:T(4,128)S(1)} %squeeze.29, f32[9,4,2048]{2,1,0:T(4,128)S(1)} %copy-done.10, f32[9,4,2048]{2,1,0:T(4,128)S(1)} %copy-done.9, f32[4,10,2048]{2,0,1:T(4,128)S(1)} %copy-done), kind=kLoop, calls=%fused_computation.42 | loop fusion | flops 573440 | bytes 1572864 | tf_op jit(solution)/shard_map/transpose | solution.py:165
  54.4 0.0 all-to-all-done
  54.4 1.6 %reduce_sum.42 = f32[2,10,256]{2,0,1:T(2,128)} reduce(f32[8,2,10,256]{3,1,2,0:T(2,128)} %all-to-all-done, f32[]{:T(128)} %constant.39.clone.1), dimensions={0}, to_apply=%region_3.4 | reduce | flops 35840 | bytes 184324 | tf_op jit(solution)/shard_map/reduce_sum | solution.py:70
  (45 shorter events, 0.8 us)
Async XLA Ops:
  0.6 2.0 %copy-start.1 = (f32[4,10,2048]{2,0,1:T(4,128)S(1)}, f32[4,10,2048]{2,0,1:T(4,128)}, u32[]{:S(2)}) copy-start(f32[4,10,2048]{2,0,1:T(4,128)} %param.13) | copy-start | bytes 983044
  0.6 2.0 %copy-start = (f32[4,10,2048]{2,0,1:T(4,128)S(1)}, f32[4,10,2048]{2,0,1:T(4,128)}, u32[]{:S(2)}) copy-start(f32[4,10,2048]{2,0,1:T(4,128)} %param.14) | copy-start | bytes 983044
  0.7 2.0 %copy-start.2 = (f32[4,10,2048]{2,0,1:T(4,128)S(1)}, f32[4,10,2048]{2,0,1:T(4,128)}, u32[]{:S(2)}) copy-start(f32[4,10,2048]{2,0,1:T(4,128)} %param.22) | copy-start | bytes 983044
  0.7 2.0 %copy-start.4 = (f32[4,10,2048]{2,0,1:T(4,128)S(1)}, f32[4,10,2048]{2,0,1:T(4,128)}, u32[]{:S(2)}) copy-start(f32[4,10,2048]{2,0,1:T(4,128)} %param.23) | copy-start | bytes 983044
  3.7 0.9 %copy-start.12 = (f32[20,2048]{1,0:T(8,128)S(1)}, f32[20,2048]{1,0:T(8,128)}, u32[]{:S(2)}) copy-start(f32[20,2048]{1,0:T(8,128)} %reshape.100) | copy-start | bytes 491524
  4.7 0.7 %copy-start.15 = (s32[4,256]{1,0:T(4,128)S(1)}, s32[4,256]{1,0:T(4,128)}, u32[]{:S(2)}) copy-start(s32[4,256]{1,0:T(4,128)} %param.20) | copy-start | bytes 12292
  7.7 0.7 %copy-start.14 = (f32[4,256]{1,0:T(4,128)S(1)}, f32[4,256]{1,0:T(4,128)}, u32[]{:S(2)}) copy-start(f32[4,256]{1,0:T(4,128)} %param.21) | copy-start | bytes 12292
  8.4 16.4 %copy-start.3 = (f32[4,10,2048]{2,0,1:T(4,128)S(1)}, f32[4,10,2048]{2,0,1:T(4,128)}, u32[]{:S(2)}) copy-start(f32[4,10,2048]{2,0,1:T(4,128)} %param.22) | copy-start | bytes 983044
  8.4 16.4 %copy-start.5 = (f32[4,10,2048]{2,0,1:T(4,128)S(1)}, f32[4,10,2048]{2,0,1:T(4,128)}, u32[]{:S(2)}) copy-start(f32[4,10,2048]{2,0,1:T(4,128)} %param.23) | copy-start | bytes 983044
  9.1 19.6 %collective-permute-start = (f32[4,10,4,256]{3,2,1,0:T(4,128)S(1)}, f32[4,10,4,256]{3,2,1,0:T(4,128)S(1)}, u32[]{:S(2)}, u32[]{:S(2)}) collective-permute-start(f32[4,10,4,256]{3,2,1,0:T(4,128)S(1)} %bitcast.123), channel_id=1, source_target_pairs={{0,8},{8,0},{16,24},{24,16},{32,40},{40,32},{48,56},{56,48},{64,72... | collective-permute-start | bytes 491528 | tf_op jit(solution)/shard_map/ppermute | solution.py:9
  17.9 10.8 %collective-permute-start.1 = (f32[4,10,4,256]{3,2,1,0:T(4,128)S(1)}, f32[4,10,4,256]{3,2,1,0:T(4,128)S(1)}, u32[]{:S(2)}, u32[]{:S(2)}) collective-permute-start(f32[4,10,4,256]{3,2,1,0:T(4,128)S(1)} %bitcast.124), channel_id=1, source_target_pairs={{0,16},{8,24},{16,0},{24,8},{32,48},{40,56},{48,32},{56,40},{64,80... | collective-permute-start | bytes 491528 | tf_op jit(solution)/shard_map/ppermute | solution.py:9
  19.9 19.2 %collective-permute-start.2 = (f32[4,10,4,256]{3,2,1,0:T(4,128)S(1)}, f32[4,10,4,256]{3,2,1,0:T(4,128)S(1)}, u32[]{:S(2)}, u32[]{:S(2)}) collective-permute-start(f32[4,10,4,256]{3,2,1,0:T(4,128)S(1)} %bitcast.125), channel_id=1, source_target_pairs={{0,32},{8,40},{16,48},{24,56},{32,0},{40,8},{48,16},{56,24},{64,96... | collective-permute-start | bytes 491528 | tf_op jit(solution)/shard_map/ppermute | solution.py:9
  21.9 17.2 %collective-permute-start.3 = (f32[4,10,4,256]{3,2,1,0:T(4,128)S(1)}, f32[4,10,4,256]{3,2,1,0:T(4,128)S(1)}, u32[]{:S(2)}, u32[]{:S(2)}) collective-permute-start(f32[4,10,4,256]{3,2,1,0:T(4,128)S(1)} %bitcast.126), channel_id=1, source_target_pairs={{0,64},{8,72},{16,80},{24,88},{32,96},{40,104},{48,112},{56,120},{... | collective-permute-start | bytes 491528 | tf_op jit(solution)/shard_map/ppermute | solution.py:9
  27.9 0.8 %copy-start.13 = (f32[4,2048]{1,0:T(4,128)S(1)}, f32[4,2048]{1,0:T(4,128)}, u32[]{:S(2)}) copy-start(f32[4,2048]{1,0:T(4,128)} %param.19) | copy-start | bytes 98308
  42.9 11.5 %all-to-all-start = ((f32[8,2,10,256]{3,1,2,0:T(2,128)}), f32[8,2,10,256]{3,1,2,0:T(2,128)}, u32[]{:S(2)}, u32[]{:S(2)}) async-start(f32[8,2,10,256]{3,1,2,0:T(2,128)} %copy.47), calls=%async_computation | async-start | bytes 327680 | tf_op jit(solution)/shard_map/all_to_all | solution.py:69
  49.6 1.2 %copy-start.7 = (f32[9,4,2048]{2,1,0:T(4,128)S(1)}, f32[9,4,2048]{2,1,0:T(4,128)}, u32[]{:S(2)}) copy-start(f32[9,4,2048]{2,1,0:T(4,128)} %get-tuple-element.63) | copy-start | bytes 884740
  50.7 1.9 %copy-start.8 = (f32[9,4,2048]{2,1,0:T(4,128)S(1)}, f32[9,4,2048]{2,1,0:T(4,128)}, u32[]{:S(2)}) copy-start(f32[9,4,2048]{2,1,0:T(4,128)} %get-tuple-element.35) | copy-start | bytes 884740
  50.8 1.8 %copy-start.6 = (f32[10,4,2048]{2,1,0:T(4,128)S(1)}, f32[10,4,2048]{2,1,0:T(4,128)}, u32[]{:S(2)}) copy-start(f32[10,4,2048]{2,1,0:T(4,128)} %squeeze.31) | copy-start | bytes 983044
  50.8 1.7 %copy-start.11 = (f32[9,4,2048]{2,1,0:T(4,128)S(1)}, f32[9,4,2048]{2,1,0:T(4,128)}, u32[]{:S(2)}) copy-start(f32[9,4,2048]{2,1,0:T(4,128)} %get-tuple-element.59) | copy-start | bytes 884740
  51.7 1.8 %copy-start.9 = (f32[9,4,2048]{2,1,0:T(4,128)S(1)}, f32[9,4,2048]{2,1,0:T(4,128)}, u32[]{:S(2)}) copy-start(f32[9,4,2048]{2,1,0:T(4,128)} %get-tuple-element.58) | copy-start | bytes 884740
  51.7 1.8 %copy-start.10 = (f32[9,4,2048]{2,1,0:T(4,128)S(1)}, f32[9,4,2048]{2,1,0:T(4,128)}, u32[]{:S(2)}) copy-start(f32[9,4,2048]{2,1,0:T(4,128)} %get-tuple-element.60) | copy-start | bytes 884740

commit v6 on v5

--- a/solution.py
+++ b/solution.py
@@ -67,7 +67,10 @@
     width = value.shape[-1] // size
     parts = jnp.moveaxis(value.reshape(value.shape[:-1] + (size, width)), -2, 0)
     got = lax.all_to_all(parts, axis, 0, 0, tiled=True)
-    return jnp.sum(got, axis=0)
+    total = got[0]
+    for index in range(1, size):
+        total = total + got[index]
+    return total
 
 
 def body(
@@ -142,17 +145,21 @@
     g_kt = jnp.sum(db * d_t, axis=1)
     vert_grads = jnp.stack([0.5 * pad_sum(g_kf, 0), 0.5 * pad_sum(g_kt, 0)])
 
-    lat_grads = exact_select(
-        param_lat.reshape(2 * layers, rounds * face), select, 0
-    ).reshape(2, layers, width)
+    placed = exact_select(
+        jnp.concatenate(
+            [
+                param_lat.reshape(2 * layers, rounds * face),
+                jnp.concatenate([update, adj_lat]).reshape(4 * n_field, rounds * face),
+            ]
+        ),
+        select,
+        0,
+    )
+    lat_grads = placed[: 2 * layers].reshape(2, layers, width)
+    lat = placed[2 * layers :].reshape(4, layers, members, width)
     grads = (vert_grads + lat_grads) * jnp.stack([cond, therm])
     owned = sum_scatter(grads, "member")
 
-    lat = exact_select(
-        jnp.concatenate([update, adj_lat]).reshape(4 * n_field, rounds * face),
-        select,
-        0,
-    ).reshape(4, layers, members, width)
 
     p_rate = spread0(flow)
     p_rate = p_rate.at[0].add(recharge)

time: 56.5 us -> 56.1 us (level)
  matrix products: 5.83 us -> 4.24 us
  local copies, waits for them, and re-layouts: 6.45 us -> 7.27 us
    dot_general x3 -> x2, matrix products: 5.83 us -> 4.24 us  [exact_select(): lax.dot_general(split2(rows), select, (((1,), (contract,)), ((), ())), pr...]
    reduce_sum x1 -> x0, other arithmetic: 1.58 us -> none  [sum_scatter(): return jnp.sum(got, axis=0)]
    add x0 -> x1, other arithmetic: none -> 1.49 us  [sum_scatter(): total = total + got[index]]
    squeeze x1, local copies, waits for them, and re-layouts: 0.09 us -> 0.82 us  [body(): new_heat = t_old + 0.1 * (t_rate + lat[1])]
    unnamed x48 -> x50, local copies, waits for them, and re-layouts: 2.75 us -> 2.74 us
  transfers between devices with their start and end apart: 5 -> 5, of which waited for: 1 -> 2; matrix products, arithmetic and copies ran while one was open for 19% -> 16% of each run, Pallas kernels for 0% -> 0%
where the time goes in v6:
time: 56.1 us; the launch traced here: 55.4 us
  starting transfers between devices  19.7 us (35%)
  other arithmetic  12.3 us (22%)
  waiting for transfers between devices  10.7 us (19%)
  local copies, waits for them, and re-layouts  7.27 us (13%)
  matrix products  4.24 us (8%)
  between operations  1.18 us (2%)
    ppermute x4, starting transfers between devices, from_partner(): return lax.ppermute(value, axis, pairs)  15.6 us
    ppermute x4, waiting for transfers between devices, from_partner(): return lax.ppermute(value, axis, pairs)  10.4 us
    dot_general x2, matrix products, exact_select(): lax.dot_general(split2(rows), select, (((1,), (contract,)), ((), ())), pr...  4.24 us
    all_to_all x1, starting transfers between devices, sum_scatter(): got = lax.all_to_all(parts, axis, 0, 0, tiled=True)  4.14 us
    transpose x4, other arithmetic, body(): return tuple((o.transpose(1, 0, 2) for o in outs)) + (owned,)  3.55 us
    unnamed x50, local copies, waits for them, and re-layouts  2.74 us
    add x1, other arithmetic, sum_scatter(): total = total + got[index]  1.49 us
    mul x1, other arithmetic, body(): therm = jnp.exp(log_therm) * (1.0 + blocked)  1.24 us
  transfers between devices with their start and end apart: 5, of which 2 were waited for; matrix products, arithmetic and copies ran while one was open for 16% of the time, Pallas kernels for 0%

profile of v6, /device:TPU:1, one launch (start us, length us, event | category | flops | bytes accessed | tf_op | source)
XLA Modules:
  0.0 55.4 jit_solution(442708861340492869)
XLA Ops:
  0.6 0.0 copy-start.1
  0.6 0.0 copy-start
  0.7 0.0 copy-start.2
  0.7 0.0 copy-start.4
  0.7 1.2 %add_multiply_fusion.3 = (f32[10,2048]{1,0:T(8,128)S(1)}, f32[10,2048]{1,0:T(8,128)S(1)}) fusion(f32[10,2048]{1,0:T(8,128)} %param.16, f32[10,2048]{1,0:T(8,128)} %param.17, s32[10,2048]{1,0:T(8,128)} %param.18, f32[10,2048]{1,0:T(8,128)} %param.15), kind=kLoop, calls=%fused_computation.79 | loop fusion | flops 122880 | bytes 491520 | tf_op jit(solution)/shard_map/mul | solution.py:97
  2.0 0.7 %reshape.104 = f32[20,2048]{1,0:T(8,128)} reshape(f32[2,10,2048]{2,1,0:T(8,128)S(1)} %pad_maximum_fusion.4) | data formatting | bytes 327680 | tf_op jit(solution)/shard_map/reshape | solution.py:110
  2.7 0.0 copy-done
  2.7 0.6 %pad_maximum_fusion = f32[4,10,4,2048]{3,2,1,0:T(4,128)S(1)} fusion(f32[1,10,4,2048]{3,2,1,0:T(4,128)S(1)} %bitcast.106, f32[1,10,4,2048]{3,2,1,0:T(4,128)S(1)} %bitcast.105, f32[1,10,4,2048]{3,2,1,0:T(4,128)S(1)} %bitcast.95, f32[1,10,4,2048]{3,2,1,0:T(4,128)S(1)} %bitcast.98), kind=kLoop, calls=%fused_computation.12 | loop fusion | flops 983040 | bytes 2621440 | tf_op jit(solution)/shard_map/stack | solution.py:109
  3.3 0.5 reshape.103
  3.7 0.0 copy-start.13
  3.7 0.1 constant_dynamic-update-slice_fusion.1
  3.8 0.8 %copy-done.13 = f32[20,2048]{1,0:T(8,128)S(1)} copy-done((f32[20,2048]{1,0:T(8,128)S(1)}, f32[20,2048]{1,0:T(8,128)}, u32[]{:S(2)}) %copy-start.13) | copy-done | bytes 163864
  4.7 0.0 copy-start.16
  4.7 0.2 reduce-precision_convert_fusion
  4.9 0.5 copy-done.16
  5.4 2.2 %fusion.1 = f32[360,1024]{1,0:T(8,128)S(1)} fusion(s32[1024]{0:T(1024)S(1)} %bitcast.132, bf16[180,2048]{1,0:T(8,128)(2,1)S(1)} %get-tuple-element.34, bf16[180,2048]{1,0:T(8,128)(2,1)S(1)} %get-tuple-element.33), kind=kOutput, calls=%fused_computation.2 | convolution fusion | flops 1514995712 | bytes 2953216 | tf_op jit(solution)/shard_map/dot_general | solution.py:39
  7.5 0.1 slice_add_fusion.1
  7.7 0.0 copy-start.15
  7.7 0.1 fusion.34
  7.8 0.2 slice.164
  8.0 0.2 slice.166
  8.1 0.2 copy-done.15
  8.4 0.0 copy-start.3
  8.4 0.0 copy-start.5
  8.4 0.1 broadcast_multiply_fusion.1
  8.5 0.5 fusion.19
  9.0 8.8 %collective-permute-start = (f32[4,10,4,256]{3,2,1,0:T(4,128)S(1)}, f32[4,10,4,256]{3,2,1,0:T(4,128)S(1)}, u32[]{:S(2)}, u32[]{:S(2)}) collective-permute-start(f32[4,10,4,256]{3,2,1,0:T(4,128)S(1)} %bitcast.125), channel_id=1, source_target_pairs={{0,8},{8,0},{16,24},{24,16},{32,40},{40,32},{48,56},{56,48},{64,72... | collective-permute-start | bytes 491528 | tf_op jit(solution)/shard_map/ppermute | solution.py:9
  17.9 1.9 %collective-permute-start.1 = (f32[4,10,4,256]{3,2,1,0:T(4,128)S(1)}, f32[4,10,4,256]{3,2,1,0:T(4,128)S(1)}, u32[]{:S(2)}, u32[]{:S(2)}) collective-permute-start(f32[4,10,4,256]{3,2,1,0:T(4,128)S(1)} %bitcast.126), channel_id=1, source_target_pairs={{0,16},{8,24},{16,0},{24,8},{32,48},{40,56},{48,32},{56,40},{64,80... | collective-permute-start | bytes 491528 | tf_op jit(solution)/shard_map/ppermute | solution.py:9
  19.9 1.9 %collective-permute-start.2 = (f32[4,10,4,256]{3,2,1,0:T(4,128)S(1)}, f32[4,10,4,256]{3,2,1,0:T(4,128)S(1)}, u32[]{:S(2)}, u32[]{:S(2)}) collective-permute-start(f32[4,10,4,256]{3,2,1,0:T(4,128)S(1)} %bitcast.127), channel_id=1, source_target_pairs={{0,32},{8,40},{16,48},{24,56},{32,0},{40,8},{48,16},{56,24},{64,96... | collective-permute-start | bytes 491528 | tf_op jit(solution)/shard_map/ppermute | solution.py:9
  21.9 3.0 %collective-permute-start.3 = (f32[4,10,4,256]{3,2,1,0:T(4,128)S(1)}, f32[4,10,4,256]{3,2,1,0:T(4,128)S(1)}, u32[]{:S(2)}, u32[]{:S(2)}) collective-permute-start(f32[4,10,4,256]{3,2,1,0:T(4,128)S(1)} %bitcast.128), channel_id=1, source_target_pairs={{0,64},{8,72},{16,80},{24,88},{32,96},{40,104},{48,112},{56,120},{... | collective-permute-start | bytes 491528 | tf_op jit(solution)/shard_map/ppermute | solution.py:9
  24.9 0.2 bitcast_multiply_fusion
  25.1 0.5 multiply_reduce_fusion.2
  25.6 1.1 %multiply_multiply_fusion = (f32[9,4,2048]{2,1,0:T(4,128)}, f32[9,4,2048]{2,1,0:T(4,128)S(1)}, f32[9,4,2048]{2,1,0:T(4,128)}) fusion(f32[9,4,2048]{2,1,0:T(4,128)S(1)} %get-tuple-element.24, f32[10,4,2048]{2,1,0:T(4,128)S(1)} %bitcast.100, f32[9,2048]{1,0:T(8,128)S(1)} %get-tuple-element.57, f32[9,4,2048]{2,1,0:T(4,128)S(1)} %get-tuple-element.23), kind=kLoop, calls=%fused_computation.55 | loop fusion | flops 368640 | bytes 2138112 | tf_op jit(solution)/shard_map/mul | solution.py:170
  26.7 0.1 pad_subtract_fusion
  26.8 1.2 %multiply_reduce_fusion.1 = (f32[9,2048]{1,0:T(8,128)S(1)}, f32[9,4,2048]{2,1,0:T(4,128)}, f32[9,4,2048]{2,1,0:T(4,128)}, f32[9,4,2048]{2,1,0:T(4,128)}) fusion(f32[9,4,2048]{2,1,0:T(4,128)S(1)} %get-tuple-element.24, f32[10,4,2048]{2,1,0:T(4,128)S(1)} %bitcast.97, f32[9,2048]{1,0:T(8,128)S(1)} %get-tuple-element.56, f32[9,4,2048]{2,1,0:T(4,128)S(1)} %get-tuple-element.26), kind=kLoop, calls=%fused_computation.50 | loop fusion | flops 571392 | bytes 2211840 | tf_op jit(solution)/shard_map/reduce_sum | solution.py:145
  28.2 0.5 copy-done.14
  28.7 0.0 collective-permute-done
  28.7 0.0 collective-permute-done.1
  28.7 10.3 %collective-permute-done.2 = f32[4,10,4,256]{3,2,1,0:T(4,128)S(1)} collective-permute-done((f32[4,10,4,256]{3,2,1,0:T(4,128)S(1)}, f32[4,10,4,256]{3,2,1,0:T(4,128)S(1)}, u32[]{:S(2)}, u32[]{:S(2)}) %collective-permute-start.2) | collective-permute-done | bytes 163872 | tf_op jit(solution)/shard_map/ppermute | solution.py:9
  39.1 0.0 collective-permute-done.3
  39.1 0.1 pad_maximum_fusion.2
  39.2 0.1 fusion.35
  39.4 0.7 %multiply_reduce_fusion = (f32[2,10,4,256]{3,2,1,0:T(4,128)S(1)}, f32[2,10,4,4,256]{4,3,2,1,0:T(4,128)S(1)}, f32[2,10,4,4,256]{4,3,2,1,0:T(4,128)S(1)}) fusion(f32[2,10,4,4,256]{4,3,2,1,0:T(4,128)S(1)} %slice.164, f32[2,10,4,4,256]{4,3,2,1,0:T(4,128)S(1)} %slice.166, f32[2,10,4,4,256]{4,2,1,0,3:T(4,128)S(1)} %get-tuple-element.41, ...), kind=kLoop, calls=%fused_computation.42 | loop fusion | flops 552960 | bytes 2211840 | tf_op jit(solution)/shard_map/reduce_sum | solution.py:130
  40.0 0.2 pad_maximum_fusion.3
  40.3 0.1 copy.54
  40.5 0.2 reduce-precision_convert_fusion.1
  40.6 2.1 %fusion = f32[360,2048]{1,0:T(8,128)S(1)} fusion(s32[1024]{0:T(1024)S(1)} %bitcast.133, bf16[180,1024]{1,0:T(8,128)(2,1)S(1)} %get-tuple-element.36, bf16[180,1024]{1,0:T(8,128)(2,1)S(1)} %get-tuple-element.35), kind=kOutput, calls=%fused_computation.1 | convolution fusion | flops 1513521152 | bytes 3690496 | tf_op jit(solution)/shard_map/dot_general | solution.py:39
  42.7 0.2 slice_add_fusion
  43.0 0.2 fusion.33
  43.1 0.1 copy.57
  43.3 0.8 %copy.46 = f32[8,2,10,256]{3,1,2,0:T(2,128)} copy(f32[8,2,10,256]{3,0,2,1:T(8,128)S(1)} %fusion.22) | data formatting | bytes 327680 | tf_op jit(solution)/shard_map/transpose | solution.py:68
  44.1 4.1 %all-to-all-start = ((f32[8,2,10,256]{3,1,2,0:T(2,128)}), f32[8,2,10,256]{3,1,2,0:T(2,128)}, u32[]{:S(2)}, u32[]{:S(2)}) async-start(f32[8,2,10,256]{3,1,2,0:T(2,128)} %copy.46), calls=%async_computation | async-start | bytes 327680 | tf_op jit(solution)/shard_map/all_to_all | solution.py:69
  48.2 0.8 %squeeze.45 = f32[10,4,2048]{2,1,0:T(4,128)} reshape(f32[40,2048]{1,0:T(8,128)S(1)} %get-tuple-element.29) | data formatting | bytes 655360 | tf_op jit(solution)/shard_map/squeeze | solution.py:170
  49.0 0.1 squeeze.44
  49.1 0.8 %squeeze.43 = f32[10,4,2048]{2,1,0:T(4,128)} reshape(f32[40,2048]{1,0:T(8,128)S(1)} %get-tuple-element.31) | data formatting | bytes 655360 | tf_op jit(solution)/shard_map/squeeze | solution.py:168
  49.9 0.1 squeeze.42
  50.1 0.8 %fusion.16 = f32[4,10,2048]{2,0,1:T(4,128)} fusion(f32[10,4,2048]{2,1,0:T(4,128)S(1)} %squeeze.44, f32[4,10,2048]{2,0,1:T(4,128)S(1)} %copy-done.3, f32[9,4,2048]{2,1,0:T(4,128)S(1)} %copy-done.8), kind=kLoop, calls=%fused_computation.37 | loop fusion | flops 245760 | bytes 1277952 | tf_op jit(solution)/shard_map/transpose | solution.py:172
  50.9 0.9 %add_bitcast_fusion.1 = f32[4,10,2048]{2,0,1:T(4,128)} fusion(f32[10,4,2048]{2,1,0:T(4,128)S(1)} %fusion.27, f32[10,4,2048]{2,1,0:T(4,128)S(1)} %squeeze.42, f32[4,10,2048]{2,0,1:T(4,128)S(1)} %copy-done.1), kind=kLoop, calls=%fused_computation.41 | loop fusion | flops 245760 | bytes 1310720 | tf_op jit(solution)/shard_map/transpose | solution.py:172
  51.8 0.0 copy-done.12
  51.8 0.9 %fusion.14 = f32[4,10,2048]{2,0,1:T(4,128)} fusion(f32[10,4,2048]{2,1,0:T(4,128)S(1)} %copy-done.7, f32[4,10,2048]{2,0,1:T(4,128)S(1)} %copy-done.5, f32[9,4,2048]{2,1,0:T(4,128)S(1)} %copy-done.9, f32[9,4,2048]{2,1,0:T(4,128)S(1)} %copy-done.12), kind=kLoop, calls=%fused_computation.33 | loop fusion | flops 491520 | bytes 1572864 | tf_op jit(solution)/shard_map/transpose | solution.py:172
  52.7 0.0 copy-done.6
  52.7 0.9 %add_bitcast_fusion = f32[4,10,2048]{2,0,1:T(4,128)} fusion(f32[10,4,2048]{2,1,0:T(4,128)S(1)} %copy-done.6, f32[9,4,2048]{2,1,0:T(4,128)S(1)} %copy-done.11, f32[9,4,2048]{2,1,0:T(4,128)S(1)} %copy-done.10, f32[4,10,2048]{2,0,1:T(4,128)S(1)} %copy-done), kind=kLoop, calls=%fused_computation.40 | loop fusion | flops 573440 | bytes 1572864 | tf_op jit(solution)/shard_map/transpose | solution.py:172
  53.6 0.3 all-to-all-done
  53.9 1.5 %fusion.28 = f32[2,10,256]{2,0,1:T(2,128)} fusion(f32[8,2,10,256]{3,1,2,0:T(2,128)} %all-to-all-done), kind=kLoop, calls=%fused_computation.93 | loop fusion | flops 35840 | bytes 184320 | tf_op jit(solution)/shard_map/add | solution.py:72
  (46 shorter events, 0.8 us)
Async XLA Ops:
  0.6 2.0 %copy-start.1 = (f32[4,10,2048]{2,0,1:T(4,128)S(1)}, f32[4,10,2048]{2,0,1:T(4,128)}, u32[]{:S(2)}) copy-start(f32[4,10,2048]{2,0,1:T(4,128)} %param.13) | copy-start | bytes 983044
  0.6 2.0 %copy-start = (f32[4,10,2048]{2,0,1:T(4,128)S(1)}, f32[4,10,2048]{2,0,1:T(4,128)}, u32[]{:S(2)}) copy-start(f32[4,10,2048]{2,0,1:T(4,128)} %param.14) | copy-start | bytes 983044
  0.7 2.0 %copy-start.2 = (f32[4,10,2048]{2,0,1:T(4,128)S(1)}, f32[4,10,2048]{2,0,1:T(4,128)}, u32[]{:S(2)}) copy-start(f32[4,10,2048]{2,0,1:T(4,128)} %param.22) | copy-start | bytes 983044
  0.7 2.0 %copy-start.4 = (f32[4,10,2048]{2,0,1:T(4,128)S(1)}, f32[4,10,2048]{2,0,1:T(4,128)}, u32[]{:S(2)}) copy-start(f32[4,10,2048]{2,0,1:T(4,128)} %param.23) | copy-start | bytes 983044
  3.7 0.9 %copy-start.13 = (f32[20,2048]{1,0:T(8,128)S(1)}, f32[20,2048]{1,0:T(8,128)}, u32[]{:S(2)}) copy-start(f32[20,2048]{1,0:T(8,128)} %reshape.104) | copy-start | bytes 491524
  4.7 0.7 %copy-start.16 = (s32[4,256]{1,0:T(4,128)S(1)}, s32[4,256]{1,0:T(4,128)}, u32[]{:S(2)}) copy-start(s32[4,256]{1,0:T(4,128)} %param.20) | copy-start | bytes 12292
  7.7 0.7 %copy-start.15 = (f32[4,256]{1,0:T(4,128)S(1)}, f32[4,256]{1,0:T(4,128)}, u32[]{:S(2)}) copy-start(f32[4,256]{1,0:T(4,128)} %param.21) | copy-start | bytes 12292
  8.4 16.4 %copy-start.3 = (f32[4,10,2048]{2,0,1:T(4,128)S(1)}, f32[4,10,2048]{2,0,1:T(4,128)}, u32[]{:S(2)}) copy-start(f32[4,10,2048]{2,0,1:T(4,128)} %param.22) | copy-start | bytes 983044
  8.4 16.4 %copy-start.5 = (f32[4,10,2048]{2,0,1:T(4,128)S(1)}, f32[4,10,2048]{2,0,1:T(4,128)}, u32[]{:S(2)}) copy-start(f32[4,10,2048]{2,0,1:T(4,128)} %param.23) | copy-start | bytes 983044
  9.0 19.7 %collective-permute-start = (f32[4,10,4,256]{3,2,1,0:T(4,128)S(1)}, f32[4,10,4,256]{3,2,1,0:T(4,128)S(1)}, u32[]{:S(2)}, u32[]{:S(2)}) collective-permute-start(f32[4,10,4,256]{3,2,1,0:T(4,128)S(1)} %bitcast.125), channel_id=1, source_target_pairs={{0,8},{8,0},{16,24},{24,16},{32,40},{40,32},{48,56},{56,48},{64,72... | collective-permute-start | bytes 491528 | tf_op jit(solution)/shard_map/ppermute | solution.py:9
  17.9 10.8 %collective-permute-start.1 = (f32[4,10,4,256]{3,2,1,0:T(4,128)S(1)}, f32[4,10,4,256]{3,2,1,0:T(4,128)S(1)}, u32[]{:S(2)}, u32[]{:S(2)}) collective-permute-start(f32[4,10,4,256]{3,2,1,0:T(4,128)S(1)} %bitcast.126), channel_id=1, source_target_pairs={{0,16},{8,24},{16,0},{24,8},{32,48},{40,56},{48,32},{56,40},{64,80... | collective-permute-start | bytes 491528 | tf_op jit(solution)/shard_map/ppermute | solution.py:9
  19.9 19.2 %collective-permute-start.2 = (f32[4,10,4,256]{3,2,1,0:T(4,128)S(1)}, f32[4,10,4,256]{3,2,1,0:T(4,128)S(1)}, u32[]{:S(2)}, u32[]{:S(2)}) collective-permute-start(f32[4,10,4,256]{3,2,1,0:T(4,128)S(1)} %bitcast.127), channel_id=1, source_target_pairs={{0,32},{8,40},{16,48},{24,56},{32,0},{40,8},{48,16},{56,24},{64,96... | collective-permute-start | bytes 491528 | tf_op jit(solution)/shard_map/ppermute | solution.py:9
  21.9 17.2 %collective-permute-start.3 = (f32[4,10,4,256]{3,2,1,0:T(4,128)S(1)}, f32[4,10,4,256]{3,2,1,0:T(4,128)S(1)}, u32[]{:S(2)}, u32[]{:S(2)}) collective-permute-start(f32[4,10,4,256]{3,2,1,0:T(4,128)S(1)} %bitcast.128), channel_id=1, source_target_pairs={{0,64},{8,72},{16,80},{24,88},{32,96},{40,104},{48,112},{56,120},{... | collective-permute-start | bytes 491528 | tf_op jit(solution)/shard_map/ppermute | solution.py:9
  27.9 0.8 %copy-start.14 = (f32[4,2048]{1,0:T(4,128)S(1)}, f32[4,2048]{1,0:T(4,128)}, u32[]{:S(2)}) copy-start(f32[4,2048]{1,0:T(4,128)} %param.19) | copy-start | bytes 98308
  44.1 6.0 %copy-start.8 = (f32[9,4,2048]{2,1,0:T(4,128)S(1)}, f32[9,4,2048]{2,1,0:T(4,128)}, u32[]{:S(2)}) copy-start(f32[9,4,2048]{2,1,0:T(4,128)} %get-tuple-element.53) | copy-start | bytes 884740
  44.1 9.9 %all-to-all-start = ((f32[8,2,10,256]{3,1,2,0:T(2,128)}), f32[8,2,10,256]{3,1,2,0:T(2,128)}, u32[]{:S(2)}, u32[]{:S(2)}) async-start(f32[8,2,10,256]{3,1,2,0:T(2,128)} %copy.46), calls=%async_computation | async-start | bytes 327680 | tf_op jit(solution)/shard_map/all_to_all | solution.py:69
  49.9 1.8 %copy-start.7 = (f32[10,4,2048]{2,1,0:T(4,128)S(1)}, f32[10,4,2048]{2,1,0:T(4,128)}, u32[]{:S(2)}) copy-start(f32[10,4,2048]{2,1,0:T(4,128)} %squeeze.45) | copy-start | bytes 983044
  49.9 1.8 %copy-start.9 = (f32[9,4,2048]{2,1,0:T(4,128)S(1)}, f32[9,4,2048]{2,1,0:T(4,128)}, u32[]{:S(2)}) copy-start(f32[9,4,2048]{2,1,0:T(4,128)} %get-tuple-element.25) | copy-start | bytes 884740
  50.0 1.8 %copy-start.12 = (f32[9,4,2048]{2,1,0:T(4,128)S(1)}, f32[9,4,2048]{2,1,0:T(4,128)}, u32[]{:S(2)}) copy-start(f32[9,4,2048]{2,1,0:T(4,128)} %get-tuple-element.49) | copy-start | bytes 884740
  50.9 1.8 %copy-start.6 = (f32[10,4,2048]{2,1,0:T(4,128)S(1)}, f32[10,4,2048]{2,1,0:T(4,128)}, u32[]{:S(2)}) copy-start(f32[10,4,2048]{2,1,0:T(4,128)} %squeeze.43) | copy-start | bytes 983044
  50.9 1.8 %copy-start.10 = (f32[9,4,2048]{2,1,0:T(4,128)S(1)}, f32[9,4,2048]{2,1,0:T(4,128)}, u32[]{:S(2)}) copy-start(f32[9,4,2048]{2,1,0:T(4,128)} %get-tuple-element.48) | copy-start | bytes 884740
  50.9 1.8 %copy-start.11 = (f32[9,4,2048]{2,1,0:T(4,128)S(1)}, f32[9,4,2048]{2,1,0:T(4,128)}, u32[]{:S(2)}) copy-start(f32[9,4,2048]{2,1,0:T(4,128)} %get-tuple-element.50) | copy-start | bytes 884740

commit v7 on v6

--- a/solution.py
+++ b/solution.py
@@ -104,13 +104,15 @@
     )
 
     n_field = members * layers
-    rows = jnp.concatenate(
-        [
-            jnp.stack([p_old, t_old, c_p, c_t]).reshape(4 * n_field, width),
-            jnp.stack([cond, therm]).reshape(2 * layers, width),
-        ]
-    )
-    picked = exact_select(rows, select, 1)
+    pieces = [x.reshape(n_field, width) for x in (p_old, t_old, c_p, c_t)]
+    pieces += [cond, therm]
+    highs = [lax.reduce_precision(x, exponent_bits=8, mantissa_bits=7) for x in pieces]
+    lows = [x - h for x, h in zip(pieces, highs)]
+    row_parts = jnp.concatenate([x.astype(jnp.bfloat16) for x in highs + lows])
+    picked = lax.dot_general(
+        row_parts, select, (((1,), (1,)), ((), ())), preferred_element_type=jnp.float32
+    )
+    picked = picked[: picked.shape[0] // 2] + picked[picked.shape[0] // 2 :]
     fields_f = picked[: 4 * n_field].reshape(4, layers, members, rounds, face)
     coefs_f = picked[4 * n_field :].reshape(2, layers, 1, rounds, face)
     wc = face_weight * coefs_f

time: 56.1 us -> 62.9 us (1.12)
  the two profiles are of different devices: /device:TPU:1 before, /device:TPU:136 now
where the time goes in v7:
time: 62.9 us; the launch traced here: 62 us
  starting transfers between devices  20.9 us (33%)
  local copies, waits for them, and re-layouts  15.7 us (25%)
  other arithmetic  14.3 us (23%)
  waiting for transfers between devices  5.88 us (9%)
  matrix products  4.02 us (6%)
  between operations  1.23 us (2%)
    ppermute x4, starting transfers between devices, from_partner(): return lax.ppermute(value, axis, pairs)  14.8 us
    concatenate x1, local copies, waits for them, and re-layouts, body(): row_parts = jnp.concatenate([x.astype(jnp.bfloat16) for x in highs + lows])  9.2 us
    all_to_all x1, starting transfers between devices, sum_scatter(): got = lax.all_to_all(parts, axis, 0, 0, tiled=True)  6.11 us
    ppermute x4, waiting for transfers between devices, from_partner(): return lax.ppermute(value, axis, pairs)  4.87 us
    transpose x4, other arithmetic, body(): return tuple((o.transpose(1, 0, 2) for o in outs)) + (owned,)  4.68 us
    convert_element_type x4, other arithmetic, body(): row_parts = jnp.concatenate([x.astype(jnp.bfloat16) for x in highs + lows])  3.06 us
    reshape x4, local copies, waits for them, and re-layouts, body(): pieces = [x.reshape(n_field, width) for x in (p_old, t_old, c_p, c_t)]  2.49 us
    dot_general x1, matrix products, exact_select(): lax.dot_general(split2(rows), select, (((1,), (contract,)), ((), ())), pr...  2.08 us
  transfers between devices with their start and end apart: 5, of which 2 were waited for; matrix products, arithmetic and copies ran while one was open for 15% of the time, Pallas kernels for 0%

profile of v7, /device:TPU:136, one launch (start us, length us, event | category | flops | bytes accessed | tf_op | source)
XLA Modules:
  0.0 62.0 jit_solution(9062957597454645509)
XLA Ops:
  0.6 0.0 copy-start.2
  0.6 0.0 copy-start.3
  0.7 0.0 copy-start.15
  0.7 1.2 %reshape.109 = f32[40,2048]{1,0:T(8,128)S(1)} reshape(f32[10,4,2048]{2,1,0:T(4,128)} %bitcast.76) | data formatting | bytes 655360 | tf_op jit(solution)/shard_map/reshape | solution.py:107
  1.9 1.1 %reshape.110 = f32[40,2048]{1,0:T(8,128)S(1)} reshape(f32[10,4,2048]{2,1,0:T(4,128)} %bitcast.79) | data formatting | bytes 655360 | tf_op jit(solution)/shard_map/reshape | solution.py:107
  3.0 0.1 reshape.111
  3.1 0.0 copy-done.3
  3.1 0.1 reshape.112
  3.3 0.7 %fusion.19 = (bf16[10,2048]{1,0:T(8,128)(2,1)}, f32[10,2048]{1,0:T(8,128)S(1)}, bf16[10,2048]{1,0:T(8,128)(2,1)}, f32[10,2048]{1,0:T(8,128)S(1)}) fusion(f32[10,2048]{1,0:T(8,128)S(1)} %copy-done.9, s32[10,2048]{1,0:T(8,128)S(1)} %copy-done.10, f32[10,2048]{1,0:T(8,128)S(1)} %copy-done.11, f32[10,2048]{1,0:T(8,128)S(1)} %copy-done.12), kind=kLoop, calls=%fused_computation.77 | loop fusion | flops 245760 | bytes 573440 | tf_op jit(solution)/shard_map/convert_element_type | solution.py:111
  4.0 0.7 %reduce-precision_convert_fusion.5 = (bf16[10,2048]{1,0:T(8,128)(2,1)}, bf16[10,2048]{1,0:T(8,128)(2,1)}) fusion(f32[10,2048]{1,0:T(8,128)S(1)} %get-tuple-element.30, f32[10,2048]{1,0:T(8,128)S(1)} %get-tuple-element.62), kind=kLoop, calls=%fused_computation.54 | loop fusion | flops 81920 | bytes 245760 | tf_op jit(solution)/shard_map/convert_element_type | solution.py:111
  4.7 0.8 %fusion.8 = (bf16[40,2048]{1,0:T(8,128)(2,1)S(1)}, bf16[40,2048]{1,0:T(8,128)(2,1)}, bf16[40,2048]{1,0:T(8,128)(2,1)}, bf16[40,2048]{1,0:T(8,128)(2,1)}) fusion(f32[40,2048]{1,0:T(8,128)S(1)} %reshape.109, f32[40,2048]{1,0:T(8,128)S(1)} %reshape.110), kind=kLoop, calls=%fused_computation.30 | loop fusion | flops 655360 | bytes 1310720 | tf_op jit(solution)/shard_map/convert_element_type | solution.py:111
  5.5 0.8 %fusion.10 = (bf16[40,2048]{1,0:T(8,128)(2,1)S(1)}, bf16[40,2048]{1,0:T(8,128)(2,1)S(1)}, bf16[40,2048]{1,0:T(8,128)(2,1)}, bf16[40,2048]{1,0:T(8,128)(2,1)}) fusion(f32[40,2048]{1,0:T(8,128)S(1)} %reshape.111, f32[40,2048]{1,0:T(8,128)S(1)} %reshape.112), kind=kLoop, calls=%fused_computation.32 | loop fusion | flops 655360 | bytes 1310720 | tf_op jit(solution)/shard_map/convert_element_type | solution.py:111
  6.4 9.2 %concatenate.19 = bf16[360,2048]{1,0:T(8,128)(2,1)S(1)} concatenate(bf16[40,2048]{1,0:T(8,128)(2,1)} %get-tuple-element.60, bf16[40,2048]{1,0:T(8,128)(2,1)} %get-tuple-element.70, bf16[40,2048]{1,0:T(8,128)(2,1)S(1)} %get-tuple-element.56, bf16[40,2048]{1,0:T(8,128)(2,1)} %get-tuple-element.72, bf16[10,2048]{1,0:T(8,128)(2,1)} %get-tuple-element.67, ...), dimensions={0} | concatenate | bytes 2949120 | tf_op jit(solution)/shard_map/concatenate | solution.py:111
  15.6 1.9 %fusion.1 = f32[360,1024]{1,0:T(8,128)S(1)} fusion(bf16[360,2048]{1,0:T(8,128)(2,1)S(1)} %concatenate.19, s32[1024]{0:T(1024)S(1)} %bitcast.111), kind=kOutput, calls=%fused_computation.2 | convolution fusion | flops 1512046592 | bytes 2953216 | tf_op jit(solution)/shard_map/dot_general | solution.py:112
  17.5 0.1 slice_add_fusion.1
  17.6 0.0 copy-start.14
  17.7 0.2 slice.164
  17.9 0.2 slice.166
  18.1 0.2 copy-done.14
  18.4 0.1 broadcast_multiply_fusion.3
  18.4 0.5 fusion.14
  19.0 4.5 %collective-permute-start.2 = (f32[4,10,4,256]{3,2,1,0:T(4,128)S(1)}, f32[4,10,4,256]{3,2,1,0:T(4,128)S(1)}, u32[]{:S(2)}, u32[]{:S(2)}) collective-permute-start(f32[4,10,4,256]{3,2,1,0:T(4,128)S(1)} %bitcast.104), channel_id=1, source_target_pairs={{0,32},{8,40},{16,48},{24,56},{32,0},{40,8},{48,16},{56,24},{64,96... | collective-permute-start | bytes 491528 | tf_op jit(solution)/shard_map/ppermute | solution.py:9
  23.5 0.0 copy-start
  23.5 0.0 copy-start.1
  23.6 5.2 %collective-permute-start.3 = (f32[4,10,4,256]{3,2,1,0:T(4,128)S(1)}, f32[4,10,4,256]{3,2,1,0:T(4,128)S(1)}, u32[]{:S(2)}, u32[]{:S(2)}) collective-permute-start(f32[4,10,4,256]{3,2,1,0:T(4,128)S(1)} %bitcast.105), channel_id=1, source_target_pairs={{0,64},{8,72},{16,80},{24,88},{32,96},{40,104},{48,112},{56,120},{... | collective-permute-start | bytes 491528 | tf_op jit(solution)/shard_map/ppermute | solution.py:9
  28.8 1.9 %collective-permute-start = (f32[4,10,4,256]{3,2,1,0:T(4,128)S(1)}, f32[4,10,4,256]{3,2,1,0:T(4,128)S(1)}, u32[]{:S(2)}, u32[]{:S(2)}) collective-permute-start(f32[4,10,4,256]{3,2,1,0:T(4,128)S(1)} %bitcast.106), channel_id=1, source_target_pairs={{0,8},{8,0},{16,24},{24,16},{32,40},{40,32},{48,56},{56,48},{64,72... | collective-permute-start | bytes 491528 | tf_op jit(solution)/shard_map/ppermute | solution.py:9
  30.8 3.2 %collective-permute-start.1 = (f32[4,10,4,256]{3,2,1,0:T(4,128)S(1)}, f32[4,10,4,256]{3,2,1,0:T(4,128)S(1)}, u32[]{:S(2)}, u32[]{:S(2)}) collective-permute-start(f32[4,10,4,256]{3,2,1,0:T(4,128)S(1)} %bitcast.107), channel_id=1, source_target_pairs={{0,16},{8,24},{16,0},{24,8},{32,48},{40,56},{48,32},{56,40},{64,80... | collective-permute-start | bytes 491528 | tf_op jit(solution)/shard_map/ppermute | solution.py:9
  34.1 0.2 broadcast_multiply_fusion
  34.3 0.4 multiply_reduce_fusion.2
  34.7 1.1 %multiply_multiply_fusion = (f32[9,4,2048]{2,1,0:T(4,128)}, f32[9,4,2048]{2,1,0:T(4,128)S(1)}, f32[9,4,2048]{2,1,0:T(4,128)}) fusion(f32[9,4,2048]{2,1,0:T(4,128)S(1)} %get-tuple-element.24, f32[10,4,2048]{2,1,0:T(4,128)S(1)} %bitcast.78, f32[9,2048]{1,0:T(8,128)S(1)} %get-tuple-element.69, f32[9,4,2048]{2,1,0:T(4,128)S(1)} %get-tuple-element.23), kind=kLoop, calls=%fused_computation.52 | loop fusion | flops 368640 | bytes 2138112 | tf_op jit(solution)/shard_map/mul | solution.py:172
  35.8 0.1 pad_subtract_fusion
  35.8 1.1 %multiply_reduce_fusion.1 = (f32[9,2048]{1,0:T(8,128)S(1)}, f32[9,4,2048]{2,1,0:T(4,128)}, f32[9,4,2048]{2,1,0:T(4,128)}, f32[9,4,2048]{2,1,0:T(4,128)}) fusion(f32[9,4,2048]{2,1,0:T(4,128)S(1)} %get-tuple-element.24, f32[10,4,2048]{2,1,0:T(4,128)S(1)} %bitcast.81, f32[9,2048]{1,0:T(8,128)S(1)} %get-tuple-element.68, f32[9,4,2048]{2,1,0:T(4,128)S(1)} %get-tuple-element.26), kind=kLoop, calls=%fused_computation.48 | loop fusion | flops 571392 | bytes 2211840 | tf_op jit(solution)/shard_map/reduce_sum | solution.py:147
  37.3 0.5 copy-done.13
  37.8 0.0 collective-permute-done.2
  37.8 4.9 %collective-permute-done.3 = f32[4,10,4,256]{3,2,1,0:T(4,128)S(1)} collective-permute-done((f32[4,10,4,256]{3,2,1,0:T(4,128)S(1)}, f32[4,10,4,256]{3,2,1,0:T(4,128)S(1)}, u32[]{:S(2)}, u32[]{:S(2)}) %collective-permute-start.3) | collective-permute-done | bytes 163872 | tf_op jit(solution)/shard_map/ppermute | solution.py:9
  42.6 0.0 collective-permute-done
  42.6 0.0 collective-permute-done.1
  42.6 0.1 pad_maximum_fusion.1
  42.8 0.1 fusion.31
  42.9 0.3 copy_subtract_fusion
  43.2 0.4 multiply_reduce_fusion
  43.6 0.2 pad_maximum_fusion.2
  43.8 0.1 copy.54
  44.0 0.1 reduce-precision_convert_fusion
  44.1 2.1 %fusion = f32[360,2048]{1,0:T(8,128)S(1)} fusion(s32[1024]{0:T(1024)S(1)} %bitcast.112, bf16[180,1024]{1,0:T(8,128)(2,1)S(1)} %get-tuple-element.38, bf16[180,1024]{1,0:T(8,128)(2,1)S(1)} %get-tuple-element.37), kind=kOutput, calls=%fused_computation.1 | convolution fusion | flops 1513521152 | bytes 3690496 | tf_op jit(solution)/shard_map/dot_general | solution.py:39
  46.2 0.2 slice_add_fusion
  46.4 0.2 fusion.29
  46.6 0.1 copy.57
  46.7 0.8 %copy.46 = f32[8,2,10,256]{3,1,2,0:T(2,128)} copy(f32[8,2,10,256]{3,0,2,1:T(8,128)S(1)} %fusion.17) | data formatting | bytes 327680 | tf_op jit(solution)/shard_map/transpose | solution.py:68
  47.5 6.1 %all-to-all-start = ((f32[8,2,10,256]{3,1,2,0:T(2,128)}), f32[8,2,10,256]{3,1,2,0:T(2,128)}, u32[]{:S(2)}, u32[]{:S(2)}) async-start(f32[8,2,10,256]{3,1,2,0:T(2,128)} %copy.46), calls=%async_computation | async-start | bytes 327680 | tf_op jit(solution)/shard_map/all_to_all | solution.py:69
  53.6 0.8 %squeeze.45 = f32[10,4,2048]{2,1,0:T(4,128)} reshape(f32[40,2048]{1,0:T(8,128)S(1)} %get-tuple-element.33) | data formatting | bytes 655360 | tf_op jit(solution)/shard_map/squeeze | solution.py:172
  54.4 0.1 squeeze.44
  54.5 0.1 squeeze.43
  54.6 0.0 copy-start.4
  54.7 0.1 squeeze.42
  54.8 0.0 copy-start.5
  54.8 0.0 copy-start.8
  54.8 2.0 %add_bitcast_fusion.1 = f32[4,10,2048]{2,0,1:T(4,128)} fusion(f32[10,4,2048]{2,1,0:T(4,128)S(1)} %squeeze.44, f32[9,4,2048]{2,1,0:T(4,128)} %get-tuple-element.63, f32[4,10,2048]{2,0,1:T(4,128)S(1)} %copy-done.2), kind=kLoop, calls=%fused_computation.37 | loop fusion | flops 245760 | bytes 1277952 | tf_op jit(solution)/shard_map/transpose | solution.py:174
  56.8 0.9 %add_bitcast_fusion.3 = f32[4,10,2048]{2,0,1:T(4,128)} fusion(f32[10,4,2048]{2,1,0:T(4,128)S(1)} %fusion.24, f32[10,4,2048]{2,1,0:T(4,128)S(1)} %squeeze.42, f32[4,10,2048]{2,0,1:T(4,128)S(1)} %copy-done), kind=kLoop, calls=%fused_computation.39 | loop fusion | flops 245760 | bytes 1310720 | tf_op jit(solution)/shard_map/transpose | solution.py:174
  57.7 0.9 %add_bitcast_fusion = f32[4,10,2048]{2,0,1:T(4,128)} fusion(f32[10,4,2048]{2,1,0:T(4,128)S(1)} %copy-done.4, f32[9,4,2048]{2,1,0:T(4,128)S(1)} %copy-done.5, f32[9,4,2048]{2,1,0:T(4,128)S(1)} %copy-done.8, f32[4,10,2048]{2,0,1:T(4,128)S(1)} %copy-done.3), kind=kLoop, calls=%fused_computation.36 | loop fusion | flops 491520 | bytes 1572864 | tf_op jit(solution)/shard_map/transpose | solution.py:174
  58.6 0.0 copy-done.6
  58.6 0.9 %add_bitcast_fusion.2 = f32[4,10,2048]{2,0,1:T(4,128)} fusion(f32[10,4,2048]{2,1,0:T(4,128)S(1)} %squeeze.43, f32[9,4,2048]{2,1,0:T(4,128)S(1)} %copy-done.7, f32[9,4,2048]{2,1,0:T(4,128)S(1)} %copy-done.6, f32[4,10,2048]{2,0,1:T(4,128)S(1)} %copy-done.1), kind=kLoop, calls=%fused_computation.38 | loop fusion | flops 573440 | bytes 1572864 | tf_op jit(solution)/shard_map/transpose | solution.py:174
  59.5 1.0 %all-to-all-done = f32[8,2,10,256]{3,1,2,0:T(2,128)} async-done(((f32[8,2,10,256]{3,1,2,0:T(2,128)}), f32[8,2,10,256]{3,1,2,0:T(2,128)}, u32[]{:S(2)}, u32[]{:S(2)}) %all-to-all-start) | async-done | bytes 163872 | tf_op jit(solution)/shard_map/all_to_all | solution.py:69
  60.5 1.5 %fusion.25 = f32[2,10,256]{2,0,1:T(2,128)} fusion(f32[8,2,10,256]{3,1,2,0:T(2,128)} %all-to-all-done), kind=kLoop, calls=%fused_computation.98 | loop fusion | flops 35840 | bytes 184320 | tf_op jit(solution)/shard_map/add | solution.py:72
  (46 shorter events, 0.8 us)
Async XLA Ops:
  0.6 2.3 %copy-start.2 = (f32[4,10,2048]{2,0,1:T(4,128)S(1)}, f32[4,10,2048]{2,0,1:T(4,128)}, u32[]{:S(2)}) copy-start(f32[4,10,2048]{2,0,1:T(4,128)} %param.22) | copy-start | bytes 983044
  0.6 2.5 %copy-start.3 = (f32[4,10,2048]{2,0,1:T(4,128)S(1)}, f32[4,10,2048]{2,0,1:T(4,128)}, u32[]{:S(2)}) copy-start(f32[4,10,2048]{2,0,1:T(4,128)} %param.23) | copy-start | bytes 983044
  0.7 2.6 %copy-start.15 = (s32[4,256]{1,0:T(4,128)S(1)}, s32[4,256]{1,0:T(4,128)}, u32[]{:S(2)}) copy-start(s32[4,256]{1,0:T(4,128)} %param.20) | copy-start | bytes 12292
  0.7 2.6 %copy-start.12 = (f32[10,2048]{1,0:T(8,128)S(1)}, f32[10,2048]{1,0:T(8,128)}, u32[]{:S(2)}) copy-start(f32[10,2048]{1,0:T(8,128)} %param.15) | copy-start | bytes 245764
  0.7 2.6 %copy-start.11 = (f32[10,2048]{1,0:T(8,128)S(1)}, f32[10,2048]{1,0:T(8,128)}, u32[]{:S(2)}) copy-start(f32[10,2048]{1,0:T(8,128)} %param.16) | copy-start | bytes 245764
  0.7 2.6 %copy-start.9 = (f32[10,2048]{1,0:T(8,128)S(1)}, f32[10,2048]{1,0:T(8,128)}, u32[]{:S(2)}) copy-start(f32[10,2048]{1,0:T(8,128)} %param.17) | copy-start | bytes 245764
  0.7 2.6 %copy-start.10 = (s32[10,2048]{1,0:T(8,128)S(1)}, s32[10,2048]{1,0:T(8,128)}, u32[]{:S(2)}) copy-start(s32[10,2048]{1,0:T(8,128)} %param.18) | copy-start | bytes 245764
  17.6 0.7 %copy-start.14 = (f32[4,256]{1,0:T(4,128)S(1)}, f32[4,256]{1,0:T(4,128)}, u32[]{:S(2)}) copy-start(f32[4,256]{1,0:T(4,128)} %param.21) | copy-start | bytes 12292
  19.0 18.8 %collective-permute-start.2 = (f32[4,10,4,256]{3,2,1,0:T(4,128)S(1)}, f32[4,10,4,256]{3,2,1,0:T(4,128)S(1)}, u32[]{:S(2)}, u32[]{:S(2)}) collective-permute-start(f32[4,10,4,256]{3,2,1,0:T(4,128)S(1)} %bitcast.104), channel_id=1, source_target_pairs={{0,32},{8,40},{16,48},{24,56},{32,0},{40,8},{48,16},{56,24},{64,96... | collective-permute-start | bytes 491528 | tf_op jit(solution)/shard_map/ppermute | solution.py:9
  23.5 10.8 %copy-start = (f32[4,10,2048]{2,0,1:T(4,128)S(1)}, f32[4,10,2048]{2,0,1:T(4,128)}, u32[]{:S(2)}) copy-start(f32[4,10,2048]{2,0,1:T(4,128)} %param.13) | copy-start | bytes 983044
  23.5 10.8 %copy-start.1 = (f32[4,10,2048]{2,0,1:T(4,128)S(1)}, f32[4,10,2048]{2,0,1:T(4,128)}, u32[]{:S(2)}) copy-start(f32[4,10,2048]{2,0,1:T(4,128)} %param.14) | copy-start | bytes 983044
  23.6 19.1 %collective-permute-start.3 = (f32[4,10,4,256]{3,2,1,0:T(4,128)S(1)}, f32[4,10,4,256]{3,2,1,0:T(4,128)S(1)}, u32[]{:S(2)}, u32[]{:S(2)}) collective-permute-start(f32[4,10,4,256]{3,2,1,0:T(4,128)S(1)} %bitcast.105), channel_id=1, source_target_pairs={{0,64},{8,72},{16,80},{24,88},{32,96},{40,104},{48,112},{56,120},{... | collective-permute-start | bytes 491528 | tf_op jit(solution)/shard_map/ppermute | solution.py:9
  28.8 13.8 %collective-permute-start = (f32[4,10,4,256]{3,2,1,0:T(4,128)S(1)}, f32[4,10,4,256]{3,2,1,0:T(4,128)S(1)}, u32[]{:S(2)}, u32[]{:S(2)}) collective-permute-start(f32[4,10,4,256]{3,2,1,0:T(4,128)S(1)} %bitcast.106), channel_id=1, source_target_pairs={{0,8},{8,0},{16,24},{24,16},{32,40},{40,32},{48,56},{56,48},{64,72... | collective-permute-start | bytes 491528 | tf_op jit(solution)/shard_map/ppermute | solution.py:9
  30.8 11.9 %collective-permute-start.1 = (f32[4,10,4,256]{3,2,1,0:T(4,128)S(1)}, f32[4,10,4,256]{3,2,1,0:T(4,128)S(1)}, u32[]{:S(2)}, u32[]{:S(2)}) collective-permute-start(f32[4,10,4,256]{3,2,1,0:T(4,128)S(1)} %bitcast.107), channel_id=1, source_target_pairs={{0,16},{8,24},{16,0},{24,8},{32,48},{40,56},{48,32},{56,40},{64,80... | collective-permute-start | bytes 491528 | tf_op jit(solution)/shard_map/ppermute | solution.py:9
  37.0 0.8 %copy-start.13 = (f32[4,2048]{1,0:T(4,128)S(1)}, f32[4,2048]{1,0:T(4,128)}, u32[]{:S(2)}) copy-start(f32[4,2048]{1,0:T(4,128)} %param.19) | copy-start | bytes 98308
  47.5 13.0 %all-to-all-start = ((f32[8,2,10,256]{3,1,2,0:T(2,128)}), f32[8,2,10,256]{3,1,2,0:T(2,128)}, u32[]{:S(2)}, u32[]{:S(2)}) async-start(f32[8,2,10,256]{3,1,2,0:T(2,128)} %copy.46), calls=%async_computation | async-start | bytes 327680 | tf_op jit(solution)/shard_map/all_to_all | solution.py:69
  54.6 3.0 %copy-start.4 = (f32[10,4,2048]{2,1,0:T(4,128)S(1)}, f32[10,4,2048]{2,1,0:T(4,128)}, u32[]{:S(2)}) copy-start(f32[10,4,2048]{2,1,0:T(4,128)} %squeeze.45) | copy-start | bytes 983044
  54.8 2.9 %copy-start.5 = (f32[9,4,2048]{2,1,0:T(4,128)S(1)}, f32[9,4,2048]{2,1,0:T(4,128)}, u32[]{:S(2)}) copy-start(f32[9,4,2048]{2,1,0:T(4,128)} %get-tuple-element.25) | copy-start | bytes 884740
  54.8 2.9 %copy-start.8 = (f32[9,4,2048]{2,1,0:T(4,128)S(1)}, f32[9,4,2048]{2,1,0:T(4,128)}, u32[]{:S(2)}) copy-start(f32[9,4,2048]{2,1,0:T(4,128)} %get-tuple-element.51) | copy-start | bytes 884740
  56.8 1.8 %copy-start.6 = (f32[9,4,2048]{2,1,0:T(4,128)S(1)}, f32[9,4,2048]{2,1,0:T(4,128)}, u32[]{:S(2)}) copy-start(f32[9,4,2048]{2,1,0:T(4,128)} %get-tuple-element.50) | copy-start | bytes 884740
  56.8 1.8 %copy-start.7 = (f32[9,4,2048]{2,1,0:T(4,128)S(1)}, f32[9,4,2048]{2,1,0:T(4,128)}, u32[]{:S(2)}) copy-start(f32[9,4,2048]{2,1,0:T(4,128)} %get-tuple-element.52) | copy-start | bytes 884740

commit v8 on v6

--- a/solution.py
+++ b/solution.py
@@ -65,12 +65,13 @@
 def sum_scatter(value, axis):
     size = lax.axis_size(axis)
     width = value.shape[-1] // size
-    parts = jnp.moveaxis(value.reshape(value.shape[:-1] + (size, width)), -2, 0)
+    rows = value.reshape(-1, size, width)
+    parts = jnp.moveaxis(rows, 1, 0)
     got = lax.all_to_all(parts, axis, 0, 0, tiled=True)
     total = got[0]
     for index in range(1, size):
         total = total + got[index]
-    return total
+    return total.reshape(value.shape[:-1] + (width,))
 
 
 def body(

time: 56.1 us -> 59.7 us (1.064)
  the two profiles are of different devices: /device:TPU:1 before, /device:TPU:136 now
where the time goes in v8:
time: 59.7 us; the launch traced here: 59.3 us
  starting transfers between devices  20.8 us (35%)
  other arithmetic  14.3 us (24%)
  waiting for transfers between devices  9.69 us (16%)
  local copies, waits for them, and re-layouts  8.98 us (15%)
  matrix products  4.24 us (7%)
  between operations  1.22 us (2%)
    ppermute x4, starting transfers between devices, from_partner(): return lax.ppermute(value, axis, pairs)  14.7 us
    ppermute x4, waiting for transfers between devices, from_partner(): return lax.ppermute(value, axis, pairs)  7.88 us
    all_to_all x1, starting transfers between devices, sum_scatter(): got = lax.all_to_all(parts, axis, 0, 0, tiled=True)  6.14 us
    unnamed x54, local copies, waits for them, and re-layouts  5.91 us
    transpose x4, other arithmetic, body(): return tuple((o.transpose(1, 0, 2) for o in outs)) + (owned,)  4.68 us
    dot_general x2, matrix products, exact_select(): lax.dot_general(split2(rows), select, (((1,), (contract,)), ((), ())), pr...  4.24 us
    all_to_all x1, waiting for transfers between devices, sum_scatter(): got = lax.all_to_all(parts, axis, 0, 0, tiled=True)  1.81 us
    another operation x1, other arithmetic, body(): far = jnp.stack(far, axis=-2)  1.3 us
  transfers between devices with their start and end apart: 5, of which 3 were waited for; matrix products, arithmetic and copies ran while one was open for 19% of the time, Pallas kernels for 0%

profile of v8, /device:TPU:136, one launch (start us, length us, event | category | flops | bytes accessed | tf_op | source)
XLA Modules:
  0.0 59.3 jit_solution(572217773429865503)
XLA Ops:
  0.7 0.0 copy-start.2
  0.7 0.0 copy-start.4
  0.7 1.2 %add_multiply_fusion.1 = (f32[10,2048]{1,0:T(8,128)S(1)}, f32[10,2048]{1,0:T(8,128)S(1)}) fusion(f32[10,2048]{1,0:T(8,128)} %param.16, f32[10,2048]{1,0:T(8,128)} %param.17, s32[10,2048]{1,0:T(8,128)} %param.18, f32[10,2048]{1,0:T(8,128)} %param.15), kind=kLoop, calls=%fused_computation.80 | loop fusion | flops 122880 | bytes 491520 | tf_op jit(solution)/shard_map/mul | solution.py:98
  1.9 0.0 copy-start.6
  2.0 0.7 %reshape.107 = f32[20,2048]{1,0:T(8,128)} reshape(f32[2,10,2048]{2,1,0:T(8,128)S(1)} %pad_maximum_fusion.4) | data formatting | bytes 327680 | tf_op jit(solution)/shard_map/reshape | solution.py:111
  2.7 0.6 pad_maximum_fusion
  3.3 0.5 reshape.106
  3.8 0.0 copy-start.14
  3.8 0.1 constant_dynamic-update-slice_fusion.1
  3.9 0.8 %copy-done.14 = f32[20,2048]{1,0:T(8,128)S(1)} copy-done((f32[20,2048]{1,0:T(8,128)S(1)}, f32[20,2048]{1,0:T(8,128)}, u32[]{:S(2)}) %copy-start.14) | copy-done | bytes 163864
  4.7 0.0 copy-start.20
  4.7 0.2 reduce-precision_convert_fusion
  4.9 0.5 copy-done.20
  5.4 2.2 %fusion.1 = f32[360,1024]{1,0:T(8,128)S(1)} fusion(s32[1024]{0:T(1024)S(1)} %bitcast.96, bf16[180,2048]{1,0:T(8,128)(2,1)S(1)} %get-tuple-element.39, bf16[180,2048]{1,0:T(8,128)(2,1)S(1)} %get-tuple-element.38), kind=kOutput, calls=%fused_computation.2 | convolution fusion | flops 1514995712 | bytes 2953216 | tf_op jit(solution)/shard_map/dot_general | solution.py:39
  7.6 0.1 slice_add_fusion.1
  7.7 0.0 copy-start.19
  7.8 0.2 slice.164
  8.0 0.2 slice.166
  8.2 0.2 copy-done.19
  8.4 0.7 %broadcast_multiply_fusion.7 = (f32[2,10,4,256]{3,2,1,0:T(4,128)S(1)}, f32[2,10,4,256]{3,2,1,0:T(4,128)}) fusion(f32[2,10,4,256]{3,2,1,0:T(4,128)S(1)} %reshape.108, f32[4,256]{1,0:T(4,128)S(1)} %copy-done.19), kind=kLoop, calls=%fused_computation.84 | loop fusion | flops 40960 | bytes 249856 | tf_op jit(solution)/shard_map/mul | solution.py:120
  9.1 0.1 broadcast_multiply_fusion.1
  9.1 0.5 fusion.19
  9.6 0.0 copy-start.7
  9.6 0.7 %copy.55 = f32[4,10,4,1,256]{4,2,1,0,3:T(4,128)} copy(f32[4,10,4,1,256]{4,3,2,1,0:T(1,128)S(1)} %get-tuple-element.48) | data formatting | bytes 327680
  10.4 1.9 %collective-permute-start = (f32[4,10,4,256]{3,2,1,0:T(4,128)}, f32[4,10,4,256]{3,2,1,0:T(4,128)}, u32[]{:S(2)}, u32[]{:S(2)}) collective-permute-start(f32[4,10,4,256]{3,2,1,0:T(4,128)} %bitcast.74), channel_id=1, source_target_pairs={{0,8},{8,0},{16,24},{24,16},{32,40},{40,32},{48,56},{56,48},{64,72... | collective-permute-start | bytes 491528 | tf_op jit(solution)/shard_map/ppermute | solution.py:9
  12.3 0.7 %copy.54 = f32[4,10,4,1,256]{4,2,1,0,3:T(4,128)} copy(f32[4,10,4,1,256]{4,3,2,1,0:T(1,128)S(1)} %get-tuple-element.49) | data formatting | bytes 327680
  13.0 2.4 %collective-permute-start.1 = (f32[4,10,4,256]{3,2,1,0:T(4,128)}, f32[4,10,4,256]{3,2,1,0:T(4,128)}, u32[]{:S(2)}, u32[]{:S(2)}) collective-permute-start(f32[4,10,4,256]{3,2,1,0:T(4,128)} %bitcast.73), channel_id=1, source_target_pairs={{0,16},{8,24},{16,0},{24,8},{32,48},{40,56},{48,32},{56,40},{64,80... | collective-permute-start | bytes 491528 | tf_op jit(solution)/shard_map/ppermute | solution.py:9
  15.4 0.7 %copy.53 = f32[4,10,4,1,256]{4,2,1,0,3:T(4,128)} copy(f32[4,10,4,1,256]{4,3,2,1,0:T(1,128)S(1)} %get-tuple-element.51) | data formatting | bytes 327680
  16.1 4.5 %collective-permute-start.2 = (f32[4,10,4,256]{3,2,1,0:T(4,128)}, f32[4,10,4,256]{3,2,1,0:T(4,128)}, u32[]{:S(2)}, u32[]{:S(2)}) collective-permute-start(f32[4,10,4,256]{3,2,1,0:T(4,128)} %bitcast.72), channel_id=1, source_target_pairs={{0,32},{8,40},{16,48},{24,56},{32,0},{40,8},{48,16},{56,24},{64,96... | collective-permute-start | bytes 491528 | tf_op jit(solution)/shard_map/ppermute | solution.py:9
  20.5 0.7 %copy.56 = f32[4,10,4,1,256]{4,2,3,1,0:T(4,128)} copy(f32[4,10,4,1,256]{4,3,2,1,0:T(1,128)S(1)} %get-tuple-element.50) | data formatting | bytes 327680
  21.3 5.9 %collective-permute-start.3 = (f32[4,10,4,256]{3,2,1,0:T(4,128)}, f32[4,10,4,256]{3,2,1,0:T(4,128)}, u32[]{:S(2)}, u32[]{:S(2)}) collective-permute-start(f32[4,10,4,256]{3,2,1,0:T(4,128)} %bitcast.75), channel_id=1, source_target_pairs={{0,64},{8,72},{16,80},{24,88},{32,96},{40,104},{48,112},{56,120},{... | collective-permute-start | bytes 491528 | tf_op jit(solution)/shard_map/ppermute | solution.py:9
  27.2 0.2 bitcast_multiply_fusion
  27.5 0.7 %fusion.23 = (f32[9,2048]{1,0:T(8,128)}, f32[9,2048]{1,0:T(8,128)}) fusion(f32[10,2048]{1,0:T(8,128)S(1)} %copy-done.7, f32[10,2048]{1,0:T(8,128)S(1)} %copy-done.9), kind=kLoop, calls=%fused_computation.75 | loop fusion | flops 73728 | bytes 442368 | tf_op jit(solution)/shard_map/mul | solution.py:134
  28.3 0.4 multiply_reduce_fusion.2
  28.7 0.5 copy-done.16
  29.2 1.1 %multiply_multiply_fusion = (f32[9,4,2048]{2,1,0:T(4,128)}, f32[9,4,2048]{2,1,0:T(4,128)S(1)}, f32[9,4,2048]{2,1,0:T(4,128)}) fusion(f32[9,4,2048]{2,1,0:T(4,128)S(1)} %get-tuple-element.29, f32[10,4,2048]{2,1,0:T(4,128)S(1)} %bitcast.81, f32[9,2048]{1,0:T(8,128)S(1)} %copy-done.16, f32[9,4,2048]{2,1,0:T(4,128)S(1)} %get-tuple-element.28), kind=kLoop, calls=%fused_computation.56 | loop fusion | flops 368640 | bytes 2138112 | tf_op jit(solution)/shard_map/mul | solution.py:171
  30.2 0.1 pad_subtract_fusion
  30.3 0.0 copy-start.18
  30.3 1.2 %multiply_reduce_fusion.1 = (f32[9,2048]{1,0:T(8,128)S(1)}, f32[9,4,2048]{2,1,0:T(4,128)}, f32[9,4,2048]{2,1,0:T(4,128)}, f32[9,4,2048]{2,1,0:T(4,128)}) fusion(f32[9,4,2048]{2,1,0:T(4,128)S(1)} %get-tuple-element.29, f32[10,4,2048]{2,1,0:T(4,128)S(1)} %bitcast.78, f32[9,2048]{1,0:T(8,128)S(1)} %copy-done.15, f32[9,4,2048]{2,1,0:T(4,128)S(1)} %get-tuple-element.31), kind=kLoop, calls=%fused_computation.50 | loop fusion | flops 571392 | bytes 2211840 | tf_op jit(solution)/shard_map/reduce_sum | solution.py:146
  31.7 1.1 %collective-permute-done.2 = f32[4,10,4,256]{3,2,1,0:T(4,128)} collective-permute-done((f32[4,10,4,256]{3,2,1,0:T(4,128)}, f32[4,10,4,256]{3,2,1,0:T(4,128)}, u32[]{:S(2)}, u32[]{:S(2)}) %collective-permute-start.2) | collective-permute-done | bytes 163872 | tf_op jit(solution)/shard_map/ppermute | solution.py:9
  32.8 6.8 %collective-permute-done.3 = f32[4,10,4,256]{3,2,1,0:T(4,128)} collective-permute-done((f32[4,10,4,256]{3,2,1,0:T(4,128)}, f32[4,10,4,256]{3,2,1,0:T(4,128)}, u32[]{:S(2)}, u32[]{:S(2)}) %collective-permute-start.3) | collective-permute-done | bytes 163872 | tf_op jit(solution)/shard_map/ppermute | solution.py:9
  39.5 1.3 %pad_maximum_fusion.2 = f32[4,10,4,4,256]{4,2,1,0,3:T(4,128)S(1)} fusion(f32[4,10,4,1,256]{4,2,1,0,3:T(4,128)} %bitcast.17, f32[4,10,4,1,256]{4,2,1,0,3:T(4,128)} %bitcast.16, f32[4,10,4,1,256]{4,2,1,0,3:T(4,128)} %bitcast.14, f32[4,10,4,1,256]{4,2,1,0,3:T(4,128)} %bitcast.12), kind=kLoop, calls=%fused_computation.27 | loop fusion | flops 491520 | bytes 1310720 | tf_op jit(solution)/shard_map/stack | solution.py:126
  40.8 0.1 fusion.34
  41.0 0.6 %multiply_reduce_fusion = (f32[2,10,4,256]{3,2,1,0:T(4,128)S(1)}, f32[2,10,4,4,256]{4,3,2,1,0:T(4,128)S(1)}, f32[2,10,4,4,256]{4,3,2,1,0:T(4,128)S(1)}) fusion(f32[2,10,4,4,256]{4,3,2,1,0:T(4,128)S(1)} %slice.164, f32[2,10,4,4,256]{4,3,2,1,0:T(4,128)S(1)} %slice.166, f32[2,10,4,4,256]{4,2,1,0,3:T(4,128)S(1)} %get-tuple-element.46, ...), kind=kLoop, calls=%fused_computation.42 | loop fusion | flops 552960 | bytes 2211840 | tf_op jit(solution)/shard_map/reduce_sum | solution.py:131
  41.6 0.2 pad_maximum_fusion.3
  41.8 0.1 copy.41
  42.0 0.2 reduce-precision_convert_fusion.1
  42.2 2.1 %fusion = f32[360,2048]{1,0:T(8,128)S(1)} fusion(s32[1024]{0:T(1024)S(1)} %bitcast.97, bf16[180,1024]{1,0:T(8,128)(2,1)S(1)} %get-tuple-element.41, bf16[180,1024]{1,0:T(8,128)(2,1)S(1)} %get-tuple-element.40), kind=kOutput, calls=%fused_computation.1 | convolution fusion | flops 1513521152 | bytes 3690496 | tf_op jit(solution)/shard_map/dot_general | solution.py:39
  44.3 0.2 slice_add_fusion
  44.5 0.2 fusion.32
  44.7 0.1 copy.42
  44.8 0.7 %copy.32 = f32[8,20,256]{2,1,0:T(8,128)} copy(f32[8,20,256]{2,0,1:T(8,128)S(1)} %fusion.22) | data formatting | bytes 327680 | tf_op jit(solution)/shard_map/transpose | solution.py:69
  45.5 6.1 %all-to-all-start = ((f32[8,20,256]{2,1,0:T(8,128)}), f32[8,20,256]{2,1,0:T(8,128)S(1)}, u32[]{:S(2)}, u32[]{:S(2)}) async-start(f32[8,20,256]{2,1,0:T(8,128)} %copy.32), calls=%async_computation | async-start | bytes 393216 | tf_op jit(solution)/shard_map/all_to_all | solution.py:70
  51.7 0.1 squeeze.45
  51.8 0.1 squeeze.44
  51.9 0.1 squeeze.43
  52.0 0.1 squeeze.42
  52.1 0.0 copy-start.10
  52.1 2.0 %fusion.16 = f32[4,10,2048]{2,0,1:T(4,128)} fusion(f32[10,4,2048]{2,1,0:T(4,128)S(1)} %squeeze.44, f32[4,10,2048]{2,0,1:T(4,128)S(1)} %copy-done.3, f32[9,4,2048]{2,1,0:T(4,128)} %get-tuple-element.58), kind=kLoop, calls=%fused_computation.37 | loop fusion | flops 245760 | bytes 1277952 | tf_op jit(solution)/shard_map/transpose | solution.py:173
  54.1 0.9 %add_bitcast_fusion.1 = f32[4,10,2048]{2,0,1:T(4,128)} fusion(f32[10,4,2048]{2,1,0:T(4,128)S(1)} %fusion.27, f32[10,4,2048]{2,1,0:T(4,128)S(1)} %squeeze.42, f32[4,10,2048]{2,0,1:T(4,128)S(1)} %copy-done.1), kind=kLoop, calls=%fused_computation.41 | loop fusion | flops 245760 | bytes 1310720 | tf_op jit(solution)/shard_map/transpose | solution.py:173
  55.0 0.9 %fusion.14 = f32[4,10,2048]{2,0,1:T(4,128)} fusion(f32[10,4,2048]{2,1,0:T(4,128)S(1)} %squeeze.45, f32[4,10,2048]{2,0,1:T(4,128)S(1)} %copy-done.5, f32[9,4,2048]{2,1,0:T(4,128)S(1)} %copy-done.10, f32[9,4,2048]{2,1,0:T(4,128)S(1)} %copy-done.13), kind=kLoop, calls=%fused_computation.33 | loop fusion | flops 491520 | bytes 1572864 | tf_op jit(solution)/shard_map/transpose | solution.py:173
  55.9 0.9 %add_bitcast_fusion = f32[4,10,2048]{2,0,1:T(4,128)} fusion(f32[10,4,2048]{2,1,0:T(4,128)S(1)} %squeeze.43, f32[9,4,2048]{2,1,0:T(4,128)S(1)} %copy-done.12, f32[9,4,2048]{2,1,0:T(4,128)S(1)} %copy-done.11, f32[4,10,2048]{2,0,1:T(4,128)S(1)} %copy-done), kind=kLoop, calls=%fused_computation.40 | loop fusion | flops 573440 | bytes 1572864 | tf_op jit(solution)/shard_map/transpose | solution.py:173
  56.8 1.8 %all-to-all-done = f32[8,20,256]{2,1,0:T(8,128)S(1)} async-done(((f32[8,20,256]{2,1,0:T(8,128)}), f32[8,20,256]{2,1,0:T(8,128)S(1)}, u32[]{:S(2)}, u32[]{:S(2)}) %all-to-all-start) | async-done | bytes 163872 | tf_op jit(solution)/shard_map/all_to_all | solution.py:70
  58.6 0.6 %copy.33 = f32[2,10,256]{2,0,1:T(2,128)} copy(f32[2,10,256]{2,1,0:T(8,128)S(1)} %reshape.113) | data formatting | bytes 40960
  (51 shorter events, 0.5 us)
Async XLA Ops:
  0.6 2.1 %copy-start.1 = (f32[4,10,2048]{2,0,1:T(4,128)S(1)}, f32[4,10,2048]{2,0,1:T(4,128)}, u32[]{:S(2)}) copy-start(f32[4,10,2048]{2,0,1:T(4,128)} %param.13) | copy-start | bytes 983044
  0.6 2.1 %copy-start = (f32[4,10,2048]{2,0,1:T(4,128)S(1)}, f32[4,10,2048]{2,0,1:T(4,128)}, u32[]{:S(2)}) copy-start(f32[4,10,2048]{2,0,1:T(4,128)} %param.14) | copy-start | bytes 983044
  0.7 2.0 %copy-start.2 = (f32[4,10,2048]{2,0,1:T(4,128)S(1)}, f32[4,10,2048]{2,0,1:T(4,128)}, u32[]{:S(2)}) copy-start(f32[4,10,2048]{2,0,1:T(4,128)} %param.22) | copy-start | bytes 983044
  0.7 2.0 %copy-start.4 = (f32[4,10,2048]{2,0,1:T(4,128)S(1)}, f32[4,10,2048]{2,0,1:T(4,128)}, u32[]{:S(2)}) copy-start(f32[4,10,2048]{2,0,1:T(4,128)} %param.23) | copy-start | bytes 983044
  1.9 0.8 %copy-start.6 = (f32[10,2048]{1,0:T(8,128)}, f32[10,2048]{1,0:T(8,128)S(1)}, u32[]{:S(2)}) copy-start(f32[10,2048]{1,0:T(8,128)S(1)} %get-tuple-element.56) | copy-start | bytes 245764
  1.9 0.8 %copy-start.8 = (f32[10,2048]{1,0:T(8,128)}, f32[10,2048]{1,0:T(8,128)S(1)}, u32[]{:S(2)}) copy-start(f32[10,2048]{1,0:T(8,128)S(1)} %get-tuple-element.57) | copy-start | bytes 245764
  3.8 0.9 %copy-start.14 = (f32[20,2048]{1,0:T(8,128)S(1)}, f32[20,2048]{1,0:T(8,128)}, u32[]{:S(2)}) copy-start(f32[20,2048]{1,0:T(8,128)} %reshape.107) | copy-start | bytes 491524
  4.7 0.7 %copy-start.20 = (s32[4,256]{1,0:T(4,128)S(1)}, s32[4,256]{1,0:T(4,128)}, u32[]{:S(2)}) copy-start(s32[4,256]{1,0:T(4,128)} %param.20) | copy-start | bytes 12292
  7.7 0.7 %copy-start.19 = (f32[4,256]{1,0:T(4,128)S(1)}, f32[4,256]{1,0:T(4,128)}, u32[]{:S(2)}) copy-start(f32[4,256]{1,0:T(4,128)} %param.21) | copy-start | bytes 12292
  9.1 18.2 %copy-start.3 = (f32[4,10,2048]{2,0,1:T(4,128)S(1)}, f32[4,10,2048]{2,0,1:T(4,128)}, u32[]{:S(2)}) copy-start(f32[4,10,2048]{2,0,1:T(4,128)} %param.22) | copy-start | bytes 983044
  9.1 18.2 %copy-start.5 = (f32[4,10,2048]{2,0,1:T(4,128)S(1)}, f32[4,10,2048]{2,0,1:T(4,128)}, u32[]{:S(2)}) copy-start(f32[4,10,2048]{2,0,1:T(4,128)} %param.23) | copy-start | bytes 983044
  9.6 17.8 %copy-start.7 = (f32[10,2048]{1,0:T(8,128)S(1)}, f32[10,2048]{1,0:T(8,128)}, u32[]{:S(2)}) copy-start(f32[10,2048]{1,0:T(8,128)} %copy-done.6) | copy-start | bytes 245764
  9.6 17.8 %copy-start.9 = (f32[10,2048]{1,0:T(8,128)S(1)}, f32[10,2048]{1,0:T(8,128)}, u32[]{:S(2)}) copy-start(f32[10,2048]{1,0:T(8,128)} %copy-done.8) | copy-start | bytes 245764
  10.4 21.3 %collective-permute-start = (f32[4,10,4,256]{3,2,1,0:T(4,128)}, f32[4,10,4,256]{3,2,1,0:T(4,128)}, u32[]{:S(2)}, u32[]{:S(2)}) collective-permute-start(f32[4,10,4,256]{3,2,1,0:T(4,128)} %bitcast.74), channel_id=1, source_target_pairs={{0,8},{8,0},{16,24},{24,16},{32,40},{40,32},{48,56},{56,48},{64,72... | collective-permute-start | bytes 491528 | tf_op jit(solution)/shard_map/ppermute | solution.py:9
  13.0 18.7 %collective-permute-start.1 = (f32[4,10,4,256]{3,2,1,0:T(4,128)}, f32[4,10,4,256]{3,2,1,0:T(4,128)}, u32[]{:S(2)}, u32[]{:S(2)}) collective-permute-start(f32[4,10,4,256]{3,2,1,0:T(4,128)} %bitcast.73), channel_id=1, source_target_pairs={{0,16},{8,24},{16,0},{24,8},{32,48},{40,56},{48,32},{56,40},{64,80... | collective-permute-start | bytes 491528 | tf_op jit(solution)/shard_map/ppermute | solution.py:9
  16.1 16.7 %collective-permute-start.2 = (f32[4,10,4,256]{3,2,1,0:T(4,128)}, f32[4,10,4,256]{3,2,1,0:T(4,128)}, u32[]{:S(2)}, u32[]{:S(2)}) collective-permute-start(f32[4,10,4,256]{3,2,1,0:T(4,128)} %bitcast.72), channel_id=1, source_target_pairs={{0,32},{8,40},{16,48},{24,56},{32,0},{40,8},{48,16},{56,24},{64,96... | collective-permute-start | bytes 491528 | tf_op jit(solution)/shard_map/ppermute | solution.py:9
  21.3 18.3 %collective-permute-start.3 = (f32[4,10,4,256]{3,2,1,0:T(4,128)}, f32[4,10,4,256]{3,2,1,0:T(4,128)}, u32[]{:S(2)}, u32[]{:S(2)}) collective-permute-start(f32[4,10,4,256]{3,2,1,0:T(4,128)} %bitcast.75), channel_id=1, source_target_pairs={{0,64},{8,72},{16,80},{24,88},{32,96},{40,104},{48,112},{56,120},{... | collective-permute-start | bytes 491528 | tf_op jit(solution)/shard_map/ppermute | solution.py:9
  28.2 0.9 %copy-start.16 = (f32[9,2048]{1,0:T(8,128)S(1)}, f32[9,2048]{1,0:T(8,128)}, u32[]{:S(2)}) copy-start(f32[9,2048]{1,0:T(8,128)} %get-tuple-element.62) | copy-start | bytes 221188
  28.7 1.6 %copy-start.15 = (f32[9,2048]{1,0:T(8,128)S(1)}, f32[9,2048]{1,0:T(8,128)}, u32[]{:S(2)}) copy-start(f32[9,2048]{1,0:T(8,128)} %get-tuple-element.61) | copy-start | bytes 221188
  30.3 1.2 %copy-start.18 = (f32[4,2048]{1,0:T(4,128)S(1)}, f32[4,2048]{1,0:T(4,128)}, u32[]{:S(2)}) copy-start(f32[4,2048]{1,0:T(4,128)} %param.19) | copy-start | bytes 98308
  31.6 9.4 %copy-start.17 = (f32[2,10,4,256]{3,2,1,0:T(4,128)S(1)}, f32[2,10,4,256]{3,2,1,0:T(4,128)}, u32[]{:S(2)}) copy-start(f32[2,10,4,256]{3,2,1,0:T(4,128)} %get-tuple-element.33) | copy-start | bytes 245764
  45.5 13.1 %all-to-all-start = ((f32[8,20,256]{2,1,0:T(8,128)}), f32[8,20,256]{2,1,0:T(8,128)S(1)}, u32[]{:S(2)}, u32[]{:S(2)}) async-start(f32[8,20,256]{2,1,0:T(8,128)} %copy.32), calls=%async_computation | async-start | bytes 393216 | tf_op jit(solution)/shard_map/all_to_all | solution.py:70
  52.1 2.9 %copy-start.10 = (f32[9,4,2048]{2,1,0:T(4,128)S(1)}, f32[9,4,2048]{2,1,0:T(4,128)}, u32[]{:S(2)}) copy-start(f32[9,4,2048]{2,1,0:T(4,128)} %get-tuple-element.30) | copy-start | bytes 884740
  52.1 2.9 %copy-start.13 = (f32[9,4,2048]{2,1,0:T(4,128)S(1)}, f32[9,4,2048]{2,1,0:T(4,128)}, u32[]{:S(2)}) copy-start(f32[9,4,2048]{2,1,0:T(4,128)} %get-tuple-element.54) | copy-start | bytes 884740
  54.1 1.8 %copy-start.11 = (f32[9,4,2048]{2,1,0:T(4,128)S(1)}, f32[9,4,2048]{2,1,0:T(4,128)}, u32[]{:S(2)}) copy-start(f32[9,4,2048]{2,1,0:T(4,128)} %get-tuple-element.53) | copy-start | bytes 884740
  54.1 1.8 %copy-start.12 = (f32[9,4,2048]{2,1,0:T(4,128)S(1)}, f32[9,4,2048]{2,1,0:T(4,128)}, u32[]{:S(2)}) copy-start(f32[9,4,2048]{2,1,0:T(4,128)} %get-tuple-element.55) | copy-start | bytes 884740

commit v9 on v6

--- a/solution.py
+++ b/solution.py
@@ -98,6 +98,9 @@
     g_p = 0.1 * c_p
     g_t = 0.1 * c_t
 
+    order = [2, 3, 0, 1] if rounds == 4 else list(range(rounds))
+    face_cols = jnp.concatenate([face_cols[i : i + 1] for i in order])
+    face_weight = jnp.concatenate([face_weight[i : i + 1] for i in order])
     cols = face_cols.reshape(rounds * face)
     select = (cols[:, None] == jnp.arange(width, dtype=jnp.int32)[None, :]).astype(
         jnp.bfloat16
@@ -121,7 +124,7 @@
 
     far = []
     for index in range(rounds):
-        far.append(from_partner(sending[..., index, :], "space", 1 << index))
+        far.append(from_partner(sending[..., index, :], "space", 1 << order[index]))
     far = jnp.stack(far, axis=-2)
 
     diff = far[:2] - own

time: 56.1 us -> 52.9 us (0.943)
  the two profiles are of different devices: /device:TPU:1 before, /device:TPU:136 now
where the time goes in v9:
time: 52.9 us; the launch traced here: 52.4 us
  starting transfers between devices  21 us (40%)
  other arithmetic  12.3 us (23%)
  local copies, waits for them, and re-layouts  7.48 us (14%)
  waiting for transfers between devices  6.16 us (12%)
  matrix products  4.24 us (8%)
  between operations  1.18 us (2%)
    ppermute x4, starting transfers between devices, from_partner(): return lax.ppermute(value, axis, pairs)  14.7 us
    all_to_all x1, starting transfers between devices, sum_scatter(): got = lax.all_to_all(parts, axis, 0, 0, tiled=True)  6.27 us
    ppermute x4, waiting for transfers between devices, from_partner(): return lax.ppermute(value, axis, pairs)  4.72 us
    dot_general x2, matrix products, exact_select(): lax.dot_general(split2(rows), select, (((1,), (contract,)), ((), ())), pr...  4.24 us
    transpose x4, other arithmetic, body(): return tuple((o.transpose(1, 0, 2) for o in outs)) + (owned,)  3.55 us
    unnamed x50, local copies, waits for them, and re-layouts  2.94 us
    add x1, other arithmetic, sum_scatter(): total = total + got[index]  1.49 us
    all_to_all x1, waiting for transfers between devices, sum_scatter(): got = lax.all_to_all(parts, axis, 0, 0, tiled=True)  1.44 us
  transfers between devices with their start and end apart: 5, of which 2 were waited for; matrix products, arithmetic and copies ran while one was open for 17% of the time, Pallas kernels for 0%

profile of v9, /device:TPU:136, one launch (start us, length us, event | category | flops | bytes accessed | tf_op | source)
XLA Modules:
  0.0 52.4 jit_solution(2377303801475778325)
XLA Ops:
  0.6 0.0 copy-start.1
  0.6 0.0 copy-start
  0.7 0.0 copy-start.2
  0.7 0.0 copy-start.4
  0.7 1.2 %add_multiply_fusion.3 = (f32[10,2048]{1,0:T(8,128)S(1)}, f32[10,2048]{1,0:T(8,128)S(1)}) fusion(f32[10,2048]{1,0:T(8,128)} %param.16, f32[10,2048]{1,0:T(8,128)} %param.17, s32[10,2048]{1,0:T(8,128)} %param.18, f32[10,2048]{1,0:T(8,128)} %param.15), kind=kLoop, calls=%fused_computation.79 | loop fusion | flops 122880 | bytes 491520 | tf_op jit(solution)/shard_map/mul | solution.py:97
  2.0 0.7 %reshape.104 = f32[20,2048]{1,0:T(8,128)} reshape(f32[2,10,2048]{2,1,0:T(8,128)S(1)} %pad_maximum_fusion.4) | data formatting | bytes 327680 | tf_op jit(solution)/shard_map/reshape | solution.py:113
  2.7 0.0 copy-done.1
  2.7 0.6 %pad_maximum_fusion = f32[4,10,4,2048]{3,2,1,0:T(4,128)S(1)} fusion(f32[1,10,4,2048]{3,2,1,0:T(4,128)S(1)} %bitcast.108, f32[1,10,4,2048]{3,2,1,0:T(4,128)S(1)} %bitcast.107, f32[1,10,4,2048]{3,2,1,0:T(4,128)S(1)} %bitcast.97, f32[1,10,4,2048]{3,2,1,0:T(4,128)S(1)} %bitcast.100), kind=kLoop, calls=%fused_computation.12 | loop fusion | flops 983040 | bytes 2621440 | tf_op jit(solution)/shard_map/stack | solution.py:112
  3.3 0.5 reshape.103
  3.7 0.0 copy-start.13
  3.7 0.1 constant_dynamic-update-slice_fusion.1
  3.8 0.8 %copy-done.13 = f32[20,2048]{1,0:T(8,128)S(1)} copy-done((f32[20,2048]{1,0:T(8,128)S(1)}, f32[20,2048]{1,0:T(8,128)}, u32[]{:S(2)}) %copy-start.13) | copy-done | bytes 163864
  4.7 0.0 copy-start.15
  4.7 0.2 reduce-precision_convert_fusion
  4.9 0.5 copy-done.15
  5.4 2.2 %fusion.1 = f32[360,1024]{1,0:T(8,128)S(1)} fusion(s32[1024]{0:T(1024)S(1)} %bitcast.132, bf16[180,2048]{1,0:T(8,128)(2,1)S(1)} %get-tuple-element.34, bf16[180,2048]{1,0:T(8,128)(2,1)S(1)} %get-tuple-element.33), kind=kOutput, calls=%fused_computation.2 | convolution fusion | flops 1514995712 | bytes 2953216 | tf_op jit(solution)/shard_map/dot_general | solution.py:39
  7.6 0.0 copy-start.16
  7.6 0.1 slice_add_fusion.1
  7.7 0.1 fusion.35
  7.8 0.4 copy-done.16
  8.3 0.2 slice.188
  8.4 0.2 slice.190
  8.6 0.0 copy-start.3
  8.6 0.0 copy-start.5
  8.7 0.1 broadcast_multiply_fusion.1
  8.7 0.5 fusion.19
  9.3 4.5 %collective-permute-start = (f32[4,10,4,256]{3,2,1,0:T(4,128)S(1)}, f32[4,10,4,256]{3,2,1,0:T(4,128)S(1)}, u32[]{:S(2)}, u32[]{:S(2)}) collective-permute-start(f32[4,10,4,256]{3,2,1,0:T(4,128)S(1)} %bitcast.127), channel_id=1, source_target_pairs={{0,32},{8,40},{16,48},{24,56},{32,0},{40,8},{48,16},{56,24},{64,96... | collective-permute-start | bytes 491528 | tf_op jit(solution)/shard_map/ppermute | solution.py:9
  13.8 5.0 %collective-permute-start.1 = (f32[4,10,4,256]{3,2,1,0:T(4,128)S(1)}, f32[4,10,4,256]{3,2,1,0:T(4,128)S(1)}, u32[]{:S(2)}, u32[]{:S(2)}) collective-permute-start(f32[4,10,4,256]{3,2,1,0:T(4,128)S(1)} %bitcast.128), channel_id=1, source_target_pairs={{0,64},{8,72},{16,80},{24,88},{32,96},{40,104},{48,112},{56,120},{... | collective-permute-start | bytes 491528 | tf_op jit(solution)/shard_map/ppermute | solution.py:9
  18.9 1.9 %collective-permute-start.2 = (f32[4,10,4,256]{3,2,1,0:T(4,128)S(1)}, f32[4,10,4,256]{3,2,1,0:T(4,128)S(1)}, u32[]{:S(2)}, u32[]{:S(2)}) collective-permute-start(f32[4,10,4,256]{3,2,1,0:T(4,128)S(1)} %bitcast.129), channel_id=1, source_target_pairs={{0,8},{8,0},{16,24},{24,16},{32,40},{40,32},{48,56},{56,48},{64,72... | collective-permute-start | bytes 491528 | tf_op jit(solution)/shard_map/ppermute | solution.py:9
  20.9 3.3 %collective-permute-start.3 = (f32[4,10,4,256]{3,2,1,0:T(4,128)S(1)}, f32[4,10,4,256]{3,2,1,0:T(4,128)S(1)}, u32[]{:S(2)}, u32[]{:S(2)}) collective-permute-start(f32[4,10,4,256]{3,2,1,0:T(4,128)S(1)} %bitcast.130), channel_id=1, source_target_pairs={{0,16},{8,24},{16,0},{24,8},{32,48},{40,56},{48,32},{56,40},{64,80... | collective-permute-start | bytes 491528 | tf_op jit(solution)/shard_map/ppermute | solution.py:9
  24.2 0.0 copy-done.3
  24.2 0.0 copy-done.5
  24.2 0.2 bitcast_multiply_fusion
  24.5 0.5 multiply_reduce_fusion.2
  25.0 1.1 %multiply_multiply_fusion = (f32[9,4,2048]{2,1,0:T(4,128)}, f32[9,4,2048]{2,1,0:T(4,128)S(1)}, f32[9,4,2048]{2,1,0:T(4,128)}) fusion(f32[9,4,2048]{2,1,0:T(4,128)S(1)} %get-tuple-element.24, f32[10,4,2048]{2,1,0:T(4,128)S(1)} %bitcast.102, f32[9,2048]{1,0:T(8,128)S(1)} %get-tuple-element.63, f32[9,4,2048]{2,1,0:T(4,128)S(1)} %get-tuple-element.23), kind=kLoop, calls=%fused_computation.55 | loop fusion | flops 368640 | bytes 2138112 | tf_op jit(solution)/shard_map/mul | solution.py:173
  26.0 0.1 pad_subtract_fusion
  26.1 1.2 %multiply_reduce_fusion.1 = (f32[9,2048]{1,0:T(8,128)S(1)}, f32[9,4,2048]{2,1,0:T(4,128)}, f32[9,4,2048]{2,1,0:T(4,128)}, f32[9,4,2048]{2,1,0:T(4,128)}) fusion(f32[9,4,2048]{2,1,0:T(4,128)S(1)} %get-tuple-element.24, f32[10,4,2048]{2,1,0:T(4,128)S(1)} %bitcast.99, f32[9,2048]{1,0:T(8,128)S(1)} %get-tuple-element.62, f32[9,4,2048]{2,1,0:T(4,128)S(1)} %get-tuple-element.26), kind=kLoop, calls=%fused_computation.50 | loop fusion | flops 571392 | bytes 2211840 | tf_op jit(solution)/shard_map/reduce_sum | solution.py:148
  27.6 0.5 copy-done.14
  28.1 0.0 collective-permute-done
  28.1 4.7 %collective-permute-done.1 = f32[4,10,4,256]{3,2,1,0:T(4,128)S(1)} collective-permute-done((f32[4,10,4,256]{3,2,1,0:T(4,128)S(1)}, f32[4,10,4,256]{3,2,1,0:T(4,128)S(1)}, u32[]{:S(2)}, u32[]{:S(2)}) %collective-permute-start.1) | collective-permute-done | bytes 163872 | tf_op jit(solution)/shard_map/ppermute | solution.py:9
  32.8 0.0 collective-permute-done.2
  32.8 0.0 collective-permute-done.3
  32.8 0.1 pad_maximum_fusion.2
  32.9 0.1 fusion.36
  33.1 0.7 %multiply_reduce_fusion = (f32[2,10,4,256]{3,2,1,0:T(4,128)S(1)}, f32[2,10,4,4,256]{4,3,2,1,0:T(4,128)S(1)}, f32[2,10,4,4,256]{4,3,2,1,0:T(4,128)S(1)}) fusion(f32[2,10,4,4,256]{4,3,2,1,0:T(4,128)S(1)} %slice.188, f32[2,10,4,4,256]{4,3,2,1,0:T(4,128)S(1)} %slice.190, f32[2,10,4,4,256]{4,2,1,0,3:T(4,128)S(1)} %get-tuple-element.41, ...), kind=kLoop, calls=%fused_computation.42 | loop fusion | flops 552960 | bytes 2211840 | tf_op jit(solution)/shard_map/reduce_sum | solution.py:133
  33.7 0.2 pad_maximum_fusion.3
  34.0 0.1 copy.54
  34.2 0.2 reduce-precision_convert_fusion.1
  34.3 2.1 %fusion = f32[360,2048]{1,0:T(8,128)S(1)} fusion(s32[1024]{0:T(1024)S(1)} %bitcast.133, bf16[180,1024]{1,0:T(8,128)(2,1)S(1)} %get-tuple-element.36, bf16[180,1024]{1,0:T(8,128)(2,1)S(1)} %get-tuple-element.35), kind=kOutput, calls=%fused_computation.1 | convolution fusion | flops 1513521152 | bytes 3690496 | tf_op jit(solution)/shard_map/dot_general | solution.py:39
  36.4 0.2 slice_add_fusion
  36.6 0.2 fusion.34
  36.8 0.1 copy.57
  37.0 0.8 %copy.46 = f32[8,2,10,256]{3,1,2,0:T(2,128)} copy(f32[8,2,10,256]{3,0,2,1:T(8,128)S(1)} %fusion.22) | data formatting | bytes 327680 | tf_op jit(solution)/shard_map/transpose | solution.py:68
  37.8 6.3 %all-to-all-start = ((f32[8,2,10,256]{3,1,2,0:T(2,128)}), f32[8,2,10,256]{3,1,2,0:T(2,128)}, u32[]{:S(2)}, u32[]{:S(2)}) async-start(f32[8,2,10,256]{3,1,2,0:T(2,128)} %copy.46), calls=%async_computation | async-start | bytes 327680 | tf_op jit(solution)/shard_map/all_to_all | solution.py:69
  44.0 0.8 %squeeze.45 = f32[10,4,2048]{2,1,0:T(4,128)} reshape(f32[40,2048]{1,0:T(8,128)S(1)} %get-tuple-element.29) | data formatting | bytes 655360 | tf_op jit(solution)/shard_map/squeeze | solution.py:173
  44.8 0.1 squeeze.44
  44.9 0.8 %squeeze.43 = f32[10,4,2048]{2,1,0:T(4,128)} reshape(f32[40,2048]{1,0:T(8,128)S(1)} %get-tuple-element.31) | data formatting | bytes 655360 | tf_op jit(solution)/shard_map/squeeze | solution.py:171
  45.8 0.1 squeeze.42
  45.9 0.8 %fusion.16 = f32[4,10,2048]{2,0,1:T(4,128)} fusion(f32[10,4,2048]{2,1,0:T(4,128)S(1)} %squeeze.44, f32[4,10,2048]{2,0,1:T(4,128)S(1)} %copy-done.3, f32[9,4,2048]{2,1,0:T(4,128)S(1)} %copy-done.8), kind=kLoop, calls=%fused_computation.37 | loop fusion | flops 245760 | bytes 1277952 | tf_op jit(solution)/shard_map/transpose | solution.py:175
  46.7 0.9 %add_bitcast_fusion.1 = f32[4,10,2048]{2,0,1:T(4,128)} fusion(f32[10,4,2048]{2,1,0:T(4,128)S(1)} %fusion.27, f32[10,4,2048]{2,1,0:T(4,128)S(1)} %squeeze.42, f32[4,10,2048]{2,0,1:T(4,128)S(1)} %copy-done.1), kind=kLoop, calls=%fused_computation.41 | loop fusion | flops 245760 | bytes 1310720 | tf_op jit(solution)/shard_map/transpose | solution.py:175
  47.6 0.9 %fusion.14 = f32[4,10,2048]{2,0,1:T(4,128)} fusion(f32[10,4,2048]{2,1,0:T(4,128)S(1)} %copy-done.7, f32[4,10,2048]{2,0,1:T(4,128)S(1)} %copy-done.5, f32[9,4,2048]{2,1,0:T(4,128)S(1)} %copy-done.9, f32[9,4,2048]{2,1,0:T(4,128)S(1)} %copy-done.12), kind=kLoop, calls=%fused_computation.33 | loop fusion | flops 491520 | bytes 1572864 | tf_op jit(solution)/shard_map/transpose | solution.py:175
  48.5 0.9 %add_bitcast_fusion = f32[4,10,2048]{2,0,1:T(4,128)} fusion(f32[10,4,2048]{2,1,0:T(4,128)S(1)} %copy-done.6, f32[9,4,2048]{2,1,0:T(4,128)S(1)} %copy-done.11, f32[9,4,2048]{2,1,0:T(4,128)S(1)} %copy-done.10, f32[4,10,2048]{2,0,1:T(4,128)S(1)} %copy-done), kind=kLoop, calls=%fused_computation.40 | loop fusion | flops 573440 | bytes 1572864 | tf_op jit(solution)/shard_map/transpose | solution.py:175
  49.4 1.4 %all-to-all-done = f32[8,2,10,256]{3,1,2,0:T(2,128)} async-done(((f32[8,2,10,256]{3,1,2,0:T(2,128)}), f32[8,2,10,256]{3,1,2,0:T(2,128)}, u32[]{:S(2)}, u32[]{:S(2)}) %all-to-all-start) | async-done | bytes 163872 | tf_op jit(solution)/shard_map/all_to_all | solution.py:69
  50.9 1.5 %fusion.28 = f32[2,10,256]{2,0,1:T(2,128)} fusion(f32[8,2,10,256]{3,1,2,0:T(2,128)} %all-to-all-done), kind=kLoop, calls=%fused_computation.93 | loop fusion | flops 35840 | bytes 184320 | tf_op jit(solution)/shard_map/add | solution.py:72
  (50 shorter events, 0.8 us)
Async XLA Ops:
  0.6 2.0 %copy-start.1 = (f32[4,10,2048]{2,0,1:T(4,128)S(1)}, f32[4,10,2048]{2,0,1:T(4,128)}, u32[]{:S(2)}) copy-start(f32[4,10,2048]{2,0,1:T(4,128)} %param.13) | copy-start | bytes 983044
  0.6 2.0 %copy-start = (f32[4,10,2048]{2,0,1:T(4,128)S(1)}, f32[4,10,2048]{2,0,1:T(4,128)}, u32[]{:S(2)}) copy-start(f32[4,10,2048]{2,0,1:T(4,128)} %param.14) | copy-start | bytes 983044
  0.7 2.0 %copy-start.2 = (f32[4,10,2048]{2,0,1:T(4,128)S(1)}, f32[4,10,2048]{2,0,1:T(4,128)}, u32[]{:S(2)}) copy-start(f32[4,10,2048]{2,0,1:T(4,128)} %param.22) | copy-start | bytes 983044
  0.7 2.0 %copy-start.4 = (f32[4,10,2048]{2,0,1:T(4,128)S(1)}, f32[4,10,2048]{2,0,1:T(4,128)}, u32[]{:S(2)}) copy-start(f32[4,10,2048]{2,0,1:T(4,128)} %param.23) | copy-start | bytes 983044
  3.7 0.9 %copy-start.13 = (f32[20,2048]{1,0:T(8,128)S(1)}, f32[20,2048]{1,0:T(8,128)}, u32[]{:S(2)}) copy-start(f32[20,2048]{1,0:T(8,128)} %reshape.104) | copy-start | bytes 491524
  4.7 0.7 %copy-start.15 = (s32[4,256]{1,0:T(4,128)S(1)}, s32[4,256]{1,0:T(4,128)}, u32[]{:S(2)}) copy-start(s32[4,256]{1,0:T(4,128)} %param.20) | copy-start | bytes 12292
  7.6 0.7 %copy-start.16 = (f32[4,256]{1,0:T(4,128)S(1)}, f32[4,256]{1,0:T(4,128)}, u32[]{:S(2)}) copy-start(f32[4,256]{1,0:T(4,128)} %param.21) | copy-start | bytes 12292
  8.6 15.6 %copy-start.3 = (f32[4,10,2048]{2,0,1:T(4,128)S(1)}, f32[4,10,2048]{2,0,1:T(4,128)}, u32[]{:S(2)}) copy-start(f32[4,10,2048]{2,0,1:T(4,128)} %param.22) | copy-start | bytes 983044
  8.6 15.6 %copy-start.5 = (f32[4,10,2048]{2,0,1:T(4,128)S(1)}, f32[4,10,2048]{2,0,1:T(4,128)}, u32[]{:S(2)}) copy-start(f32[4,10,2048]{2,0,1:T(4,128)} %param.23) | copy-start | bytes 983044
  9.3 18.8 %collective-permute-start = (f32[4,10,4,256]{3,2,1,0:T(4,128)S(1)}, f32[4,10,4,256]{3,2,1,0:T(4,128)S(1)}, u32[]{:S(2)}, u32[]{:S(2)}) collective-permute-start(f32[4,10,4,256]{3,2,1,0:T(4,128)S(1)} %bitcast.127), channel_id=1, source_target_pairs={{0,32},{8,40},{16,48},{24,56},{32,0},{40,8},{48,16},{56,24},{64,96... | collective-permute-start | bytes 491528 | tf_op jit(solution)/shard_map/ppermute | solution.py:9
  13.8 18.9 %collective-permute-start.1 = (f32[4,10,4,256]{3,2,1,0:T(4,128)S(1)}, f32[4,10,4,256]{3,2,1,0:T(4,128)S(1)}, u32[]{:S(2)}, u32[]{:S(2)}) collective-permute-start(f32[4,10,4,256]{3,2,1,0:T(4,128)S(1)} %bitcast.128), channel_id=1, source_target_pairs={{0,64},{8,72},{16,80},{24,88},{32,96},{40,104},{48,112},{56,120},{... | collective-permute-start | bytes 491528 | tf_op jit(solution)/shard_map/ppermute | solution.py:9
  18.9 13.8 %collective-permute-start.2 = (f32[4,10,4,256]{3,2,1,0:T(4,128)S(1)}, f32[4,10,4,256]{3,2,1,0:T(4,128)S(1)}, u32[]{:S(2)}, u32[]{:S(2)}) collective-permute-start(f32[4,10,4,256]{3,2,1,0:T(4,128)S(1)} %bitcast.129), channel_id=1, source_target_pairs={{0,8},{8,0},{16,24},{24,16},{32,40},{40,32},{48,56},{56,48},{64,72... | collective-permute-start | bytes 491528 | tf_op jit(solution)/shard_map/ppermute | solution.py:9
  20.9 11.9 %collective-permute-start.3 = (f32[4,10,4,256]{3,2,1,0:T(4,128)S(1)}, f32[4,10,4,256]{3,2,1,0:T(4,128)S(1)}, u32[]{:S(2)}, u32[]{:S(2)}) collective-permute-start(f32[4,10,4,256]{3,2,1,0:T(4,128)S(1)} %bitcast.130), channel_id=1, source_target_pairs={{0,16},{8,24},{16,0},{24,8},{32,48},{40,56},{48,32},{56,40},{64,80... | collective-permute-start | bytes 491528 | tf_op jit(solution)/shard_map/ppermute | solution.py:9
  27.3 0.8 %copy-start.14 = (f32[4,2048]{1,0:T(4,128)S(1)}, f32[4,2048]{1,0:T(4,128)}, u32[]{:S(2)}) copy-start(f32[4,2048]{1,0:T(4,128)} %param.19) | copy-start | bytes 98308
  37.8 8.1 %copy-start.8 = (f32[9,4,2048]{2,1,0:T(4,128)S(1)}, f32[9,4,2048]{2,1,0:T(4,128)}, u32[]{:S(2)}) copy-start(f32[9,4,2048]{2,1,0:T(4,128)} %get-tuple-element.53) | copy-start | bytes 884740
  37.8 13.1 %all-to-all-start = ((f32[8,2,10,256]{3,1,2,0:T(2,128)}), f32[8,2,10,256]{3,1,2,0:T(2,128)}, u32[]{:S(2)}, u32[]{:S(2)}) async-start(f32[8,2,10,256]{3,1,2,0:T(2,128)} %copy.46), calls=%async_computation | async-start | bytes 327680 | tf_op jit(solution)/shard_map/all_to_all | solution.py:69
  45.8 1.8 %copy-start.7 = (f32[10,4,2048]{2,1,0:T(4,128)S(1)}, f32[10,4,2048]{2,1,0:T(4,128)}, u32[]{:S(2)}) copy-start(f32[10,4,2048]{2,1,0:T(4,128)} %squeeze.45) | copy-start | bytes 983044
  45.8 1.8 %copy-start.9 = (f32[9,4,2048]{2,1,0:T(4,128)S(1)}, f32[9,4,2048]{2,1,0:T(4,128)}, u32[]{:S(2)}) copy-start(f32[9,4,2048]{2,1,0:T(4,128)} %get-tuple-element.25) | copy-start | bytes 884740
  45.9 1.8 %copy-start.12 = (f32[9,4,2048]{2,1,0:T(4,128)S(1)}, f32[9,4,2048]{2,1,0:T(4,128)}, u32[]{:S(2)}) copy-start(f32[9,4,2048]{2,1,0:T(4,128)} %get-tuple-element.49) | copy-start | bytes 884740
  46.7 1.8 %copy-start.6 = (f32[10,4,2048]{2,1,0:T(4,128)S(1)}, f32[10,4,2048]{2,1,0:T(4,128)}, u32[]{:S(2)}) copy-start(f32[10,4,2048]{2,1,0:T(4,128)} %squeeze.43) | copy-start | bytes 983044
  46.7 1.8 %copy-start.10 = (f32[9,4,2048]{2,1,0:T(4,128)S(1)}, f32[9,4,2048]{2,1,0:T(4,128)}, u32[]{:S(2)}) copy-start(f32[9,4,2048]{2,1,0:T(4,128)} %get-tuple-element.48) | copy-start | bytes 884740
  46.7 1.8 %copy-start.11 = (f32[9,4,2048]{2,1,0:T(4,128)S(1)}, f32[9,4,2048]{2,1,0:T(4,128)}, u32[]{:S(2)}) copy-start(f32[9,4,2048]{2,1,0:T(4,128)} %get-tuple-element.50) | copy-start | bytes 884740

commit v10 on v9

--- a/solution.py
+++ b/solution.py
@@ -98,7 +98,7 @@
     g_p = 0.1 * c_p
     g_t = 0.1 * c_t
 
-    order = [2, 3, 0, 1] if rounds == 4 else list(range(rounds))
+    order = [2, 3, 1, 0] if rounds == 4 else list(range(rounds))
     face_cols = jnp.concatenate([face_cols[i : i + 1] for i in order])
     face_weight = jnp.concatenate([face_weight[i : i + 1] for i in order])
     cols = face_cols.reshape(rounds * face)

time: 52.9 us -> 56 us (1.059)
  the two profiles are of different devices: /device:TPU:136 before, /device:TPU:8 now
where the time goes in v10:
time: 56 us; the launch traced here: 55.4 us
  starting transfers between devices  21 us (38%)
  other arithmetic  12.2 us (22%)
  local copies, waits for them, and re-layouts  10.6 us (19%)
  waiting for transfers between devices  6.2 us (11%)
  matrix products  4.23 us (8%)
  between operations  1.18 us (2%)
    ppermute x4, starting transfers between devices, from_partner(): return lax.ppermute(value, axis, pairs)  14.7 us
    all_to_all x1, starting transfers between devices, sum_scatter(): got = lax.all_to_all(parts, axis, 0, 0, tiled=True)  6.23 us
    ppermute x4, waiting for transfers between devices, from_partner(): return lax.ppermute(value, axis, pairs)  4.76 us
    dot_general x2, matrix products, exact_select(): lax.dot_general(split2(rows), select, (((1,), (contract,)), ((), ())), pr...  4.23 us
    transpose x4, other arithmetic, body(): return tuple((o.transpose(1, 0, 2) for o in outs)) + (owned,)  3.55 us
    unnamed x50, local copies, waits for them, and re-layouts  2.52 us
    slice x2, local copies, waits for them, and re-layouts, body(): face_cols = jnp.concatenate([face_cols[i:i + 1] for i in order])  2.06 us
    add x1, other arithmetic, sum_scatter(): total = total + got[index]  1.49 us
  transfers between devices with their start and end apart: 5, of which 2 were waited for; matrix products, arithmetic and copies ran while one was open for 16% of the time, Pallas kernels for 0%

profile of v10, /device:TPU:8, one launch (start us, length us, event | category | flops | bytes accessed | tf_op | source)
XLA Modules:
  0.0 55.4 jit_solution(9743164978449884364)
XLA Ops:
  0.6 0.0 copy-start.1
  0.7 0.0 copy-start.2
  0.7 0.0 copy-start.4
  0.7 1.4 %fusion.38 = (s32[1,256]{1,0:T(1,128)}, s32[1,256]{1,0:T(1,128)}) fusion(s32[4,256]{1,0:T(4,128)} %param.20), kind=kLoop, calls=%fused_computation.112 | loop fusion | bytes 4096 | tf_op jit(solution)/shard_map/slice | solution.py:102
  2.0 0.7 %slice.186 = s32[2,256]{1,0:T(2,128)S(1)} slice(s32[4,256]{1,0:T(4,128)} %param.20), slice={[2:4], [0:256]} | slice | bytes 4096 | tf_op jit(solution)/shard_map/slice | solution.py:102
  2.7 0.8 %fusion.37 = (f32[1,256]{1,0:T(1,128)S(1)}, f32[1,256]{1,0:T(1,128)S(1)}) fusion(f32[4,256]{1,0:T(4,128)} %param.21), kind=kLoop, calls=%fused_computation.111 | loop fusion | bytes 4096 | tf_op jit(solution)/shard_map/slice | solution.py:103
  3.5 0.7 %slice.183 = f32[2,256]{1,0:T(2,128)S(1)} slice(f32[4,256]{1,0:T(4,128)} %param.21), slice={[2:4], [0:256]} | slice | bytes 4096 | tf_op jit(solution)/shard_map/slice | solution.py:103
  4.2 1.1 %add_multiply_fusion.3 = (f32[10,2048]{1,0:T(8,128)S(1)}, f32[10,2048]{1,0:T(8,128)S(1)}) fusion(f32[10,2048]{1,0:T(8,128)} %param.16, f32[10,2048]{1,0:T(8,128)} %param.17, s32[10,2048]{1,0:T(8,128)} %param.18, f32[10,2048]{1,0:T(8,128)} %param.15), kind=kLoop, calls=%fused_computation.79 | loop fusion | flops 122880 | bytes 491520 | tf_op jit(solution)/shard_map/mul | solution.py:97
  5.4 0.7 %reshape.104 = f32[20,2048]{1,0:T(8,128)} reshape(f32[2,10,2048]{2,1,0:T(8,128)S(1)} %pad_maximum_fusion.4) | data formatting | bytes 327680 | tf_op jit(solution)/shard_map/reshape | solution.py:113
  6.1 0.6 %pad_maximum_fusion = f32[4,10,4,2048]{3,2,1,0:T(4,128)S(1)} fusion(f32[1,10,4,2048]{3,2,1,0:T(4,128)S(1)} %bitcast.108, f32[1,10,4,2048]{3,2,1,0:T(4,128)S(1)} %bitcast.107, f32[1,10,4,2048]{3,2,1,0:T(4,128)S(1)} %bitcast.97, f32[1,10,4,2048]{3,2,1,0:T(4,128)S(1)} %bitcast.100), kind=kLoop, calls=%fused_computation.12 | loop fusion | flops 983040 | bytes 2621440 | tf_op jit(solution)/shard_map/stack | solution.py:112
  6.7 0.5 reshape.103
  7.1 0.0 copy-start.13
  7.1 0.1 constant_dynamic-update-slice_fusion.1
  7.2 0.8 %copy-done.13 = f32[20,2048]{1,0:T(8,128)S(1)} copy-done((f32[20,2048]{1,0:T(8,128)S(1)}, f32[20,2048]{1,0:T(8,128)}, u32[]{:S(2)}) %copy-start.13) | copy-done | bytes 163864
  8.1 0.0 copy-start.15
  8.1 0.0 copy-start.16
  8.1 0.2 reduce-precision_convert_fusion
  8.3 0.5 copy-done.15
  8.8 0.0 copy-done.16
  8.8 2.2 %fusion.1 = f32[360,1024]{1,0:T(8,128)S(1)} fusion(s32[1024]{0:T(1024)S(1)} %bitcast.132, bf16[180,2048]{1,0:T(8,128)(2,1)S(1)} %get-tuple-element.34, bf16[180,2048]{1,0:T(8,128)(2,1)S(1)} %get-tuple-element.33), kind=kOutput, calls=%fused_computation.2 | convolution fusion | flops 1514995712 | bytes 2953216 | tf_op jit(solution)/shard_map/dot_general | solution.py:39
  11.0 0.1 slice_add_fusion.1
  11.1 0.1 fusion.35
  11.2 0.2 slice.192
  11.4 0.2 slice.194
  11.6 0.0 copy-start.3
  11.6 0.0 copy-start.5
  11.6 0.1 broadcast_multiply_fusion.1
  11.7 0.5 fusion.19
  12.3 4.5 %collective-permute-start = (f32[4,10,4,256]{3,2,1,0:T(4,128)S(1)}, f32[4,10,4,256]{3,2,1,0:T(4,128)S(1)}, u32[]{:S(2)}, u32[]{:S(2)}) collective-permute-start(f32[4,10,4,256]{3,2,1,0:T(4,128)S(1)} %bitcast.127), channel_id=1, source_target_pairs={{0,32},{8,40},{16,48},{24,56},{32,0},{40,8},{48,16},{56,24},{64,96... | collective-permute-start | bytes 491528 | tf_op jit(solution)/shard_map/ppermute | solution.py:9
  16.8 5.0 %collective-permute-start.1 = (f32[4,10,4,256]{3,2,1,0:T(4,128)S(1)}, f32[4,10,4,256]{3,2,1,0:T(4,128)S(1)}, u32[]{:S(2)}, u32[]{:S(2)}) collective-permute-start(f32[4,10,4,256]{3,2,1,0:T(4,128)S(1)} %bitcast.128), channel_id=1, source_target_pairs={{0,64},{8,72},{16,80},{24,88},{32,96},{40,104},{48,112},{56,120},{... | collective-permute-start | bytes 491528 | tf_op jit(solution)/shard_map/ppermute | solution.py:9
  21.9 3.3 %collective-permute-start.2 = (f32[4,10,4,256]{3,2,1,0:T(4,128)S(1)}, f32[4,10,4,256]{3,2,1,0:T(4,128)S(1)}, u32[]{:S(2)}, u32[]{:S(2)}) collective-permute-start(f32[4,10,4,256]{3,2,1,0:T(4,128)S(1)} %bitcast.129), channel_id=1, source_target_pairs={{0,16},{8,24},{16,0},{24,8},{32,48},{40,56},{48,32},{56,40},{64,80... | collective-permute-start | bytes 491528 | tf_op jit(solution)/shard_map/ppermute | solution.py:9
  25.3 1.9 %collective-permute-start.3 = (f32[4,10,4,256]{3,2,1,0:T(4,128)S(1)}, f32[4,10,4,256]{3,2,1,0:T(4,128)S(1)}, u32[]{:S(2)}, u32[]{:S(2)}) collective-permute-start(f32[4,10,4,256]{3,2,1,0:T(4,128)S(1)} %bitcast.130), channel_id=1, source_target_pairs={{0,8},{8,0},{16,24},{24,16},{32,40},{40,32},{48,56},{56,48},{64,72... | collective-permute-start | bytes 491528 | tf_op jit(solution)/shard_map/ppermute | solution.py:9
  27.2 0.2 bitcast_multiply_fusion
  27.5 0.5 multiply_reduce_fusion.2
  28.0 1.1 %multiply_multiply_fusion = (f32[9,4,2048]{2,1,0:T(4,128)}, f32[9,4,2048]{2,1,0:T(4,128)S(1)}, f32[9,4,2048]{2,1,0:T(4,128)}) fusion(f32[9,4,2048]{2,1,0:T(4,128)S(1)} %get-tuple-element.24, f32[10,4,2048]{2,1,0:T(4,128)S(1)} %bitcast.102, f32[9,2048]{1,0:T(8,128)S(1)} %get-tuple-element.63, f32[9,4,2048]{2,1,0:T(4,128)S(1)} %get-tuple-element.23), kind=kLoop, calls=%fused_computation.55 | loop fusion | flops 368640 | bytes 2138112 | tf_op jit(solution)/shard_map/mul | solution.py:173
  29.0 0.1 pad_subtract_fusion
  29.1 1.2 %multiply_reduce_fusion.1 = (f32[9,2048]{1,0:T(8,128)S(1)}, f32[9,4,2048]{2,1,0:T(4,128)}, f32[9,4,2048]{2,1,0:T(4,128)}, f32[9,4,2048]{2,1,0:T(4,128)}) fusion(f32[9,4,2048]{2,1,0:T(4,128)S(1)} %get-tuple-element.24, f32[10,4,2048]{2,1,0:T(4,128)S(1)} %bitcast.99, f32[9,2048]{1,0:T(8,128)S(1)} %get-tuple-element.62, f32[9,4,2048]{2,1,0:T(4,128)S(1)} %get-tuple-element.26), kind=kLoop, calls=%fused_computation.50 | loop fusion | flops 571392 | bytes 2211840 | tf_op jit(solution)/shard_map/reduce_sum | solution.py:148
  30.6 0.5 copy-done.14
  31.0 0.0 collective-permute-done
  31.1 4.7 %collective-permute-done.1 = f32[4,10,4,256]{3,2,1,0:T(4,128)S(1)} collective-permute-done((f32[4,10,4,256]{3,2,1,0:T(4,128)S(1)}, f32[4,10,4,256]{3,2,1,0:T(4,128)S(1)}, u32[]{:S(2)}, u32[]{:S(2)}) %collective-permute-start.1) | collective-permute-done | bytes 163872 | tf_op jit(solution)/shard_map/ppermute | solution.py:9
  35.8 0.0 collective-permute-done.2
  35.8 0.0 collective-permute-done.3
  35.8 0.1 pad_maximum_fusion.2
  36.0 0.1 fusion.36
  36.1 0.7 %multiply_reduce_fusion = (f32[2,10,4,256]{3,2,1,0:T(4,128)S(1)}, f32[2,10,4,4,256]{4,3,2,1,0:T(4,128)S(1)}, f32[2,10,4,4,256]{4,3,2,1,0:T(4,128)S(1)}) fusion(f32[2,10,4,4,256]{4,3,2,1,0:T(4,128)S(1)} %slice.192, f32[2,10,4,4,256]{4,3,2,1,0:T(4,128)S(1)} %slice.194, f32[2,10,4,4,256]{4,2,1,0,3:T(4,128)S(1)} %get-tuple-element.41, ...), kind=kLoop, calls=%fused_computation.42 | loop fusion | flops 552960 | bytes 2211840 | tf_op jit(solution)/shard_map/reduce_sum | solution.py:133
  36.8 0.2 pad_maximum_fusion.3
  37.0 0.1 copy.54
  37.2 0.2 reduce-precision_convert_fusion.1
  37.4 2.1 %fusion = f32[360,2048]{1,0:T(8,128)S(1)} fusion(s32[1024]{0:T(1024)S(1)} %bitcast.133, bf16[180,1024]{1,0:T(8,128)(2,1)S(1)} %get-tuple-element.36, bf16[180,1024]{1,0:T(8,128)(2,1)S(1)} %get-tuple-element.35), kind=kOutput, calls=%fused_computation.1 | convolution fusion | flops 1513521152 | bytes 3690496 | tf_op jit(solution)/shard_map/dot_general | solution.py:39
  39.5 0.2 slice_add_fusion
  39.7 0.2 fusion.34
  39.9 0.1 copy.57
  40.0 0.8 %copy.46 = f32[8,2,10,256]{3,1,2,0:T(2,128)} copy(f32[8,2,10,256]{3,0,2,1:T(8,128)S(1)} %fusion.22) | data formatting | bytes 327680 | tf_op jit(solution)/shard_map/transpose | solution.py:68
  40.8 6.2 %all-to-all-start = ((f32[8,2,10,256]{3,1,2,0:T(2,128)}), f32[8,2,10,256]{3,1,2,0:T(2,128)}, u32[]{:S(2)}, u32[]{:S(2)}) async-start(f32[8,2,10,256]{3,1,2,0:T(2,128)} %copy.46), calls=%async_computation | async-start | bytes 327680 | tf_op jit(solution)/shard_map/all_to_all | solution.py:69
  47.0 0.8 %squeeze.45 = f32[10,4,2048]{2,1,0:T(4,128)} reshape(f32[40,2048]{1,0:T(8,128)S(1)} %get-tuple-element.29) | data formatting | bytes 655360 | tf_op jit(solution)/shard_map/squeeze | solution.py:173
  47.8 0.1 squeeze.44
  47.9 0.8 %squeeze.43 = f32[10,4,2048]{2,1,0:T(4,128)} reshape(f32[40,2048]{1,0:T(8,128)S(1)} %get-tuple-element.31) | data formatting | bytes 655360 | tf_op jit(solution)/shard_map/squeeze | solution.py:171
  48.8 0.1 squeeze.42
  48.9 0.8 %fusion.16 = f32[4,10,2048]{2,0,1:T(4,128)} fusion(f32[10,4,2048]{2,1,0:T(4,128)S(1)} %squeeze.44, f32[4,10,2048]{2,0,1:T(4,128)S(1)} %copy-done.3, f32[9,4,2048]{2,1,0:T(4,128)S(1)} %copy-done.8), kind=kLoop, calls=%fused_computation.37 | loop fusion | flops 245760 | bytes 1277952 | tf_op jit(solution)/shard_map/transpose | solution.py:175
  49.7 0.9 %add_bitcast_fusion.1 = f32[4,10,2048]{2,0,1:T(4,128)} fusion(f32[10,4,2048]{2,1,0:T(4,128)S(1)} %fusion.27, f32[10,4,2048]{2,1,0:T(4,128)S(1)} %squeeze.42, f32[4,10,2048]{2,0,1:T(4,128)S(1)} %copy-done.1), kind=kLoop, calls=%fused_computation.41 | loop fusion | flops 245760 | bytes 1310720 | tf_op jit(solution)/shard_map/transpose | solution.py:175
  50.6 0.9 %fusion.14 = f32[4,10,2048]{2,0,1:T(4,128)} fusion(f32[10,4,2048]{2,1,0:T(4,128)S(1)} %copy-done.7, f32[4,10,2048]{2,0,1:T(4,128)S(1)} %copy-done.5, f32[9,4,2048]{2,1,0:T(4,128)S(1)} %copy-done.9, f32[9,4,2048]{2,1,0:T(4,128)S(1)} %copy-done.12), kind=kLoop, calls=%fused_computation.33 | loop fusion | flops 491520 | bytes 1572864 | tf_op jit(solution)/shard_map/transpose | solution.py:175
  51.5 0.9 %add_bitcast_fusion = f32[4,10,2048]{2,0,1:T(4,128)} fusion(f32[10,4,2048]{2,1,0:T(4,128)S(1)} %copy-done.6, f32[9,4,2048]{2,1,0:T(4,128)S(1)} %copy-done.11, f32[9,4,2048]{2,1,0:T(4,128)S(1)} %copy-done.10, f32[4,10,2048]{2,0,1:T(4,128)S(1)} %copy-done), kind=kLoop, calls=%fused_computation.40 | loop fusion | flops 573440 | bytes 1572864 | tf_op jit(solution)/shard_map/transpose | solution.py:175
  52.4 1.4 %all-to-all-done = f32[8,2,10,256]{3,1,2,0:T(2,128)} async-done(((f32[8,2,10,256]{3,1,2,0:T(2,128)}), f32[8,2,10,256]{3,1,2,0:T(2,128)}, u32[]{:S(2)}, u32[]{:S(2)}) %all-to-all-start) | async-done | bytes 163872 | tf_op jit(solution)/shard_map/all_to_all | solution.py:69
  53.9 1.5 %fusion.28 = f32[2,10,256]{2,0,1:T(2,128)} fusion(f32[8,2,10,256]{3,1,2,0:T(2,128)} %all-to-all-done), kind=kLoop, calls=%fused_computation.93 | loop fusion | flops 35840 | bytes 184320 | tf_op jit(solution)/shard_map/add | solution.py:72
  (52 shorter events, 0.8 us)
Async XLA Ops:
  0.6 5.4 %copy-start.1 = (f32[4,10,2048]{2,0,1:T(4,128)S(1)}, f32[4,10,2048]{2,0,1:T(4,128)}, u32[]{:S(2)}) copy-start(f32[4,10,2048]{2,0,1:T(4,128)} %param.13) | copy-start | bytes 983044
  0.6 5.4 %copy-start = (f32[4,10,2048]{2,0,1:T(4,128)S(1)}, f32[4,10,2048]{2,0,1:T(4,128)}, u32[]{:S(2)}) copy-start(f32[4,10,2048]{2,0,1:T(4,128)} %param.14) | copy-start | bytes 983044
  0.7 5.4 %copy-start.2 = (f32[4,10,2048]{2,0,1:T(4,128)S(1)}, f32[4,10,2048]{2,0,1:T(4,128)}, u32[]{:S(2)}) copy-start(f32[4,10,2048]{2,0,1:T(4,128)} %param.22) | copy-start | bytes 983044
  0.7 5.4 %copy-start.4 = (f32[4,10,2048]{2,0,1:T(4,128)S(1)}, f32[4,10,2048]{2,0,1:T(4,128)}, u32[]{:S(2)}) copy-start(f32[4,10,2048]{2,0,1:T(4,128)} %param.23) | copy-start | bytes 983044
  7.1 0.9 %copy-start.13 = (f32[20,2048]{1,0:T(8,128)S(1)}, f32[20,2048]{1,0:T(8,128)}, u32[]{:S(2)}) copy-start(f32[20,2048]{1,0:T(8,128)} %reshape.104) | copy-start | bytes 491524
  8.1 0.7 %copy-start.15 = (s32[1,256]{1,0:T(1,128)S(1)}, s32[1,256]{1,0:T(1,128)}, u32[]{:S(2)}) copy-start(s32[1,256]{1,0:T(1,128)} %get-tuple-element.58) | copy-start | bytes 3076
  8.1 0.7 %copy-start.16 = (s32[1,256]{1,0:T(1,128)S(1)}, s32[1,256]{1,0:T(1,128)}, u32[]{:S(2)}) copy-start(s32[1,256]{1,0:T(1,128)} %get-tuple-element.59) | copy-start | bytes 3076
  11.6 15.6 %copy-start.3 = (f32[4,10,2048]{2,0,1:T(4,128)S(1)}, f32[4,10,2048]{2,0,1:T(4,128)}, u32[]{:S(2)}) copy-start(f32[4,10,2048]{2,0,1:T(4,128)} %param.22) | copy-start | bytes 983044
  11.6 15.6 %copy-start.5 = (f32[4,10,2048]{2,0,1:T(4,128)S(1)}, f32[4,10,2048]{2,0,1:T(4,128)}, u32[]{:S(2)}) copy-start(f32[4,10,2048]{2,0,1:T(4,128)} %param.23) | copy-start | bytes 983044
  12.3 18.8 %collective-permute-start = (f32[4,10,4,256]{3,2,1,0:T(4,128)S(1)}, f32[4,10,4,256]{3,2,1,0:T(4,128)S(1)}, u32[]{:S(2)}, u32[]{:S(2)}) collective-permute-start(f32[4,10,4,256]{3,2,1,0:T(4,128)S(1)} %bitcast.127), channel_id=1, source_target_pairs={{0,32},{8,40},{16,48},{24,56},{32,0},{40,8},{48,16},{56,24},{64,96... | collective-permute-start | bytes 491528 | tf_op jit(solution)/shard_map/ppermute | solution.py:9
  16.8 19.0 %collective-permute-start.1 = (f32[4,10,4,256]{3,2,1,0:T(4,128)S(1)}, f32[4,10,4,256]{3,2,1,0:T(4,128)S(1)}, u32[]{:S(2)}, u32[]{:S(2)}) collective-permute-start(f32[4,10,4,256]{3,2,1,0:T(4,128)S(1)} %bitcast.128), channel_id=1, source_target_pairs={{0,64},{8,72},{16,80},{24,88},{32,96},{40,104},{48,112},{56,120},{... | collective-permute-start | bytes 491528 | tf_op jit(solution)/shard_map/ppermute | solution.py:9
  21.9 13.9 %collective-permute-start.2 = (f32[4,10,4,256]{3,2,1,0:T(4,128)S(1)}, f32[4,10,4,256]{3,2,1,0:T(4,128)S(1)}, u32[]{:S(2)}, u32[]{:S(2)}) collective-permute-start(f32[4,10,4,256]{3,2,1,0:T(4,128)S(1)} %bitcast.129), channel_id=1, source_target_pairs={{0,16},{8,24},{16,0},{24,8},{32,48},{40,56},{48,32},{56,40},{64,80... | collective-permute-start | bytes 491528 | tf_op jit(solution)/shard_map/ppermute | solution.py:9
  25.3 10.6 %collective-permute-start.3 = (f32[4,10,4,256]{3,2,1,0:T(4,128)S(1)}, f32[4,10,4,256]{3,2,1,0:T(4,128)S(1)}, u32[]{:S(2)}, u32[]{:S(2)}) collective-permute-start(f32[4,10,4,256]{3,2,1,0:T(4,128)S(1)} %bitcast.130), channel_id=1, source_target_pairs={{0,8},{8,0},{16,24},{24,16},{32,40},{40,32},{48,56},{56,48},{64,72... | collective-permute-start | bytes 491528 | tf_op jit(solution)/shard_map/ppermute | solution.py:9
  30.3 0.8 %copy-start.14 = (f32[4,2048]{1,0:T(4,128)S(1)}, f32[4,2048]{1,0:T(4,128)}, u32[]{:S(2)}) copy-start(f32[4,2048]{1,0:T(4,128)} %param.19) | copy-start | bytes 98308
  40.8 8.1 %copy-start.8 = (f32[9,4,2048]{2,1,0:T(4,128)S(1)}, f32[9,4,2048]{2,1,0:T(4,128)}, u32[]{:S(2)}) copy-start(f32[9,4,2048]{2,1,0:T(4,128)} %get-tuple-element.53) | copy-start | bytes 884740
  40.8 13.1 %all-to-all-start = ((f32[8,2,10,256]{3,1,2,0:T(2,128)}), f32[8,2,10,256]{3,1,2,0:T(2,128)}, u32[]{:S(2)}, u32[]{:S(2)}) async-start(f32[8,2,10,256]{3,1,2,0:T(2,128)} %copy.46), calls=%async_computation | async-start | bytes 327680 | tf_op jit(solution)/shard_map/all_to_all | solution.py:69
  48.8 1.8 %copy-start.7 = (f32[10,4,2048]{2,1,0:T(4,128)S(1)}, f32[10,4,2048]{2,1,0:T(4,128)}, u32[]{:S(2)}) copy-start(f32[10,4,2048]{2,1,0:T(4,128)} %squeeze.45) | copy-start | bytes 983044
  48.8 1.8 %copy-start.9 = (f32[9,4,2048]{2,1,0:T(4,128)S(1)}, f32[9,4,2048]{2,1,0:T(4,128)}, u32[]{:S(2)}) copy-start(f32[9,4,2048]{2,1,0:T(4,128)} %get-tuple-element.25) | copy-start | bytes 884740
  48.9 1.8 %copy-start.12 = (f32[9,4,2048]{2,1,0:T(4,128)S(1)}, f32[9,4,2048]{2,1,0:T(4,128)}, u32[]{:S(2)}) copy-start(f32[9,4,2048]{2,1,0:T(4,128)} %get-tuple-element.49) | copy-start | bytes 884740
  49.7 1.8 %copy-start.6 = (f32[10,4,2048]{2,1,0:T(4,128)S(1)}, f32[10,4,2048]{2,1,0:T(4,128)}, u32[]{:S(2)}) copy-start(f32[10,4,2048]{2,1,0:T(4,128)} %squeeze.43) | copy-start | bytes 983044
  49.7 1.8 %copy-start.10 = (f32[9,4,2048]{2,1,0:T(4,128)S(1)}, f32[9,4,2048]{2,1,0:T(4,128)}, u32[]{:S(2)}) copy-start(f32[9,4,2048]{2,1,0:T(4,128)} %get-tuple-element.48) | copy-start | bytes 884740
  49.7 1.8 %copy-start.11 = (f32[9,4,2048]{2,1,0:T(4,128)S(1)}, f32[9,4,2048]{2,1,0:T(4,128)}, u32[]{:S(2)}) copy-start(f32[9,4,2048]{2,1,0:T(4,128)} %get-tuple-element.50) | copy-start | bytes 884740

commit v11 on v10

--- a/solution.py
+++ b/solution.py
@@ -98,7 +98,7 @@
     g_p = 0.1 * c_p
     g_t = 0.1 * c_t
 
-    order = [2, 3, 1, 0] if rounds == 4 else list(range(rounds))
+    order = [3, 2, 0, 1] if rounds == 4 else list(range(rounds))
     face_cols = jnp.concatenate([face_cols[i : i + 1] for i in order])
     face_weight = jnp.concatenate([face_weight[i : i + 1] for i in order])
     cols = face_cols.reshape(rounds * face)

time: 56 us -> 55.1 us (0.984)
  the two profiles are of different devices: /device:TPU:8 before, /device:TPU:128 now
where the time goes in v11:
time: 55.1 us; the launch traced here: 54.6 us
  starting transfers between devices  21.2 us (38%)
  other arithmetic  12.2 us (22%)
  local copies, waits for them, and re-layouts  8.85 us (16%)
  waiting for transfers between devices  6.9 us (13%)
  matrix products  4.25 us (8%)
  between operations  1.17 us (2%)
    ppermute x4, starting transfers between devices, from_partner(): return lax.ppermute(value, axis, pairs)  14.9 us
    all_to_all x1, starting transfers between devices, sum_scatter(): got = lax.all_to_all(parts, axis, 0, 0, tiled=True)  6.25 us
    ppermute x4, waiting for transfers between devices, from_partner(): return lax.ppermute(value, axis, pairs)  5.46 us
    dot_general x2, matrix products, exact_select(): lax.dot_general(split2(rows), select, (((1,), (contract,)), ((), ())), pr...  4.25 us
    transpose x4, other arithmetic, body(): return tuple((o.transpose(1, 0, 2) for o in outs)) + (owned,)  3.55 us
    unnamed x46, local copies, waits for them, and re-layouts  2.03 us
    add x1, other arithmetic, sum_scatter(): total = total + got[index]  1.49 us
    all_to_all x1, waiting for transfers between devices, sum_scatter(): got = lax.all_to_all(parts, axis, 0, 0, tiled=True)  1.44 us
  transfers between devices with their start and end apart: 5, of which 3 were waited for; matrix products, arithmetic and copies ran while one was open for 16% of the time, Pallas kernels for 0%

profile of v11, /device:TPU:128, one launch (start us, length us, event | category | flops | bytes accessed | tf_op | source)
XLA Modules:
  0.0 54.6 jit_solution(502162190457823343)
XLA Ops:
  0.7 0.0 copy-start.2
  0.7 0.0 copy-start.4
  0.7 0.8 %fusion.38 = (s32[1,256]{1,0:T(1,128)S(1)}, s32[1,256]{1,0:T(1,128)S(1)}) fusion(s32[4,256]{1,0:T(4,128)} %param.20), kind=kLoop, calls=%fused_computation.112 | loop fusion | bytes 4096 | tf_op jit(solution)/shard_map/slice | solution.py:102
  1.5 0.8 %fusion.37 = (f32[1,256]{1,0:T(1,128)S(1)}, f32[1,256]{1,0:T(1,128)S(1)}) fusion(f32[4,256]{1,0:T(4,128)} %param.21), kind=kLoop, calls=%fused_computation.111 | loop fusion | bytes 4096 | tf_op jit(solution)/shard_map/slice | solution.py:103
  2.2 1.1 %add_multiply_fusion.3 = (f32[10,2048]{1,0:T(8,128)S(1)}, f32[10,2048]{1,0:T(8,128)S(1)}) fusion(f32[10,2048]{1,0:T(8,128)} %param.16, f32[10,2048]{1,0:T(8,128)} %param.17, s32[10,2048]{1,0:T(8,128)} %param.18, f32[10,2048]{1,0:T(8,128)} %param.15), kind=kLoop, calls=%fused_computation.79 | loop fusion | flops 122880 | bytes 491520 | tf_op jit(solution)/shard_map/mul | solution.py:97
  3.4 0.7 %reshape.104 = f32[20,2048]{1,0:T(8,128)} reshape(f32[2,10,2048]{2,1,0:T(8,128)S(1)} %pad_maximum_fusion.4) | data formatting | bytes 327680 | tf_op jit(solution)/shard_map/reshape | solution.py:113
  4.1 0.0 copy-done.1
  4.1 0.6 %pad_maximum_fusion = f32[4,10,4,2048]{3,2,1,0:T(4,128)S(1)} fusion(f32[1,10,4,2048]{3,2,1,0:T(4,128)S(1)} %bitcast.108, f32[1,10,4,2048]{3,2,1,0:T(4,128)S(1)} %bitcast.107, f32[1,10,4,2048]{3,2,1,0:T(4,128)S(1)} %bitcast.97, f32[1,10,4,2048]{3,2,1,0:T(4,128)S(1)} %bitcast.100), kind=kLoop, calls=%fused_computation.12 | loop fusion | flops 983040 | bytes 2621440 | tf_op jit(solution)/shard_map/stack | solution.py:112
  4.7 0.5 reshape.103
  5.2 0.0 copy-start.13
  5.2 0.1 constant_dynamic-update-slice_fusion.1
  5.3 0.8 %copy-done.13 = f32[20,2048]{1,0:T(8,128)S(1)} copy-done((f32[20,2048]{1,0:T(8,128)S(1)}, f32[20,2048]{1,0:T(8,128)}, u32[]{:S(2)}) %copy-start.13) | copy-done | bytes 163864
  6.1 0.0 slice-start.1
  6.2 0.2 reduce-precision_convert_fusion
  6.3 0.5 slice-done.1
  6.8 2.2 %fusion.1 = f32[360,1024]{1,0:T(8,128)S(1)} fusion(s32[1024]{0:T(1024)S(1)} %bitcast.132, bf16[180,2048]{1,0:T(8,128)(2,1)S(1)} %get-tuple-element.34, bf16[180,2048]{1,0:T(8,128)(2,1)S(1)} %get-tuple-element.33), kind=kOutput, calls=%fused_computation.2 | convolution fusion | flops 1514995712 | bytes 2953216 | tf_op jit(solution)/shard_map/dot_general | solution.py:39
  9.0 0.1 slice_add_fusion.1
  9.2 0.0 slice-start
  9.2 0.1 fusion.35
  9.3 0.2 slice.192
  9.5 0.2 slice.194
  9.6 0.2 slice-done
  9.9 0.0 copy-start.3
  9.9 0.0 copy-start.5
  9.9 0.1 broadcast_multiply_fusion.1
  10.0 0.5 fusion.19
  10.6 7.7 %collective-permute-start = (f32[4,10,4,256]{3,2,1,0:T(4,128)S(1)}, f32[4,10,4,256]{3,2,1,0:T(4,128)S(1)}, u32[]{:S(2)}, u32[]{:S(2)}) collective-permute-start(f32[4,10,4,256]{3,2,1,0:T(4,128)S(1)} %bitcast.127), channel_id=1, source_target_pairs={{0,64},{8,72},{16,80},{24,88},{32,96},{40,104},{48,112},{56,120},{... | collective-permute-start | bytes 491528 | tf_op jit(solution)/shard_map/ppermute | solution.py:9
  18.3 2.7 %collective-permute-start.1 = (f32[4,10,4,256]{3,2,1,0:T(4,128)S(1)}, f32[4,10,4,256]{3,2,1,0:T(4,128)S(1)}, u32[]{:S(2)}, u32[]{:S(2)}) collective-permute-start(f32[4,10,4,256]{3,2,1,0:T(4,128)S(1)} %bitcast.128), channel_id=1, source_target_pairs={{0,32},{8,40},{16,48},{24,56},{32,0},{40,8},{48,16},{56,24},{64,96... | collective-permute-start | bytes 491528 | tf_op jit(solution)/shard_map/ppermute | solution.py:9
  21.1 1.9 %collective-permute-start.2 = (f32[4,10,4,256]{3,2,1,0:T(4,128)S(1)}, f32[4,10,4,256]{3,2,1,0:T(4,128)S(1)}, u32[]{:S(2)}, u32[]{:S(2)}) collective-permute-start(f32[4,10,4,256]{3,2,1,0:T(4,128)S(1)} %bitcast.129), channel_id=1, source_target_pairs={{0,8},{8,0},{16,24},{24,16},{32,40},{40,32},{48,56},{56,48},{64,72... | collective-permute-start | bytes 491528 | tf_op jit(solution)/shard_map/ppermute | solution.py:9
  23.1 2.6 %collective-permute-start.3 = (f32[4,10,4,256]{3,2,1,0:T(4,128)S(1)}, f32[4,10,4,256]{3,2,1,0:T(4,128)S(1)}, u32[]{:S(2)}, u32[]{:S(2)}) collective-permute-start(f32[4,10,4,256]{3,2,1,0:T(4,128)S(1)} %bitcast.130), channel_id=1, source_target_pairs={{0,16},{8,24},{16,0},{24,8},{32,48},{40,56},{48,32},{56,40},{64,80... | collective-permute-start | bytes 491528 | tf_op jit(solution)/shard_map/ppermute | solution.py:9
  25.7 0.2 bitcast_multiply_fusion
  26.0 0.5 multiply_reduce_fusion.2
  26.4 1.1 %multiply_multiply_fusion = (f32[9,4,2048]{2,1,0:T(4,128)}, f32[9,4,2048]{2,1,0:T(4,128)S(1)}, f32[9,4,2048]{2,1,0:T(4,128)}) fusion(f32[9,4,2048]{2,1,0:T(4,128)S(1)} %get-tuple-element.24, f32[10,4,2048]{2,1,0:T(4,128)S(1)} %bitcast.102, f32[9,2048]{1,0:T(8,128)S(1)} %get-tuple-element.63, f32[9,4,2048]{2,1,0:T(4,128)S(1)} %get-tuple-element.23), kind=kLoop, calls=%fused_computation.55 | loop fusion | flops 368640 | bytes 2138112 | tf_op jit(solution)/shard_map/mul | solution.py:173
  27.5 0.1 pad_subtract_fusion
  27.6 1.1 %multiply_reduce_fusion.1 = (f32[9,2048]{1,0:T(8,128)S(1)}, f32[9,4,2048]{2,1,0:T(4,128)}, f32[9,4,2048]{2,1,0:T(4,128)}, f32[9,4,2048]{2,1,0:T(4,128)}) fusion(f32[9,4,2048]{2,1,0:T(4,128)S(1)} %get-tuple-element.24, f32[10,4,2048]{2,1,0:T(4,128)S(1)} %bitcast.99, f32[9,2048]{1,0:T(8,128)S(1)} %get-tuple-element.62, f32[9,4,2048]{2,1,0:T(4,128)S(1)} %get-tuple-element.26), kind=kLoop, calls=%fused_computation.50 | loop fusion | flops 571392 | bytes 2211840 | tf_op jit(solution)/shard_map/reduce_sum | solution.py:148
  29.0 0.5 copy-done.14
  29.5 0.0 collective-permute-done
  29.5 4.3 %collective-permute-done.1 = f32[4,10,4,256]{3,2,1,0:T(4,128)S(1)} collective-permute-done((f32[4,10,4,256]{3,2,1,0:T(4,128)S(1)}, f32[4,10,4,256]{3,2,1,0:T(4,128)S(1)}, u32[]{:S(2)}, u32[]{:S(2)}) %collective-permute-start.1) | collective-permute-done | bytes 163872 | tf_op jit(solution)/shard_map/ppermute | solution.py:9
  33.8 0.0 collective-permute-done.2
  33.8 1.2 %collective-permute-done.3 = f32[4,10,4,256]{3,2,1,0:T(4,128)S(1)} collective-permute-done((f32[4,10,4,256]{3,2,1,0:T(4,128)S(1)}, f32[4,10,4,256]{3,2,1,0:T(4,128)S(1)}, u32[]{:S(2)}, u32[]{:S(2)}) %collective-permute-start.3) | collective-permute-done | bytes 163872 | tf_op jit(solution)/shard_map/ppermute | solution.py:9
  35.0 0.1 pad_maximum_fusion.2
  35.1 0.1 fusion.36
  35.3 0.7 %multiply_reduce_fusion = (f32[2,10,4,256]{3,2,1,0:T(4,128)S(1)}, f32[2,10,4,4,256]{4,3,2,1,0:T(4,128)S(1)}, f32[2,10,4,4,256]{4,3,2,1,0:T(4,128)S(1)}) fusion(f32[2,10,4,4,256]{4,3,2,1,0:T(4,128)S(1)} %slice.192, f32[2,10,4,4,256]{4,3,2,1,0:T(4,128)S(1)} %slice.194, f32[2,10,4,4,256]{4,2,1,0,3:T(4,128)S(1)} %get-tuple-element.41, ...), kind=kLoop, calls=%fused_computation.42 | loop fusion | flops 552960 | bytes 2211840 | tf_op jit(solution)/shard_map/reduce_sum | solution.py:133
  35.9 0.2 pad_maximum_fusion.3
  36.2 0.1 copy.54
  36.4 0.2 reduce-precision_convert_fusion.1
  36.5 2.1 %fusion = f32[360,2048]{1,0:T(8,128)S(1)} fusion(s32[1024]{0:T(1024)S(1)} %bitcast.133, bf16[180,1024]{1,0:T(8,128)(2,1)S(1)} %get-tuple-element.36, bf16[180,1024]{1,0:T(8,128)(2,1)S(1)} %get-tuple-element.35), kind=kOutput, calls=%fused_computation.1 | convolution fusion | flops 1513521152 | bytes 3690496 | tf_op jit(solution)/shard_map/dot_general | solution.py:39
  38.6 0.2 slice_add_fusion
  38.8 0.2 fusion.34
  39.0 0.1 copy.57
  39.2 0.8 %copy.46 = f32[8,2,10,256]{3,1,2,0:T(2,128)} copy(f32[8,2,10,256]{3,0,2,1:T(8,128)S(1)} %fusion.22) | data formatting | bytes 327680 | tf_op jit(solution)/shard_map/transpose | solution.py:68
  40.0 6.2 %all-to-all-start = ((f32[8,2,10,256]{3,1,2,0:T(2,128)}), f32[8,2,10,256]{3,1,2,0:T(2,128)}, u32[]{:S(2)}, u32[]{:S(2)}) async-start(f32[8,2,10,256]{3,1,2,0:T(2,128)} %copy.46), calls=%async_computation | async-start | bytes 327680 | tf_op jit(solution)/shard_map/all_to_all | solution.py:69
  46.2 0.8 %squeeze.45 = f32[10,4,2048]{2,1,0:T(4,128)} reshape(f32[40,2048]{1,0:T(8,128)S(1)} %get-tuple-element.29) | data formatting | bytes 655360 | tf_op jit(solution)/shard_map/squeeze | solution.py:173
  47.0 0.1 squeeze.44
  47.1 0.8 %squeeze.43 = f32[10,4,2048]{2,1,0:T(4,128)} reshape(f32[40,2048]{1,0:T(8,128)S(1)} %get-tuple-element.31) | data formatting | bytes 655360 | tf_op jit(solution)/shard_map/squeeze | solution.py:171
  47.9 0.1 squeeze.42
  48.1 0.8 %fusion.16 = f32[4,10,2048]{2,0,1:T(4,128)} fusion(f32[10,4,2048]{2,1,0:T(4,128)S(1)} %squeeze.44, f32[4,10,2048]{2,0,1:T(4,128)S(1)} %copy-done.3, f32[9,4,2048]{2,1,0:T(4,128)S(1)} %copy-done.8), kind=kLoop, calls=%fused_computation.37 | loop fusion | flops 245760 | bytes 1277952 | tf_op jit(solution)/shard_map/transpose | solution.py:175
  48.9 0.9 %add_bitcast_fusion.1 = f32[4,10,2048]{2,0,1:T(4,128)} fusion(f32[10,4,2048]{2,1,0:T(4,128)S(1)} %fusion.27, f32[10,4,2048]{2,1,0:T(4,128)S(1)} %squeeze.42, f32[4,10,2048]{2,0,1:T(4,128)S(1)} %copy-done.1), kind=kLoop, calls=%fused_computation.41 | loop fusion | flops 245760 | bytes 1310720 | tf_op jit(solution)/shard_map/transpose | solution.py:175
  49.8 0.9 %fusion.14 = f32[4,10,2048]{2,0,1:T(4,128)} fusion(f32[10,4,2048]{2,1,0:T(4,128)S(1)} %copy-done.7, f32[4,10,2048]{2,0,1:T(4,128)S(1)} %copy-done.5, f32[9,4,2048]{2,1,0:T(4,128)S(1)} %copy-done.9, f32[9,4,2048]{2,1,0:T(4,128)S(1)} %copy-done.12), kind=kLoop, calls=%fused_computation.33 | loop fusion | flops 491520 | bytes 1572864 | tf_op jit(solution)/shard_map/transpose | solution.py:175
  50.7 0.0 copy-done.6
  50.7 0.0 copy-done.11
  50.7 0.9 %add_bitcast_fusion = f32[4,10,2048]{2,0,1:T(4,128)} fusion(f32[10,4,2048]{2,1,0:T(4,128)S(1)} %copy-done.6, f32[9,4,2048]{2,1,0:T(4,128)S(1)} %copy-done.11, f32[9,4,2048]{2,1,0:T(4,128)S(1)} %copy-done.10, f32[4,10,2048]{2,0,1:T(4,128)S(1)} %copy-done), kind=kLoop, calls=%fused_computation.40 | loop fusion | flops 573440 | bytes 1572864 | tf_op jit(solution)/shard_map/transpose | solution.py:175
  51.6 1.4 %all-to-all-done = f32[8,2,10,256]{3,1,2,0:T(2,128)} async-done(((f32[8,2,10,256]{3,1,2,0:T(2,128)}), f32[8,2,10,256]{3,1,2,0:T(2,128)}, u32[]{:S(2)}, u32[]{:S(2)}) %all-to-all-start) | async-done | bytes 163872 | tf_op jit(solution)/shard_map/all_to_all | solution.py:69
  53.1 1.5 %fusion.28 = f32[2,10,256]{2,0,1:T(2,128)} fusion(f32[8,2,10,256]{3,1,2,0:T(2,128)} %all-to-all-done), kind=kLoop, calls=%fused_computation.93 | loop fusion | flops 35840 | bytes 184320 | tf_op jit(solution)/shard_map/add | solution.py:72
  (50 shorter events, 0.8 us)
Async XLA Ops:
  0.6 3.5 %copy-start.1 = (f32[4,10,2048]{2,0,1:T(4,128)S(1)}, f32[4,10,2048]{2,0,1:T(4,128)}, u32[]{:S(2)}) copy-start(f32[4,10,2048]{2,0,1:T(4,128)} %param.13) | copy-start | bytes 983044
  0.6 3.5 %copy-start = (f32[4,10,2048]{2,0,1:T(4,128)S(1)}, f32[4,10,2048]{2,0,1:T(4,128)}, u32[]{:S(2)}) copy-start(f32[4,10,2048]{2,0,1:T(4,128)} %param.14) | copy-start | bytes 983044
  0.7 3.5 %copy-start.2 = (f32[4,10,2048]{2,0,1:T(4,128)S(1)}, f32[4,10,2048]{2,0,1:T(4,128)}, u32[]{:S(2)}) copy-start(f32[4,10,2048]{2,0,1:T(4,128)} %param.22) | copy-start | bytes 983044
  0.7 3.5 %copy-start.4 = (f32[4,10,2048]{2,0,1:T(4,128)S(1)}, f32[4,10,2048]{2,0,1:T(4,128)}, u32[]{:S(2)}) copy-start(f32[4,10,2048]{2,0,1:T(4,128)} %param.23) | copy-start | bytes 983044
  5.2 0.9 %copy-start.13 = (f32[20,2048]{1,0:T(8,128)S(1)}, f32[20,2048]{1,0:T(8,128)}, u32[]{:S(2)}) copy-start(f32[20,2048]{1,0:T(8,128)} %reshape.104) | copy-start | bytes 491524
  6.1 0.7 %slice-start.1 = ((s32[4,256]{1,0:T(4,128)}), s32[2,256]{1,0:T(2,128)S(1)}, s32[]{:S(2)}) async-start(s32[4,256]{1,0:T(4,128)} %param.20), calls=%async_computation.2 | async-start | bytes 4096 | tf_op jit(solution)/shard_map/slice | solution.py:102
  9.2 0.7 %slice-start = ((f32[4,256]{1,0:T(4,128)}), f32[2,256]{1,0:T(2,128)S(1)}, s32[]{:S(2)}) async-start(f32[4,256]{1,0:T(4,128)} %param.21), calls=%async_computation.1 | async-start | bytes 4096 | tf_op jit(solution)/shard_map/slice | solution.py:103
  9.9 15.8 %copy-start.3 = (f32[4,10,2048]{2,0,1:T(4,128)S(1)}, f32[4,10,2048]{2,0,1:T(4,128)}, u32[]{:S(2)}) copy-start(f32[4,10,2048]{2,0,1:T(4,128)} %param.22) | copy-start | bytes 983044
  9.9 15.8 %copy-start.5 = (f32[4,10,2048]{2,0,1:T(4,128)S(1)}, f32[4,10,2048]{2,0,1:T(4,128)}, u32[]{:S(2)}) copy-start(f32[4,10,2048]{2,0,1:T(4,128)} %param.23) | copy-start | bytes 983044
  10.6 19.0 %collective-permute-start = (f32[4,10,4,256]{3,2,1,0:T(4,128)S(1)}, f32[4,10,4,256]{3,2,1,0:T(4,128)S(1)}, u32[]{:S(2)}, u32[]{:S(2)}) collective-permute-start(f32[4,10,4,256]{3,2,1,0:T(4,128)S(1)} %bitcast.127), channel_id=1, source_target_pairs={{0,64},{8,72},{16,80},{24,88},{32,96},{40,104},{48,112},{56,120},{... | collective-permute-start | bytes 491528 | tf_op jit(solution)/shard_map/ppermute | solution.py:9
  18.3 15.4 %collective-permute-start.1 = (f32[4,10,4,256]{3,2,1,0:T(4,128)S(1)}, f32[4,10,4,256]{3,2,1,0:T(4,128)S(1)}, u32[]{:S(2)}, u32[]{:S(2)}) collective-permute-start(f32[4,10,4,256]{3,2,1,0:T(4,128)S(1)} %bitcast.128), channel_id=1, source_target_pairs={{0,32},{8,40},{16,48},{24,56},{32,0},{40,8},{48,16},{56,24},{64,96... | collective-permute-start | bytes 491528 | tf_op jit(solution)/shard_map/ppermute | solution.py:9
  21.1 12.7 %collective-permute-start.2 = (f32[4,10,4,256]{3,2,1,0:T(4,128)S(1)}, f32[4,10,4,256]{3,2,1,0:T(4,128)S(1)}, u32[]{:S(2)}, u32[]{:S(2)}) collective-permute-start(f32[4,10,4,256]{3,2,1,0:T(4,128)S(1)} %bitcast.129), channel_id=1, source_target_pairs={{0,8},{8,0},{16,24},{24,16},{32,40},{40,32},{48,56},{56,48},{64,72... | collective-permute-start | bytes 491528 | tf_op jit(solution)/shard_map/ppermute | solution.py:9
  23.1 11.9 %collective-permute-start.3 = (f32[4,10,4,256]{3,2,1,0:T(4,128)S(1)}, f32[4,10,4,256]{3,2,1,0:T(4,128)S(1)}, u32[]{:S(2)}, u32[]{:S(2)}) collective-permute-start(f32[4,10,4,256]{3,2,1,0:T(4,128)S(1)} %bitcast.130), channel_id=1, source_target_pairs={{0,16},{8,24},{16,0},{24,8},{32,48},{40,56},{48,32},{56,40},{64,80... | collective-permute-start | bytes 491528 | tf_op jit(solution)/shard_map/ppermute | solution.py:9
  28.7 0.8 %copy-start.14 = (f32[4,2048]{1,0:T(4,128)S(1)}, f32[4,2048]{1,0:T(4,128)}, u32[]{:S(2)}) copy-start(f32[4,2048]{1,0:T(4,128)} %param.19) | copy-start | bytes 98308
  40.0 8.1 %copy-start.8 = (f32[9,4,2048]{2,1,0:T(4,128)S(1)}, f32[9,4,2048]{2,1,0:T(4,128)}, u32[]{:S(2)}) copy-start(f32[9,4,2048]{2,1,0:T(4,128)} %get-tuple-element.53) | copy-start | bytes 884740
  40.0 13.1 %all-to-all-start = ((f32[8,2,10,256]{3,1,2,0:T(2,128)}), f32[8,2,10,256]{3,1,2,0:T(2,128)}, u32[]{:S(2)}, u32[]{:S(2)}) async-start(f32[8,2,10,256]{3,1,2,0:T(2,128)} %copy.46), calls=%async_computation | async-start | bytes 327680 | tf_op jit(solution)/shard_map/all_to_all | solution.py:69
  47.9 1.8 %copy-start.7 = (f32[10,4,2048]{2,1,0:T(4,128)S(1)}, f32[10,4,2048]{2,1,0:T(4,128)}, u32[]{:S(2)}) copy-start(f32[10,4,2048]{2,1,0:T(4,128)} %squeeze.45) | copy-start | bytes 983044
  47.9 1.8 %copy-start.9 = (f32[9,4,2048]{2,1,0:T(4,128)S(1)}, f32[9,4,2048]{2,1,0:T(4,128)}, u32[]{:S(2)}) copy-start(f32[9,4,2048]{2,1,0:T(4,128)} %get-tuple-element.25) | copy-start | bytes 884740
  48.0 1.8 %copy-start.12 = (f32[9,4,2048]{2,1,0:T(4,128)S(1)}, f32[9,4,2048]{2,1,0:T(4,128)}, u32[]{:S(2)}) copy-start(f32[9,4,2048]{2,1,0:T(4,128)} %get-tuple-element.49) | copy-start | bytes 884740
  48.9 1.8 %copy-start.6 = (f32[10,4,2048]{2,1,0:T(4,128)S(1)}, f32[10,4,2048]{2,1,0:T(4,128)}, u32[]{:S(2)}) copy-start(f32[10,4,2048]{2,1,0:T(4,128)} %squeeze.43) | copy-start | bytes 983044
  48.9 1.8 %copy-start.10 = (f32[9,4,2048]{2,1,0:T(4,128)S(1)}, f32[9,4,2048]{2,1,0:T(4,128)}, u32[]{:S(2)}) copy-start(f32[9,4,2048]{2,1,0:T(4,128)} %get-tuple-element.48) | copy-start | bytes 884740
  48.9 1.8 %copy-start.11 = (f32[9,4,2048]{2,1,0:T(4,128)S(1)}, f32[9,4,2048]{2,1,0:T(4,128)}, u32[]{:S(2)}) copy-start(f32[9,4,2048]{2,1,0:T(4,128)} %get-tuple-element.50) | copy-start | bytes 884740

commit v12 on v11

--- a/solution.py
+++ b/solution.py
@@ -98,7 +98,7 @@
     g_p = 0.1 * c_p
     g_t = 0.1 * c_t
 
-    order = [3, 2, 0, 1] if rounds == 4 else list(range(rounds))
+    order = [2, 0, 3, 1] if rounds == 4 else list(range(rounds))
     face_cols = jnp.concatenate([face_cols[i : i + 1] for i in order])
     face_weight = jnp.concatenate([face_weight[i : i + 1] for i in order])
     cols = face_cols.reshape(rounds * face)

time: 55.1 us -> 54.4 us (0.987)
  local copies, waits for them, and re-layouts: 8.85 us -> 7.81 us
    slice x3 -> x1, local copies, waits for them, and re-layouts: 0.99 us -> 0.01 us  [body(): face_weight = jnp.concatenate([face_weight[i:i + 1] for i in order])]
    slice x3 -> x1, local copies, waits for them, and re-layouts: 1.3 us -> 0.84 us  [body(): face_cols = jnp.concatenate([face_cols[i:i + 1] for i in order])]
    unnamed x46 -> x48, local copies, waits for them, and re-layouts: 2.03 us -> 2.44 us
where the time goes in v12:
time: 54.4 us; the launch traced here: 53.8 us
  starting transfers between devices  21.2 us (39%)
  other arithmetic  12.2 us (22%)
  local copies, waits for them, and re-layouts  7.81 us (14%)
  waiting for transfers between devices  7.18 us (13%)
  matrix products  4.24 us (8%)
  between operations  1.18 us (2%)
    ppermute x4, starting transfers between devices, from_partner(): return lax.ppermute(value, axis, pairs)  14.9 us
    all_to_all x1, starting transfers between devices, sum_scatter(): got = lax.all_to_all(parts, axis, 0, 0, tiled=True)  6.23 us
    ppermute x4, waiting for transfers between devices, from_partner(): return lax.ppermute(value, axis, pairs)  5.74 us
    dot_general x2, matrix products, exact_select(): lax.dot_general(split2(rows), select, (((1,), (contract,)), ((), ())), pr...  4.24 us
    transpose x4, other arithmetic, body(): return tuple((o.transpose(1, 0, 2) for o in outs)) + (owned,)  3.55 us
    unnamed x48, local copies, waits for them, and re-layouts  2.44 us
    add x1, other arithmetic, sum_scatter(): total = total + got[index]  1.49 us
    all_to_all x1, waiting for transfers between devices, sum_scatter(): got = lax.all_to_all(parts, axis, 0, 0, tiled=True)  1.44 us
  transfers between devices with their start and end apart: 5, of which 3 were waited for; matrix products, arithmetic and copies ran while one was open for 16% of the time, Pallas kernels for 0%

profile of v12, /device:TPU:128, one launch (start us, length us, event | category | flops | bytes accessed | tf_op | source)
XLA Modules:
  0.0 53.8 jit_solution(17445054221938296083)
XLA Ops:
  0.6 0.0 copy-start.1
  0.6 0.0 copy-start
  0.7 0.0 copy-start.2
  0.7 0.0 copy-start.4
  0.7 0.8 %fusion.38 = (s32[1,256]{1,0:T(1,128)S(1)}, s32[1,256]{1,0:T(1,128)S(1)}, s32[1,256]{1,0:T(1,128)S(1)}, s32[1,256]{1,0:T(1,128)S(1)}) fusion(s32[4,256]{1,0:T(4,128)} %param.20), kind=kLoop, calls=%fused_computation.112 | loop fusion | bytes 8192 | tf_op jit(solution)/shard_map/slice | solution.py:102
  1.5 1.1 %add_multiply_fusion.3 = (f32[10,2048]{1,0:T(8,128)S(1)}, f32[10,2048]{1,0:T(8,128)S(1)}) fusion(f32[10,2048]{1,0:T(8,128)} %param.16, f32[10,2048]{1,0:T(8,128)} %param.17, s32[10,2048]{1,0:T(8,128)} %param.18, f32[10,2048]{1,0:T(8,128)} %param.15), kind=kLoop, calls=%fused_computation.79 | loop fusion | flops 122880 | bytes 491520 | tf_op jit(solution)/shard_map/mul | solution.py:97
  2.7 0.7 %reshape.104 = f32[20,2048]{1,0:T(8,128)} reshape(f32[2,10,2048]{2,1,0:T(8,128)S(1)} %pad_maximum_fusion.4) | data formatting | bytes 327680 | tf_op jit(solution)/shard_map/reshape | solution.py:113
  3.4 0.0 copy-done.1
  3.4 0.0 copy-done
  3.4 0.6 %pad_maximum_fusion = f32[4,10,4,2048]{3,2,1,0:T(4,128)S(1)} fusion(f32[1,10,4,2048]{3,2,1,0:T(4,128)S(1)} %bitcast.108, f32[1,10,4,2048]{3,2,1,0:T(4,128)S(1)} %bitcast.107, f32[1,10,4,2048]{3,2,1,0:T(4,128)S(1)} %bitcast.97, f32[1,10,4,2048]{3,2,1,0:T(4,128)S(1)} %bitcast.100), kind=kLoop, calls=%fused_computation.12 | loop fusion | flops 983040 | bytes 2621440 | tf_op jit(solution)/shard_map/stack | solution.py:112
  4.0 0.5 reshape.103
  4.5 0.0 copy-start.13
  4.5 0.1 constant_dynamic-update-slice_fusion.1
  4.6 0.8 %copy-done.13 = f32[20,2048]{1,0:T(8,128)S(1)} copy-done((f32[20,2048]{1,0:T(8,128)S(1)}, f32[20,2048]{1,0:T(8,128)}, u32[]{:S(2)}) %copy-start.13) | copy-done | bytes 163864
  5.4 0.2 reduce-precision_convert_fusion
  5.6 2.2 %fusion.1 = f32[360,1024]{1,0:T(8,128)S(1)} fusion(s32[1024]{0:T(1024)S(1)} %bitcast.132, bf16[180,2048]{1,0:T(8,128)(2,1)S(1)} %get-tuple-element.34, bf16[180,2048]{1,0:T(8,128)(2,1)S(1)} %get-tuple-element.33), kind=kOutput, calls=%fused_computation.2 | convolution fusion | flops 1514995712 | bytes 2953216 | tf_op jit(solution)/shard_map/dot_general | solution.py:39
  7.8 0.0 copy-start.15
  7.8 0.1 slice_add_fusion.1
  8.0 0.1 fusion.35
  8.1 0.4 copy-done.15
  8.5 0.2 slice.196
  8.7 0.2 slice.198
  8.9 0.0 copy-start.3
  8.9 0.0 copy-start.5
  8.9 0.1 broadcast_multiply_fusion.1
  9.0 0.5 fusion.19
  9.5 4.5 %collective-permute-start = (f32[4,10,4,256]{3,2,1,0:T(4,128)S(1)}, f32[4,10,4,256]{3,2,1,0:T(4,128)S(1)}, u32[]{:S(2)}, u32[]{:S(2)}) collective-permute-start(f32[4,10,4,256]{3,2,1,0:T(4,128)S(1)} %bitcast.127), channel_id=1, source_target_pairs={{0,32},{8,40},{16,48},{24,56},{32,0},{40,8},{48,16},{56,24},{64,96... | collective-permute-start | bytes 491528 | tf_op jit(solution)/shard_map/ppermute | solution.py:9
  14.1 1.9 %collective-permute-start.1 = (f32[4,10,4,256]{3,2,1,0:T(4,128)S(1)}, f32[4,10,4,256]{3,2,1,0:T(4,128)S(1)}, u32[]{:S(2)}, u32[]{:S(2)}) collective-permute-start(f32[4,10,4,256]{3,2,1,0:T(4,128)S(1)} %bitcast.128), channel_id=1, source_target_pairs={{0,8},{8,0},{16,24},{24,16},{32,40},{40,32},{48,56},{56,48},{64,72... | collective-permute-start | bytes 491528 | tf_op jit(solution)/shard_map/ppermute | solution.py:9
  16.1 5.9 %collective-permute-start.2 = (f32[4,10,4,256]{3,2,1,0:T(4,128)S(1)}, f32[4,10,4,256]{3,2,1,0:T(4,128)S(1)}, u32[]{:S(2)}, u32[]{:S(2)}) collective-permute-start(f32[4,10,4,256]{3,2,1,0:T(4,128)S(1)} %bitcast.129), channel_id=1, source_target_pairs={{0,64},{8,72},{16,80},{24,88},{32,96},{40,104},{48,112},{56,120},{... | collective-permute-start | bytes 491528 | tf_op jit(solution)/shard_map/ppermute | solution.py:9
  22.1 2.6 %collective-permute-start.3 = (f32[4,10,4,256]{3,2,1,0:T(4,128)S(1)}, f32[4,10,4,256]{3,2,1,0:T(4,128)S(1)}, u32[]{:S(2)}, u32[]{:S(2)}) collective-permute-start(f32[4,10,4,256]{3,2,1,0:T(4,128)S(1)} %bitcast.130), channel_id=1, source_target_pairs={{0,16},{8,24},{16,0},{24,8},{32,48},{40,56},{48,32},{56,40},{64,80... | collective-permute-start | bytes 491528 | tf_op jit(solution)/shard_map/ppermute | solution.py:9
  24.7 0.2 bitcast_multiply_fusion
  25.0 0.5 multiply_reduce_fusion.2
  25.4 1.1 %multiply_multiply_fusion = (f32[9,4,2048]{2,1,0:T(4,128)}, f32[9,4,2048]{2,1,0:T(4,128)S(1)}, f32[9,4,2048]{2,1,0:T(4,128)}) fusion(f32[9,4,2048]{2,1,0:T(4,128)S(1)} %get-tuple-element.24, f32[10,4,2048]{2,1,0:T(4,128)S(1)} %bitcast.102, f32[9,2048]{1,0:T(8,128)S(1)} %get-tuple-element.67, f32[9,4,2048]{2,1,0:T(4,128)S(1)} %get-tuple-element.23), kind=kLoop, calls=%fused_computation.55 | loop fusion | flops 368640 | bytes 2138112 | tf_op jit(solution)/shard_map/mul | solution.py:173
  26.5 0.1 pad_subtract_fusion
  26.6 1.2 %multiply_reduce_fusion.1 = (f32[9,2048]{1,0:T(8,128)S(1)}, f32[9,4,2048]{2,1,0:T(4,128)}, f32[9,4,2048]{2,1,0:T(4,128)}, f32[9,4,2048]{2,1,0:T(4,128)}) fusion(f32[9,4,2048]{2,1,0:T(4,128)S(1)} %get-tuple-element.24, f32[10,4,2048]{2,1,0:T(4,128)S(1)} %bitcast.99, f32[9,2048]{1,0:T(8,128)S(1)} %get-tuple-element.66, f32[9,4,2048]{2,1,0:T(4,128)S(1)} %get-tuple-element.26), kind=kLoop, calls=%fused_computation.50 | loop fusion | flops 571392 | bytes 2211840 | tf_op jit(solution)/shard_map/reduce_sum | solution.py:148
  28.0 0.5 copy-done.14
  28.5 0.0 collective-permute-done
  28.5 0.0 collective-permute-done.1
  28.5 0.5 collective-permute-done.2
  29.0 5.3 %collective-permute-done.3 = f32[4,10,4,256]{3,2,1,0:T(4,128)S(1)} collective-permute-done((f32[4,10,4,256]{3,2,1,0:T(4,128)S(1)}, f32[4,10,4,256]{3,2,1,0:T(4,128)S(1)}, u32[]{:S(2)}, u32[]{:S(2)}) %collective-permute-start.3) | collective-permute-done | bytes 163872 | tf_op jit(solution)/shard_map/ppermute | solution.py:9
  34.3 0.1 pad_maximum_fusion.2
  34.4 0.1 fusion.36
  34.5 0.7 %multiply_reduce_fusion = (f32[2,10,4,256]{3,2,1,0:T(4,128)S(1)}, f32[2,10,4,4,256]{4,3,2,1,0:T(4,128)S(1)}, f32[2,10,4,4,256]{4,3,2,1,0:T(4,128)S(1)}) fusion(f32[2,10,4,4,256]{4,3,2,1,0:T(4,128)S(1)} %slice.196, f32[2,10,4,4,256]{4,3,2,1,0:T(4,128)S(1)} %slice.198, f32[2,10,4,4,256]{4,2,1,0,3:T(4,128)S(1)} %get-tuple-element.41, ...), kind=kLoop, calls=%fused_computation.42 | loop fusion | flops 552960 | bytes 2211840 | tf_op jit(solution)/shard_map/reduce_sum | solution.py:133
  35.2 0.2 pad_maximum_fusion.3
  35.5 0.1 copy.54
  35.7 0.2 reduce-precision_convert_fusion.1
  35.8 2.1 %fusion = f32[360,2048]{1,0:T(8,128)S(1)} fusion(s32[1024]{0:T(1024)S(1)} %bitcast.133, bf16[180,1024]{1,0:T(8,128)(2,1)S(1)} %get-tuple-element.36, bf16[180,1024]{1,0:T(8,128)(2,1)S(1)} %get-tuple-element.35), kind=kOutput, calls=%fused_computation.1 | convolution fusion | flops 1513521152 | bytes 3690496 | tf_op jit(solution)/shard_map/dot_general | solution.py:39
  37.9 0.2 slice_add_fusion
  38.1 0.2 fusion.34
  38.3 0.1 copy.57
  38.5 0.8 %copy.46 = f32[8,2,10,256]{3,1,2,0:T(2,128)} copy(f32[8,2,10,256]{3,0,2,1:T(8,128)S(1)} %fusion.22) | data formatting | bytes 327680 | tf_op jit(solution)/shard_map/transpose | solution.py:68
  39.2 6.2 %all-to-all-start = ((f32[8,2,10,256]{3,1,2,0:T(2,128)}), f32[8,2,10,256]{3,1,2,0:T(2,128)}, u32[]{:S(2)}, u32[]{:S(2)}) async-start(f32[8,2,10,256]{3,1,2,0:T(2,128)} %copy.46), calls=%async_computation | async-start | bytes 327680 | tf_op jit(solution)/shard_map/all_to_all | solution.py:69
  45.5 0.8 %squeeze.45 = f32[10,4,2048]{2,1,0:T(4,128)} reshape(f32[40,2048]{1,0:T(8,128)S(1)} %get-tuple-element.29) | data formatting | bytes 655360 | tf_op jit(solution)/shard_map/squeeze | solution.py:173
  46.3 0.1 squeeze.44
  46.4 0.8 %squeeze.43 = f32[10,4,2048]{2,1,0:T(4,128)} reshape(f32[40,2048]{1,0:T(8,128)S(1)} %get-tuple-element.31) | data formatting | bytes 655360 | tf_op jit(solution)/shard_map/squeeze | solution.py:171
  47.2 0.1 squeeze.42
  47.3 0.8 %fusion.16 = f32[4,10,2048]{2,0,1:T(4,128)} fusion(f32[10,4,2048]{2,1,0:T(4,128)S(1)} %squeeze.44, f32[4,10,2048]{2,0,1:T(4,128)S(1)} %copy-done.3, f32[9,4,2048]{2,1,0:T(4,128)S(1)} %copy-done.8), kind=kLoop, calls=%fused_computation.37 | loop fusion | flops 245760 | bytes 1277952 | tf_op jit(solution)/shard_map/transpose | solution.py:175
  48.2 0.9 %add_bitcast_fusion.1 = f32[4,10,2048]{2,0,1:T(4,128)} fusion(f32[10,4,2048]{2,1,0:T(4,128)S(1)} %fusion.27, f32[10,4,2048]{2,1,0:T(4,128)S(1)} %squeeze.42, f32[4,10,2048]{2,0,1:T(4,128)S(1)} %copy-done.1), kind=kLoop, calls=%fused_computation.41 | loop fusion | flops 245760 | bytes 1310720 | tf_op jit(solution)/shard_map/transpose | solution.py:175
  49.1 0.9 %fusion.14 = f32[4,10,2048]{2,0,1:T(4,128)} fusion(f32[10,4,2048]{2,1,0:T(4,128)S(1)} %copy-done.7, f32[4,10,2048]{2,0,1:T(4,128)S(1)} %copy-done.5, f32[9,4,2048]{2,1,0:T(4,128)S(1)} %copy-done.9, f32[9,4,2048]{2,1,0:T(4,128)S(1)} %copy-done.12), kind=kLoop, calls=%fused_computation.33 | loop fusion | flops 491520 | bytes 1572864 | tf_op jit(solution)/shard_map/transpose | solution.py:175
  50.0 0.0 copy-done.6
  50.0 0.0 copy-done.11
  50.0 0.9 %add_bitcast_fusion = f32[4,10,2048]{2,0,1:T(4,128)} fusion(f32[10,4,2048]{2,1,0:T(4,128)S(1)} %copy-done.6, f32[9,4,2048]{2,1,0:T(4,128)S(1)} %copy-done.11, f32[9,4,2048]{2,1,0:T(4,128)S(1)} %copy-done.10, f32[4,10,2048]{2,0,1:T(4,128)S(1)} %copy-done), kind=kLoop, calls=%fused_computation.40 | loop fusion | flops 573440 | bytes 1572864 | tf_op jit(solution)/shard_map/transpose | solution.py:175
  50.9 1.4 %all-to-all-done = f32[8,2,10,256]{3,1,2,0:T(2,128)} async-done(((f32[8,2,10,256]{3,1,2,0:T(2,128)}), f32[8,2,10,256]{3,1,2,0:T(2,128)}, u32[]{:S(2)}, u32[]{:S(2)}) %all-to-all-start) | async-done | bytes 163872 | tf_op jit(solution)/shard_map/all_to_all | solution.py:69
  52.3 1.5 %fusion.28 = f32[2,10,256]{2,0,1:T(2,128)} fusion(f32[8,2,10,256]{3,1,2,0:T(2,128)} %all-to-all-done), kind=kLoop, calls=%fused_computation.93 | loop fusion | flops 35840 | bytes 184320 | tf_op jit(solution)/shard_map/add | solution.py:72
  (48 shorter events, 0.8 us)
Async XLA Ops:
  0.6 2.8 %copy-start.1 = (f32[4,10,2048]{2,0,1:T(4,128)S(1)}, f32[4,10,2048]{2,0,1:T(4,128)}, u32[]{:S(2)}) copy-start(f32[4,10,2048]{2,0,1:T(4,128)} %param.13) | copy-start | bytes 983044
  0.6 2.8 %copy-start = (f32[4,10,2048]{2,0,1:T(4,128)S(1)}, f32[4,10,2048]{2,0,1:T(4,128)}, u32[]{:S(2)}) copy-start(f32[4,10,2048]{2,0,1:T(4,128)} %param.14) | copy-start | bytes 983044
  0.7 2.8 %copy-start.2 = (f32[4,10,2048]{2,0,1:T(4,128)S(1)}, f32[4,10,2048]{2,0,1:T(4,128)}, u32[]{:S(2)}) copy-start(f32[4,10,2048]{2,0,1:T(4,128)} %param.22) | copy-start | bytes 983044
  0.7 2.8 %copy-start.4 = (f32[4,10,2048]{2,0,1:T(4,128)S(1)}, f32[4,10,2048]{2,0,1:T(4,128)}, u32[]{:S(2)}) copy-start(f32[4,10,2048]{2,0,1:T(4,128)} %param.23) | copy-start | bytes 983044
  4.5 0.9 %copy-start.13 = (f32[20,2048]{1,0:T(8,128)S(1)}, f32[20,2048]{1,0:T(8,128)}, u32[]{:S(2)}) copy-start(f32[20,2048]{1,0:T(8,128)} %reshape.104) | copy-start | bytes 491524
  7.8 0.7 %copy-start.15 = (f32[4,256]{1,0:T(4,128)S(1)}, f32[4,256]{1,0:T(4,128)}, u32[]{:S(2)}) copy-start(f32[4,256]{1,0:T(4,128)} %param.21) | copy-start | bytes 12292
  8.9 15.8 %copy-start.3 = (f32[4,10,2048]{2,0,1:T(4,128)S(1)}, f32[4,10,2048]{2,0,1:T(4,128)}, u32[]{:S(2)}) copy-start(f32[4,10,2048]{2,0,1:T(4,128)} %param.22) | copy-start | bytes 983044
  8.9 15.8 %copy-start.5 = (f32[4,10,2048]{2,0,1:T(4,128)S(1)}, f32[4,10,2048]{2,0,1:T(4,128)}, u32[]{:S(2)}) copy-start(f32[4,10,2048]{2,0,1:T(4,128)} %param.23) | copy-start | bytes 983044
  9.5 19.0 %collective-permute-start = (f32[4,10,4,256]{3,2,1,0:T(4,128)S(1)}, f32[4,10,4,256]{3,2,1,0:T(4,128)S(1)}, u32[]{:S(2)}, u32[]{:S(2)}) collective-permute-start(f32[4,10,4,256]{3,2,1,0:T(4,128)S(1)} %bitcast.127), channel_id=1, source_target_pairs={{0,32},{8,40},{16,48},{24,56},{32,0},{40,8},{48,16},{56,24},{64,96... | collective-permute-start | bytes 491528 | tf_op jit(solution)/shard_map/ppermute | solution.py:9
  14.1 14.4 %collective-permute-start.1 = (f32[4,10,4,256]{3,2,1,0:T(4,128)S(1)}, f32[4,10,4,256]{3,2,1,0:T(4,128)S(1)}, u32[]{:S(2)}, u32[]{:S(2)}) collective-permute-start(f32[4,10,4,256]{3,2,1,0:T(4,128)S(1)} %bitcast.128), channel_id=1, source_target_pairs={{0,8},{8,0},{16,24},{24,16},{32,40},{40,32},{48,56},{56,48},{64,72... | collective-permute-start | bytes 491528 | tf_op jit(solution)/shard_map/ppermute | solution.py:9
  16.1 12.9 %collective-permute-start.2 = (f32[4,10,4,256]{3,2,1,0:T(4,128)S(1)}, f32[4,10,4,256]{3,2,1,0:T(4,128)S(1)}, u32[]{:S(2)}, u32[]{:S(2)}) collective-permute-start(f32[4,10,4,256]{3,2,1,0:T(4,128)S(1)} %bitcast.129), channel_id=1, source_target_pairs={{0,64},{8,72},{16,80},{24,88},{32,96},{40,104},{48,112},{56,120},{... | collective-permute-start | bytes 491528 | tf_op jit(solution)/shard_map/ppermute | solution.py:9
  22.1 12.2 %collective-permute-start.3 = (f32[4,10,4,256]{3,2,1,0:T(4,128)S(1)}, f32[4,10,4,256]{3,2,1,0:T(4,128)S(1)}, u32[]{:S(2)}, u32[]{:S(2)}) collective-permute-start(f32[4,10,4,256]{3,2,1,0:T(4,128)S(1)} %bitcast.130), channel_id=1, source_target_pairs={{0,16},{8,24},{16,0},{24,8},{32,48},{40,56},{48,32},{56,40},{64,80... | collective-permute-start | bytes 491528 | tf_op jit(solution)/shard_map/ppermute | solution.py:9
  27.7 0.8 %copy-start.14 = (f32[4,2048]{1,0:T(4,128)S(1)}, f32[4,2048]{1,0:T(4,128)}, u32[]{:S(2)}) copy-start(f32[4,2048]{1,0:T(4,128)} %param.19) | copy-start | bytes 98308
  39.2 8.1 %copy-start.8 = (f32[9,4,2048]{2,1,0:T(4,128)S(1)}, f32[9,4,2048]{2,1,0:T(4,128)}, u32[]{:S(2)}) copy-start(f32[9,4,2048]{2,1,0:T(4,128)} %get-tuple-element.53) | copy-start | bytes 884740
  39.2 13.1 %all-to-all-start = ((f32[8,2,10,256]{3,1,2,0:T(2,128)}), f32[8,2,10,256]{3,1,2,0:T(2,128)}, u32[]{:S(2)}, u32[]{:S(2)}) async-start(f32[8,2,10,256]{3,1,2,0:T(2,128)} %copy.46), calls=%async_computation | async-start | bytes 327680 | tf_op jit(solution)/shard_map/all_to_all | solution.py:69
  47.2 1.8 %copy-start.7 = (f32[10,4,2048]{2,1,0:T(4,128)S(1)}, f32[10,4,2048]{2,1,0:T(4,128)}, u32[]{:S(2)}) copy-start(f32[10,4,2048]{2,1,0:T(4,128)} %squeeze.45) | copy-start | bytes 983044
  47.2 1.8 %copy-start.9 = (f32[9,4,2048]{2,1,0:T(4,128)S(1)}, f32[9,4,2048]{2,1,0:T(4,128)}, u32[]{:S(2)}) copy-start(f32[9,4,2048]{2,1,0:T(4,128)} %get-tuple-element.25) | copy-start | bytes 884740
  47.3 1.8 %copy-start.12 = (f32[9,4,2048]{2,1,0:T(4,128)S(1)}, f32[9,4,2048]{2,1,0:T(4,128)}, u32[]{:S(2)}) copy-start(f32[9,4,2048]{2,1,0:T(4,128)} %get-tuple-element.49) | copy-start | bytes 884740
  48.2 1.8 %copy-start.6 = (f32[10,4,2048]{2,1,0:T(4,128)S(1)}, f32[10,4,2048]{2,1,0:T(4,128)}, u32[]{:S(2)}) copy-start(f32[10,4,2048]{2,1,0:T(4,128)} %squeeze.43) | copy-start | bytes 983044
  48.2 1.8 %copy-start.10 = (f32[9,4,2048]{2,1,0:T(4,128)S(1)}, f32[9,4,2048]{2,1,0:T(4,128)}, u32[]{:S(2)}) copy-start(f32[9,4,2048]{2,1,0:T(4,128)} %get-tuple-element.48) | copy-start | bytes 884740
  48.2 1.8 %copy-start.11 = (f32[9,4,2048]{2,1,0:T(4,128)S(1)}, f32[9,4,2048]{2,1,0:T(4,128)}, u32[]{:S(2)}) copy-start(f32[9,4,2048]{2,1,0:T(4,128)} %get-tuple-element.50) | copy-start | bytes 884740

commit v13 on v5

--- a/solution.py
+++ b/solution.py
@@ -67,7 +67,10 @@
     width = value.shape[-1] // size
     parts = jnp.moveaxis(value.reshape(value.shape[:-1] + (size, width)), -2, 0)
     got = lax.all_to_all(parts, axis, 0, 0, tiled=True)
-    return jnp.sum(got, axis=0)
+    total = got[0]
+    for index in range(1, size):
+        total = total + got[index]
+    return total
 
 
 def body(
@@ -95,6 +98,9 @@
     g_p = 0.1 * c_p
     g_t = 0.1 * c_t
 
+    order = [2, 3, 0, 1] if rounds == 4 else list(range(rounds))
+    face_cols = jnp.concatenate([face_cols[i : i + 1] for i in order])
+    face_weight = jnp.concatenate([face_weight[i : i + 1] for i in order])
     cols = face_cols.reshape(rounds * face)
     select = (cols[:, None] == jnp.arange(width, dtype=jnp.int32)[None, :]).astype(
         jnp.bfloat16
@@ -118,7 +124,7 @@
 
     far = []
     for index in range(rounds):
-        far.append(from_partner(sending[..., index, :], "space", 1 << index))
+        far.append(from_partner(sending[..., index, :], "space", 1 << order[index]))
     far = jnp.stack(far, axis=-2)
 
     diff = far[:2] - own
@@ -147,12 +153,12 @@
     ).reshape(2, layers, width)
     grads = (vert_grads + lat_grads) * jnp.stack([cond, therm])
     owned = sum_scatter(grads, "member")
-
     lat = exact_select(
         jnp.concatenate([update, adj_lat]).reshape(4 * n_field, rounds * face),
         select,
         0,
     ).reshape(4, layers, members, width)
+
 
     p_rate = spread0(flow)
     p_rate = p_rate.at[0].add(recharge)

time: 56.5 us -> 52.6 us (0.931)
  the two profiles are of different devices: /device:TPU:1 before, /device:TPU:138 now
where the time goes in v13:
time: 52.6 us; the launch traced here: 52.1 us
  starting transfers between devices  21.3 us (40%)
  other arithmetic  12.3 us (23%)
  local copies, waits for them, and re-layouts  6.65 us (13%)
  matrix products  5.83 us (11%)
  waiting for transfers between devices  4.73 us (9%)
  between operations  1.21 us (2%)
    ppermute x4, starting transfers between devices, from_partner(): return lax.ppermute(value, axis, pairs)  14.7 us
    all_to_all x1, starting transfers between devices, sum_scatter(): got = lax.all_to_all(parts, axis, 0, 0, tiled=True)  6.65 us
    dot_general x3, matrix products, exact_select(): lax.dot_general(split2(rows), select, (((1,), (contract,)), ((), ())), pr...  5.83 us
    ppermute x4, waiting for transfers between devices, from_partner(): return lax.ppermute(value, axis, pairs)  4.73 us
    transpose x4, other arithmetic, body(): return tuple((o.transpose(1, 0, 2) for o in outs)) + (owned,)  3.55 us
    unnamed x48, local copies, waits for them, and re-layouts  2.94 us
    add x1, other arithmetic, sum_scatter(): total = total + got[index]  1.49 us
    mul x1, other arithmetic, body(): therm = jnp.exp(log_therm) * (1.0 + blocked)  1.24 us
  transfers between devices with their start and end apart: 5, of which 1 were waited for; matrix products, arithmetic and copies ran while one was open for 20% of the time, Pallas kernels for 0%

profile of v13, /device:TPU:138, one launch (start us, length us, event | category | flops | bytes accessed | tf_op | source)
XLA Modules:
  0.0 52.1 jit_solution(17300645635517294003)
XLA Ops:
  0.7 0.0 copy-start.2
  0.7 0.0 copy-start.4
  0.7 1.2 %add_multiply_fusion.3 = (f32[10,2048]{1,0:T(8,128)S(1)}, f32[10,2048]{1,0:T(8,128)S(1)}) fusion(f32[10,2048]{1,0:T(8,128)} %param.16, f32[10,2048]{1,0:T(8,128)} %param.17, s32[10,2048]{1,0:T(8,128)} %param.18, f32[10,2048]{1,0:T(8,128)} %param.15), kind=kLoop, calls=%fused_computation.83 | loop fusion | flops 122880 | bytes 491520 | tf_op jit(solution)/shard_map/mul | solution.py:97
  2.0 0.7 %reshape.104 = f32[20,2048]{1,0:T(8,128)} reshape(f32[2,10,2048]{2,1,0:T(8,128)S(1)} %pad_maximum_fusion.3) | data formatting | bytes 327680 | tf_op jit(solution)/shard_map/reshape | solution.py:113
  2.7 0.0 copy-done
  2.7 0.6 %pad_maximum_fusion = f32[4,10,4,2048]{3,2,1,0:T(4,128)S(1)} fusion(f32[1,10,4,2048]{3,2,1,0:T(4,128)S(1)} %bitcast.108, f32[1,10,4,2048]{3,2,1,0:T(4,128)S(1)} %bitcast.107, f32[1,10,4,2048]{3,2,1,0:T(4,128)S(1)} %bitcast.97, f32[1,10,4,2048]{3,2,1,0:T(4,128)S(1)} %bitcast.100), kind=kLoop, calls=%fused_computation.14 | loop fusion | flops 983040 | bytes 2621440 | tf_op jit(solution)/shard_map/stack | solution.py:112
  3.3 0.5 reshape.103
  3.7 0.0 copy-start.12
  3.7 0.1 constant_dynamic-update-slice_fusion.1
  3.8 0.8 %copy-done.12 = f32[20,2048]{1,0:T(8,128)S(1)} copy-done((f32[20,2048]{1,0:T(8,128)S(1)}, f32[20,2048]{1,0:T(8,128)}, u32[]{:S(2)}) %copy-start.12) | copy-done | bytes 163864
  4.7 0.0 copy-start.14
  4.7 0.2 reduce-precision_convert_fusion
  4.9 0.5 copy-done.14
  5.4 2.2 %fusion.2 = f32[360,1024]{1,0:T(8,128)S(1)} fusion(s32[1024]{0:T(1024)S(1)} %bitcast.132, bf16[180,2048]{1,0:T(8,128)(2,1)S(1)} %get-tuple-element.30, bf16[180,2048]{1,0:T(8,128)(2,1)S(1)} %get-tuple-element.29), kind=kOutput, calls=%fused_computation.3 | convolution fusion | flops 1514995712 | bytes 2953216 | tf_op jit(solution)/shard_map/dot_general | solution.py:39
  7.6 0.0 copy-start.15
  7.6 0.1 slice_add_fusion.1
  7.7 0.1 fusion.42
  7.8 0.4 copy-done.15
  8.3 0.2 slice.189
  8.4 0.2 slice.187
  8.6 0.0 copy-start.3
  8.7 0.0 copy-start.5
  8.7 0.1 broadcast_multiply_fusion
  8.7 0.5 fusion.21
  9.3 4.5 %collective-permute-start = (f32[4,10,4,256]{3,2,1,0:T(4,128)S(1)}, f32[4,10,4,256]{3,2,1,0:T(4,128)S(1)}, u32[]{:S(2)}, u32[]{:S(2)}) collective-permute-start(f32[4,10,4,256]{3,2,1,0:T(4,128)S(1)} %bitcast.127), channel_id=1, source_target_pairs={{0,32},{8,40},{16,48},{24,56},{32,0},{40,8},{48,16},{56,24},{64,96... | collective-permute-start | bytes 491528 | tf_op jit(solution)/shard_map/ppermute | solution.py:9
  13.8 5.0 %collective-permute-start.1 = (f32[4,10,4,256]{3,2,1,0:T(4,128)S(1)}, f32[4,10,4,256]{3,2,1,0:T(4,128)S(1)}, u32[]{:S(2)}, u32[]{:S(2)}) collective-permute-start(f32[4,10,4,256]{3,2,1,0:T(4,128)S(1)} %bitcast.128), channel_id=1, source_target_pairs={{0,64},{8,72},{16,80},{24,88},{32,96},{40,104},{48,112},{56,120},{... | collective-permute-start | bytes 491528 | tf_op jit(solution)/shard_map/ppermute | solution.py:9
  18.9 1.9 %collective-permute-start.2 = (f32[4,10,4,256]{3,2,1,0:T(4,128)S(1)}, f32[4,10,4,256]{3,2,1,0:T(4,128)S(1)}, u32[]{:S(2)}, u32[]{:S(2)}) collective-permute-start(f32[4,10,4,256]{3,2,1,0:T(4,128)S(1)} %bitcast.129), channel_id=1, source_target_pairs={{0,8},{8,0},{16,24},{24,16},{32,40},{40,32},{48,56},{56,48},{64,72... | collective-permute-start | bytes 491528 | tf_op jit(solution)/shard_map/ppermute | solution.py:9
  20.9 3.3 %collective-permute-start.3 = (f32[4,10,4,256]{3,2,1,0:T(4,128)S(1)}, f32[4,10,4,256]{3,2,1,0:T(4,128)S(1)}, u32[]{:S(2)}, u32[]{:S(2)}) collective-permute-start(f32[4,10,4,256]{3,2,1,0:T(4,128)S(1)} %bitcast.130), channel_id=1, source_target_pairs={{0,16},{8,24},{16,0},{24,8},{32,48},{40,56},{48,32},{56,40},{64,80... | collective-permute-start | bytes 491528 | tf_op jit(solution)/shard_map/ppermute | solution.py:9
  24.2 0.2 bitcast_multiply_fusion
  24.5 0.5 multiply_reduce_fusion.2
  24.9 1.1 %multiply_multiply_fusion = (f32[9,4,2048]{2,1,0:T(4,128)}, f32[9,4,2048]{2,1,0:T(4,128)S(1)}, f32[9,4,2048]{2,1,0:T(4,128)}) fusion(f32[9,4,2048]{2,1,0:T(4,128)S(1)} %get-tuple-element.24, f32[10,4,2048]{2,1,0:T(4,128)S(1)} %bitcast.102, f32[9,2048]{1,0:T(8,128)S(1)} %get-tuple-element.65, f32[9,4,2048]{2,1,0:T(4,128)S(1)} %get-tuple-element.23), kind=kLoop, calls=%fused_computation.56 | loop fusion | flops 368640 | bytes 2138112 | tf_op jit(solution)/shard_map/mul | solution.py:169
  26.0 0.1 pad_subtract_fusion
  26.1 1.2 %multiply_reduce_fusion.1 = (f32[9,2048]{1,0:T(8,128)S(1)}, f32[9,4,2048]{2,1,0:T(4,128)}, f32[9,4,2048]{2,1,0:T(4,128)}, f32[9,4,2048]{2,1,0:T(4,128)}) fusion(f32[9,4,2048]{2,1,0:T(4,128)S(1)} %get-tuple-element.24, f32[10,4,2048]{2,1,0:T(4,128)S(1)} %bitcast.99, f32[9,2048]{1,0:T(8,128)S(1)} %get-tuple-element.64, f32[9,4,2048]{2,1,0:T(4,128)S(1)} %get-tuple-element.26), kind=kLoop, calls=%fused_computation.51 | loop fusion | flops 571392 | bytes 2211840 | tf_op jit(solution)/shard_map/reduce_sum | solution.py:148
  27.6 0.5 copy-done.13
  28.0 0.0 collective-permute-done
  28.1 4.7 %collective-permute-done.1 = f32[4,10,4,256]{3,2,1,0:T(4,128)S(1)} collective-permute-done((f32[4,10,4,256]{3,2,1,0:T(4,128)S(1)}, f32[4,10,4,256]{3,2,1,0:T(4,128)S(1)}, u32[]{:S(2)}, u32[]{:S(2)}) %collective-permute-start.1) | collective-permute-done | bytes 163872 | tf_op jit(solution)/shard_map/ppermute | solution.py:9
  32.8 0.0 collective-permute-done.2
  32.8 0.0 collective-permute-done.3
  32.8 0.1 pad_maximum_fusion.1
  32.9 0.1 fusion.43
  33.1 0.7 %multiply_reduce_fusion = (f32[2,10,4,256]{3,2,1,0:T(4,128)S(1)}, f32[2,10,4,4,256]{4,3,2,1,0:T(4,128)S(1)}, f32[2,10,4,4,256]{4,3,2,1,0:T(4,128)S(1)}) fusion(f32[2,10,4,4,256]{4,3,2,1,0:T(4,128)S(1)} %slice.189, f32[2,10,4,4,256]{4,3,2,1,0:T(4,128)S(1)} %slice.187, f32[2,10,4,4,256]{4,2,1,0,3:T(4,128)S(1)} %get-tuple-element.41, ...), kind=kLoop, calls=%fused_computation.41 | loop fusion | flops 552960 | bytes 2211840 | tf_op jit(solution)/shard_map/reduce_sum | solution.py:133
  33.8 1.8 %fusion = f32[40,2048]{1,0:T(8,128)S(1)} fusion(s32[1024]{0:T(1024)S(1)} %bitcast.133, bf16[20,1024]{1,0:T(8,128)(2,1)S(1)} %get-tuple-element.55, bf16[20,1024]{1,0:T(8,128)(2,1)S(1)} %get-tuple-element.54), kind=kOutput, calls=%fused_computation.1 | convolution fusion | flops 170033152 | bytes 413696 | tf_op jit(solution)/shard_map/dot_general | solution.py:39
  35.6 0.1 copy.57
  35.8 0.8 %copy.46 = f32[8,2,10,256]{3,1,2,0:T(2,128)} copy(f32[8,2,10,256]{3,0,2,1:T(8,128)S(1)} %fusion.24) | data formatting | bytes 327680 | tf_op jit(solution)/shard_map/transpose | solution.py:68
  36.6 6.6 %all-to-all-start = ((f32[8,2,10,256]{3,1,2,0:T(2,128)}), f32[8,2,10,256]{3,1,2,0:T(2,128)}, u32[]{:S(2)}, u32[]{:S(2)}) async-start(f32[8,2,10,256]{3,1,2,0:T(2,128)} %copy.46), calls=%async_computation | async-start | bytes 327680 | tf_op jit(solution)/shard_map/all_to_all | solution.py:69
  43.2 0.2 pad_maximum_fusion.2
  43.4 0.1 copy.52
  43.6 0.1 reduce-precision_convert_fusion.1
  43.7 1.9 %fusion.1 = f32[320,2048]{1,0:T(8,128)S(1)} fusion(s32[1024]{0:T(1024)S(1)} %bitcast.134, bf16[160,1024]{1,0:T(8,128)(2,1)S(1)} %get-tuple-element.40, bf16[160,1024]{1,0:T(8,128)(2,1)S(1)} %get-tuple-element.39), kind=kOutput, calls=%fused_computation.2 | convolution fusion | flops 1345585152 | bytes 3280896 | tf_op jit(solution)/shard_map/dot_general | solution.py:39
  45.6 0.1 slice_add_fusion
  45.7 0.1 fusion.41
  45.8 0.0 copy-start.7
  45.8 0.8 %squeeze.45 = f32[10,4,2048]{2,1,0:T(4,128)} reshape(f32[40,2048]{1,0:T(8,128)S(1)} %get-tuple-element.31) | data formatting | bytes 655360 | tf_op jit(solution)/shard_map/squeeze | solution.py:169
  46.6 0.1 squeeze.44
  46.7 0.1 squeeze.43
  46.8 0.0 copy-start.8
  46.9 0.1 squeeze.42
  47.0 0.0 copy-start.6
  47.0 0.8 %fusion.18 = f32[4,10,2048]{2,0,1:T(4,128)} fusion(f32[10,4,2048]{2,1,0:T(4,128)S(1)} %squeeze.44, f32[4,10,2048]{2,0,1:T(4,128)S(1)} %copy-done.3, f32[9,4,2048]{2,1,0:T(4,128)S(1)} %copy-done.7), kind=kLoop, calls=%fused_computation.38 | loop fusion | flops 245760 | bytes 1277952 | tf_op jit(solution)/shard_map/transpose | solution.py:171
  47.8 0.9 %add_bitcast_fusion.1 = f32[4,10,2048]{2,0,1:T(4,128)} fusion(f32[10,4,2048]{2,1,0:T(4,128)S(1)} %fusion.33, f32[10,4,2048]{2,1,0:T(4,128)S(1)} %squeeze.42, f32[4,10,2048]{2,0,1:T(4,128)S(1)} %copy-done.1), kind=kLoop, calls=%fused_computation.43 | loop fusion | flops 245760 | bytes 1310720 | tf_op jit(solution)/shard_map/transpose | solution.py:171
  48.7 0.9 %fusion.16 = f32[4,10,2048]{2,0,1:T(4,128)} fusion(f32[10,4,2048]{2,1,0:T(4,128)S(1)} %copy-done.6, f32[4,10,2048]{2,0,1:T(4,128)S(1)} %copy-done.5, f32[9,4,2048]{2,1,0:T(4,128)S(1)} %copy-done.8, f32[9,4,2048]{2,1,0:T(4,128)S(1)} %copy-done.11), kind=kLoop, calls=%fused_computation.34 | loop fusion | flops 491520 | bytes 1572864 | tf_op jit(solution)/shard_map/transpose | solution.py:171
  49.6 0.9 %add_bitcast_fusion = f32[4,10,2048]{2,0,1:T(4,128)} fusion(f32[10,4,2048]{2,1,0:T(4,128)S(1)} %squeeze.43, f32[9,4,2048]{2,1,0:T(4,128)S(1)} %copy-done.10, f32[9,4,2048]{2,1,0:T(4,128)S(1)} %copy-done.9, f32[4,10,2048]{2,0,1:T(4,128)S(1)} %copy-done), kind=kLoop, calls=%fused_computation.42 | loop fusion | flops 573440 | bytes 1572864 | tf_op jit(solution)/shard_map/transpose | solution.py:171
  50.6 0.0 all-to-all-done
  50.6 1.5 %fusion.34 = f32[2,10,256]{2,0,1:T(2,128)} fusion(f32[8,2,10,256]{3,1,2,0:T(2,128)} %all-to-all-done), kind=kLoop, calls=%fused_computation.100 | loop fusion | flops 35840 | bytes 184320 | tf_op jit(solution)/shard_map/add | solution.py:72
  (49 shorter events, 0.8 us)
Async XLA Ops:
  0.6 2.0 %copy-start.1 = (f32[4,10,2048]{2,0,1:T(4,128)S(1)}, f32[4,10,2048]{2,0,1:T(4,128)}, u32[]{:S(2)}) copy-start(f32[4,10,2048]{2,0,1:T(4,128)} %param.13) | copy-start | bytes 983044
  0.6 2.0 %copy-start = (f32[4,10,2048]{2,0,1:T(4,128)S(1)}, f32[4,10,2048]{2,0,1:T(4,128)}, u32[]{:S(2)}) copy-start(f32[4,10,2048]{2,0,1:T(4,128)} %param.14) | copy-start | bytes 983044
  0.7 2.0 %copy-start.2 = (f32[4,10,2048]{2,0,1:T(4,128)S(1)}, f32[4,10,2048]{2,0,1:T(4,128)}, u32[]{:S(2)}) copy-start(f32[4,10,2048]{2,0,1:T(4,128)} %param.22) | copy-start | bytes 983044
  0.7 2.0 %copy-start.4 = (f32[4,10,2048]{2,0,1:T(4,128)S(1)}, f32[4,10,2048]{2,0,1:T(4,128)}, u32[]{:S(2)}) copy-start(f32[4,10,2048]{2,0,1:T(4,128)} %param.23) | copy-start | bytes 983044
  3.7 0.9 %copy-start.12 = (f32[20,2048]{1,0:T(8,128)S(1)}, f32[20,2048]{1,0:T(8,128)}, u32[]{:S(2)}) copy-start(f32[20,2048]{1,0:T(8,128)} %reshape.104) | copy-start | bytes 491524
  4.7 0.7 %copy-start.14 = (s32[4,256]{1,0:T(4,128)S(1)}, s32[4,256]{1,0:T(4,128)}, u32[]{:S(2)}) copy-start(s32[4,256]{1,0:T(4,128)} %param.20) | copy-start | bytes 12292
  7.6 0.7 %copy-start.15 = (f32[4,256]{1,0:T(4,128)S(1)}, f32[4,256]{1,0:T(4,128)}, u32[]{:S(2)}) copy-start(f32[4,256]{1,0:T(4,128)} %param.21) | copy-start | bytes 12292
  8.6 15.5 %copy-start.3 = (f32[4,10,2048]{2,0,1:T(4,128)S(1)}, f32[4,10,2048]{2,0,1:T(4,128)}, u32[]{:S(2)}) copy-start(f32[4,10,2048]{2,0,1:T(4,128)} %param.22) | copy-start | bytes 983044
  8.7 15.5 %copy-start.5 = (f32[4,10,2048]{2,0,1:T(4,128)S(1)}, f32[4,10,2048]{2,0,1:T(4,128)}, u32[]{:S(2)}) copy-start(f32[4,10,2048]{2,0,1:T(4,128)} %param.23) | copy-start | bytes 983044
  9.3 18.8 %collective-permute-start = (f32[4,10,4,256]{3,2,1,0:T(4,128)S(1)}, f32[4,10,4,256]{3,2,1,0:T(4,128)S(1)}, u32[]{:S(2)}, u32[]{:S(2)}) collective-permute-start(f32[4,10,4,256]{3,2,1,0:T(4,128)S(1)} %bitcast.127), channel_id=1, source_target_pairs={{0,32},{8,40},{16,48},{24,56},{32,0},{40,8},{48,16},{56,24},{64,96... | collective-permute-start | bytes 491528 | tf_op jit(solution)/shard_map/ppermute | solution.py:9
  13.8 18.9 %collective-permute-start.1 = (f32[4,10,4,256]{3,2,1,0:T(4,128)S(1)}, f32[4,10,4,256]{3,2,1,0:T(4,128)S(1)}, u32[]{:S(2)}, u32[]{:S(2)}) collective-permute-start(f32[4,10,4,256]{3,2,1,0:T(4,128)S(1)} %bitcast.128), channel_id=1, source_target_pairs={{0,64},{8,72},{16,80},{24,88},{32,96},{40,104},{48,112},{56,120},{... | collective-permute-start | bytes 491528 | tf_op jit(solution)/shard_map/ppermute | solution.py:9
  18.9 13.8 %collective-permute-start.2 = (f32[4,10,4,256]{3,2,1,0:T(4,128)S(1)}, f32[4,10,4,256]{3,2,1,0:T(4,128)S(1)}, u32[]{:S(2)}, u32[]{:S(2)}) collective-permute-start(f32[4,10,4,256]{3,2,1,0:T(4,128)S(1)} %bitcast.129), channel_id=1, source_target_pairs={{0,8},{8,0},{16,24},{24,16},{32,40},{40,32},{48,56},{56,48},{64,72... | collective-permute-start | bytes 491528 | tf_op jit(solution)/shard_map/ppermute | solution.py:9
  20.9 11.9 %collective-permute-start.3 = (f32[4,10,4,256]{3,2,1,0:T(4,128)S(1)}, f32[4,10,4,256]{3,2,1,0:T(4,128)S(1)}, u32[]{:S(2)}, u32[]{:S(2)}) collective-permute-start(f32[4,10,4,256]{3,2,1,0:T(4,128)S(1)} %bitcast.130), channel_id=1, source_target_pairs={{0,16},{8,24},{16,0},{24,8},{32,48},{40,56},{48,32},{56,40},{64,80... | collective-permute-start | bytes 491528 | tf_op jit(solution)/shard_map/ppermute | solution.py:9
  27.3 0.8 %copy-start.13 = (f32[4,2048]{1,0:T(4,128)S(1)}, f32[4,2048]{1,0:T(4,128)}, u32[]{:S(2)}) copy-start(f32[4,2048]{1,0:T(4,128)} %param.19) | copy-start | bytes 98308
  36.6 14.0 %all-to-all-start = ((f32[8,2,10,256]{3,1,2,0:T(2,128)}), f32[8,2,10,256]{3,1,2,0:T(2,128)}, u32[]{:S(2)}, u32[]{:S(2)}) async-start(f32[8,2,10,256]{3,1,2,0:T(2,128)} %copy.46), calls=%async_computation | async-start | bytes 327680 | tf_op jit(solution)/shard_map/all_to_all | solution.py:69
  45.8 1.2 %copy-start.7 = (f32[9,4,2048]{2,1,0:T(4,128)S(1)}, f32[9,4,2048]{2,1,0:T(4,128)}, u32[]{:S(2)}) copy-start(f32[9,4,2048]{2,1,0:T(4,128)} %get-tuple-element.53) | copy-start | bytes 884740
  46.8 1.9 %copy-start.8 = (f32[9,4,2048]{2,1,0:T(4,128)S(1)}, f32[9,4,2048]{2,1,0:T(4,128)}, u32[]{:S(2)}) copy-start(f32[9,4,2048]{2,1,0:T(4,128)} %get-tuple-element.25) | copy-start | bytes 884740
  47.0 1.8 %copy-start.6 = (f32[10,4,2048]{2,1,0:T(4,128)S(1)}, f32[10,4,2048]{2,1,0:T(4,128)}, u32[]{:S(2)}) copy-start(f32[10,4,2048]{2,1,0:T(4,128)} %squeeze.45) | copy-start | bytes 983044
  47.0 1.7 %copy-start.11 = (f32[9,4,2048]{2,1,0:T(4,128)S(1)}, f32[9,4,2048]{2,1,0:T(4,128)}, u32[]{:S(2)}) copy-start(f32[9,4,2048]{2,1,0:T(4,128)} %get-tuple-element.49) | copy-start | bytes 884740
  47.8 1.8 %copy-start.9 = (f32[9,4,2048]{2,1,0:T(4,128)S(1)}, f32[9,4,2048]{2,1,0:T(4,128)}, u32[]{:S(2)}) copy-start(f32[9,4,2048]{2,1,0:T(4,128)} %get-tuple-element.48) | copy-start | bytes 884740
  47.8 1.8 %copy-start.10 = (f32[9,4,2048]{2,1,0:T(4,128)S(1)}, f32[9,4,2048]{2,1,0:T(4,128)}, u32[]{:S(2)}) copy-start(f32[9,4,2048]{2,1,0:T(4,128)} %get-tuple-element.50) | copy-start | bytes 884740

commit v14 on v13

--- a/solution.py
+++ b/solution.py
@@ -153,11 +153,13 @@
     ).reshape(2, layers, width)
     grads = (vert_grads + lat_grads) * jnp.stack([cond, therm])
     owned = sum_scatter(grads, "member")
-    lat = exact_select(
-        jnp.concatenate([update, adj_lat]).reshape(4 * n_field, rounds * face),
+    lat_parts = lax.dot_general(
+        split2(jnp.concatenate([update, adj_lat]).reshape(4 * n_field, rounds * face)),
         select,
-        0,
-    ).reshape(4, layers, members, width)
+        (((1,), (0,)), ((), ())),
+        preferred_element_type=jnp.float32,
+    ).reshape(2, 4, layers, members, width)
+    lat = [lat_parts[0, i] + lat_parts[1, i] for i in range(4)]
 
 
     p_rate = spread0(flow)

time: 52.6 us -> 55.7 us (1.059)
  local copies, waits for them, and re-layouts: 6.65 us -> 8.19 us
  matrix products: 5.83 us -> 7.31 us
    dot_general x0 -> x1, matrix products: none -> 3.36 us  [body(): lax.dot_general(split2(jnp.concatenate([update, adj_lat]).reshape(4 * n_f...]
    reshape x0 -> x1, local copies, waits for them, and re-layouts: none -> 2.78 us  [body(): lat_parts = lax.dot_general(split2(jnp.concatenate([update, adj_lat]).res...]
    dot_general x3 -> x2, matrix products: 5.83 us -> 3.94 us  [exact_select(): lax.dot_general(split2(rows), select, (((1,), (contract,)), ((), ())), pr...]
    transpose x4 -> x2, other arithmetic: 3.55 us -> 4.79 us  [body(): return tuple((o.transpose(1, 0, 2) for o in outs)) + (owned,)]
    squeeze x4 -> x0, local copies, waits for them, and re-layouts: 1.1 us -> none  [the longest x1 0.82 us: body(): lat[3]]
    add x1, other arithmetic: 1.49 us -> 0.64 us  [sum_scatter(): total = total + got[index]]
    unnamed x48 -> x40, local copies, waits for them, and re-layouts: 2.94 us -> 2.9 us
  transfers between devices with their start and end apart: 5 -> 5, of which waited for: 1 -> 1; matrix products, arithmetic and copies ran while one was open for 20% -> 27% of each run, Pallas kernels for 0% -> 0%
where the time goes in v14:
time: 55.7 us; the launch traced here: 55.1 us
  starting transfers between devices  21.4 us (38%)
  other arithmetic  12.3 us (22%)
  local copies, waits for them, and re-layouts  8.19 us (15%)
  matrix products  7.31 us (13%)
  waiting for transfers between devices  4.83 us (9%)
  between operations  1.15 us (2%)
    ppermute x4, starting transfers between devices, from_partner(): return lax.ppermute(value, axis, pairs)  14.7 us
    all_to_all x1, starting transfers between devices, sum_scatter(): got = lax.all_to_all(parts, axis, 0, 0, tiled=True)  6.65 us
    ppermute x4, waiting for transfers between devices, from_partner(): return lax.ppermute(value, axis, pairs)  4.83 us
    transpose x2, other arithmetic, body(): return tuple((o.transpose(1, 0, 2) for o in outs)) + (owned,)  4.79 us
    dot_general x2, matrix products, exact_select(): lax.dot_general(split2(rows), select, (((1,), (contract,)), ((), ())), pr...  3.94 us
    dot_general x1, matrix products, body(): lax.dot_general(split2(jnp.concatenate([update, adj_lat]).reshape(4 * n_f...  3.36 us
    unnamed x40, local copies, waits for them, and re-layouts  2.9 us
    reshape x1, local copies, waits for them, and re-layouts, body(): lat_parts = lax.dot_general(split2(jnp.concatenate([update, adj_lat]).res...  2.78 us
  transfers between devices with their start and end apart: 5, of which 1 were waited for; matrix products, arithmetic and copies ran while one was open for 27% of the time, Pallas kernels for 0%

profile of v14, /device:TPU:138, one launch (start us, length us, event | category | flops | bytes accessed | tf_op | source)
XLA Modules:
  0.0 55.1 jit_solution(12395849969937037785)
XLA Ops:
  0.6 0.0 copy-start.1
  0.6 0.0 copy-start
  0.7 0.0 copy-start.4
  0.7 0.0 copy-start.2
  0.7 1.2 %add_multiply_fusion.3 = (f32[10,2048]{1,0:T(8,128)S(1)}, f32[10,2048]{1,0:T(8,128)S(1)}) fusion(f32[10,2048]{1,0:T(8,128)} %param.16, f32[10,2048]{1,0:T(8,128)} %param.17, s32[10,2048]{1,0:T(8,128)} %param.18, f32[10,2048]{1,0:T(8,128)} %param.15), kind=kLoop, calls=%fused_computation.96 | loop fusion | flops 122880 | bytes 491520 | tf_op jit(solution)/shard_map/mul | solution.py:97
  2.0 0.7 %reshape.102 = f32[20,2048]{1,0:T(8,128)} reshape(f32[2,10,2048]{2,1,0:T(8,128)S(1)} %pad_maximum_fusion.3) | data formatting | bytes 327680 | tf_op jit(solution)/shard_map/reshape | solution.py:113
  2.7 0.0 copy-done.1
  2.7 0.0 copy-done
  2.7 0.0 copy-done.4
  2.7 0.0 copy-done.2
  2.7 0.4 pad_maximum_fusion
  3.1 0.5 reshape.101
  3.6 0.0 copy-start.8
  3.6 0.1 constant_dynamic-update-slice_fusion.1
  3.7 0.8 %copy-done.8 = f32[20,2048]{1,0:T(8,128)S(1)} copy-done((f32[20,2048]{1,0:T(8,128)S(1)}, f32[20,2048]{1,0:T(8,128)}, u32[]{:S(2)}) %copy-start.8) | copy-done | bytes 163864
  4.5 0.0 copy-start.10
  4.5 0.2 reduce-precision_convert_fusion
  4.8 0.4 copy-done.10
  5.2 2.2 %fusion.2 = f32[360,1024]{1,0:T(8,128)S(1)} fusion(s32[1024]{0:T(1024)S(1)} %bitcast.160, bf16[180,2048]{1,0:T(8,128)(2,1)S(1)} %get-tuple-element.33, bf16[180,2048]{1,0:T(8,128)(2,1)S(1)} %get-tuple-element.32), kind=kOutput, calls=%fused_computation.3 | convolution fusion | flops 1514995712 | bytes 2953216 | tf_op jit(solution)/shard_map/dot_general | solution.py:39
  7.4 0.0 copy-start.11
  7.4 0.1 slice_add_fusion
  7.7 0.4 copy-done.11
  8.1 0.2 slice.191
  8.3 0.2 slice.189
  8.5 0.0 copy-start.3
  8.5 0.0 copy-start.5
  8.5 0.1 broadcast_multiply_fusion
  8.6 0.5 fusion.33
  9.1 4.5 %collective-permute-start = (f32[4,10,4,256]{3,2,1,0:T(4,128)S(1)}, f32[4,10,4,256]{3,2,1,0:T(4,128)S(1)}, u32[]{:S(2)}, u32[]{:S(2)}) collective-permute-start(f32[4,10,4,256]{3,2,1,0:T(4,128)S(1)} %bitcast.155), channel_id=1, source_target_pairs={{0,32},{8,40},{16,48},{24,56},{32,0},{40,8},{48,16},{56,24},{64,96... | collective-permute-start | bytes 491528 | tf_op jit(solution)/shard_map/ppermute | solution.py:9
  13.7 5.0 %collective-permute-start.1 = (f32[4,10,4,256]{3,2,1,0:T(4,128)S(1)}, f32[4,10,4,256]{3,2,1,0:T(4,128)S(1)}, u32[]{:S(2)}, u32[]{:S(2)}) collective-permute-start(f32[4,10,4,256]{3,2,1,0:T(4,128)S(1)} %bitcast.156), channel_id=1, source_target_pairs={{0,64},{8,72},{16,80},{24,88},{32,96},{40,104},{48,112},{56,120},{... | collective-permute-start | bytes 491528 | tf_op jit(solution)/shard_map/ppermute | solution.py:9
  18.8 1.9 %collective-permute-start.2 = (f32[4,10,4,256]{3,2,1,0:T(4,128)S(1)}, f32[4,10,4,256]{3,2,1,0:T(4,128)S(1)}, u32[]{:S(2)}, u32[]{:S(2)}) collective-permute-start(f32[4,10,4,256]{3,2,1,0:T(4,128)S(1)} %bitcast.157), channel_id=1, source_target_pairs={{0,8},{8,0},{16,24},{24,16},{32,40},{40,32},{48,56},{56,48},{64,72... | collective-permute-start | bytes 491528 | tf_op jit(solution)/shard_map/ppermute | solution.py:9
  20.8 3.3 %collective-permute-start.3 = (f32[4,10,4,256]{3,2,1,0:T(4,128)S(1)}, f32[4,10,4,256]{3,2,1,0:T(4,128)S(1)}, u32[]{:S(2)}, u32[]{:S(2)}) collective-permute-start(f32[4,10,4,256]{3,2,1,0:T(4,128)S(1)} %bitcast.158), channel_id=1, source_target_pairs={{0,16},{8,24},{16,0},{24,8},{32,48},{40,56},{48,32},{56,40},{64,80... | collective-permute-start | bytes 491528 | tf_op jit(solution)/shard_map/ppermute | solution.py:9
  24.0 0.0 copy-done.3
  24.0 0.0 copy-done.5
  24.1 0.2 bitcast_multiply_fusion
  24.3 0.4 multiply_reduce_fusion.2
  24.7 1.1 %multiply_multiply_fusion = (f32[9,4,2048]{2,1,0:T(4,128)}, f32[9,4,2048]{2,1,0:T(4,128)S(1)}, f32[9,4,2048]{2,1,0:T(4,128)}) fusion(f32[9,4,2048]{2,1,0:T(4,128)S(1)} %get-tuple-element.24, f32[10,4,2048]{2,1,0:T(4,128)S(1)} %bitcast.130, f32[9,2048]{1,0:T(8,128)S(1)} %get-tuple-element.64, f32[9,4,2048]{2,1,0:T(4,128)S(1)} %get-tuple-element.23), kind=kLoop, calls=%fused_computation.69 | loop fusion | flops 368640 | bytes 2138112 | tf_op jit(solution)/shard_map/mul | solution.py:171
  25.8 0.1 pad_subtract_fusion
  25.9 1.1 %multiply_reduce_fusion.1 = (f32[9,2048]{1,0:T(8,128)S(1)}, f32[9,4,2048]{2,1,0:T(4,128)}, f32[9,4,2048]{2,1,0:T(4,128)}, f32[9,4,2048]{2,1,0:T(4,128)}) fusion(f32[9,4,2048]{2,1,0:T(4,128)S(1)} %get-tuple-element.24, f32[10,4,2048]{2,1,0:T(4,128)S(1)} %bitcast.127, f32[9,2048]{1,0:T(8,128)S(1)} %get-tuple-element.63, f32[9,4,2048]{2,1,0:T(4,128)S(1)} %get-tuple-element.26), kind=kLoop, calls=%fused_computation.64 | loop fusion | flops 571392 | bytes 2211840 | tf_op jit(solution)/shard_map/reduce_sum | solution.py:148
  27.3 0.5 copy-done.9
  27.8 0.0 copy-start.6
  27.8 0.0 collective-permute-done
  27.8 4.8 %collective-permute-done.1 = f32[4,10,4,256]{3,2,1,0:T(4,128)S(1)} collective-permute-done((f32[4,10,4,256]{3,2,1,0:T(4,128)S(1)}, f32[4,10,4,256]{3,2,1,0:T(4,128)S(1)}, u32[]{:S(2)}, u32[]{:S(2)}) %collective-permute-start.1) | collective-permute-done | bytes 163872 | tf_op jit(solution)/shard_map/ppermute | solution.py:9
  32.6 0.0 collective-permute-done.2
  32.6 0.0 collective-permute-done.3
  32.6 0.1 pad_maximum_fusion.1
  32.8 0.1 fusion.54
  32.9 0.7 %multiply_reduce_fusion = (f32[2,10,4,256]{3,2,1,0:T(4,128)S(1)}, f32[2,10,4,4,256]{4,3,2,1,0:T(4,128)S(1)}, f32[2,10,4,4,256]{4,3,2,1,0:T(4,128)S(1)}) fusion(f32[2,10,4,4,256]{4,3,2,1,0:T(4,128)S(1)} %slice.191, f32[2,10,4,4,256]{4,3,2,1,0:T(4,128)S(1)} %slice.189, f32[2,10,4,4,256]{4,2,1,0,3:T(4,128)S(1)} %get-tuple-element.40, ...), kind=kLoop, calls=%fused_computation.56 | loop fusion | flops 552960 | bytes 2211840 | tf_op jit(solution)/shard_map/reduce_sum | solution.py:133
  33.6 0.0 copy-done.6
  33.7 1.8 %fusion = f32[40,2048]{1,0:T(8,128)S(1)} fusion(s32[1024]{0:T(1024)S(1)} %bitcast.161, bf16[20,1024]{1,0:T(8,128)(2,1)S(1)} %get-tuple-element.54, bf16[20,1024]{1,0:T(8,128)(2,1)S(1)} %get-tuple-element.53), kind=kOutput, calls=%fused_computation.1 | convolution fusion | flops 170033152 | bytes 413696 | tf_op jit(solution)/shard_map/dot_general | solution.py:39
  35.5 0.1 copy.57
  35.6 0.8 %copy.46 = f32[8,2,10,256]{3,1,2,0:T(2,128)} copy(f32[8,2,10,256]{3,0,2,1:T(8,128)S(1)} %fusion.36) | data formatting | bytes 327680 | tf_op jit(solution)/shard_map/transpose | solution.py:68
  36.4 6.6 %all-to-all-start = ((f32[8,2,10,256]{3,1,2,0:T(2,128)}), f32[8,2,10,256]{3,1,2,0:T(2,128)S(1)}, u32[]{:S(2)}, u32[]{:S(2)}) async-start(f32[8,2,10,256]{3,1,2,0:T(2,128)} %copy.46), calls=%async_computation | async-start | bytes 327680 | tf_op jit(solution)/shard_map/all_to_all | solution.py:69
  43.1 0.2 pad_maximum_fusion.2
  43.3 0.1 copy.52
  43.4 0.1 reduce-precision_convert_fusion.1
  43.6 3.4 %fusion.1 = f32[320,2048]{1,0:T(8,128)} fusion(s32[1024]{0:T(1024)S(1)} %bitcast.162, bf16[160,1024]{1,0:T(8,128)(2,1)S(1)} %get-tuple-element.39, bf16[160,1024]{1,0:T(8,128)(2,1)S(1)} %get-tuple-element.38), kind=kOutput, calls=%fused_computation.2 | convolution fusion | flops 1345585152 | bytes 3280896 | tf_op jit(solution)/shard_map/dot_general | solution.py:156
  46.9 2.8 %reshape.105 = f32[2,4,10,4,2048]{4,3,2,1,0:T(4,128)S(1)} reshape(f32[320,2048]{1,0:T(8,128)} %fusion.1) | data formatting | bytes 5242880 | tf_op jit(solution)/shard_map/reshape | solution.py:161
  49.7 0.0 copy-start.7
  49.7 3.9 %fusion.16 = (f32[4,10,2048]{2,0,1:T(4,128)}, f32[4,10,2048]{2,0,1:T(4,128)}, f32[4,10,2048]{2,0,1:T(4,128)}) fusion(f32[2,4,10,4,2048]{4,3,2,1,0:T(4,128)S(1)} %reshape.105, f32[4,10,2048]{2,0,1:T(4,128)} %param.23, f32[9,4,2048]{2,1,0:T(4,128)} %get-tuple-element.25, f32[9,4,2048]{2,1,0:T(4,128)} %get-tuple-element.48, ...), kind=kLoop, calls=%fused_computation.32 | loop fusion | flops 1556480 | bytes 5406720 | tf_op jit(solution)/shard_map/transpose | solution.py:173
  53.6 0.0 copy-done.7
  53.6 0.9 %fusion.29 = f32[4,10,2048]{2,0,1:T(4,128)} fusion(f32[10,4,2048]{2,1,0:T(4,128)S(1)} %copy-done.7, f32[2,4,10,4,2048]{4,3,2,1,0:T(4,128)S(1)} %reshape.105, f32[4,10,2048]{2,0,1:T(4,128)S(1)} %copy-done.1), kind=kLoop, calls=%fused_computation.48 | loop fusion | flops 327680 | bytes 1638400 | tf_op jit(solution)/shard_map/transpose | solution.py:173
  54.5 0.0 all-to-all-done
  54.5 0.6 %fusion.46 = f32[2,10,256]{2,0,1:T(2,128)} fusion(f32[8,2,10,256]{3,1,2,0:T(2,128)S(1)} %all-to-all-done), kind=kLoop, calls=%fused_computation.113 | loop fusion | flops 35840 | bytes 184320 | tf_op jit(solution)/shard_map/add | solution.py:72
  (34 shorter events, 0.8 us)
Async XLA Ops:
  0.6 2.0 %copy-start.1 = (f32[4,10,2048]{2,0,1:T(4,128)S(1)}, f32[4,10,2048]{2,0,1:T(4,128)}, u32[]{:S(2)}) copy-start(f32[4,10,2048]{2,0,1:T(4,128)} %param.13) | copy-start | bytes 983044
  0.6 2.0 %copy-start = (f32[4,10,2048]{2,0,1:T(4,128)S(1)}, f32[4,10,2048]{2,0,1:T(4,128)}, u32[]{:S(2)}) copy-start(f32[4,10,2048]{2,0,1:T(4,128)} %param.14) | copy-start | bytes 983044
  0.7 2.0 %copy-start.4 = (f32[4,10,2048]{2,0,1:T(4,128)S(1)}, f32[4,10,2048]{2,0,1:T(4,128)}, u32[]{:S(2)}) copy-start(f32[4,10,2048]{2,0,1:T(4,128)} %param.22) | copy-start | bytes 983044
  0.7 2.0 %copy-start.2 = (f32[4,10,2048]{2,0,1:T(4,128)S(1)}, f32[4,10,2048]{2,0,1:T(4,128)}, u32[]{:S(2)}) copy-start(f32[4,10,2048]{2,0,1:T(4,128)} %param.23) | copy-start | bytes 983044
  3.6 0.9 %copy-start.8 = (f32[20,2048]{1,0:T(8,128)S(1)}, f32[20,2048]{1,0:T(8,128)}, u32[]{:S(2)}) copy-start(f32[20,2048]{1,0:T(8,128)} %reshape.102) | copy-start | bytes 491524
  4.5 0.7 %copy-start.10 = (s32[4,256]{1,0:T(4,128)S(1)}, s32[4,256]{1,0:T(4,128)}, u32[]{:S(2)}) copy-start(s32[4,256]{1,0:T(4,128)} %param.20) | copy-start | bytes 12292
  7.4 0.7 %copy-start.11 = (f32[4,256]{1,0:T(4,128)S(1)}, f32[4,256]{1,0:T(4,128)}, u32[]{:S(2)}) copy-start(f32[4,256]{1,0:T(4,128)} %param.21) | copy-start | bytes 12292
  8.5 15.5 %copy-start.3 = (f32[4,10,2048]{2,0,1:T(4,128)S(1)}, f32[4,10,2048]{2,0,1:T(4,128)}, u32[]{:S(2)}) copy-start(f32[4,10,2048]{2,0,1:T(4,128)} %param.23) | copy-start | bytes 983044
  8.5 15.5 %copy-start.5 = (f32[4,10,2048]{2,0,1:T(4,128)S(1)}, f32[4,10,2048]{2,0,1:T(4,128)}, u32[]{:S(2)}) copy-start(f32[4,10,2048]{2,0,1:T(4,128)} %param.22) | copy-start | bytes 983044
  9.1 18.7 %collective-permute-start = (f32[4,10,4,256]{3,2,1,0:T(4,128)S(1)}, f32[4,10,4,256]{3,2,1,0:T(4,128)S(1)}, u32[]{:S(2)}, u32[]{:S(2)}) collective-permute-start(f32[4,10,4,256]{3,2,1,0:T(4,128)S(1)} %bitcast.155), channel_id=1, source_target_pairs={{0,32},{8,40},{16,48},{24,56},{32,0},{40,8},{48,16},{56,24},{64,96... | collective-permute-start | bytes 491528 | tf_op jit(solution)/shard_map/ppermute | solution.py:9
  13.7 18.9 %collective-permute-start.1 = (f32[4,10,4,256]{3,2,1,0:T(4,128)S(1)}, f32[4,10,4,256]{3,2,1,0:T(4,128)S(1)}, u32[]{:S(2)}, u32[]{:S(2)}) collective-permute-start(f32[4,10,4,256]{3,2,1,0:T(4,128)S(1)} %bitcast.156), channel_id=1, source_target_pairs={{0,64},{8,72},{16,80},{24,88},{32,96},{40,104},{48,112},{56,120},{... | collective-permute-start | bytes 491528 | tf_op jit(solution)/shard_map/ppermute | solution.py:9
  18.8 13.9 %collective-permute-start.2 = (f32[4,10,4,256]{3,2,1,0:T(4,128)S(1)}, f32[4,10,4,256]{3,2,1,0:T(4,128)S(1)}, u32[]{:S(2)}, u32[]{:S(2)}) collective-permute-start(f32[4,10,4,256]{3,2,1,0:T(4,128)S(1)} %bitcast.157), channel_id=1, source_target_pairs={{0,8},{8,0},{16,24},{24,16},{32,40},{40,32},{48,56},{56,48},{64,72... | collective-permute-start | bytes 491528 | tf_op jit(solution)/shard_map/ppermute | solution.py:9
  20.8 11.9 %collective-permute-start.3 = (f32[4,10,4,256]{3,2,1,0:T(4,128)S(1)}, f32[4,10,4,256]{3,2,1,0:T(4,128)S(1)}, u32[]{:S(2)}, u32[]{:S(2)}) collective-permute-start(f32[4,10,4,256]{3,2,1,0:T(4,128)S(1)} %bitcast.158), channel_id=1, source_target_pairs={{0,16},{8,24},{16,0},{24,8},{32,48},{40,56},{48,32},{56,40},{64,80... | collective-permute-start | bytes 491528 | tf_op jit(solution)/shard_map/ppermute | solution.py:9
  27.0 0.8 %copy-start.9 = (f32[4,2048]{1,0:T(4,128)S(1)}, f32[4,2048]{1,0:T(4,128)}, u32[]{:S(2)}) copy-start(f32[4,2048]{1,0:T(4,128)} %param.19) | copy-start | bytes 98308
  27.8 5.8 %copy-start.6 = (f32[10,4,2048]{2,1,0:T(4,128)}, f32[10,4,2048]{2,1,0:T(4,128)S(1)}, u32[]{:S(2)}) copy-start(f32[10,4,2048]{2,1,0:T(4,128)S(1)} %fusion.45) | copy-start | bytes 983044
  36.4 18.1 %all-to-all-start = ((f32[8,2,10,256]{3,1,2,0:T(2,128)}), f32[8,2,10,256]{3,1,2,0:T(2,128)S(1)}, u32[]{:S(2)}, u32[]{:S(2)}) async-start(f32[8,2,10,256]{3,1,2,0:T(2,128)} %copy.46), calls=%async_computation | async-start | bytes 327680 | tf_op jit(solution)/shard_map/all_to_all | solution.py:69
  49.7 3.9 %copy-start.7 = (f32[10,4,2048]{2,1,0:T(4,128)S(1)}, f32[10,4,2048]{2,1,0:T(4,128)}, u32[]{:S(2)}) copy-start(f32[10,4,2048]{2,1,0:T(4,128)} %copy-done.6) | copy-start | bytes 983044
